TPU v7x, 128 devices: a whole 4x4x4 slice. The times are simulated.
128 devices in a mesh: pair: 32 (over z, x, core), vgrp: 4 (over y).
Axes of the slice: x: 4, y: 4, z: 4, core: 2. Of those that a mesh axis runs over, the one named last changes fastest.
Arguments:
- amplitudes: bfloat16 [64, 768, 768], P('pair'), may hold values from -6 to 6
- cholesky_vectors: bfloat16 [4, 32, 768, 768], P('vgrp', 'pair'), may hold values from -0.21875 to 0.21875
- owner_order: int32 [4, 4], replicated, may hold values from 0 to 31, as said below
Outputs:
- residual: float32 [64, 768, 768], P('pair', 'vgrp')
Inputs may be any that keep to these rules, and one draw needn't show every extreme that they name: `owner_order`: within one row the 4 entries are distinct; in every draw some row names both 0 and 31.
All inputs are finite; a program needn't handle non-finite values.
Results may differ from a plain program's by a relative error of at most 0.0029.
Values may be sent and summed in bfloat16 or wider, within the bound.
No kernel may reach another device: no remote copies, remote signals or barrier semaphores. Data moves between devices by JAX's collectives and lax.ppermute only.
A program may use at most 64 MiB of HBM per device.

v0:
```python
import jax
import jax.numpy as jnp
from jax import lax
from jax.sharding import PartitionSpec as P


def spread(block, axis, source):
    block = jnp.where(lax.axis_index(axis) == source, block, jnp.zeros_like(block))
    return lax.psum(block, axis)


def on_device(amplitudes, cholesky_vectors, owner_order):
    vgrp_index = lax.axis_index("vgrp")
    owned_slots = lax.dynamic_index_in_dim(owner_order, vgrp_index, 0, keepdims=False)
    own_vector = cholesky_vectors[0, 0]
    slot_count = owned_slots.shape[0]
    accumulated = jnp.zeros(amplitudes.shape, jnp.float32)
    for slot in range(slot_count):
        vector = spread(own_vector, "pair", owned_slots[slot])
        half_product = jnp.einsum(
            "ac,pcd->pad", vector, amplitudes, preferred_element_type=jnp.float32
        ).astype(jnp.bfloat16)
        accumulated = accumulated + jnp.einsum(
            "pad,bd->pab", half_product, vector, preferred_element_type=jnp.float32
        )
    return lax.psum_scatter(accumulated, "vgrp", scatter_dimension=1, tiled=True)


def solution(mesh):
    placed = (P("pair", None, None), P("vgrp", "pair", None, None), P())
    return jax.shard_map(
        on_device, mesh=mesh, in_specs=placed, out_specs=P("pair", "vgrp", None), check_vma=False
    )
```

profile of v0, /device:TPU:1, one launch (start us, length us, event | category | flops | bytes accessed | tf_op | source)
XLA Modules:
  0.0 218.5 jit_solution(8663369854278851356)
XLA Ops:
  6.5 0.0 copy-start
  6.5 0.0 all-reduce.3.cloned.1.call-start
  6.5 0.8 constant_dynamic-slice_fusion
  7.4 0.7 fusion.42
  10.6 3.6 %select_bitcast_fusion.3 = (bf16[768,768]{1,0:T(8,128)(2,1)}, bf16[768,768]{1,0:T(8,128)(2,1)}, bf16[768,768]{1,0:T(8,128)(2,1)}, bf16[768,768]{1,0:T(8,128)(2,1)}) fusion(bf16[1,1,768,768]{3,2,1,0:T(8,128)(2,1)} %param.4, pred[]{:T(512)S(6)} %eq.12, pred[]{:T(512)S(6)} %eq.13, pred[]{:T(512)S(6)} %eq.15, pred[]{:T(512)S(6)} %eq.14), kind=kLoop, calls=%fused_computation.28 | loop fusion | flops 2359296 | bytes 5898244 | tf_op jit(solution)/shard_map/jit(_where)/select_n | solution.py:8
  14.1 0.0 all-reduce.3.cloned.1.call-update
  14.1 0.0 reduce-scatter.2.cloned.1.call-start
  14.2 116.3 %all-reduce.3.cloned.1.call-done = (bf16[768,768]{1,0:T(8,128)(2,1)}, bf16[768,768]{1,0:T(8,128)(2,1)}, bf16[768,768]{1,0:T(8,128)(2,1)}, bf16[768,768]{1,0:T(8,128)(2,1)}) async-done(((bf16[768,768]{1,0:T(8,128)(2,1)}, bf16[768,768]{1,0:T(8,128)(2,1)}, bf16[768,768]{1,0:T(8,128)(2,1)}, bf16[768,768]{1,0:T(8,128)(2,1)}), (bf16[768,768]{1,0:T(8,128)(2,1)}, bf16[768,768]{1,0:T(8,128)(2,1)}, ...) | async-done | bytes 4718608 | tf_op jit(solution)/shard_map/psum | solution.py:9
  130.5 0.0 copy-done
  130.5 0.0 copy-start.2
  130.5 7.7 %fusion = f32[2,768,768]{2,1,0:T(8,128)} fusion(bf16[768,768]{1,0:T(8,128)(2,1)} %get-tuple-element.5, bf16[2,768,768]{2,1,0:T(8,128)(2,1)S(1)} %copy-done), kind=kOutput, calls=%fused_computation.1 | convolution fusion | flops 3625058304 | bytes 8257536 | tf_op jit(solution)/shard_map/pad,bd->pab/dot_general | solution.py:23
  138.2 0.0 copy-done.2
  138.2 6.0 %fusion.2 = f32[2,768,768]{2,1,0:T(8,128)} fusion(bf16[768,768]{1,0:T(8,128)(2,1)S(1)} %copy-done.2, bf16[2,768,768]{2,1,0:T(8,128)(2,1)S(1)} %copy-done), kind=kOutput, calls=%fused_computation.3 | convolution fusion | flops 3625058304 | bytes 8257536 | tf_op jit(solution)/shard_map/pad,bd->pab/dot_general | solution.py:23
  144.2 0.0 copy-start.1
  144.2 7.8 %fusion.4 = f32[2,768,768]{2,1,0:T(8,128)} fusion(bf16[768,768]{1,0:T(8,128)(2,1)} %get-tuple-element.7, bf16[2,768,768]{2,1,0:T(8,128)(2,1)S(1)} %copy-done), kind=kOutput, calls=%fused_computation.5 | convolution fusion | flops 3625058304 | bytes 8257536 | tf_op jit(solution)/shard_map/pad,bd->pab/dot_general | solution.py:23
  152.0 0.0 copy-done.1
  152.0 8.8 %add_add_fusion = f32[2,768,768]{2,1,0:T(8,128)} fusion(f32[2,768,768]{2,1,0:T(8,128)} %fusion, f32[2,768,768]{2,1,0:T(8,128)} %fusion.2, f32[2,768,768]{2,1,0:T(8,128)} %fusion.4, bf16[768,768]{1,0:T(8,128)(2,1)S(1)} %copy-done.1, bf16[2,768,768]{2,1,0:T(8,128)(2,1)S(1)} %copy-done), kind=kOutput, calls=%fused_computation | convolution fusion | flops 3628597248 | bytes 22413312 | tf_op jit(solution)/shard_map/pad,bd->pab/dot_general | solution.py:23
  160.8 0.0 reduce-scatter.2.cloned.1.call-update
  160.8 50.8 %reduce-scatter.2.cloned.1.call-done = f32[2,192,768]{2,1,0:T(8,128)} async-done(((f32[2,768,768]{2,1,0:T(8,128)}), f32[2,192,768]{2,1,0:T(8,128)}) %reduce-scatter.2.cloned.1.call-update) | async-done | bytes 1179664 | tf_op jit(solution)/shard_map/reduce_scatter | solution.py:26
Async XLA Ops:
  6.5 123.9 %copy-start = (bf16[2,768,768]{2,1,0:T(8,128)(2,1)S(1)}, bf16[2,768,768]{2,1,0:T(8,128)(2,1)}, u32[]{:S(2)}) copy-start(bf16[2,768,768]{2,1,0:T(8,128)(2,1)} %param.3) | copy-start | bytes 7077892
  6.5 123.9 %all-reduce.3.cloned.1.call-start = ((), (), s32[]{:S(2)}) async-start(), calls=%async_computation.2 | async-start | bytes 9437184 | tf_op jit(solution)/shard_map/psum | solution.py:9
  14.1 197.5 %reduce-scatter.2.cloned.1.call-start = ((), (), s32[]{:S(2)}) async-start(), calls=%async_computation.1 | async-start | bytes 5898240 | tf_op jit(solution)/shard_map/reduce_scatter | solution.py:26
  130.5 7.7 %copy-start.2 = (bf16[768,768]{1,0:T(8,128)(2,1)S(1)}, bf16[768,768]{1,0:T(8,128)(2,1)}, u32[]{:S(2)}) copy-start(bf16[768,768]{1,0:T(8,128)(2,1)} %get-tuple-element.6) | copy-start | bytes 3538948
  144.2 7.8 %copy-start.1 = (bf16[768,768]{1,0:T(8,128)(2,1)S(1)}, bf16[768,768]{1,0:T(8,128)(2,1)}, u32[]{:S(2)}) copy-start(bf16[768,768]{1,0:T(8,128)(2,1)} %get-tuple-element.8) | copy-start | bytes 3538948
Sparse Core Ops, SparseCore 0:
  14.3 116.1 all-reduce.2
  160.9 50.6 reduce-scatter.1
where the time goes:
time: 219 us; the launch traced here: 218 us
  waiting for transfers between devices  167 us (76%)
  matrix products  30.3 us (14%)
  between operations  15.9 us (7%)
  other arithmetic  3.55 us (2%)
    psum x1, waiting for transfers between devices, spread(): return lax.psum(block, axis)  116 us
    reduce_scatter x1, waiting for transfers between devices, on_device(): lax.psum_scatter(accumulated, 'vgrp', scatter_dimension=1, tiled=True)  50.8 us
    dot_general x4, matrix products, on_device(): jnp.einsum('pad,bd->pab', half_product, vector, preferred_element_type=jn...  30.3 us
  transfers between devices with their start and end apart: 2, of which 2 were waited for; matrix products, arithmetic and copies ran while one was open for 0% of the time, Pallas kernels for 0%

commit v1 on v0

v1 whole, which is shorter than its diff:
```python
import jax
import jax.numpy as jnp
from jax import lax
from jax.sharding import Mesh
from jax.sharding import PartitionSpec as P

PAIR = ("z", "x", "core")
CHIPS = ("z", "x")


def gather_slots(own_vector, owned_slots):
    rows, cols = own_vector.shape
    devices = lax.psum(1, PAIR)
    cores = lax.psum(1, "core")
    piece = rows // devices
    pieces = own_vector.reshape(devices, piece, cols)
    pieces = lax.all_to_all(pieces, PAIR, 0, 0, tiled=True)
    picked = jnp.take(pieces, owned_slots, axis=0)
    mine = lax.all_gather(picked, CHIPS, axis=0, tiled=False)
    core = lax.axis_index("core")
    other = lax.ppermute(mine, "core", [(0, 1), (1, 0)])
    low = jnp.where(core == 0, mine, other)
    high = jnp.where(core == 0, other, mine)
    full = jnp.stack([low, high], axis=1)
    slots = owned_slots.shape[0]
    full = jnp.transpose(full, (2, 0, 1, 3, 4))
    return full.reshape(slots, rows, cols)


def on_device(amplitudes, cholesky_vectors, owner_order):
    vgrp_index = lax.axis_index("vgrp")
    owned_slots = lax.dynamic_index_in_dim(owner_order, vgrp_index, 0, keepdims=False)
    vectors = gather_slots(cholesky_vectors[0, 0], owned_slots)
    accumulated = jnp.zeros(amplitudes.shape, jnp.float32)
    for slot in range(owned_slots.shape[0]):
        vector = vectors[slot]
        half_product = jnp.einsum(
            "ac,pcd->pad", vector, amplitudes, preferred_element_type=jnp.float32
        ).astype(jnp.bfloat16)
        accumulated = accumulated + jnp.einsum(
            "pad,bd->pab", half_product, vector, preferred_element_type=jnp.float32
        )
    return lax.psum_scatter(accumulated, "vgrp", scatter_dimension=1, tiled=True)


def solution(mesh):
    pair, vgrp = mesh.devices.shape
    cores = 2
    chips = pair // cores
    side = int(round(chips ** 0.5))
    devices = mesh.devices.reshape(chips // side, side, cores, vgrp)
    fine = Mesh(devices, ("z", "x", "core", "vgrp"))
    placed = (P(PAIR, None, None), P("vgrp", PAIR, None, None), P())
    return jax.shard_map(
        on_device, mesh=fine, in_specs=placed, out_specs=P(PAIR, "vgrp", None), check_vma=False
    )
```

time: 219 us -> 180 us (0.82)
  waiting for transfers between devices: 167 us -> 115 us
  starting transfers between devices: 0.04 us -> 11.8 us
  between operations: 15.9 us -> 13.5 us
    psum x1 -> x0, waiting for transfers between devices: 116 us -> none  [spread(): return lax.psum(block, axis)]
    all_gather x0 -> x1, waiting for transfers between devices: none -> 41.8 us  [gather_slots(): mine = lax.all_gather(picked, CHIPS, axis=0, tiled=False)]
    all_to_all x0 -> x1, waiting for transfers between devices: none -> 18.4 us  [gather_slots(): pieces = lax.all_to_all(pieces, PAIR, 0, 0, tiled=True)]
    all_to_all x0 -> x1, starting transfers between devices: none -> 9.55 us  [gather_slots(): pieces = lax.all_to_all(pieces, PAIR, 0, 0, tiled=True)]
    ppermute x0 -> x1, waiting for transfers between devices: none -> 4.5 us  [gather_slots(): other = lax.ppermute(mine, 'core', [(0, 1), (1, 0)])]
    another operation x0 -> x1, other arithmetic: none -> 2.68 us  [gather_slots(): full = jnp.stack([low, high], axis=1)]
  transfers between devices with their start and end apart: 2 -> 4, of which waited for: 2 -> 4; matrix products, arithmetic and copies ran while one was open for 0% -> 0% of each run, Pallas kernels for 0% -> 0%
where the time goes in v1:
time: 180 us
  waiting for transfers between devices  115 us (64%)
  matrix products  31.8 us (18%)
  between operations  13.5 us (8%)
  starting transfers between devices  11.8 us (7%)
  other arithmetic  4.77 us (3%)
  local copies, waits for them, and re-layouts  3.11 us (2%)
    reduce_scatter x1, waiting for transfers between devices, on_device(): lax.psum_scatter(accumulated, 'vgrp', scatter_dimension=1, tiled=True)  50.1 us
    all_gather x1, waiting for transfers between devices, gather_slots(): mine = lax.all_gather(picked, CHIPS, axis=0, tiled=False)  41.8 us
    dot_general x4, matrix products, on_device(): jnp.einsum('pad,bd->pab', half_product, vector, preferred_element_type=jn...  31.8 us
    all_to_all x1, waiting for transfers between devices, gather_slots(): pieces = lax.all_to_all(pieces, PAIR, 0, 0, tiled=True)  18.4 us
    all_to_all x1, starting transfers between devices, gather_slots(): pieces = lax.all_to_all(pieces, PAIR, 0, 0, tiled=True)  9.55 us
    ppermute x1, waiting for transfers between devices, gather_slots(): other = lax.ppermute(mine, 'core', [(0, 1), (1, 0)])  4.5 us
  transfers between devices with their start and end apart: 4, of which 4 were waited for; matrix products, arithmetic and copies ran while one was open for 0% of the time, Pallas kernels for 0%

profile of v1, /device:TPU:1, one launch (start us, length us, event | category | flops | bytes accessed | tf_op | source)
XLA Modules:
  0.0 179.7 jit_solution(6533274493731231810)
XLA Ops:
  6.5 0.0 copy-start
  6.5 0.0 copy-start.1
  6.5 9.6 %all-to-all-start = ((bf16[32,24,768]{2,1,0:T(8,128)(2,1)}), bf16[32,24,768]{2,1,0:T(8,128)(2,1)S(1)}, u32[]{:S(2)}, u32[]{:S(2)}) async-start(bf16[32,24,768]{2,1,0:T(8,128)(2,1)} %bitcast.59), calls=%async_computation | async-start | bytes 2359296 | tf_op jit(solution)/shard_map/all_to_all | solution.py:17
  16.1 0.0 all-gather.2.cloned.1.call-start
  16.2 0.0 copy-done.1
  16.2 18.4 %all-to-all-done = bf16[32,24,768]{2,1,0:T(8,128)(2,1)S(1)} async-done(((bf16[32,24,768]{2,1,0:T(8,128)(2,1)}), bf16[32,24,768]{2,1,0:T(8,128)(2,1)S(1)}, u32[]{:S(2)}, u32[]{:S(2)}) %all-to-all-start) | async-done | bytes 1179680 | tf_op jit(solution)/shard_map/all_to_all | solution.py:17
  34.6 1.2 gather_fusion
  35.8 1.7 bitcast_select_fusion
  37.5 0.0 all-gather.2.cloned.1.call-update
  37.5 0.0 reduce-scatter.2.cloned.1.call-start
  37.6 41.8 %all-gather.2.cloned.1.call-done = bf16[16,4,24,768]{3,2,0,1:T(8,128)(2,1)} async-done(((bf16[1,4,24,768]{3,2,0,1:T(8,128)(2,1)}), bf16[16,4,24,768]{3,2,0,1:T(8,128)(2,1)}) %all-gather.2.cloned.1.call-update) | async-done | bytes 2359312 | tf_op jit(solution)/shard_map/all_gather | solution.py:19
  79.3 2.1 %collective-permute-start = (bf16[16,4,24,768]{3,2,0,1:T(8,128)(2,1)}, bf16[16,4,24,768]{3,2,0,1:T(8,128)(2,1)}, u32[]{:S(2)}, u32[]{:S(2)}) collective-permute-start(bf16[16,4,24,768]{3,2,0,1:T(8,128)(2,1)} %all-gather.2.cloned.1.call-done), channel_id=1, source_target_pairs={{0,4},{4,0},{1,5},{5,1},{2,6},{6,2},{3,7},{7,3},{8,12},{12,8},{9,1... | collective-permute-start | bytes 7077896 | tf_op jit(solution)/shard_map/ppermute | solution.py:21
  81.4 4.5 %collective-permute-done = bf16[16,4,24,768]{3,2,0,1:T(8,128)(2,1)} collective-permute-done((bf16[16,4,24,768]{3,2,0,1:T(8,128)(2,1)}, bf16[16,4,24,768]{3,2,0,1:T(8,128)(2,1)}, u32[]{:S(2)}, u32[]{:S(2)}) %collective-permute-start) | collective-permute-done | bytes 2359328 | tf_op jit(solution)/shard_map/ppermute | solution.py:21
  86.0 2.7 %select_bitcast_fusion.1 = (bf16[16,1,4,24,768]{4,3,1,0,2:T(8,128)(2,1)S(1)}, bf16[16,1,4,24,768]{4,3,1,0,2:T(8,128)(2,1)S(1)}) fusion(bf16[16,4,24,768]{3,2,0,1:T(8,128)(2,1)} %all-gather.2.cloned.1.call-done, bf16[16,4,24,768]{3,2,0,1:T(8,128)(2,1)} %collective-permute-done, pred[]{:T(512)S(6)} %eq.4), kind=kLoop, calls=%fused_computation.16 | loop fusion | flops 2359296 | bytes 9437185 | tf_op jit(solution)/shard_map/stack | solution.py:24
  88.6 0.4 maximum_bitcast_fusion
  89.1 1.9 %fusion.23 = (bf16[1,16,2,24,768]{4,3,2,1,0:T(8,128)(2,1)S(1)}, bf16[1,16,2,24,768]{4,3,2,1,0:T(8,128)(2,1)}, bf16[1,16,2,24,768]{4,3,2,1,0:T(8,128)(2,1)}, bf16[1,16,2,24,768]{4,3,2,1,0:T(8,128)(2,1)}) fusion(bf16[4,16,2,24,768]{4,3,2,1,0:T(8,128)(2,1)S(1)} %maximum_bitcast_fusion), kind=kLoop, calls=%fused_computation.28 | loop fusion | bytes 9437184 | tf_op jit(solution)/shard_map/slice | solution.py:36
  90.9 0.0 copy-done
  90.9 7.7 %fusion.2 = f32[2,768,768]{2,1,0:T(8,128)} fusion(bf16[768,768,1]{1,0,2:T(8,128)(2,1)} %bitcast.58, bf16[2,768,768]{2,1,0:T(8,128)(2,1)S(1)} %copy-done), kind=kOutput, calls=%fused_computation.5 | convolution fusion | flops 3625058304 | bytes 8257536 | tf_op jit(solution)/shard_map/pad,bd->pab/dot_general | solution.py:40
  98.6 7.6 %fusion.4 = f32[2,768,768]{2,1,0:T(8,128)} fusion(bf16[768,768,1]{1,0,2:T(8,128)(2,1)} %bitcast.57, bf16[2,768,768]{2,1,0:T(8,128)(2,1)S(1)} %copy-done), kind=kOutput, calls=%fused_computation.7 | convolution fusion | flops 3625058304 | bytes 8257536 | tf_op jit(solution)/shard_map/pad,bd->pab/dot_general | solution.py:40
  106.2 7.7 %fusion.6 = f32[2,768,768]{2,1,0:T(8,128)} fusion(bf16[768,768,1]{1,0,2:T(8,128)(2,1)} %bitcast.56, bf16[2,768,768]{2,1,0:T(8,128)(2,1)S(1)} %copy-done), kind=kOutput, calls=%fused_computation.9 | convolution fusion | flops 3625058304 | bytes 8257536 | tf_op jit(solution)/shard_map/pad,bd->pab/dot_general | solution.py:40
  113.9 8.8 %add_add_fusion = f32[2,768,768]{2,1,0:T(8,128)} fusion(f32[2,768,768]{2,1,0:T(8,128)} %fusion.2, f32[2,768,768]{2,1,0:T(8,128)} %fusion.6, f32[2,768,768]{2,1,0:T(8,128)} %fusion.4, bf16[768,768,1]{1,0,2:T(8,128)(2,1)S(1)} %bitcast.55, bf16[2,768,768]{2,1,0:T(8,128)(2,1)S(1)} %copy-done), kind=kOutput, calls=%fused_computation.2 | convolution fusion | flops 3628597248 | bytes 22413312 | tf_op jit(solution)/shard_map/pad,bd->pab/dot_general | solution.py:40
  122.8 0.0 reduce-scatter.2.cloned.1.call-update
  122.8 50.1 %reduce-scatter.2.cloned.1.call-done = f32[2,192,768]{2,1,0:T(8,128)} async-done(((f32[2,768,768]{2,1,0:T(8,128)}), f32[2,192,768]{2,1,0:T(8,128)}) %reduce-scatter.2.cloned.1.call-update) | async-done | bytes 1179664 | tf_op jit(solution)/shard_map/reduce_scatter | solution.py:43
  (3 shorter events, 0.0 us)
Async XLA Ops:
  6.5 84.4 %copy-start = (bf16[2,768,768]{2,1,0:T(8,128)(2,1)S(1)}, bf16[2,768,768]{2,1,0:T(8,128)(2,1)}, u32[]{:S(2)}) copy-start(bf16[2,768,768]{2,1,0:T(8,128)(2,1)} %param.3) | copy-start | bytes 7077892
  6.5 9.6 %copy-start.1 = (s32[4,4]{1,0:T(4,128)S(1)}, s32[4,4]{1,0:T(4,128)}, u32[]{:S(2)}) copy-start(s32[4,4]{1,0:T(4,128)} %param.5) | copy-start | bytes 196
  6.5 28.1 %all-to-all-start = ((bf16[32,24,768]{2,1,0:T(8,128)(2,1)}), bf16[32,24,768]{2,1,0:T(8,128)(2,1)S(1)}, u32[]{:S(2)}, u32[]{:S(2)}) async-start(bf16[32,24,768]{2,1,0:T(8,128)(2,1)} %bitcast.59), calls=%async_computation | async-start | bytes 2359296 | tf_op jit(solution)/shard_map/all_to_all | solution.py:17
  16.1 63.2 %all-gather.2.cloned.1.call-start = ((), (), s32[]{:S(2)}) async-start(), calls=%async_computation.2 | async-start | bytes 2506752 | tf_op jit(solution)/shard_map/all_gather | solution.py:19
  37.5 135.4 %reduce-scatter.2.cloned.1.call-start = ((), (), s32[]{:S(2)}) async-start(), calls=%async_computation.3 | async-start | bytes 5898240 | tf_op jit(solution)/shard_map/reduce_scatter | solution.py:43
  79.3 6.6 %collective-permute-start = (bf16[16,4,24,768]{3,2,0,1:T(8,128)(2,1)}, bf16[16,4,24,768]{3,2,0,1:T(8,128)(2,1)}, u32[]{:S(2)}, u32[]{:S(2)}) collective-permute-start(bf16[16,4,24,768]{3,2,0,1:T(8,128)(2,1)} %all-gather.2.cloned.1.call-done), channel_id=1, source_target_pairs={{0,4},{4,0},{1,5},{5,1},{2,6},{6,2},{3,7},{7,3},{8,12},{12,8},{9,1... | collective-permute-start | bytes 7077896 | tf_op jit(solution)/shard_map/ppermute | solution.py:21
Sparse Core Ops, SparseCore 0:
  37.6 41.6 all-gather.1
  122.9 49.9 reduce-scatter.1

commit v2 on v1

v2 whole, which is shorter than its diff:
```python
import jax
import jax.numpy as jnp
from jax import lax
from jax.sharding import Mesh
from jax.sharding import PartitionSpec as P

PAIR = ("z", "x", "core")
CHIPS = ("z", "x")
RING = 4


def ring_axis(stage, core):
    return "x" if (stage == 1) == (core == 0) else "z"


def ring_perm(sizes, stage, step):
    nz, nx, nc = sizes
    perm = []
    for z in range(nz):
        for x in range(nx):
            for c in range(nc):
                if ring_axis(stage, c) == "x":
                    dz, dx = z, (x + step) % nx
                else:
                    dz, dx = (z + step) % nz, x
                perm.append(((z * nx + x) * nc + c, (dz * nx + dx) * nc + c))
    return perm


def ring_gather(piece, sizes, stage):
    half = piece.shape[0] // 2
    from_prev = lax.ppermute(piece, PAIR, ring_perm(sizes, stage, 1))
    from_next = lax.ppermute(piece, PAIR, ring_perm(sizes, stage, -1))
    far_low = lax.ppermute(from_prev[:half], PAIR, ring_perm(sizes, stage, 1))
    far_high = lax.ppermute(from_next[half:], PAIR, ring_perm(sizes, stage, -1))
    far = jnp.concatenate([far_low, far_high], axis=0)
    return jnp.stack([piece, from_next, far, from_prev], axis=0)


def gather_slots(own_vector, owned_slots, sizes):
    nz, nx, nc = sizes
    rows, cols = own_vector.shape
    devices = nz * nx * nc
    piece = rows // devices
    slots = owned_slots.shape[0]
    pieces = own_vector.reshape(devices, piece, cols)
    pieces = lax.all_to_all(pieces, PAIR, 0, 0, tiled=True)
    picked = jnp.take(pieces, owned_slots, axis=0)
    first = ring_gather(picked, sizes, 1)
    both = ring_gather(first, sizes, 2)
    swap = [(q, q ^ 1) for q in range(devices)]
    other = lax.ppermute(both, PAIR, swap)
    chips = nz * nx
    stacked = jnp.concatenate(
        [both.reshape((chips,) + both.shape[2:]), other.reshape((chips,) + both.shape[2:])], axis=0
    )
    z = lax.axis_index("z")
    x = lax.axis_index("x")
    core = lax.axis_index("core")
    q = jnp.arange(devices, dtype=jnp.int32)
    zq, xq, cq = q // (nx * nc), (q // nc) % nx, q % nc
    dz, dx = (zq - z) % nz, (xq - x) % nx
    inner = jnp.where(cq == 0, dz * nx + dx, dx * nz + dz)
    index = jnp.where(cq == core, 0, chips) + inner
    ordered = jnp.take(stacked, index, axis=0)
    ordered = jnp.transpose(ordered, (0, 2, 1, 3))
    return ordered.reshape(rows, slots, cols)


def on_device(amplitudes, cholesky_vectors, owner_order, sizes):
    vgrp = lax.axis_index("vgrp")
    groups = lax.psum(1, "vgrp")
    owned_slots = lax.dynamic_index_in_dim(owner_order, vgrp, 0, keepdims=False)
    vectors = gather_slots(cholesky_vectors[0, 0], owned_slots, sizes)
    rows, slots, cols = vectors.shape
    block = rows // groups
    flat = vectors.reshape(rows, slots * cols)

    def partial(pair, index):
        start = pl_multiple(index * block)
        mine = lax.dynamic_slice_in_dim(flat, start, block, axis=0)
        half = jnp.dot(
            mine.reshape(block * slots, cols), amplitudes[pair], preferred_element_type=jnp.float32
        ).astype(jnp.bfloat16)
        return lax.dot_general(
            half.reshape(block, slots * cols), flat, (((1,), (1,)), ((), ())),
            preferred_element_type=jnp.float32,
        )

    outs = []
    arrived = [None, None]
    directions = (1, -1)
    for step in range(RING):
        sums = []
        for pair, direction in enumerate(directions):
            index = (vgrp - direction * (1 + step)) % groups
            total = partial(pair, index)
            if arrived[pair] is not None:
                total = total + arrived[pair].astype(jnp.float32)
            sums.append(total)
        if step < RING - 1:
            for pair, direction in enumerate(directions):
                shift = [(g, (g + direction) % RING) for g in range(RING)]
                arrived[pair] = lax.ppermute(sums[pair].astype(jnp.bfloat16), "vgrp", shift)
        else:
            outs = sums
    return jnp.stack(outs, axis=0)


def pl_multiple(value):
    return value


def solution(mesh):
    pair, vgrp = mesh.devices.shape
    cores = 2
    chips = pair // cores
    side = RING
    assert chips == side * side and vgrp == RING
    devices = mesh.devices.reshape(chips // side, side, cores, vgrp)
    fine = Mesh(devices, ("z", "x", "core", "vgrp"))
    sizes = (chips // side, side, cores)
    placed = (P(PAIR, None, None), P("vgrp", PAIR, None, None), P())

    def body(amplitudes, cholesky_vectors, owner_order):
        return on_device(amplitudes, cholesky_vectors, owner_order, sizes)

    return jax.shard_map(
        body, mesh=fine, in_specs=placed, out_specs=P(PAIR, "vgrp", None), check_vma=False
    )
```

time: 180 us -> 208 us (1.16); the launches traced: 180 us -> 205 us
  waiting for transfers between devices: 115 us -> 48.3 us
  local copies, waits for them, and re-layouts: 3.11 us -> 52.9 us
  matrix products: 31.8 us -> 61.9 us
  starting transfers between devices: 11.8 us -> 30.3 us
  between operations: 13.5 us -> 0.36 us
  other arithmetic: 4.77 us -> 11 us
    reduce_scatter x1 -> x0, waiting for transfers between devices: 50.1 us -> none  [on_device(): lax.psum_scatter(accumulated, 'vgrp', scatter_dimension=1, tiled=True)]
    all_gather x1 -> x0, waiting for transfers between devices: 41.8 us -> none  [gather_slots(): mine = lax.all_gather(picked, CHIPS, axis=0, tiled=False)]
    reshape x0 -> x16, local copies, waits for them, and re-layouts: none -> 39.6 us  [the longest x8 20.2 us: partial(): half.reshape(block, slots * cols)]
    dot_general x4 -> x16, matrix products: 31.8 us -> 61.9 us  [the longest x8 35.9 us: partial(): lax.dot_general(half.reshape(block, slots * cols), flat, (((1,), (1,)), (...]
    ppermute x1 -> x15, waiting for transfers between devices: 4.5 us -> 29.8 us  [the longest x2 7.56 us: ring_gather(): from_next = lax.ppermute(piece, PAIR, ring_perm(sizes, stage, -1))]
    ppermute x1 -> x15, starting transfers between devices: 2.12 us -> 20.8 us  [the longest x6 6.94 us: on_device(): arrived[pair] = lax.ppermute(sums[pair].astype(jnp.bfloat16), 'vgrp', shift)]
    gather x0 -> x1, local copies, waits for them, and re-layouts: none -> 5.36 us  [gather_slots(): ordered = jnp.take(stacked, index, axis=0)]
    concatenate x0 -> x1, other arithmetic: none -> 4.23 us  [gather_slots(): jnp.concatenate([both.reshape((chips,) + both.shape[2:]), other.reshape((...]
  transfers between devices with their start and end apart: 4 -> 16, of which waited for: 4 -> 10; matrix products, arithmetic and copies ran while one was open for 0% -> 43% of each run, Pallas kernels for 0% -> 0%
where the time goes in v2:
time: 208 us; the launch traced here: 205 us
  matrix products  61.9 us (30%)
  local copies, waits for them, and re-layouts  52.9 us (25%)
  waiting for transfers between devices  48.3 us (23%)
  starting transfers between devices  30.3 us (15%)
  other arithmetic  11 us (5%)
    dot_general x8, matrix products, partial(): lax.dot_general(half.reshape(block, slots * cols), flat, (((1,), (1,)), (...  35.9 us
    dot_general x8, matrix products, partial(): jnp.dot(mine.reshape(block * slots, cols), amplitudes[pair], preferred_el...  26 us
    reshape x8, local copies, waits for them, and re-layouts, partial(): half.reshape(block, slots * cols)  20.2 us
    reshape x8, local copies, waits for them, and re-layouts, partial(): mine.reshape(block * slots, cols)  19.4 us
    all_to_all x1, waiting for transfers between devices, gather_slots(): pieces = lax.all_to_all(pieces, PAIR, 0, 0, tiled=True)  18.5 us
    all_to_all x1, starting transfers between devices, gather_slots(): pieces = lax.all_to_all(pieces, PAIR, 0, 0, tiled=True)  9.55 us
    ppermute x2, waiting for transfers between devices, ring_gather(): from_next = lax.ppermute(piece, PAIR, ring_perm(sizes, stage, -1))  7.56 us
    ppermute x6, starting transfers between devices, on_device(): arrived[pair] = lax.ppermute(sums[pair].astype(jnp.bfloat16), 'vgrp', shift)  6.94 us
  transfers between devices with their start and end apart: 16, of which 10 were waited for; matrix products, arithmetic and copies ran while one was open for 43% of the time, Pallas kernels for 0%

profile of v2, /device:TPU:1, one launch (start us, length us, event | category | flops | bytes accessed | tf_op | source)
XLA Modules:
  0.0 204.8 jit_solution(7686084874262000163)
XLA Ops:
  0.0 9.6 %all-to-all-start = ((bf16[32,24,768]{2,1,0:T(8,128)(2,1)}), bf16[32,24,768]{2,1,0:T(8,128)(2,1)S(1)}, u32[]{:S(2)}, u32[]{:S(2)}) async-start(bf16[32,24,768]{2,1,0:T(8,128)(2,1)} %bitcast.89), calls=%async_computation | async-start | bytes 2359296 | tf_op jit(solution)/shard_map/all_to_all | solution.py:47
  9.6 18.5 %all-to-all-done = bf16[32,24,768]{2,1,0:T(8,128)(2,1)S(1)} async-done(((bf16[32,24,768]{2,1,0:T(8,128)(2,1)}), bf16[32,24,768]{2,1,0:T(8,128)(2,1)S(1)}, u32[]{:S(2)}, u32[]{:S(2)}) %all-to-all-start) | async-done | bytes 1179680 | tf_op jit(solution)/shard_map/all_to_all | solution.py:47
  40.4 7.6 %collective-permute-done.4 = bf16[4,4,24,768]{3,2,1,0:T(8,128)(2,1)S(1)} collective-permute-done((bf16[4,4,24,768]{3,2,1,0:T(8,128)(2,1)S(1)}, bf16[4,4,24,768]{3,2,1,0:T(8,128)(2,1)S(1)}, u32[]{:S(2)}, u32[]{:S(2)}) %collective-permute-start.4) | collective-permute-done | bytes 589856 | tf_op jit(solution)/shard_map/ppermute | solution.py:33
  50.4 3.6 %collective-permute-done.7 = bf16[2,4,24,768]{3,2,1,0:T(8,128)(2,1)S(1)} collective-permute-done((bf16[2,4,24,768]{3,2,1,0:T(8,128)(2,1)S(1)}, bf16[2,4,24,768]{3,2,1,0:T(8,128)(2,1)S(1)}, u32[]{:S(2)}, u32[]{:S(2)}) %collective-permute-start.7) | collective-permute-done | bytes 294944 | tf_op jit(solution)/shard_map/ppermute | solution.py:35
  54.0 3.2 %collective-permute-done.6 = bf16[2,4,24,768]{3,2,1,0:T(8,128)(2,1)S(1)} collective-permute-done((bf16[2,4,24,768]{3,2,1,0:T(8,128)(2,1)S(1)}, bf16[2,4,24,768]{3,2,1,0:T(8,128)(2,1)S(1)}, u32[]{:S(2)}, u32[]{:S(2)}) %collective-permute-start.6) | collective-permute-done | bytes 294944 | tf_op jit(solution)/shard_map/ppermute | solution.py:34
  57.5 4.5 %collective-permute-start.8 = (bf16[4,4,4,24,768]{4,3,2,1,0:T(8,128)(2,1)S(1)}, bf16[4,4,4,24,768]{4,3,2,1,0:T(8,128)(2,1)}, u32[]{:S(2)}, u32[]{:S(2)}) collective-permute-start(bf16[4,4,4,24,768]{4,3,2,1,0:T(8,128)(2,1)S(1)} %pad_maximum_fusion.1), channel_id=1, source_target_pairs={{0,4},{4,0},{8,12},{12,8},{16,20},{20,16},{24,28},{28,24},{32,36},... | collective-permute-start | bytes 7077896 | tf_op jit(solution)/shard_map/ppermute | solution.py:52
  62.1 4.2 %collective-permute-done.8 = bf16[4,4,4,24,768]{4,3,2,1,0:T(8,128)(2,1)} collective-permute-done((bf16[4,4,4,24,768]{4,3,2,1,0:T(8,128)(2,1)S(1)}, bf16[4,4,4,24,768]{4,3,2,1,0:T(8,128)(2,1)}, u32[]{:S(2)}, u32[]{:S(2)}) %collective-permute-start.8) | collective-permute-done | bytes 2359328 | tf_op jit(solution)/shard_map/ppermute | solution.py:52
  66.3 4.2 %pad_maximum_fusion = bf16[32,4,24,768]{3,2,1,0:T(8,128)(2,1)} fusion(bf16[16,4,24,768]{3,2,1,0:T(8,128)(2,1)} %bitcast.13, bf16[16,4,24,768]{3,2,1,0:T(8,128)(2,1)S(1)} %bitcast.86), kind=kLoop, calls=%fused_computation.2 | loop fusion | flops 2359296 | bytes 9437184 | tf_op jit(solution)/shard_map/concatenate | solution.py:54
  70.5 5.4 %gather_fusion.1 = bf16[32,4,24,768]{3,2,1,0:T(8,128)(2,1)} fusion(bf16[32,4,24,768]{3,2,1,0:T(8,128)(2,1)} %pad_maximum_fusion, s32[1024]{0:T(1024)S(1)} %pad_clamp_fusion), kind=kCustom, calls=%fused_computation.1 | custom fusion | bytes 9437312 | tf_op jit(solution)/shard_map/jit(_take)/gather | solution.py:65
  89.2 3.7 %convolution_convert_fusion.4 = bf16[768,768]{1,0:T(8,128)(2,1)} fusion(bf16[768,768]{1,0:T(8,128)(2,1)} %reshape.322, bf16[2,768,768]{2,1,0:T(8,128)(2,1)} %param.3), kind=kOutput, calls=%fused_computation.9 | convolution fusion | flops 906559488 | bytes 3538944 | tf_op jit(solution)/shard_map/dot_general | solution.py:82
  92.9 3.1 %reshape.323 = bf16[192,3072]{1,0:T(8,128)(2,1)} reshape(bf16[768,768]{1,0:T(8,128)(2,1)} %convolution_convert_fusion.4) | data formatting | bytes 2359296 | tf_op jit(solution)/shard_map/reshape | solution.py:86
  96.0 5.1 %convolution_convert_fusion.9 = bf16[192,768]{1,0:T(8,128)(2,1)} fusion(bf16[192,3072]{1,0:T(8,128)(2,1)} %reshape.323, bf16[768,3072]{1,0:T(8,128)(2,1)} %bitcast.75), kind=kOutput, calls=%fused_computation.14 | convolution fusion | flops 906117120 | bytes 6193152 | tf_op jit(solution)/shard_map/dot_general | solution.py:85
  102.5 3.1 %reshape.330 = bf16[768,768]{1,0:T(8,128)(2,1)} reshape(bf16[192,3072]{1,0:T(8,128)(2,1)} %get-tuple-element.6) | data formatting | bytes 2359296 | tf_op jit(solution)/shard_map/reshape | solution.py:83
  105.6 3.8 %convolution_convert_fusion = bf16[768,768]{1,0:T(8,128)(2,1)} fusion(bf16[768,768]{1,0:T(8,128)(2,1)} %reshape.330, bf16[2,768,768]{2,1,0:T(8,128)(2,1)} %param.3), kind=kOutput, calls=%fused_computation.5 | convolution fusion | flops 906559488 | bytes 3538944 | tf_op jit(solution)/shard_map/dot_general | solution.py:82
  109.4 3.1 %reshape.331 = bf16[192,3072]{1,0:T(8,128)(2,1)} reshape(bf16[768,768]{1,0:T(8,128)(2,1)} %convolution_convert_fusion) | data formatting | bytes 2359296 | tf_op jit(solution)/shard_map/reshape | solution.py:86
  112.5 5.1 %convolution_convert_fusion.8 = bf16[192,768]{1,0:T(8,128)(2,1)} fusion(bf16[192,3072]{1,0:T(8,128)(2,1)} %reshape.331, bf16[768,3072]{1,0:T(8,128)(2,1)} %bitcast.76), kind=kOutput, calls=%fused_computation.13 | convolution fusion | flops 906117120 | bytes 6193152 | tf_op jit(solution)/shard_map/dot_general | solution.py:85
  119.1 3.1 %reshape.328 = bf16[768,768]{1,0:T(8,128)(2,1)} reshape(bf16[192,3072]{1,0:T(8,128)(2,1)} %get-tuple-element.7) | data formatting | bytes 2359296 | tf_op jit(solution)/shard_map/reshape | solution.py:83
  122.2 3.8 %convolution_convert_fusion.1 = bf16[768,768]{1,0:T(8,128)(2,1)} fusion(bf16[768,768]{1,0:T(8,128)(2,1)} %reshape.328, bf16[2,768,768]{2,1,0:T(8,128)(2,1)} %param.3), kind=kOutput, calls=%fused_computation.6 | convolution fusion | flops 906559488 | bytes 3538944 | tf_op jit(solution)/shard_map/dot_general | solution.py:82
  129.1 3.1 %reshape.326 = bf16[768,768]{1,0:T(8,128)(2,1)} reshape(bf16[192,3072]{1,0:T(8,128)(2,1)} %get-tuple-element.8) | data formatting | bytes 2359296 | tf_op jit(solution)/shard_map/reshape | solution.py:83
  132.2 3.8 %convolution_convert_fusion.2 = bf16[768,768]{1,0:T(8,128)(2,1)} fusion(bf16[768,768]{1,0:T(8,128)(2,1)} %reshape.326, bf16[2,768,768]{2,1,0:T(8,128)(2,1)} %param.3), kind=kOutput, calls=%fused_computation.7 | convolution fusion | flops 906559488 | bytes 3538944 | tf_op jit(solution)/shard_map/dot_general | solution.py:82
  136.0 3.1 %reshape.327 = bf16[192,3072]{1,0:T(8,128)(2,1)} reshape(bf16[768,768]{1,0:T(8,128)(2,1)} %convolution_convert_fusion.2) | data formatting | bytes 2359296 | tf_op jit(solution)/shard_map/reshape | solution.py:86
  139.1 5.2 %fusion.34 = f32[192,768]{1,0:T(8,128)} fusion(bf16[192,3072]{1,0:T(8,128)(2,1)} %reshape.327, bf16[768,3072]{1,0:T(8,128)(2,1)} %bitcast.77), kind=kOutput, calls=%fused_computation.112 | convolution fusion | flops 905969664 | bytes 6488064 | tf_op jit(solution)/shard_map/dot_general | solution.py:85
  144.3 3.1 %reshape.324 = bf16[768,768]{1,0:T(8,128)(2,1)} reshape(bf16[192,3072]{1,0:T(8,128)(2,1)} %get-tuple-element.9) | data formatting | bytes 2359296 | tf_op jit(solution)/shard_map/reshape | solution.py:83
  147.4 3.8 %convolution_convert_fusion.3 = bf16[768,768]{1,0:T(8,128)(2,1)} fusion(bf16[768,768]{1,0:T(8,128)(2,1)} %reshape.324, bf16[2,768,768]{2,1,0:T(8,128)(2,1)} %param.3), kind=kOutput, calls=%fused_computation.8 | convolution fusion | flops 906559488 | bytes 3538944 | tf_op jit(solution)/shard_map/dot_general | solution.py:82
  151.2 3.1 %reshape.325 = bf16[192,3072]{1,0:T(8,128)(2,1)} reshape(bf16[768,768]{1,0:T(8,128)(2,1)} %convolution_convert_fusion.3) | data formatting | bytes 2359296 | tf_op jit(solution)/shard_map/reshape | solution.py:86
  154.3 5.2 %fusion.33 = f32[192,768]{1,0:T(8,128)} fusion(bf16[192,3072]{1,0:T(8,128)(2,1)} %reshape.325, bf16[768,3072]{1,0:T(8,128)(2,1)} %bitcast.78), kind=kOutput, calls=%fused_computation.111 | convolution fusion | flops 905969664 | bytes 6488064 | tf_op jit(solution)/shard_map/dot_general | solution.py:85
  166.1 3.4 %convolution_convert_fusion.6 = bf16[768,768]{1,0:T(8,128)(2,1)} fusion(bf16[768,768]{1,0:T(8,128)(2,1)S(1)} %reshape.318, bf16[2,768,768]{2,1,0:T(8,128)(2,1)} %param.3), kind=kOutput, calls=%fused_computation.11 | convolution fusion | flops 906559488 | bytes 3538944 | tf_op jit(solution)/shard_map/dot_general | solution.py:82
  173.4 4.2 %fusion.32 = f32[192,768]{1,0:T(8,128)S(1)} fusion(bf16[192,3072]{1,0:T(8,128)(2,1)S(1)} %reshape.319, bf16[768,3072]{1,0:T(8,128)(2,1)} %bitcast.79), kind=kOutput, calls=%fused_computation.110 | convolution fusion | flops 905969664 | bytes 6488064 | tf_op jit(solution)/shard_map/dot_general | solution.py:85
  177.6 3.5 %add_convert_fusion.1 = bf16[192,768]{1,0:T(8,128)(2,1)} fusion(bf16[192,768]{1,0:T(8,128)(2,1)} %collective-permute-done.12, bf16[192,3072]{1,0:T(8,128)(2,1)S(1)} %copy-done.1, bf16[768,3072]{1,0:T(8,128)(2,1)S(1)} %bitcast.83), kind=kOutput, calls=%fused_computation.36 | convolution fusion | flops 906412032 | bytes 6488064 | tf_op jit(solution)/shard_map/dot_general | solution.py:85
  182.6 3.4 %add_convert_fusion.3 = bf16[192,768]{1,0:T(8,128)(2,1)} fusion(bf16[192,768]{1,0:T(8,128)(2,1)} %collective-permute-done.9, bf16[192,3072]{1,0:T(8,128)(2,1)S(1)} %copy-done.2, bf16[768,3072]{1,0:T(8,128)(2,1)S(1)} %bitcast.84), kind=kOutput, calls=%fused_computation.39 | convolution fusion | flops 906412032 | bytes 6488064 | tf_op jit(solution)/shard_map/dot_general | solution.py:85
  196.0 4.1 %fusion.31 = f32[192,768]{1,0:T(8,128)S(1)} fusion(bf16[192,3072]{1,0:T(8,128)(2,1)S(1)} %reshape.317, bf16[768,3072]{1,0:T(8,128)(2,1)} %bitcast.80), kind=kOutput, calls=%fused_computation.109 | convolution fusion | flops 905969664 | bytes 6488064 | tf_op jit(solution)/shard_map/dot_general | solution.py:85
  200.1 3.5 %collective-permute-done.11 = bf16[192,768]{1,0:T(8,128)(2,1)S(1)} collective-permute-done((bf16[192,768]{1,0:T(8,128)(2,1)S(1)}, bf16[192,768]{1,0:T(8,128)(2,1)S(1)}, u32[]{:S(2)}, u32[]{:S(2)}) %collective-permute-start.11) | collective-permute-done | bytes 294944 | tf_op jit(solution)/shard_map/ppermute | solution.py:104
  (81 shorter events, 57.3 us)
Async XLA Ops:
  0.0 9.6 %copy-start.7 = (s32[4,4]{1,0:T(4,128)S(1)}, s32[4,4]{1,0:T(4,128)}, u32[]{:S(2)}) copy-start(s32[4,4]{1,0:T(4,128)} %param.5) | copy-start | bytes 196
  0.0 28.1 %all-to-all-start = ((bf16[32,24,768]{2,1,0:T(8,128)(2,1)}), bf16[32,24,768]{2,1,0:T(8,128)(2,1)S(1)}, u32[]{:S(2)}, u32[]{:S(2)}) async-start(bf16[32,24,768]{2,1,0:T(8,128)(2,1)} %bitcast.89), calls=%async_computation | async-start | bytes 2359296 | tf_op jit(solution)/shard_map/all_to_all | solution.py:47
  28.7 5.6 %collective-permute-start.1 = (bf16[4,24,768]{2,1,0:T(8,128)(2,1)S(1)}, bf16[4,24,768]{2,1,0:T(8,128)(2,1)S(1)}, u32[]{:S(2)}, u32[]{:S(2)}) collective-permute-start(bf16[4,24,768]{2,1,0:T(8,128)(2,1)S(1)} %broadcast_select_fusion), channel_id=1, source_target_pairs={{0,8},{4,36},{8,16},{12,44},{16,24},{20,52},{24,0},{28,60},{32,40}... | collective-permute-start | bytes 442376 | tf_op jit(solution)/shard_map/ppermute | solution.py:32
  28.8 5.5 %collective-permute-start = (bf16[4,24,768]{2,1,0:T(8,128)(2,1)S(1)}, bf16[4,24,768]{2,1,0:T(8,128)(2,1)S(1)}, u32[]{:S(2)}, u32[]{:S(2)}) collective-permute-start(bf16[4,24,768]{2,1,0:T(8,128)(2,1)S(1)} %broadcast_select_fusion), channel_id=1, source_target_pairs={{0,24},{4,100},{8,0},{12,108},{16,8},{20,116},{24,16},{28,124},{32... | collective-permute-start | bytes 442376 | tf_op jit(solution)/shard_map/ppermute | solution.py:33
  34.3 4.4 %collective-permute-start.2 = (bf16[2,24,768]{2,1,0:T(8,128)(2,1)S(1)}, bf16[2,24,768]{2,1,0:T(8,128)(2,1)S(1)}, u32[]{:S(2)}, u32[]{:S(2)}) collective-permute-start(bf16[2,24,768]{2,1,0:T(8,128)(2,1)S(1)} %slice.34), channel_id=1, source_target_pairs={{0,8},{4,36},{8,16},{12,44},{16,24},{20,52},{24,0},{28,60},{32,40}... | collective-permute-start | bytes 221192 | tf_op jit(solution)/shard_map/ppermute | solution.py:34
  34.4 4.4 %collective-permute-start.3 = (bf16[2,24,768]{2,1,0:T(8,128)(2,1)S(1)}, bf16[2,24,768]{2,1,0:T(8,128)(2,1)S(1)}, u32[]{:S(2)}, u32[]{:S(2)}) collective-permute-start(bf16[2,24,768]{2,1,0:T(8,128)(2,1)S(1)} %slice.35), channel_id=1, source_target_pairs={{0,24},{4,100},{8,0},{12,108},{16,8},{20,116},{24,16},{28,124},{32... | collective-permute-start | bytes 221192 | tf_op jit(solution)/shard_map/ppermute | solution.py:35
  38.9 9.1 %collective-permute-start.4 = (bf16[4,4,24,768]{3,2,1,0:T(8,128)(2,1)S(1)}, bf16[4,4,24,768]{3,2,1,0:T(8,128)(2,1)S(1)}, u32[]{:S(2)}, u32[]{:S(2)}) collective-permute-start(bf16[4,4,24,768]{3,2,1,0:T(8,128)(2,1)S(1)} %get-tuple-element.14), channel_id=1, source_target_pairs={{0,96},{4,28},{8,104},{12,4},{16,112},{20,12},{24,120},{28,20},{32... | collective-permute-start | bytes 1769480 | tf_op jit(solution)/shard_map/ppermute | solution.py:33
  40.0 10.3 %collective-permute-start.5 = (bf16[4,4,24,768]{3,2,1,0:T(8,128)(2,1)S(1)}, bf16[4,4,24,768]{3,2,1,0:T(8,128)(2,1)S(1)}, u32[]{:S(2)}, u32[]{:S(2)}) collective-permute-start(bf16[4,4,24,768]{3,2,1,0:T(8,128)(2,1)S(1)} %get-tuple-element.14), channel_id=1, source_target_pairs={{0,32},{4,12},{8,40},{12,20},{16,48},{20,28},{24,56},{28,4},{32,64... | collective-permute-start | bytes 1769480 | tf_op jit(solution)/shard_map/ppermute | solution.py:32
  48.0 6.0 %collective-permute-start.7 = (bf16[2,4,24,768]{3,2,1,0:T(8,128)(2,1)S(1)}, bf16[2,4,24,768]{3,2,1,0:T(8,128)(2,1)S(1)}, u32[]{:S(2)}, u32[]{:S(2)}) collective-permute-start(bf16[2,4,24,768]{3,2,1,0:T(8,128)(2,1)S(1)} %slice.37), channel_id=1, source_target_pairs={{0,96},{4,28},{8,104},{12,4},{16,112},{20,12},{24,120},{28,20},{32... | collective-permute-start | bytes 884744 | tf_op jit(solution)/shard_map/ppermute | solution.py:35
  50.3 6.9 %collective-permute-start.6 = (bf16[2,4,24,768]{3,2,1,0:T(8,128)(2,1)S(1)}, bf16[2,4,24,768]{3,2,1,0:T(8,128)(2,1)S(1)}, u32[]{:S(2)}, u32[]{:S(2)}) collective-permute-start(bf16[2,4,24,768]{3,2,1,0:T(8,128)(2,1)S(1)} %slice.36), channel_id=1, source_target_pairs={{0,32},{4,12},{8,40},{12,20},{16,48},{20,28},{24,56},{28,4},{32,64... | collective-permute-start | bytes 884744 | tf_op jit(solution)/shard_map/ppermute | solution.py:34
  57.5 8.8 %collective-permute-start.8 = (bf16[4,4,4,24,768]{4,3,2,1,0:T(8,128)(2,1)S(1)}, bf16[4,4,4,24,768]{4,3,2,1,0:T(8,128)(2,1)}, u32[]{:S(2)}, u32[]{:S(2)}) collective-permute-start(bf16[4,4,4,24,768]{4,3,2,1,0:T(8,128)(2,1)S(1)} %pad_maximum_fusion.1), channel_id=1, source_target_pairs={{0,4},{4,0},{8,12},{12,8},{16,20},{20,16},{24,28},{28,24},{32,36},... | collective-permute-start | bytes 7077896 | tf_op jit(solution)/shard_map/ppermute | solution.py:52
  82.1 3.9 %copy-start = (bf16[96,8,4,768]{3,1,2,0:T(8,128)(2,1)}, bf16[96,8,4,768]{3,1,2,0:T(8,128)(2,1)S(1)}, u32[]{:S(2)}) copy-start(bf16[96,8,4,768]{3,1,2,0:T(8,128)(2,1)S(1)} %copy.5) | copy-start | bytes 14155780
  101.2 81.4 %collective-permute-start.9 = (bf16[192,768]{1,0:T(8,128)(2,1)}, bf16[192,768]{1,0:T(8,128)(2,1)}, u32[]{:S(2)}, u32[]{:S(2)}) collective-permute-start(bf16[192,768]{1,0:T(8,128)(2,1)} %convolution_convert_fusion.9), channel_id=1, source_target_pairs={{0,1},{1,2},{2,3},{3,0},{4,5},{5,6},{6,7},{7,4},{8,9},{9,10},{10,1... | collective-permute-start | bytes 884744 | tf_op jit(solution)/shard_map/ppermute | solution.py:104
  117.6 60.0 %collective-permute-start.12 = (bf16[192,768]{1,0:T(8,128)(2,1)}, bf16[192,768]{1,0:T(8,128)(2,1)}, u32[]{:S(2)}, u32[]{:S(2)}) collective-permute-start(bf16[192,768]{1,0:T(8,128)(2,1)} %convolution_convert_fusion.8), channel_id=1, source_target_pairs={{0,3},{1,0},{2,1},{3,2},{4,7},{5,4},{6,5},{7,6},{8,11},{9,8},{10,9... | collective-permute-start | bytes 884744 | tf_op jit(solution)/shard_map/ppermute | solution.py:104
  171.8 5.8 %slice-start = ((s8[4718592]{0:T(1024)(128)(4,1)}), s8[524288]{0:T(1024)(128)(4,1)S(1)}, s32[]{:S(2)}) async-start(s8[4718592]{0:T(1024)(128)(4,1)} %bitcast.81), calls=%async_computation.1 | async-start | bytes 1048576
  173.4 4.2 %slice-start.1 = ((s8[4718592]{0:T(1024)(128)(4,1)}), s8[4194304]{0:T(1024)(128)(4,1)S(1)}, s32[]{:S(2)}) async-start(s8[4718592]{0:T(1024)(128)(4,1)} %bitcast.81), calls=%async_computation.2 | async-start | bytes 8388608
  173.4 4.2 %copy-start.1 = (bf16[192,3072]{1,0:T(8,128)(2,1)S(1)}, bf16[192,3072]{1,0:T(8,128)(2,1)}, u32[]{:S(2)}) copy-start(bf16[192,3072]{1,0:T(8,128)(2,1)} %reshape.329) | copy-start | bytes 3538948
  177.6 5.0 %copy-start.2 = (bf16[192,3072]{1,0:T(8,128)(2,1)S(1)}, bf16[192,3072]{1,0:T(8,128)(2,1)}, u32[]{:S(2)}) copy-start(bf16[192,3072]{1,0:T(8,128)(2,1)} %reshape.321) | copy-start | bytes 3538948
  181.1 4.9 %copy-start.3 = (bf16[768,768]{1,0:T(8,128)(2,1)S(1)}, bf16[768,768]{1,0:T(8,128)(2,1)}, u32[]{:S(2)}) copy-start(bf16[768,768]{1,0:T(8,128)(2,1)} %reshape.316) | copy-start | bytes 3538948
  181.1 4.9 %copy-start.6 = (bf16[2,768,768]{2,1,0:T(8,128)(2,1)S(1)}, bf16[2,768,768]{2,1,0:T(8,128)(2,1)}, u32[]{:S(2)}) copy-start(bf16[2,768,768]{2,1,0:T(8,128)(2,1)} %param.3) | copy-start | bytes 7077892
  181.1 8.0 %collective-permute-start.13 = (bf16[192,768]{1,0:T(8,128)(2,1)}, bf16[192,768]{1,0:T(8,128)(2,1)}, u32[]{:S(2)}, u32[]{:S(2)}) collective-permute-start(bf16[192,768]{1,0:T(8,128)(2,1)} %add_convert_fusion.1), channel_id=1, source_target_pairs={{0,3},{1,0},{2,1},{3,2},{4,7},{5,4},{6,5},{7,6},{8,11},{9,8},{10,9... | collective-permute-start | bytes 884744 | tf_op jit(solution)/shard_map/ppermute | solution.py:104
  186.0 8.9 %collective-permute-start.10 = (bf16[192,768]{1,0:T(8,128)(2,1)}, bf16[192,768]{1,0:T(8,128)(2,1)}, u32[]{:S(2)}, u32[]{:S(2)}) collective-permute-start(bf16[192,768]{1,0:T(8,128)(2,1)} %add_convert_fusion.3), channel_id=1, source_target_pairs={{0,1},{1,2},{2,3},{3,0},{4,5},{5,6},{6,7},{7,4},{8,9},{9,10},{10,1... | collective-permute-start | bytes 884744 | tf_op jit(solution)/shard_map/ppermute | solution.py:104
  187.1 2.1 %copy-start.4 = (f32[192,768]{1,0:T(8,128)S(1)}, f32[192,768]{1,0:T(8,128)}, u32[]{:S(2)}) copy-start(f32[192,768]{1,0:T(8,128)} %fusion.34) | copy-start | bytes 1769476
  190.2 9.9 %collective-permute-start.14 = (bf16[192,768]{1,0:T(8,128)(2,1)S(1)}, bf16[192,768]{1,0:T(8,128)(2,1)S(1)}, u32[]{:S(2)}, u32[]{:S(2)}) collective-permute-start(bf16[192,768]{1,0:T(8,128)(2,1)S(1)} %add_convert_fusion), channel_id=1, source_target_pairs={{0,3},{1,0},{2,1},{3,2},{4,7},{5,4},{6,5},{7,6},{8,11},{9,8},{10,9... | collective-permute-start | bytes 884744 | tf_op jit(solution)/shard_map/ppermute | solution.py:104
  195.9 4.2 %copy-start.5 = (f32[192,768]{1,0:T(8,128)S(1)}, f32[192,768]{1,0:T(8,128)}, u32[]{:S(2)}) copy-start(f32[192,768]{1,0:T(8,128)} %fusion.33) | copy-start | bytes 1769476
  195.9 7.8 %collective-permute-start.11 = (bf16[192,768]{1,0:T(8,128)(2,1)S(1)}, bf16[192,768]{1,0:T(8,128)(2,1)S(1)}, u32[]{:S(2)}, u32[]{:S(2)}) collective-permute-start(bf16[192,768]{1,0:T(8,128)(2,1)S(1)} %add_convert_fusion.2), channel_id=1, source_target_pairs={{0,1},{1,2},{2,3},{3,0},{4,5},{5,6},{6,7},{7,4},{8,9},{9,10},{10,1... | collective-permute-start | bytes 884744 | tf_op jit(solution)/shard_map/ppermute | solution.py:104

commit v3 on v1

--- a/solution.py
+++ b/solution.py
@@ -11,7 +11,6 @@
 def gather_slots(own_vector, owned_slots):
     rows, cols = own_vector.shape
     devices = lax.psum(1, PAIR)
-    cores = lax.psum(1, "core")
     piece = rows // devices
     pieces = own_vector.reshape(devices, piece, cols)
     pieces = lax.all_to_all(pieces, PAIR, 0, 0, tiled=True)
@@ -27,20 +26,47 @@
     return full.reshape(slots, rows, cols)
 
 
+def shifted(value, step, groups):
+    return lax.ppermute(value, "vgrp", [(g, (g + step) % groups) for g in range(groups)])
+
+
+def scatter_sum(total, vgrp, groups):
+    rows, cols = total.shape
+    block = rows // groups
+    blocks = total.reshape(groups, block, cols)
+
+    def pick(offset):
+        return lax.dynamic_index_in_dim(blocks, (vgrp + offset) % groups, 0, keepdims=False)
+
+    ahead = shifted(pick(1).astype(jnp.bfloat16), 1, groups)
+    behind = shifted(pick(-1).astype(jnp.bfloat16), -1, groups)
+    far = pick(2).astype(jnp.bfloat16)
+    half = block // 2
+    far_low = shifted(shifted(far[:half], 1, groups), 1, groups)
+    far_high = shifted(shifted(far[half:], -1, groups), -1, groups)
+    far = jnp.concatenate([far_low, far_high], axis=0)
+    return pick(0) + ahead.astype(jnp.float32) + behind.astype(jnp.float32) + far.astype(jnp.float32)
+
+
 def on_device(amplitudes, cholesky_vectors, owner_order):
-    vgrp_index = lax.axis_index("vgrp")
-    owned_slots = lax.dynamic_index_in_dim(owner_order, vgrp_index, 0, keepdims=False)
+    vgrp = lax.axis_index("vgrp")
+    groups = lax.psum(1, "vgrp")
+    owned_slots = lax.dynamic_index_in_dim(owner_order, vgrp, 0, keepdims=False)
     vectors = gather_slots(cholesky_vectors[0, 0], owned_slots)
-    accumulated = jnp.zeros(amplitudes.shape, jnp.float32)
-    for slot in range(owned_slots.shape[0]):
-        vector = vectors[slot]
-        half_product = jnp.einsum(
-            "ac,pcd->pad", vector, amplitudes, preferred_element_type=jnp.float32
-        ).astype(jnp.bfloat16)
-        accumulated = accumulated + jnp.einsum(
-            "pad,bd->pab", half_product, vector, preferred_element_type=jnp.float32
-        )
-    return lax.psum_scatter(accumulated, "vgrp", scatter_dimension=1, tiled=True)
+    outs = []
+    for pair in range(amplitudes.shape[0]):
+        amplitude = amplitudes[pair]
+        total = jnp.zeros(amplitude.shape, jnp.float32)
+        for slot in range(owned_slots.shape[0]):
+            vector = vectors[slot]
+            half_product = jnp.dot(
+                vector, amplitude, preferred_element_type=jnp.float32
+            ).astype(jnp.bfloat16)
+            total = total + lax.dot_general(
+                half_product, vector, (((1,), (1,)), ((), ())), preferred_element_type=jnp.float32
+            )
+        outs.append(scatter_sum(total, vgrp, groups))
+    return jnp.stack(outs, axis=0)
 
 
 def solution(mesh):

time: 180 us -> 171 us (0.950); the launches traced: 180 us -> 168 us
  waiting for transfers between devices: 115 us -> 79 us
  starting transfers between devices: 11.8 us -> 23.5 us
  matrix products: 31.8 us -> 41.5 us
  local copies, waits for them, and re-layouts: 3.11 us -> 5.26 us
    reduce_scatter x1 -> x0, waiting for transfers between devices: 50.1 us -> none  [on_device(): lax.psum_scatter(accumulated, 'vgrp', scatter_dimension=1, tiled=True)]
    ppermute x0 -> x12, waiting for transfers between devices: none -> 14.4 us  [shifted(): lax.ppermute(value, 'vgrp', [(g, (g + step) % groups) for g in range(grou...]
    ppermute x0 -> x12, starting transfers between devices: none -> 11.8 us  [shifted(): lax.ppermute(value, 'vgrp', [(g, (g + step) % groups) for g in range(grou...]
    dot_general x4 -> x8, matrix products: 31.8 us -> 41.5 us  [on_device(): lax.dot_general(half_product, vector, (((1,), (1,)), ((), ())), preferred...]
    another operation x0 -> x3, other arithmetic: none -> 2.46 us  [on_device(): return jnp.stack(outs, axis=0)]
    convert_element_type x0 -> x2, local copies, waits for them, and re-layouts: none -> 1.97 us  [scatter_sum(): far = pick(2).astype(jnp.bfloat16)]
  transfers between devices with their start and end apart: 4 -> 15, of which waited for: 4 -> 8; matrix products, arithmetic and copies ran while one was open for 0% -> 5% of each run, Pallas kernels for 0% -> 0%
where the time goes in v3:
time: 171 us; the launch traced here: 168 us
  waiting for transfers between devices  79 us (46%)
  matrix products  41.5 us (24%)
  starting transfers between devices  23.5 us (14%)
  between operations  13.5 us (8%)
  other arithmetic  5.62 us (3%)
  local copies, waits for them, and re-layouts  5.26 us (3%)
    all_gather x1, waiting for transfers between devices, gather_slots(): mine = lax.all_gather(picked, CHIPS, axis=0, tiled=False)  41.8 us
    dot_general x8, matrix products, on_device(): lax.dot_general(half_product, vector, (((1,), (1,)), ((), ())), preferred...  41.5 us
    all_to_all x1, waiting for transfers between devices, gather_slots(): pieces = lax.all_to_all(pieces, PAIR, 0, 0, tiled=True)  18.4 us
    ppermute x12, waiting for transfers between devices, shifted(): lax.ppermute(value, 'vgrp', [(g, (g + step) % groups) for g in range(grou...  14.4 us
    ppermute x12, starting transfers between devices, shifted(): lax.ppermute(value, 'vgrp', [(g, (g + step) % groups) for g in range(grou...  11.8 us
    all_to_all x1, starting transfers between devices, gather_slots(): pieces = lax.all_to_all(pieces, PAIR, 0, 0, tiled=True)  9.55 us
    ppermute x1, waiting for transfers between devices, gather_slots(): other = lax.ppermute(mine, 'core', [(0, 1), (1, 0)])  4.37 us
  transfers between devices with their start and end apart: 15, of which 8 were waited for; matrix products, arithmetic and copies ran while one was open for 5% of the time, Pallas kernels for 0%

profile of v3, /device:TPU:1, one launch (start us, length us, event | category | flops | bytes accessed | tf_op | source)
XLA Modules:
  0.0 168.4 jit_solution(16881885528507519255)
XLA Ops:
  6.5 9.6 %all-to-all-start = ((bf16[32,24,768]{2,1,0:T(8,128)(2,1)}), bf16[32,24,768]{2,1,0:T(8,128)(2,1)S(1)}, u32[]{:S(2)}, u32[]{:S(2)}) async-start(bf16[32,24,768]{2,1,0:T(8,128)(2,1)} %bitcast.117), calls=%async_computation | async-start | bytes 2359296 | tf_op jit(solution)/shard_map/all_to_all | solution.py:16
  16.2 18.4 %all-to-all-done = bf16[32,24,768]{2,1,0:T(8,128)(2,1)S(1)} async-done(((bf16[32,24,768]{2,1,0:T(8,128)(2,1)}), bf16[32,24,768]{2,1,0:T(8,128)(2,1)S(1)}, u32[]{:S(2)}, u32[]{:S(2)}) %all-to-all-start) | async-done | bytes 1179680 | tf_op jit(solution)/shard_map/all_to_all | solution.py:16
  36.0 41.8 %all-gather.2.cloned.1.call-done = bf16[16,4,24,768]{3,2,0,1:T(8,128)(2,1)} async-done(((bf16[1,4,24,768]{3,2,0,1:T(8,128)(2,1)}), bf16[16,4,24,768]{3,2,0,1:T(8,128)(2,1)}) %all-gather.2.cloned.1.call-update) | async-done | bytes 2359312 | tf_op jit(solution)/shard_map/all_gather | solution.py:18
  77.8 2.1 %collective-permute-start = (bf16[16,4,24,768]{3,2,0,1:T(8,128)(2,1)}, bf16[16,4,24,768]{3,2,0,1:T(8,128)(2,1)S(1)}, u32[]{:S(2)}, u32[]{:S(2)}) collective-permute-start(bf16[16,4,24,768]{3,2,0,1:T(8,128)(2,1)} %all-gather.2.cloned.1.call-done), channel_id=1, source_target_pairs={{0,4},{4,0},{1,5},{5,1},{2,6},{6,2},{3,7},{7,3},{8,12},{12,8},{9,1... | collective-permute-start | bytes 7077896 | tf_op jit(solution)/shard_map/ppermute | solution.py:20
  79.9 4.4 %collective-permute-done = bf16[16,4,24,768]{3,2,0,1:T(8,128)(2,1)S(1)} collective-permute-done((bf16[16,4,24,768]{3,2,0,1:T(8,128)(2,1)}, bf16[16,4,24,768]{3,2,0,1:T(8,128)(2,1)S(1)}, u32[]{:S(2)}, u32[]{:S(2)}) %collective-permute-start) | collective-permute-done | bytes 2359328 | tf_op jit(solution)/shard_map/ppermute | solution.py:20
  84.3 2.0 %select_bitcast_fusion.1 = (bf16[16,1,4,24,768]{4,3,1,0,2:T(8,128)(2,1)S(1)}, bf16[16,1,4,24,768]{4,3,1,0,2:T(8,128)(2,1)S(1)}) fusion(bf16[16,4,24,768]{3,2,0,1:T(8,128)(2,1)} %all-gather.2.cloned.1.call-done, bf16[16,4,24,768]{3,2,0,1:T(8,128)(2,1)S(1)} %collective-permute-done, pred[]{:T(512)S(6)} %eq.13), kind=kLoop, calls=%fused_computation.5 | loop fusion | flops 2359296 | bytes 9437185 | tf_op jit(solution)/shard_map/stack | solution.py:23
  86.7 1.3 fusion.55
  88.0 5.5 %fusion.9 = f32[768,768]{1,0:T(8,128)} fusion(bf16[768,768]{1,0:T(8,128)(2,1)} %bitcast.115, bf16[2,768,768]{2,1,0:T(8,128)(2,1)} %param.3), kind=kOutput, calls=%fused_computation.23 | convolution fusion | flops 1812529152 | bytes 5898240 | tf_op jit(solution)/shard_map/dot_general | solution.py:65
  93.5 5.5 %fusion.18 = f32[768,768]{1,0:T(8,128)} fusion(bf16[768,768]{1,0:T(8,128)(2,1)} %bitcast.116, bf16[2,768,768]{2,1,0:T(8,128)(2,1)} %param.3), kind=kOutput, calls=%fused_computation.26 | convolution fusion | flops 1812529152 | bytes 5898240 | tf_op jit(solution)/shard_map/dot_general | solution.py:65
  99.1 4.8 %fusion.12 = f32[768,768]{1,0:T(8,128)} fusion(bf16[768,768]{1,0:T(8,128)(2,1)S(1)} %bitcast.113, bf16[2,768,768]{2,1,0:T(8,128)(2,1)} %param.3), kind=kOutput, calls=%fused_computation.24 | convolution fusion | flops 1812529152 | bytes 5898240 | tf_op jit(solution)/shard_map/dot_general | solution.py:65
  103.8 4.8 %fusion.21 = f32[768,768]{1,0:T(8,128)} fusion(bf16[768,768]{1,0:T(8,128)(2,1)S(1)} %bitcast.114, bf16[2,768,768]{2,1,0:T(8,128)(2,1)} %param.3), kind=kOutput, calls=%fused_computation.27 | convolution fusion | flops 1812529152 | bytes 5898240 | tf_op jit(solution)/shard_map/dot_general | solution.py:65
  108.7 4.8 %fusion.15 = f32[768,768]{1,0:T(8,128)} fusion(bf16[768,768]{1,0:T(8,128)(2,1)S(1)} %bitcast.111, bf16[2,768,768]{2,1,0:T(8,128)(2,1)} %param.3), kind=kOutput, calls=%fused_computation.25 | convolution fusion | flops 1812529152 | bytes 5898240 | tf_op jit(solution)/shard_map/dot_general | solution.py:65
  113.5 4.9 %fusion.24 = f32[768,768]{1,0:T(8,128)} fusion(bf16[768,768]{1,0:T(8,128)(2,1)S(1)} %bitcast.112, bf16[2,768,768]{2,1,0:T(8,128)(2,1)} %param.3), kind=kOutput, calls=%fused_computation.28 | convolution fusion | flops 1812529152 | bytes 5898240 | tf_op jit(solution)/shard_map/dot_general | solution.py:65
  118.4 5.5 %add_add_fusion.1 = f32[768,768]{1,0:T(8,128)S(1)} fusion(f32[768,768]{1,0:T(8,128)} %fusion.15, f32[768,768]{1,0:T(8,128)} %fusion.9, f32[768,768]{1,0:T(8,128)} %fusion.12, bf16[768,768]{1,0:T(8,128)(2,1)S(1)} %bitcast.109, bf16[2,768,768]{2,1,0:T(8,128)(2,1)} %param.3), kind=kOutput, calls=%fused_computation.3 | convolution fusion | flops 1814298624 | bytes 12976128 | tf_op jit(solution)/shard_map/dot_general | solution.py:65
  123.9 1.1 dynamic-slice_convert_fusion.3
  125.7 1.2 collective-permute-start.3
  126.9 1.5 collective-permute-start.5
  128.4 5.5 %add_add_fusion = f32[768,768]{1,0:T(8,128)S(1)} fusion(f32[768,768]{1,0:T(8,128)} %fusion.24, f32[768,768]{1,0:T(8,128)} %fusion.18, f32[768,768]{1,0:T(8,128)} %fusion.21, bf16[768,768]{1,0:T(8,128)(2,1)S(1)} %bitcast.110, bf16[2,768,768]{2,1,0:T(8,128)(2,1)} %param.3), kind=kOutput, calls=%fused_computation.2 | convolution fusion | flops 1814298624 | bytes 12976128 | tf_op jit(solution)/shard_map/dot_general | solution.py:65
  134.0 0.9 dynamic-slice_convert_fusion
  135.0 1.2 collective-permute-start.1
  136.2 1.6 collective-permute-start.2
  137.7 1.4 collective-permute-start.11
  139.2 1.5 collective-permute-done.9
  140.7 1.1 collective-permute-start.6
  141.8 4.8 %collective-permute-done.11 = bf16[96,768]{1,0:T(8,128)(2,1)S(1)} collective-permute-done((bf16[96,768]{1,0:T(8,128)(2,1)S(1)}, bf16[96,768]{1,0:T(8,128)(2,1)S(1)}, u32[]{:S(2)}, u32[]{:S(2)}) %collective-permute-start.11) | collective-permute-done | bytes 147488 | tf_op jit(solution)/shard_map/ppermute | solution.py:30
  147.5 2.6 %collective-permute-done.4 = bf16[96,768]{1,0:T(8,128)(2,1)S(1)} collective-permute-done((bf16[96,768]{1,0:T(8,128)(2,1)}, bf16[96,768]{1,0:T(8,128)(2,1)S(1)}, u32[]{:S(2)}, u32[]{:S(2)}) %collective-permute-start.4) | collective-permute-done | bytes 147488 | tf_op jit(solution)/shard_map/ppermute | solution.py:30
  150.8 1.4 collective-permute-start.10
  152.3 1.3 collective-permute-start.12
  153.6 1.3 fusion.49
  154.8 3.2 %collective-permute-done.10 = bf16[96,768]{1,0:T(8,128)(2,1)S(1)} collective-permute-done((bf16[96,768]{1,0:T(8,128)(2,1)}, bf16[96,768]{1,0:T(8,128)(2,1)S(1)}, u32[]{:S(2)}, u32[]{:S(2)}) %collective-permute-start.10) | collective-permute-done | bytes 147488 | tf_op jit(solution)/shard_map/ppermute | solution.py:30
  158.1 2.3 %collective-permute-done.12 = bf16[96,768]{1,0:T(8,128)(2,1)S(1)} collective-permute-done((bf16[96,768]{1,0:T(8,128)(2,1)}, bf16[96,768]{1,0:T(8,128)(2,1)S(1)}, u32[]{:S(2)}, u32[]{:S(2)}) %collective-permute-start.12) | collective-permute-done | bytes 147488 | tf_op jit(solution)/shard_map/ppermute | solution.py:30
  160.5 1.1 pad_maximum_fusion
  (32 shorter events, 4.5 us)
Async XLA Ops:
  6.5 9.6 %copy-start.4 = (s32[4,4]{1,0:T(4,128)S(1)}, s32[4,4]{1,0:T(4,128)}, u32[]{:S(2)}) copy-start(s32[4,4]{1,0:T(4,128)} %param.5) | copy-start | bytes 196
  6.5 28.1 %all-to-all-start = ((bf16[32,24,768]{2,1,0:T(8,128)(2,1)}), bf16[32,24,768]{2,1,0:T(8,128)(2,1)S(1)}, u32[]{:S(2)}, u32[]{:S(2)}) async-start(bf16[32,24,768]{2,1,0:T(8,128)(2,1)} %bitcast.117), calls=%async_computation | async-start | bytes 2359296 | tf_op jit(solution)/shard_map/all_to_all | solution.py:16
  16.1 61.7 %all-gather.2.cloned.1.call-start = ((), (), s32[]{:S(2)}) async-start(), calls=%async_computation.1 | async-start | bytes 2506752 | tf_op jit(solution)/shard_map/all_gather | solution.py:18
  77.8 6.5 %collective-permute-start = (bf16[16,4,24,768]{3,2,0,1:T(8,128)(2,1)}, bf16[16,4,24,768]{3,2,0,1:T(8,128)(2,1)S(1)}, u32[]{:S(2)}, u32[]{:S(2)}) collective-permute-start(bf16[16,4,24,768]{3,2,0,1:T(8,128)(2,1)} %all-gather.2.cloned.1.call-done), channel_id=1, source_target_pairs={{0,4},{4,0},{1,5},{5,1},{2,6},{6,2},{3,7},{7,3},{8,12},{12,8},{9,1... | collective-permute-start | bytes 7077896 | tf_op jit(solution)/shard_map/ppermute | solution.py:20
  123.9 1.8 %copy-start = (f32[768,768]{1,0:T(8,128)}, f32[768,768]{1,0:T(8,128)S(1)}, u32[]{:S(2)}) copy-start(f32[768,768]{1,0:T(8,128)S(1)} %add_add_fusion.1) | copy-start | bytes 7077892
  125.7 12.0 %collective-permute-start.3 = (bf16[96,768]{1,0:T(8,128)(2,1)}, bf16[96,768]{1,0:T(8,128)(2,1)}, u32[]{:S(2)}, u32[]{:S(2)}) collective-permute-start(bf16[96,768]{1,0:T(8,128)(2,1)} %get-tuple-element.17), channel_id=1, source_target_pairs={{0,1},{1,2},{2,3},{3,0},{4,5},{5,6},{6,7},{7,4},{8,9},{9,10},{10,1... | collective-permute-start | bytes 442376 | tf_op jit(solution)/shard_map/ppermute | solution.py:30
  126.9 12.2 %collective-permute-start.5 = (bf16[96,768]{1,0:T(8,128)(2,1)}, bf16[96,768]{1,0:T(8,128)(2,1)}, u32[]{:S(2)}, u32[]{:S(2)}) collective-permute-start(bf16[96,768]{1,0:T(8,128)(2,1)} %get-tuple-element.18), channel_id=1, source_target_pairs={{0,3},{1,0},{2,1},{3,2},{4,7},{5,4},{6,5},{7,6},{8,11},{9,8},{10,9... | collective-permute-start | bytes 442376 | tf_op jit(solution)/shard_map/ppermute | solution.py:30
  134.9 5.8 %collective-permute-start.9 = (bf16[96,768]{1,0:T(8,128)(2,1)S(1)}, bf16[96,768]{1,0:T(8,128)(2,1)S(1)}, u32[]{:S(2)}, u32[]{:S(2)}) collective-permute-start(bf16[96,768]{1,0:T(8,128)(2,1)S(1)} %get-tuple-element.19), channel_id=1, source_target_pairs={{0,1},{1,2},{2,3},{3,0},{4,5},{5,6},{6,7},{7,4},{8,9},{9,10},{10,1... | collective-permute-start | bytes 442376 | tf_op jit(solution)/shard_map/ppermute | solution.py:30
  135.0 17.3 %collective-permute-start.1 = (bf16[192,768]{1,0:T(8,128)(2,1)}, bf16[192,768]{1,0:T(8,128)(2,1)S(1)}, u32[]{:S(2)}, u32[]{:S(2)}) collective-permute-start(bf16[192,768]{1,0:T(8,128)(2,1)} %get-tuple-element.13), channel_id=1, source_target_pairs={{0,1},{1,2},{2,3},{3,0},{4,5},{5,6},{6,7},{7,4},{8,9},{9,10},{10,1... | collective-permute-start | bytes 884744 | tf_op jit(solution)/shard_map/ppermute | solution.py:30
  136.2 17.4 %collective-permute-start.2 = (bf16[192,768]{1,0:T(8,128)(2,1)}, bf16[192,768]{1,0:T(8,128)(2,1)S(1)}, u32[]{:S(2)}, u32[]{:S(2)}) collective-permute-start(bf16[192,768]{1,0:T(8,128)(2,1)} %get-tuple-element.12), channel_id=1, source_target_pairs={{0,3},{1,0},{2,1},{3,2},{4,7},{5,4},{6,5},{7,6},{8,11},{9,8},{10,9... | collective-permute-start | bytes 884744 | tf_op jit(solution)/shard_map/ppermute | solution.py:30
  137.7 8.9 %collective-permute-start.11 = (bf16[96,768]{1,0:T(8,128)(2,1)S(1)}, bf16[96,768]{1,0:T(8,128)(2,1)S(1)}, u32[]{:S(2)}, u32[]{:S(2)}) collective-permute-start(bf16[96,768]{1,0:T(8,128)(2,1)S(1)} %get-tuple-element.20), channel_id=1, source_target_pairs={{0,3},{1,0},{2,1},{3,2},{4,7},{5,4},{6,5},{7,6},{8,11},{9,8},{10,9... | collective-permute-start | bytes 442376 | tf_op jit(solution)/shard_map/ppermute | solution.py:30
  139.1 11.0 %collective-permute-start.4 = (bf16[96,768]{1,0:T(8,128)(2,1)}, bf16[96,768]{1,0:T(8,128)(2,1)S(1)}, u32[]{:S(2)}, u32[]{:S(2)}) collective-permute-start(bf16[96,768]{1,0:T(8,128)(2,1)} %collective-permute-done.3), channel_id=1, source_target_pairs={{0,1},{1,2},{2,3},{3,0},{4,5},{5,6},{6,7},{7,4},{8,9},{9,10},{10,1... | collective-permute-start | bytes 442376 | tf_op jit(solution)/shard_map/ppermute | solution.py:30
  140.7 10.1 %copy-start.2 = (bf16[96,768]{1,0:T(8,128)(2,1)}, bf16[96,768]{1,0:T(8,128)(2,1)S(1)}, u32[]{:S(2)}) copy-start(bf16[96,768]{1,0:T(8,128)(2,1)S(1)} %collective-permute-done.9) | copy-start | bytes 442372
  140.7 10.2 %collective-permute-start.6 = (bf16[96,768]{1,0:T(8,128)(2,1)}, bf16[96,768]{1,0:T(8,128)(2,1)}, u32[]{:S(2)}, u32[]{:S(2)}) collective-permute-start(bf16[96,768]{1,0:T(8,128)(2,1)} %collective-permute-done.5), channel_id=1, source_target_pairs={{0,3},{1,0},{2,1},{3,2},{4,7},{5,4},{6,5},{7,6},{8,11},{9,8},{10,9... | collective-permute-start | bytes 442376 | tf_op jit(solution)/shard_map/ppermute | solution.py:30
  146.6 4.2 %copy-start.3 = (bf16[96,768]{1,0:T(8,128)(2,1)}, bf16[96,768]{1,0:T(8,128)(2,1)S(1)}, u32[]{:S(2)}) copy-start(bf16[96,768]{1,0:T(8,128)(2,1)S(1)} %collective-permute-done.11) | copy-start | bytes 442372
  146.6 13.7 %collective-permute-start.7 = (bf16[192,768]{1,0:T(8,128)(2,1)}, bf16[192,768]{1,0:T(8,128)(2,1)S(1)}, u32[]{:S(2)}, u32[]{:S(2)}) collective-permute-start(bf16[192,768]{1,0:T(8,128)(2,1)} %get-tuple-element.16), channel_id=1, source_target_pairs={{0,1},{1,2},{2,3},{3,0},{4,5},{5,6},{6,7},{7,4},{8,9},{9,10},{10,1... | collective-permute-start | bytes 884744 | tf_op jit(solution)/shard_map/ppermute | solution.py:30
  150.1 0.7 copy-start.1
  150.8 9.6 %collective-permute-start.8 = (bf16[192,768]{1,0:T(8,128)(2,1)}, bf16[192,768]{1,0:T(8,128)(2,1)S(1)}, u32[]{:S(2)}, u32[]{:S(2)}) collective-permute-start(bf16[192,768]{1,0:T(8,128)(2,1)} %get-tuple-element.15), channel_id=1, source_target_pairs={{0,3},{1,0},{2,1},{3,2},{4,7},{5,4},{6,5},{7,6},{8,11},{9,8},{10,9... | collective-permute-start | bytes 884744 | tf_op jit(solution)/shard_map/ppermute | solution.py:30
  150.8 7.2 %collective-permute-start.10 = (bf16[96,768]{1,0:T(8,128)(2,1)}, bf16[96,768]{1,0:T(8,128)(2,1)S(1)}, u32[]{:S(2)}, u32[]{:S(2)}) collective-permute-start(bf16[96,768]{1,0:T(8,128)(2,1)} %copy-done.2), channel_id=1, source_target_pairs={{0,1},{1,2},{2,3},{3,0},{4,5},{5,6},{6,7},{7,4},{8,9},{9,10},{10,1... | collective-permute-start | bytes 442376 | tf_op jit(solution)/shard_map/ppermute | solution.py:30
  152.3 8.1 %collective-permute-start.12 = (bf16[96,768]{1,0:T(8,128)(2,1)}, bf16[96,768]{1,0:T(8,128)(2,1)S(1)}, u32[]{:S(2)}, u32[]{:S(2)}) collective-permute-start(bf16[96,768]{1,0:T(8,128)(2,1)} %copy-done.3), channel_id=1, source_target_pairs={{0,3},{1,0},{2,1},{3,2},{4,7},{5,4},{6,5},{7,6},{8,11},{9,8},{10,9... | collective-permute-start | bytes 442376 | tf_op jit(solution)/shard_map/ppermute | solution.py:30
Sparse Core Ops, SparseCore 0:
  36.1 41.6 all-gather.1

commit v4 on v1

--- a/solution.py
+++ b/solution.py
@@ -11,7 +11,6 @@
 def gather_slots(own_vector, owned_slots):
     rows, cols = own_vector.shape
     devices = lax.psum(1, PAIR)
-    cores = lax.psum(1, "core")
     piece = rows // devices
     pieces = own_vector.reshape(devices, piece, cols)
     pieces = lax.all_to_all(pieces, PAIR, 0, 0, tiled=True)
@@ -27,20 +26,46 @@
     return full.reshape(slots, rows, cols)
 
 
+def shifted(value, step, groups):
+    return lax.ppermute(value, "vgrp", [(g, (g + step) % groups) for g in range(groups)])
+
+
+def scatter_sum(total, vgrp, groups):
+    pairs, rows, cols = total.shape
+    block = rows // groups
+    half = block // 2
+    blocks = total.reshape(pairs, groups, block, cols)
+
+    def pick(offset):
+        return lax.dynamic_index_in_dim(blocks, (vgrp + offset) % groups, 1, keepdims=False)
+
+    far = pick(2).astype(jnp.bfloat16)
+    ahead = jnp.concatenate([pick(1).astype(jnp.bfloat16), far[:, :half]], axis=1)
+    behind = jnp.concatenate([pick(-1).astype(jnp.bfloat16), far[:, half:]], axis=1)
+    ahead = shifted(ahead, 1, groups)
+    behind = shifted(behind, -1, groups)
+    far_low = shifted(ahead[:, block:], 1, groups)
+    far_high = shifted(behind[:, block:], -1, groups)
+    far = jnp.concatenate([far_low, far_high], axis=1).astype(jnp.float32)
+    near = ahead[:, :block].astype(jnp.float32) + behind[:, :block].astype(jnp.float32)
+    return pick(0) + near + far
+
+
 def on_device(amplitudes, cholesky_vectors, owner_order):
-    vgrp_index = lax.axis_index("vgrp")
-    owned_slots = lax.dynamic_index_in_dim(owner_order, vgrp_index, 0, keepdims=False)
+    vgrp = lax.axis_index("vgrp")
+    groups = lax.psum(1, "vgrp")
+    owned_slots = lax.dynamic_index_in_dim(owner_order, vgrp, 0, keepdims=False)
     vectors = gather_slots(cholesky_vectors[0, 0], owned_slots)
-    accumulated = jnp.zeros(amplitudes.shape, jnp.float32)
+    total = jnp.zeros(amplitudes.shape, jnp.float32)
     for slot in range(owned_slots.shape[0]):
         vector = vectors[slot]
         half_product = jnp.einsum(
             "ac,pcd->pad", vector, amplitudes, preferred_element_type=jnp.float32
         ).astype(jnp.bfloat16)
-        accumulated = accumulated + jnp.einsum(
+        total = total + jnp.einsum(
             "pad,bd->pab", half_product, vector, preferred_element_type=jnp.float32
         )
-    return lax.psum_scatter(accumulated, "vgrp", scatter_dimension=1, tiled=True)
+    return scatter_sum(total, vgrp, groups)
 
 
 def solution(mesh):

time: 180 us -> 169 us (0.939)
  waiting for transfers between devices: 115 us -> 89.1 us
  starting transfers between devices: 11.8 us -> 17.2 us
  local copies, waits for them, and re-layouts: 3.11 us -> 7.66 us
  other arithmetic: 4.77 us -> 7.63 us
    reduce_scatter x1 -> x0, waiting for transfers between devices: 50.1 us -> none  [on_device(): lax.psum_scatter(accumulated, 'vgrp', scatter_dimension=1, tiled=True)]
    ppermute x0 -> x4, waiting for transfers between devices: none -> 24.4 us  [shifted(): lax.ppermute(value, 'vgrp', [(g, (g + step) % groups) for g in range(grou...]
    ppermute x0 -> x4, starting transfers between devices: none -> 5.49 us  [shifted(): lax.ppermute(value, 'vgrp', [(g, (g + step) % groups) for g in range(grou...]
    add x0 -> x1, other arithmetic: none -> 2.74 us  [scatter_sum(): return pick(0) + near + far]
    convert_element_type x0 -> x1, local copies, waits for them, and re-layouts: none -> 2.16 us  [scatter_sum(): pick(1).astype(jnp.bfloat16)]
  transfers between devices with their start and end apart: 4 -> 7, of which waited for: 4 -> 6; matrix products, arithmetic and copies ran while one was open for 0% -> 1% of each run, Pallas kernels for 0% -> 0%
where the time goes in v4:
time: 169 us; the launch traced here: 167 us
  waiting for transfers between devices  89.1 us (53%)
  matrix products  31.8 us (19%)
  starting transfers between devices  17.2 us (10%)
  between operations  13.5 us (8%)
  local copies, waits for them, and re-layouts  7.66 us (5%)
  other arithmetic  7.63 us (5%)
    all_gather x1, waiting for transfers between devices, gather_slots(): mine = lax.all_gather(picked, CHIPS, axis=0, tiled=False)  41.8 us
    dot_general x4, matrix products, on_device(): jnp.einsum('pad,bd->pab', half_product, vector, preferred_element_type=jn...  31.8 us
    ppermute x4, waiting for transfers between devices, shifted(): lax.ppermute(value, 'vgrp', [(g, (g + step) % groups) for g in range(grou...  24.4 us
    all_to_all x1, waiting for transfers between devices, gather_slots(): pieces = lax.all_to_all(pieces, PAIR, 0, 0, tiled=True)  18.4 us
    all_to_all x1, starting transfers between devices, gather_slots(): pieces = lax.all_to_all(pieces, PAIR, 0, 0, tiled=True)  9.55 us
    ppermute x4, starting transfers between devices, shifted(): lax.ppermute(value, 'vgrp', [(g, (g + step) % groups) for g in range(grou...  5.49 us
    ppermute x1, waiting for transfers between devices, gather_slots(): other = lax.ppermute(mine, 'core', [(0, 1), (1, 0)])  4.5 us
  transfers between devices with their start and end apart: 7, of which 6 were waited for; matrix products, arithmetic and copies ran while one was open for 1% of the time, Pallas kernels for 0%

profile of v4, /device:TPU:1, one launch (start us, length us, event | category | flops | bytes accessed | tf_op | source)
XLA Modules:
  0.0 167.0 jit_solution(6349637030922192742)
XLA Ops:
  6.5 0.0 copy-start
  6.5 9.6 %all-to-all-start = ((bf16[32,24,768]{2,1,0:T(8,128)(2,1)}), bf16[32,24,768]{2,1,0:T(8,128)(2,1)S(1)}, u32[]{:S(2)}, u32[]{:S(2)}) async-start(bf16[32,24,768]{2,1,0:T(8,128)(2,1)} %bitcast.84), calls=%async_computation | async-start | bytes 2359296 | tf_op jit(solution)/shard_map/all_to_all | solution.py:16
  16.1 0.0 all-gather.2.cloned.1.call-start
  16.2 18.4 %all-to-all-done = bf16[32,24,768]{2,1,0:T(8,128)(2,1)S(1)} async-done(((bf16[32,24,768]{2,1,0:T(8,128)(2,1)}), bf16[32,24,768]{2,1,0:T(8,128)(2,1)S(1)}, u32[]{:S(2)}, u32[]{:S(2)}) %all-to-all-start) | async-done | bytes 1179680 | tf_op jit(solution)/shard_map/all_to_all | solution.py:16
  34.6 1.2 gather_fusion
  35.8 1.7 bitcast_select_fusion
  37.5 0.0 all-gather.2.cloned.1.call-update
  37.5 41.8 %all-gather.2.cloned.1.call-done = bf16[16,4,24,768]{3,2,0,1:T(8,128)(2,1)} async-done(((bf16[1,4,24,768]{3,2,0,1:T(8,128)(2,1)}), bf16[16,4,24,768]{3,2,0,1:T(8,128)(2,1)}) %all-gather.2.cloned.1.call-update) | async-done | bytes 2359312 | tf_op jit(solution)/shard_map/all_gather | solution.py:18
  79.3 2.1 %collective-permute-start = (bf16[16,4,24,768]{3,2,0,1:T(8,128)(2,1)}, bf16[16,4,24,768]{3,2,0,1:T(8,128)(2,1)}, u32[]{:S(2)}, u32[]{:S(2)}) collective-permute-start(bf16[16,4,24,768]{3,2,0,1:T(8,128)(2,1)} %all-gather.2.cloned.1.call-done), channel_id=1, source_target_pairs={{0,4},{4,0},{1,5},{5,1},{2,6},{6,2},{3,7},{7,3},{8,12},{12,8},{9,1... | collective-permute-start | bytes 7077896 | tf_op jit(solution)/shard_map/ppermute | solution.py:20
  81.4 4.5 %collective-permute-done = bf16[16,4,24,768]{3,2,0,1:T(8,128)(2,1)} collective-permute-done((bf16[16,4,24,768]{3,2,0,1:T(8,128)(2,1)}, bf16[16,4,24,768]{3,2,0,1:T(8,128)(2,1)}, u32[]{:S(2)}, u32[]{:S(2)}) %collective-permute-start) | collective-permute-done | bytes 2359328 | tf_op jit(solution)/shard_map/ppermute | solution.py:20
  86.0 2.7 %select_bitcast_fusion.1 = (bf16[16,1,4,24,768]{4,3,1,0,2:T(8,128)(2,1)S(1)}, bf16[16,1,4,24,768]{4,3,1,0,2:T(8,128)(2,1)S(1)}) fusion(bf16[16,4,24,768]{3,2,0,1:T(8,128)(2,1)} %all-gather.2.cloned.1.call-done, bf16[16,4,24,768]{3,2,0,1:T(8,128)(2,1)} %collective-permute-done, pred[]{:T(512)S(6)} %eq.9), kind=kLoop, calls=%fused_computation.16 | loop fusion | flops 2359296 | bytes 9437185 | tf_op jit(solution)/shard_map/stack | solution.py:23
  88.6 0.4 maximum_bitcast_fusion
  89.1 1.9 %fusion.27 = (bf16[1,16,2,24,768]{4,3,2,1,0:T(8,128)(2,1)S(1)}, bf16[1,16,2,24,768]{4,3,2,1,0:T(8,128)(2,1)}, bf16[1,16,2,24,768]{4,3,2,1,0:T(8,128)(2,1)}, bf16[1,16,2,24,768]{4,3,2,1,0:T(8,128)(2,1)}) fusion(bf16[4,16,2,24,768]{4,3,2,1,0:T(8,128)(2,1)S(1)} %maximum_bitcast_fusion), kind=kLoop, calls=%fused_computation.38 | loop fusion | bytes 9437184 | tf_op jit(solution)/shard_map/slice | solution.py:61
  90.9 7.6 %fusion.2 = f32[2,768,768]{2,1,0:T(8,128)} fusion(bf16[768,768,1]{1,0,2:T(8,128)(2,1)} %bitcast.83, bf16[2,768,768]{2,1,0:T(8,128)(2,1)S(1)} %copy-done), kind=kOutput, calls=%fused_computation.5 | convolution fusion | flops 3625058304 | bytes 8257536 | tf_op jit(solution)/shard_map/pad,bd->pab/dot_general | solution.py:65
  98.6 7.6 %fusion.4 = f32[2,768,768]{2,1,0:T(8,128)} fusion(bf16[768,768,1]{1,0,2:T(8,128)(2,1)} %bitcast.82, bf16[2,768,768]{2,1,0:T(8,128)(2,1)S(1)} %copy-done), kind=kOutput, calls=%fused_computation.7 | convolution fusion | flops 3625058304 | bytes 8257536 | tf_op jit(solution)/shard_map/pad,bd->pab/dot_general | solution.py:65
  106.2 7.7 %fusion.6 = f32[2,768,768]{2,1,0:T(8,128)} fusion(bf16[768,768,1]{1,0,2:T(8,128)(2,1)} %bitcast.81, bf16[2,768,768]{2,1,0:T(8,128)(2,1)S(1)} %copy-done), kind=kOutput, calls=%fused_computation.9 | convolution fusion | flops 3625058304 | bytes 8257536 | tf_op jit(solution)/shard_map/pad,bd->pab/dot_general | solution.py:65
  113.9 8.8 %add_add_fusion = f32[2,768,768]{2,1,0:T(8,128)} fusion(f32[2,768,768]{2,1,0:T(8,128)} %fusion.2, f32[2,768,768]{2,1,0:T(8,128)} %fusion.6, f32[2,768,768]{2,1,0:T(8,128)} %fusion.4, bf16[768,768,1]{1,0,2:T(8,128)(2,1)S(1)} %bitcast.80, bf16[2,768,768]{2,1,0:T(8,128)(2,1)S(1)} %copy-done), kind=kOutput, calls=%fused_computation.2 | convolution fusion | flops 3628597248 | bytes 22413312 | tf_op jit(solution)/shard_map/pad,bd->pab/dot_general | solution.py:65
  122.8 2.2 %fusion.23 = (bf16[2,192,768]{2,1,0:T(8,128)(2,1)S(1)}, bf16[2,192,768]{2,1,0:T(8,128)(2,1)S(1)}, bf16[2,192,768]{2,1,0:T(8,128)(2,1)S(1)}) fusion(f32[2,4,192,768]{3,2,1,0:T(8,128)} %bitcast.78, s32[]{:T(128)S(6)} %select_n.85, s32[]{:T(128)S(6)} %select_n.87, s32[]{:T(128)S(6)} %select_n.89), kind=kLoop, calls=%fused_computation.28 | loop fusion | bytes 3538956 | tf_op jit(solution)/shard_map/convert_element_type | solution.py:43
  125.0 0.1 pad_maximum_fusion
  125.0 1.3 collective-permute-start.1
  126.3 0.1 pad_maximum_fusion.1
  126.4 1.5 collective-permute-start.2
  127.9 19.2 %collective-permute-done.1 = bf16[2,288,768]{2,1,0:T(8,128)(2,1)S(1)} collective-permute-done((bf16[2,288,768]{2,1,0:T(8,128)(2,1)S(1)}, bf16[2,288,768]{2,1,0:T(8,128)(2,1)S(1)}, u32[]{:S(2)}, u32[]{:S(2)}) %collective-permute-start.1) | collective-permute-done | bytes 884768 | tf_op jit(solution)/shard_map/ppermute | solution.py:30
  147.1 0.7 slice.54
  147.9 0.0 collective-permute-start.3
  147.9 0.0 collective-permute-done.2
  147.9 0.9 copy-done.1
  148.8 0.7 slice.55
  149.5 2.7 %collective-permute-start.4 = (bf16[2,96,768]{2,1,0:T(8,128)(2,1)}, bf16[2,96,768]{2,1,0:T(8,128)(2,1)}, u32[]{:S(2)}, u32[]{:S(2)}) collective-permute-start(bf16[2,96,768]{2,1,0:T(8,128)(2,1)} %slice.55), channel_id=1, source_target_pairs={{0,3},{1,0},{2,1},{3,2},{4,7},{5,4},{6,5},{7,6},{8,11},{9,8},{10,9... | collective-permute-start | bytes 884744 | tf_op jit(solution)/shard_map/ppermute | solution.py:30
  152.2 4.4 %collective-permute-done.3 = bf16[2,96,768]{2,1,0:T(8,128)(2,1)S(1)} collective-permute-done((bf16[2,96,768]{2,1,0:T(8,128)(2,1)}, bf16[2,96,768]{2,1,0:T(8,128)(2,1)S(1)}, u32[]{:S(2)}, u32[]{:S(2)}) %collective-permute-start.3) | collective-permute-done | bytes 294944 | tf_op jit(solution)/shard_map/ppermute | solution.py:30
  156.6 0.7 collective-permute-done.4
  157.4 2.7 %fusion.14 = f32[2,192,768]{2,1,0:T(8,128)} fusion(f32[2,4,192,768]{3,2,1,0:T(8,128)} %bitcast.79, s32[]{:T(128)S(6)} %select_n.83, bf16[2,288,768]{2,1,0:T(8,128)(2,1)} %copy-done.1, bf16[2,288,768]{2,1,0:T(8,128)(2,1)S(1)} %collective-permute-done.1, bf16[2,96,768]{2,1,0:T(8,128)(2,1)} %collective-permute-done.4, ...), kind=kLoop, calls=%fused_computation.21 | loop fusion | flops 2654208 | bytes 4128772 | tf_op jit(solution)/shard_map/add | solution.py:51
  (8 shorter events, 0.1 us)
Async XLA Ops:
  6.5 84.4 %copy-start = (bf16[2,768,768]{2,1,0:T(8,128)(2,1)S(1)}, bf16[2,768,768]{2,1,0:T(8,128)(2,1)}, u32[]{:S(2)}) copy-start(bf16[2,768,768]{2,1,0:T(8,128)(2,1)} %param.3) | copy-start | bytes 7077892
  6.5 9.6 %copy-start.2 = (s32[4,4]{1,0:T(4,128)S(1)}, s32[4,4]{1,0:T(4,128)}, u32[]{:S(2)}) copy-start(s32[4,4]{1,0:T(4,128)} %param.5) | copy-start | bytes 196
  6.5 28.1 %all-to-all-start = ((bf16[32,24,768]{2,1,0:T(8,128)(2,1)}), bf16[32,24,768]{2,1,0:T(8,128)(2,1)S(1)}, u32[]{:S(2)}, u32[]{:S(2)}) async-start(bf16[32,24,768]{2,1,0:T(8,128)(2,1)} %bitcast.84), calls=%async_computation | async-start | bytes 2359296 | tf_op jit(solution)/shard_map/all_to_all | solution.py:16
  16.1 63.2 %all-gather.2.cloned.1.call-start = ((), (), s32[]{:S(2)}) async-start(), calls=%async_computation.1 | async-start | bytes 2506752 | tf_op jit(solution)/shard_map/all_gather | solution.py:18
  79.3 6.6 %collective-permute-start = (bf16[16,4,24,768]{3,2,0,1:T(8,128)(2,1)}, bf16[16,4,24,768]{3,2,0,1:T(8,128)(2,1)}, u32[]{:S(2)}, u32[]{:S(2)}) collective-permute-start(bf16[16,4,24,768]{3,2,0,1:T(8,128)(2,1)} %all-gather.2.cloned.1.call-done), channel_id=1, source_target_pairs={{0,4},{4,0},{1,5},{5,1},{2,6},{6,2},{3,7},{7,3},{8,12},{12,8},{9,1... | collective-permute-start | bytes 7077896 | tf_op jit(solution)/shard_map/ppermute | solution.py:20
  125.0 22.1 %collective-permute-start.1 = (bf16[2,288,768]{2,1,0:T(8,128)(2,1)S(1)}, bf16[2,288,768]{2,1,0:T(8,128)(2,1)S(1)}, u32[]{:S(2)}, u32[]{:S(2)}) collective-permute-start(bf16[2,288,768]{2,1,0:T(8,128)(2,1)S(1)} %pad_maximum_fusion), channel_id=1, source_target_pairs={{0,1},{1,2},{2,3},{3,0},{4,5},{5,6},{6,7},{7,4},{8,9},{9,10},{10,1... | collective-permute-start | bytes 2654216 | tf_op jit(solution)/shard_map/ppermute | solution.py:30
  126.4 21.5 %collective-permute-start.2 = (bf16[2,288,768]{2,1,0:T(8,128)(2,1)S(1)}, bf16[2,288,768]{2,1,0:T(8,128)(2,1)S(1)}, u32[]{:S(2)}, u32[]{:S(2)}) collective-permute-start(bf16[2,288,768]{2,1,0:T(8,128)(2,1)S(1)} %pad_maximum_fusion.1), channel_id=1, source_target_pairs={{0,3},{1,0},{2,1},{3,2},{4,7},{5,4},{6,5},{7,6},{8,11},{9,8},{10,9... | collective-permute-start | bytes 2654216 | tf_op jit(solution)/shard_map/ppermute | solution.py:30
  147.9 8.8 %collective-permute-start.3 = (bf16[2,96,768]{2,1,0:T(8,128)(2,1)}, bf16[2,96,768]{2,1,0:T(8,128)(2,1)S(1)}, u32[]{:S(2)}, u32[]{:S(2)}) collective-permute-start(bf16[2,96,768]{2,1,0:T(8,128)(2,1)} %slice.54), channel_id=1, source_target_pairs={{0,1},{1,2},{2,3},{3,0},{4,5},{5,6},{6,7},{7,4},{8,9},{9,10},{10,1... | collective-permute-start | bytes 884744 | tf_op jit(solution)/shard_map/ppermute | solution.py:30
  147.9 0.9 copy-start.1
  149.5 7.8 %collective-permute-start.4 = (bf16[2,96,768]{2,1,0:T(8,128)(2,1)}, bf16[2,96,768]{2,1,0:T(8,128)(2,1)}, u32[]{:S(2)}, u32[]{:S(2)}) collective-permute-start(bf16[2,96,768]{2,1,0:T(8,128)(2,1)} %slice.55), channel_id=1, source_target_pairs={{0,3},{1,0},{2,1},{3,2},{4,7},{5,4},{6,5},{7,6},{8,11},{9,8},{10,9... | collective-permute-start | bytes 884744 | tf_op jit(solution)/shard_map/ppermute | solution.py:30
Sparse Core Ops, SparseCore 0:
  37.6 41.6 all-gather.1

commit v5 on v1

--- a/solution.py
+++ b/solution.py
@@ -11,7 +11,6 @@
 def gather_slots(own_vector, owned_slots):
     rows, cols = own_vector.shape
     devices = lax.psum(1, PAIR)
-    cores = lax.psum(1, "core")
     piece = rows // devices
     pieces = own_vector.reshape(devices, piece, cols)
     pieces = lax.all_to_all(pieces, PAIR, 0, 0, tiled=True)
@@ -27,20 +26,43 @@
     return full.reshape(slots, rows, cols)
 
 
+def shifted(value, step, groups):
+    return lax.ppermute(value, "vgrp", [(g, (g + step) % groups) for g in range(groups)])
+
+
 def on_device(amplitudes, cholesky_vectors, owner_order):
-    vgrp_index = lax.axis_index("vgrp")
-    owned_slots = lax.dynamic_index_in_dim(owner_order, vgrp_index, 0, keepdims=False)
+    vgrp = lax.axis_index("vgrp")
+    groups = lax.psum(1, "vgrp")
+    owned_slots = lax.dynamic_index_in_dim(owner_order, vgrp, 0, keepdims=False)
     vectors = gather_slots(cholesky_vectors[0, 0], owned_slots)
-    accumulated = jnp.zeros(amplitudes.shape, jnp.float32)
-    for slot in range(owned_slots.shape[0]):
-        vector = vectors[slot]
-        half_product = jnp.einsum(
-            "ac,pcd->pad", vector, amplitudes, preferred_element_type=jnp.float32
-        ).astype(jnp.bfloat16)
-        accumulated = accumulated + jnp.einsum(
-            "pad,bd->pab", half_product, vector, preferred_element_type=jnp.float32
-        )
-    return lax.psum_scatter(accumulated, "vgrp", scatter_dimension=1, tiled=True)
+    slots, rows, cols = vectors.shape
+    block = rows // groups
+    half = block // 2
+
+    def partial(offset):
+        start = ((vgrp + offset) % groups) * block
+        mine = lax.dynamic_slice_in_dim(vectors, start, block, axis=1)
+        total = None
+        for slot in range(slots):
+            half_product = jnp.einsum(
+                "ac,pcd->pad", mine[slot], amplitudes, preferred_element_type=jnp.float32
+            ).astype(jnp.bfloat16)
+            term = jnp.einsum(
+                "pad,bd->pab", half_product, vectors[slot], preferred_element_type=jnp.float32
+            )
+            total = term if total is None else total + term
+        return total
+
+    far = partial(2).astype(jnp.bfloat16)
+    far_low = shifted(far[:, :half], 1, groups)
+    far_high = shifted(far[:, half:], -1, groups)
+    far_low = shifted(far_low, 1, groups)
+    far_high = shifted(far_high, -1, groups)
+    ahead = shifted(partial(1).astype(jnp.bfloat16), 1, groups)
+    behind = shifted(partial(-1).astype(jnp.bfloat16), -1, groups)
+    own = partial(0)
+    far = jnp.concatenate([far_low, far_high], axis=1).astype(jnp.float32)
+    return own + ahead.astype(jnp.float32) + behind.astype(jnp.float32) + far
 
 
 def solution(mesh):

time: 180 us -> 180 us (level); the launches traced: 180 us -> 178 us
  waiting for transfers between devices: 115 us -> 72.8 us
  matrix products: 31.8 us -> 59.5 us
  starting transfers between devices: 11.8 us -> 19.7 us
  other arithmetic: 4.77 us -> 7.1 us
  local copies, waits for them, and re-layouts: 3.11 us -> 5.02 us
    reduce_scatter x1 -> x0, waiting for transfers between devices: 50.1 us -> none  [on_device(): lax.psum_scatter(accumulated, 'vgrp', scatter_dimension=1, tiled=True)]
    dot_general x4 -> x16, matrix products: 31.8 us -> 59.5 us  [partial(): jnp.einsum('pad,bd->pab', half_product, vectors[slot], preferred_element_...]
    ppermute x0 -> x6, waiting for transfers between devices: none -> 8.06 us  [shifted(): lax.ppermute(value, 'vgrp', [(g, (g + step) % groups) for g in range(grou...]
    ppermute x0 -> x6, starting transfers between devices: none -> 8.03 us  [shifted(): lax.ppermute(value, 'vgrp', [(g, (g + step) % groups) for g in range(grou...]
    another operation x1 -> x2, other arithmetic: 2.68 us -> 5.42 us  [gather_slots(): full = jnp.stack([low, high], axis=1)]
    slice x1 -> x2, local copies, waits for them, and re-layouts: 1.88 us -> 3.8 us  [the longest x1 1.91 us: partial(): vectors[slot]]
  transfers between devices with their start and end apart: 4 -> 9, of which waited for: 4 -> 5; matrix products, arithmetic and copies ran while one was open for 0% -> 21% of each run, Pallas kernels for 0% -> 0%
where the time goes in v5:
time: 180 us; the launch traced here: 178 us
  waiting for transfers between devices  72.8 us (40%)
  matrix products  59.5 us (33%)
  starting transfers between devices  19.7 us (11%)
  between operations  13.5 us (8%)
  other arithmetic  7.1 us (4%)
  local copies, waits for them, and re-layouts  5.02 us (3%)
    dot_general x16, matrix products, partial(): jnp.einsum('pad,bd->pab', half_product, vectors[slot], preferred_element_...  59.5 us
    all_gather x1, waiting for transfers between devices, gather_slots(): mine = lax.all_gather(picked, CHIPS, axis=0, tiled=False)  41.8 us
    all_to_all x1, waiting for transfers between devices, gather_slots(): pieces = lax.all_to_all(pieces, PAIR, 0, 0, tiled=True)  18.4 us
    all_to_all x1, starting transfers between devices, gather_slots(): pieces = lax.all_to_all(pieces, PAIR, 0, 0, tiled=True)  9.55 us
    ppermute x6, waiting for transfers between devices, shifted(): lax.ppermute(value, 'vgrp', [(g, (g + step) % groups) for g in range(grou...  8.06 us
    ppermute x6, starting transfers between devices, shifted(): lax.ppermute(value, 'vgrp', [(g, (g + step) % groups) for g in range(grou...  8.03 us
    another operation x2, other arithmetic, gather_slots(): full = jnp.stack([low, high], axis=1)  5.42 us
    ppermute x1, waiting for transfers between devices, gather_slots(): other = lax.ppermute(mine, 'core', [(0, 1), (1, 0)])  4.5 us
  transfers between devices with their start and end apart: 9, of which 5 were waited for; matrix products, arithmetic and copies ran while one was open for 21% of the time, Pallas kernels for 0%

profile of v5, /device:TPU:1, one launch (start us, length us, event | category | flops | bytes accessed | tf_op | source)
XLA Modules:
  0.0 177.7 jit_solution(15594841789729798023)
XLA Ops:
  6.5 9.6 %all-to-all-start = ((bf16[32,24,768]{2,1,0:T(8,128)(2,1)}), bf16[32,24,768]{2,1,0:T(8,128)(2,1)S(1)}, u32[]{:S(2)}, u32[]{:S(2)}) async-start(bf16[32,24,768]{2,1,0:T(8,128)(2,1)} %bitcast.243), calls=%async_computation | async-start | bytes 2359296 | tf_op jit(solution)/shard_map/all_to_all | solution.py:16
  16.2 18.4 %all-to-all-done = bf16[32,24,768]{2,1,0:T(8,128)(2,1)S(1)} async-done(((bf16[32,24,768]{2,1,0:T(8,128)(2,1)}), bf16[32,24,768]{2,1,0:T(8,128)(2,1)S(1)}, u32[]{:S(2)}, u32[]{:S(2)}) %all-to-all-start) | async-done | bytes 1179680 | tf_op jit(solution)/shard_map/all_to_all | solution.py:16
  34.6 1.2 gather_fusion
  35.8 1.7 bitcast_select_fusion
  37.5 41.8 %all-gather.2.cloned.1.call-done = bf16[16,4,24,768]{3,2,0,1:T(8,128)(2,1)} async-done(((bf16[1,4,24,768]{3,2,0,1:T(8,128)(2,1)}), bf16[16,4,24,768]{3,2,0,1:T(8,128)(2,1)}) %all-gather.2.cloned.1.call-update) | async-done | bytes 2359312 | tf_op jit(solution)/shard_map/all_gather | solution.py:18
  79.3 2.1 %collective-permute-start = (bf16[16,4,24,768]{3,2,0,1:T(8,128)(2,1)}, bf16[16,4,24,768]{3,2,0,1:T(8,128)(2,1)}, u32[]{:S(2)}, u32[]{:S(2)}) collective-permute-start(bf16[16,4,24,768]{3,2,0,1:T(8,128)(2,1)} %all-gather.2.cloned.1.call-done), channel_id=1, source_target_pairs={{0,4},{4,0},{1,5},{5,1},{2,6},{6,2},{3,7},{7,3},{8,12},{12,8},{9,1... | collective-permute-start | bytes 7077896 | tf_op jit(solution)/shard_map/ppermute | solution.py:20
  81.4 4.5 %collective-permute-done = bf16[16,4,24,768]{3,2,0,1:T(8,128)(2,1)} collective-permute-done((bf16[16,4,24,768]{3,2,0,1:T(8,128)(2,1)}, bf16[16,4,24,768]{3,2,0,1:T(8,128)(2,1)}, u32[]{:S(2)}, u32[]{:S(2)}) %collective-permute-start) | collective-permute-done | bytes 2359328 | tf_op jit(solution)/shard_map/ppermute | solution.py:20
  86.0 2.7 %select_bitcast_fusion.1 = (bf16[16,1,4,24,768]{4,3,1,0,2:T(8,128)(2,1)S(1)}, bf16[16,1,4,24,768]{4,3,1,0,2:T(8,128)(2,1)S(1)}) fusion(bf16[16,4,24,768]{3,2,0,1:T(8,128)(2,1)} %all-gather.2.cloned.1.call-done, bf16[16,4,24,768]{3,2,0,1:T(8,128)(2,1)} %collective-permute-done, pred[]{:T(512)S(6)} %eq.9), kind=kLoop, calls=%fused_computation.3 | loop fusion | flops 2359296 | bytes 9437185 | tf_op jit(solution)/shard_map/stack | solution.py:23
  88.6 2.7 %pad_maximum_fusion = (bf16[16,2,4,24,768]{4,3,1,0,2:T(8,128)(2,1)}, bf16[4,16,2,24,768]{4,3,2,1,0:T(8,128)(2,1)S(1)}) fusion(bf16[16,1,4,24,768]{4,3,1,0,2:T(8,128)(2,1)S(1)} %get-tuple-element.12, bf16[16,1,4,24,768]{4,3,1,0,2:T(8,128)(2,1)S(1)} %get-tuple-element.11), kind=kLoop, calls=%fused_computation.1 | loop fusion | flops 2359296 | bytes 14155776 | tf_op jit(solution)/shard_map/stack | solution.py:23
  91.4 1.9 %fusion.57 = (bf16[1,16,2,24,768]{4,3,2,1,0:T(8,128)(2,1)}, bf16[1,16,2,24,768]{4,3,2,1,0:T(8,128)(2,1)S(1)}, bf16[1,16,2,24,768]{4,3,2,1,0:T(8,128)(2,1)}, bf16[1,16,2,24,768]{4,3,2,1,0:T(8,128)(2,1)}) fusion(bf16[4,16,2,24,768]{4,3,2,1,0:T(8,128)(2,1)S(1)} %get-tuple-element.10), kind=kLoop, calls=%fused_computation.96 | loop fusion | bytes 9437184 | tf_op jit(solution)/shard_map/slice | solution.py:51
  93.3 3.5 %fusion.4 = f32[2,192,768]{2,1,0:T(8,128)} fusion(bf16[768,768,1]{1,0,2:T(8,128)(2,1)} %bitcast.239, bf16[2,768,768]{2,1,0:T(8,128)(2,1)S(1)} %copy-done, bf16[4,768,768]{2,1,0:T(8,128)(2,1)} %bitcast.219, s32[]{:T(128)S(6)} %select_n.82), kind=kOutput, calls=%fused_computation.36 | convolution fusion | flops 906264576 | bytes 5013508 | tf_op jit(solution)/shard_map/pad,bd->pab/dot_general | solution.py:50
  96.8 3.6 %fusion.19 = f32[2,192,768]{2,1,0:T(8,128)} fusion(bf16[768,768,1]{1,0,2:T(8,128)(2,1)} %bitcast.240, bf16[2,768,768]{2,1,0:T(8,128)(2,1)S(1)} %copy-done, bf16[4,768,768]{2,1,0:T(8,128)(2,1)} %bitcast.220, s32[]{:T(128)S(6)} %select_n.88), kind=kOutput, calls=%fused_computation.51 | convolution fusion | flops 906264576 | bytes 5013508 | tf_op jit(solution)/shard_map/pad,bd->pab/dot_general | solution.py:50
  100.4 3.9 %convolution_add_fusion.2 = f32[2,192,768]{2,1,0:T(8,128)} fusion(f32[2,192,768]{2,1,0:T(8,128)} %fusion.19, bf16[768,768,1]{1,0,2:T(8,128)(2,1)} %bitcast.215, bf16[2,768,768]{2,1,0:T(8,128)(2,1)S(1)} %copy-done, bf16[4,768,768]{2,1,0:T(8,128)(2,1)} %bitcast.221, s32[]{:T(128)S(6)} %add.127, s32[]{:T(128)S(6)} %select_n.88), kind=kOutput, calls=%fused_computation.6 | convolution fusion | flops 906559488 | bytes 6193160 | tf_op jit(solution)/shard_map/pad,bd->pab/dot_general | solution.py:50
  104.3 3.6 %convolution_add_fusion.1 = f32[2,192,768]{2,1,0:T(8,128)} fusion(f32[2,192,768]{2,1,0:T(8,128)} %convolution_add_fusion.2, bf16[768,768,1]{1,0,2:T(8,128)(2,1)S(1)} %bitcast.211, bf16[2,768,768]{2,1,0:T(8,128)(2,1)S(1)} %copy-done, bf16[4,768,768]{2,1,0:T(8,128)(2,1)} %bitcast.222, s32[]{:T(128)S(6)} %add.128, s32[]{:T(128)S(6)} %select_n.88), kind=kOutput, calls=%fused_computation.5 | convolution fusion | flops 906559488 | bytes 6193160 | tf_op jit(solution)/shard_map/pad,bd->pab/dot_general | solution.py:50
  107.9 3.6 %fusion.2 = bf16[2,192,768]{2,1,0:T(8,128)(2,1)} fusion(f32[2,192,768]{2,1,0:T(8,128)} %convolution_add_fusion.1, bf16[768,768,1]{1,0,2:T(8,128)(2,1)} %bitcast.235, bf16[2,768,768]{2,1,0:T(8,128)(2,1)S(1)} %copy-done, bf16[4,768,768]{2,1,0:T(8,128)(2,1)} %bitcast.223, s32[]{:T(128)S(6)} %add.129, s32[]{:T(128)S(6)} %select_n.88), kind=kOutput, calls=%fused_computation.18 | convolution fusion | flops 906854400 | bytes 5603336 | tf_op jit(solution)/shard_map/pad,bd->pab/dot_general | solution.py:50
  111.5 1.9 %fusion.58 = (bf16[2,96,768]{2,1,0:T(8,128)(2,1)}, bf16[2,96,768]{2,1,0:T(8,128)(2,1)}) fusion(bf16[2,192,768]{2,1,0:T(8,128)(2,1)} %fusion.2), kind=kLoop, calls=%fused_computation.97 | loop fusion | bytes 1179648 | tf_op jit(solution)/shard_map/slice | solution.py:57
  114.6 1.5 collective-permute-start.5
  116.1 3.6 %fusion.9 = f32[2,192,768]{2,1,0:T(8,128)} fusion(bf16[768,768,1]{1,0,2:T(8,128)(2,1)} %bitcast.241, bf16[2,768,768]{2,1,0:T(8,128)(2,1)S(1)} %copy-done, bf16[4,768,768]{2,1,0:T(8,128)(2,1)} %bitcast.224, s32[]{:T(128)S(6)} %select_n.84), kind=kOutput, calls=%fused_computation.41 | convolution fusion | flops 906264576 | bytes 5013508 | tf_op jit(solution)/shard_map/pad,bd->pab/dot_general | solution.py:50
  119.7 3.9 %convolution_add_fusion.8 = f32[2,192,768]{2,1,0:T(8,128)} fusion(f32[2,192,768]{2,1,0:T(8,128)} %fusion.9, bf16[768,768,1]{1,0,2:T(8,128)(2,1)} %bitcast.216, bf16[2,768,768]{2,1,0:T(8,128)(2,1)S(1)} %copy-done, bf16[4,768,768]{2,1,0:T(8,128)(2,1)} %bitcast.225, s32[]{:T(128)S(6)} %add.127, s32[]{:T(128)S(6)} %select_n.84), kind=kOutput, calls=%fused_computation.12 | convolution fusion | flops 906559488 | bytes 6193160 | tf_op jit(solution)/shard_map/pad,bd->pab/dot_general | solution.py:50
  123.6 3.6 %convolution_add_fusion.7 = f32[2,192,768]{2,1,0:T(8,128)} fusion(f32[2,192,768]{2,1,0:T(8,128)} %convolution_add_fusion.8, bf16[768,768,1]{1,0,2:T(8,128)(2,1)S(1)} %bitcast.212, bf16[2,768,768]{2,1,0:T(8,128)(2,1)S(1)} %copy-done, bf16[4,768,768]{2,1,0:T(8,128)(2,1)} %bitcast.226, s32[]{:T(128)S(6)} %add.128, s32[]{:T(128)S(6)} %select_n.84), kind=kOutput, calls=%fused_computation.11 | convolution fusion | flops 906559488 | bytes 6193160 | tf_op jit(solution)/shard_map/pad,bd->pab/dot_general | solution.py:50
  127.2 3.7 %fusion = bf16[2,192,768]{2,1,0:T(8,128)(2,1)} fusion(f32[2,192,768]{2,1,0:T(8,128)} %convolution_add_fusion.7, bf16[768,768,1]{1,0,2:T(8,128)(2,1)} %bitcast.236, bf16[2,768,768]{2,1,0:T(8,128)(2,1)S(1)} %copy-done, bf16[4,768,768]{2,1,0:T(8,128)(2,1)} %bitcast.227, s32[]{:T(128)S(6)} %add.129, s32[]{:T(128)S(6)} %select_n.84), kind=kOutput, calls=%fused_computation.16 | convolution fusion | flops 906854400 | bytes 5603336 | tf_op jit(solution)/shard_map/pad,bd->pab/dot_general | solution.py:50
  130.8 3.6 %fusion.14 = f32[2,192,768]{2,1,0:T(8,128)} fusion(bf16[768,768,1]{1,0,2:T(8,128)(2,1)} %bitcast.242, bf16[2,768,768]{2,1,0:T(8,128)(2,1)S(1)} %copy-done, bf16[4,768,768]{2,1,0:T(8,128)(2,1)} %bitcast.228, s32[]{:T(128)S(6)} %select_n.86), kind=kOutput, calls=%fused_computation.46 | convolution fusion | flops 906264576 | bytes 5013508 | tf_op jit(solution)/shard_map/pad,bd->pab/dot_general | solution.py:50
  134.4 3.9 %convolution_add_fusion.5 = f32[2,192,768]{2,1,0:T(8,128)} fusion(f32[2,192,768]{2,1,0:T(8,128)} %fusion.14, bf16[768,768,1]{1,0,2:T(8,128)(2,1)} %bitcast.217, bf16[2,768,768]{2,1,0:T(8,128)(2,1)S(1)} %copy-done, bf16[4,768,768]{2,1,0:T(8,128)(2,1)} %bitcast.229, s32[]{:T(128)S(6)} %add.127, s32[]{:T(128)S(6)} %select_n.86), kind=kOutput, calls=%fused_computation.9 | convolution fusion | flops 906559488 | bytes 6193160 | tf_op jit(solution)/shard_map/pad,bd->pab/dot_general | solution.py:50
  138.3 3.6 %convolution_add_fusion.4 = f32[2,192,768]{2,1,0:T(8,128)} fusion(f32[2,192,768]{2,1,0:T(8,128)} %convolution_add_fusion.5, bf16[768,768,1]{1,0,2:T(8,128)(2,1)S(1)} %bitcast.213, bf16[2,768,768]{2,1,0:T(8,128)(2,1)S(1)} %copy-done, bf16[4,768,768]{2,1,0:T(8,128)(2,1)} %bitcast.230, s32[]{:T(128)S(6)} %add.128, s32[]{:T(128)S(6)} %select_n.86), kind=kOutput, calls=%fused_computation.8 | convolution fusion | flops 906559488 | bytes 6193160 | tf_op jit(solution)/shard_map/pad,bd->pab/dot_general | solution.py:50
  141.9 3.7 %fusion.1 = bf16[2,192,768]{2,1,0:T(8,128)(2,1)} fusion(f32[2,192,768]{2,1,0:T(8,128)} %convolution_add_fusion.4, bf16[768,768,1]{1,0,2:T(8,128)(2,1)} %bitcast.237, bf16[2,768,768]{2,1,0:T(8,128)(2,1)S(1)} %copy-done, bf16[4,768,768]{2,1,0:T(8,128)(2,1)} %bitcast.231, s32[]{:T(128)S(6)} %add.129, s32[]{:T(128)S(6)} %select_n.86), kind=kOutput, calls=%fused_computation.17 | convolution fusion | flops 906854400 | bytes 5603336 | tf_op jit(solution)/shard_map/pad,bd->pab/dot_general | solution.py:50
  145.6 2.7 %collective-permute-start.2 = (bf16[2,192,768]{2,1,0:T(8,128)(2,1)}, bf16[2,192,768]{2,1,0:T(8,128)(2,1)}, u32[]{:S(2)}, u32[]{:S(2)}) collective-permute-start(bf16[2,192,768]{2,1,0:T(8,128)(2,1)} %fusion.1), channel_id=1, source_target_pairs={{0,3},{1,0},{2,1},{3,2},{4,7},{5,4},{6,5},{7,6},{8,11},{9,8},{10,9... | collective-permute-start | bytes 1769480 | tf_op jit(solution)/shard_map/ppermute | solution.py:30
  148.3 3.9 %convolution_add_fusion.11 = f32[2,192,768]{2,1,0:T(8,128)} fusion(f32[2,192,768]{2,1,0:T(8,128)} %fusion.4, bf16[768,768,1]{1,0,2:T(8,128)(2,1)} %bitcast.218, bf16[2,768,768]{2,1,0:T(8,128)(2,1)S(1)} %copy-done, bf16[4,768,768]{2,1,0:T(8,128)(2,1)} %bitcast.232, s32[]{:T(128)S(6)} %add.127, s32[]{:T(128)S(6)} %select_n.82), kind=kOutput, calls=%fused_computation.15 | convolution fusion | flops 906559488 | bytes 6193160 | tf_op jit(solution)/shard_map/pad,bd->pab/dot_general | solution.py:50
  152.1 2.7 %collective-permute-start.6 = (bf16[2,96,768]{2,1,0:T(8,128)(2,1)}, bf16[2,96,768]{2,1,0:T(8,128)(2,1)}, u32[]{:S(2)}, u32[]{:S(2)}) collective-permute-start(bf16[2,96,768]{2,1,0:T(8,128)(2,1)} %collective-permute-done.5), channel_id=1, source_target_pairs={{0,3},{1,0},{2,1},{3,2},{4,7},{5,4},{6,5},{7,6},{8,11},{9,8},{10,9... | collective-permute-start | bytes 884744 | tf_op jit(solution)/shard_map/ppermute | solution.py:30
  154.8 3.5 %convolution_add_fusion.10 = f32[2,192,768]{2,1,0:T(8,128)} fusion(f32[2,192,768]{2,1,0:T(8,128)} %convolution_add_fusion.11, bf16[768,768,1]{1,0,2:T(8,128)(2,1)S(1)} %bitcast.214, bf16[2,768,768]{2,1,0:T(8,128)(2,1)S(1)} %copy-done, bf16[4,768,768]{2,1,0:T(8,128)(2,1)} %bitcast.233, s32[]{:T(128)S(6)} %add.128, s32[]{:T(128)S(6)} %select_n.82), kind=kOutput, calls=%fused_computation.14 | convolution fusion | flops 906559488 | bytes 6193160 | tf_op jit(solution)/shard_map/pad,bd->pab/dot_general | solution.py:50
  158.3 2.4 %collective-permute-done.4 = bf16[2,96,768]{2,1,0:T(8,128)(2,1)} collective-permute-done((bf16[2,96,768]{2,1,0:T(8,128)(2,1)}, bf16[2,96,768]{2,1,0:T(8,128)(2,1)}, u32[]{:S(2)}, u32[]{:S(2)}) %collective-permute-start.4) | collective-permute-done | bytes 294944 | tf_op jit(solution)/shard_map/ppermute | solution.py:30
  160.7 5.6 %collective-permute-done.6 = bf16[2,96,768]{2,1,0:T(8,128)(2,1)} collective-permute-done((bf16[2,96,768]{2,1,0:T(8,128)(2,1)}, bf16[2,96,768]{2,1,0:T(8,128)(2,1)}, u32[]{:S(2)}, u32[]{:S(2)}) %collective-permute-start.6) | collective-permute-done | bytes 294944 | tf_op jit(solution)/shard_map/ppermute | solution.py:30
  166.4 4.5 %convert_add_fusion = f32[2,192,768]{2,1,0:T(8,128)} fusion(bf16[2,192,768]{2,1,0:T(8,128)(2,1)} %collective-permute-done.2, bf16[2,192,768]{2,1,0:T(8,128)(2,1)} %collective-permute-done.1, bf16[2,96,768]{2,1,0:T(8,128)(2,1)} %collective-permute-done.6, bf16[2,96,768]{2,1,0:T(8,128)(2,1)} %collective-permute-done.4, ...), kind=kOutput, calls=%fused_computation.55 | convolution fusion | flops 909213696 | bytes 7962632 | tf_op jit(solution)/shard_map/pad,bd->pab/dot_general | solution.py:50
  (16 shorter events, 1.3 us)
Async XLA Ops:
  6.5 86.8 %copy-start = (bf16[2,768,768]{2,1,0:T(8,128)(2,1)S(1)}, bf16[2,768,768]{2,1,0:T(8,128)(2,1)}, u32[]{:S(2)}) copy-start(bf16[2,768,768]{2,1,0:T(8,128)(2,1)} %param.3) | copy-start | bytes 7077892
  6.5 9.6 %copy-start.1 = (s32[4,4]{1,0:T(4,128)S(1)}, s32[4,4]{1,0:T(4,128)}, u32[]{:S(2)}) copy-start(s32[4,4]{1,0:T(4,128)} %param.5) | copy-start | bytes 196
  6.5 28.1 %all-to-all-start = ((bf16[32,24,768]{2,1,0:T(8,128)(2,1)}), bf16[32,24,768]{2,1,0:T(8,128)(2,1)S(1)}, u32[]{:S(2)}, u32[]{:S(2)}) async-start(bf16[32,24,768]{2,1,0:T(8,128)(2,1)} %bitcast.243), calls=%async_computation | async-start | bytes 2359296 | tf_op jit(solution)/shard_map/all_to_all | solution.py:16
  16.1 63.2 %all-gather.2.cloned.1.call-start = ((), (), s32[]{:S(2)}) async-start(), calls=%async_computation.1 | async-start | bytes 2506752 | tf_op jit(solution)/shard_map/all_gather | solution.py:18
  79.3 6.6 %collective-permute-start = (bf16[16,4,24,768]{3,2,0,1:T(8,128)(2,1)}, bf16[16,4,24,768]{3,2,0,1:T(8,128)(2,1)}, u32[]{:S(2)}, u32[]{:S(2)}) collective-permute-start(bf16[16,4,24,768]{3,2,0,1:T(8,128)(2,1)} %all-gather.2.cloned.1.call-done), channel_id=1, source_target_pairs={{0,4},{4,0},{1,5},{5,1},{2,6},{6,2},{3,7},{7,3},{8,12},{12,8},{9,1... | collective-permute-start | bytes 7077896 | tf_op jit(solution)/shard_map/ppermute | solution.py:20
  113.4 38.7 %collective-permute-start.3 = (bf16[2,96,768]{2,1,0:T(8,128)(2,1)}, bf16[2,96,768]{2,1,0:T(8,128)(2,1)}, u32[]{:S(2)}, u32[]{:S(2)}) collective-permute-start(bf16[2,96,768]{2,1,0:T(8,128)(2,1)} %get-tuple-element.13), channel_id=1, source_target_pairs={{0,1},{1,2},{2,3},{3,0},{4,5},{5,6},{6,7},{7,4},{8,9},{9,10},{10,1... | collective-permute-start | bytes 884744 | tf_op jit(solution)/shard_map/ppermute | solution.py:30
  114.6 37.5 %collective-permute-start.5 = (bf16[2,96,768]{2,1,0:T(8,128)(2,1)}, bf16[2,96,768]{2,1,0:T(8,128)(2,1)}, u32[]{:S(2)}, u32[]{:S(2)}) collective-permute-start(bf16[2,96,768]{2,1,0:T(8,128)(2,1)} %get-tuple-element.14), channel_id=1, source_target_pairs={{0,3},{1,0},{2,1},{3,2},{4,7},{5,4},{6,5},{7,6},{8,11},{9,8},{10,9... | collective-permute-start | bytes 884744 | tf_op jit(solution)/shard_map/ppermute | solution.py:30
  130.8 35.6 %collective-permute-start.1 = (bf16[2,192,768]{2,1,0:T(8,128)(2,1)}, bf16[2,192,768]{2,1,0:T(8,128)(2,1)}, u32[]{:S(2)}, u32[]{:S(2)}) collective-permute-start(bf16[2,192,768]{2,1,0:T(8,128)(2,1)} %fusion), channel_id=1, source_target_pairs={{0,1},{1,2},{2,3},{3,0},{4,5},{5,6},{6,7},{7,4},{8,9},{9,10},{10,1... | collective-permute-start | bytes 1769480 | tf_op jit(solution)/shard_map/ppermute | solution.py:30
  145.6 20.8 %collective-permute-start.2 = (bf16[2,192,768]{2,1,0:T(8,128)(2,1)}, bf16[2,192,768]{2,1,0:T(8,128)(2,1)}, u32[]{:S(2)}, u32[]{:S(2)}) collective-permute-start(bf16[2,192,768]{2,1,0:T(8,128)(2,1)} %fusion.1), channel_id=1, source_target_pairs={{0,3},{1,0},{2,1},{3,2},{4,7},{5,4},{6,5},{7,6},{8,11},{9,8},{10,9... | collective-permute-start | bytes 1769480 | tf_op jit(solution)/shard_map/ppermute | solution.py:30
  152.1 8.6 %collective-permute-start.4 = (bf16[2,96,768]{2,1,0:T(8,128)(2,1)}, bf16[2,96,768]{2,1,0:T(8,128)(2,1)}, u32[]{:S(2)}, u32[]{:S(2)}) collective-permute-start(bf16[2,96,768]{2,1,0:T(8,128)(2,1)} %collective-permute-done.3), channel_id=1, source_target_pairs={{0,1},{1,2},{2,3},{3,0},{4,5},{5,6},{6,7},{7,4},{8,9},{9,10},{10,1... | collective-permute-start | bytes 884744 | tf_op jit(solution)/shard_map/ppermute | solution.py:30
  152.1 14.2 %collective-permute-start.6 = (bf16[2,96,768]{2,1,0:T(8,128)(2,1)}, bf16[2,96,768]{2,1,0:T(8,128)(2,1)}, u32[]{:S(2)}, u32[]{:S(2)}) collective-permute-start(bf16[2,96,768]{2,1,0:T(8,128)(2,1)} %collective-permute-done.5), channel_id=1, source_target_pairs={{0,3},{1,0},{2,1},{3,2},{4,7},{5,4},{6,5},{7,6},{8,11},{9,8},{10,9... | collective-permute-start | bytes 884744 | tf_op jit(solution)/shard_map/ppermute | solution.py:30
Sparse Core Ops, SparseCore 0:
  37.6 41.6 all-gather.1

commit v6 on v4

--- a/solution.py
+++ b/solution.py
@@ -33,22 +33,16 @@
 def scatter_sum(total, vgrp, groups):
     pairs, rows, cols = total.shape
     block = rows // groups
-    half = block // 2
     blocks = total.reshape(pairs, groups, block, cols)
 
     def pick(offset):
         return lax.dynamic_index_in_dim(blocks, (vgrp + offset) % groups, 1, keepdims=False)
 
-    far = pick(2).astype(jnp.bfloat16)
-    ahead = jnp.concatenate([pick(1).astype(jnp.bfloat16), far[:, :half]], axis=1)
-    behind = jnp.concatenate([pick(-1).astype(jnp.bfloat16), far[:, half:]], axis=1)
-    ahead = shifted(ahead, 1, groups)
-    behind = shifted(behind, -1, groups)
-    far_low = shifted(ahead[:, block:], 1, groups)
-    far_high = shifted(behind[:, block:], -1, groups)
-    far = jnp.concatenate([far_low, far_high], axis=1).astype(jnp.float32)
-    near = ahead[:, :block].astype(jnp.float32) + behind[:, :block].astype(jnp.float32)
-    return pick(0) + near + far
+    ahead = shifted(pick(1).astype(jnp.bfloat16), 1, groups)
+    behind = shifted(pick(-1).astype(jnp.bfloat16), -1, groups)
+    far = shifted(pick(2).astype(jnp.bfloat16), 2, groups)
+    near = ahead.astype(jnp.float32) + behind.astype(jnp.float32)
+    return pick(0) + near + far.astype(jnp.float32)
 
 
 def on_device(amplitudes, cholesky_vectors, owner_order):

time: 169 us -> 166 us (0.982)
    ppermute x4 -> x3, starting transfers between devices: 5.49 us -> 4.2 us  [shifted(): lax.ppermute(value, 'vgrp', [(g, (g + step) % groups) for g in range(grou...]
    ppermute x4 -> x3, waiting for transfers between devices: 24.4 us -> 25.5 us  [shifted(): lax.ppermute(value, 'vgrp', [(g, (g + step) % groups) for g in range(grou...]
  transfers between devices with their start and end apart: 7 -> 6, of which waited for: 6 -> 5; matrix products, arithmetic and copies ran while one was open for 1% -> 0% of each run, Pallas kernels for 0% -> 0%
where the time goes in v6:
time: 166 us; the launch traced here: 165 us
  waiting for transfers between devices  90.2 us (54%)
  matrix products  31.8 us (19%)
  starting transfers between devices  15.9 us (10%)
  between operations  13.5 us (8%)
  other arithmetic  7.47 us (4%)
  local copies, waits for them, and re-layouts  6.35 us (4%)
    all_gather x1, waiting for transfers between devices, gather_slots(): mine = lax.all_gather(picked, CHIPS, axis=0, tiled=False)  41.8 us
    dot_general x4, matrix products, on_device(): jnp.einsum('pad,bd->pab', half_product, vector, preferred_element_type=jn...  31.8 us
    ppermute x3, waiting for transfers between devices, shifted(): lax.ppermute(value, 'vgrp', [(g, (g + step) % groups) for g in range(grou...  25.5 us
    all_to_all x1, waiting for transfers between devices, gather_slots(): pieces = lax.all_to_all(pieces, PAIR, 0, 0, tiled=True)  18.4 us
    all_to_all x1, starting transfers between devices, gather_slots(): pieces = lax.all_to_all(pieces, PAIR, 0, 0, tiled=True)  9.55 us
    ppermute x1, waiting for transfers between devices, gather_slots(): other = lax.ppermute(mine, 'core', [(0, 1), (1, 0)])  4.5 us
    ppermute x3, starting transfers between devices, shifted(): lax.ppermute(value, 'vgrp', [(g, (g + step) % groups) for g in range(grou...  4.2 us
  transfers between devices with their start and end apart: 6, of which 5 were waited for; matrix products, arithmetic and copies ran while one was open for 0% of the time, Pallas kernels for 0%

profile of v6, /device:TPU:1, one launch (start us, length us, event | category | flops | bytes accessed | tf_op | source)
XLA Modules:
  0.0 165.2 jit_solution(2939116574654734975)
XLA Ops:
  6.5 0.0 copy-start
  6.5 0.0 copy-start.1
  6.5 9.6 %all-to-all-start = ((bf16[32,24,768]{2,1,0:T(8,128)(2,1)}), bf16[32,24,768]{2,1,0:T(8,128)(2,1)S(1)}, u32[]{:S(2)}, u32[]{:S(2)}) async-start(bf16[32,24,768]{2,1,0:T(8,128)(2,1)} %bitcast.84), calls=%async_computation | async-start | bytes 2359296 | tf_op jit(solution)/shard_map/all_to_all | solution.py:16
  16.1 0.0 all-gather.2.cloned.1.call-start
  16.2 0.0 copy-done.1
  16.2 18.4 %all-to-all-done = bf16[32,24,768]{2,1,0:T(8,128)(2,1)S(1)} async-done(((bf16[32,24,768]{2,1,0:T(8,128)(2,1)}), bf16[32,24,768]{2,1,0:T(8,128)(2,1)S(1)}, u32[]{:S(2)}, u32[]{:S(2)}) %all-to-all-start) | async-done | bytes 1179680 | tf_op jit(solution)/shard_map/all_to_all | solution.py:16
  34.6 1.2 gather_fusion
  35.8 1.7 bitcast_select_fusion
  37.5 0.0 all-gather.2.cloned.1.call-update
  37.5 41.8 %all-gather.2.cloned.1.call-done = bf16[16,4,24,768]{3,2,0,1:T(8,128)(2,1)} async-done(((bf16[1,4,24,768]{3,2,0,1:T(8,128)(2,1)}), bf16[16,4,24,768]{3,2,0,1:T(8,128)(2,1)}) %all-gather.2.cloned.1.call-update) | async-done | bytes 2359312 | tf_op jit(solution)/shard_map/all_gather | solution.py:18
  79.3 2.1 %collective-permute-start = (bf16[16,4,24,768]{3,2,0,1:T(8,128)(2,1)}, bf16[16,4,24,768]{3,2,0,1:T(8,128)(2,1)}, u32[]{:S(2)}, u32[]{:S(2)}) collective-permute-start(bf16[16,4,24,768]{3,2,0,1:T(8,128)(2,1)} %all-gather.2.cloned.1.call-done), channel_id=1, source_target_pairs={{0,4},{4,0},{1,5},{5,1},{2,6},{6,2},{3,7},{7,3},{8,12},{12,8},{9,1... | collective-permute-start | bytes 7077896 | tf_op jit(solution)/shard_map/ppermute | solution.py:20
  81.4 4.5 %collective-permute-done = bf16[16,4,24,768]{3,2,0,1:T(8,128)(2,1)} collective-permute-done((bf16[16,4,24,768]{3,2,0,1:T(8,128)(2,1)}, bf16[16,4,24,768]{3,2,0,1:T(8,128)(2,1)}, u32[]{:S(2)}, u32[]{:S(2)}) %collective-permute-start) | collective-permute-done | bytes 2359328 | tf_op jit(solution)/shard_map/ppermute | solution.py:20
  86.0 2.7 %select_bitcast_fusion.1 = (bf16[16,1,4,24,768]{4,3,1,0,2:T(8,128)(2,1)S(1)}, bf16[16,1,4,24,768]{4,3,1,0,2:T(8,128)(2,1)S(1)}) fusion(bf16[16,4,24,768]{3,2,0,1:T(8,128)(2,1)} %all-gather.2.cloned.1.call-done, bf16[16,4,24,768]{3,2,0,1:T(8,128)(2,1)} %collective-permute-done, pred[]{:T(512)S(6)} %eq.9), kind=kLoop, calls=%fused_computation.16 | loop fusion | flops 2359296 | bytes 9437185 | tf_op jit(solution)/shard_map/stack | solution.py:23
  88.6 0.4 maximum_bitcast_fusion
  89.1 1.9 %fusion.27 = (bf16[1,16,2,24,768]{4,3,2,1,0:T(8,128)(2,1)S(1)}, bf16[1,16,2,24,768]{4,3,2,1,0:T(8,128)(2,1)}, bf16[1,16,2,24,768]{4,3,2,1,0:T(8,128)(2,1)}, bf16[1,16,2,24,768]{4,3,2,1,0:T(8,128)(2,1)}) fusion(bf16[4,16,2,24,768]{4,3,2,1,0:T(8,128)(2,1)S(1)} %maximum_bitcast_fusion), kind=kLoop, calls=%fused_computation.36 | loop fusion | bytes 9437184 | tf_op jit(solution)/shard_map/slice | solution.py:55
  90.9 0.0 copy-done
  90.9 7.7 %fusion.2 = f32[2,768,768]{2,1,0:T(8,128)} fusion(bf16[768,768,1]{1,0,2:T(8,128)(2,1)} %bitcast.83, bf16[2,768,768]{2,1,0:T(8,128)(2,1)S(1)} %copy-done), kind=kOutput, calls=%fused_computation.5 | convolution fusion | flops 3625058304 | bytes 8257536 | tf_op jit(solution)/shard_map/pad,bd->pab/dot_general | solution.py:59
  98.6 7.6 %fusion.4 = f32[2,768,768]{2,1,0:T(8,128)} fusion(bf16[768,768,1]{1,0,2:T(8,128)(2,1)} %bitcast.82, bf16[2,768,768]{2,1,0:T(8,128)(2,1)S(1)} %copy-done), kind=kOutput, calls=%fused_computation.7 | convolution fusion | flops 3625058304 | bytes 8257536 | tf_op jit(solution)/shard_map/pad,bd->pab/dot_general | solution.py:59
  106.2 7.7 %fusion.6 = f32[2,768,768]{2,1,0:T(8,128)} fusion(bf16[768,768,1]{1,0,2:T(8,128)(2,1)} %bitcast.81, bf16[2,768,768]{2,1,0:T(8,128)(2,1)S(1)} %copy-done), kind=kOutput, calls=%fused_computation.9 | convolution fusion | flops 3625058304 | bytes 8257536 | tf_op jit(solution)/shard_map/pad,bd->pab/dot_general | solution.py:59
  113.9 8.8 %add_add_fusion = f32[2,768,768]{2,1,0:T(8,128)} fusion(f32[2,768,768]{2,1,0:T(8,128)} %fusion.2, f32[2,768,768]{2,1,0:T(8,128)} %fusion.6, f32[2,768,768]{2,1,0:T(8,128)} %fusion.4, bf16[768,768,1]{1,0,2:T(8,128)(2,1)S(1)} %bitcast.80, bf16[2,768,768]{2,1,0:T(8,128)(2,1)S(1)} %copy-done), kind=kOutput, calls=%fused_computation.2 | convolution fusion | flops 3628597248 | bytes 22413312 | tf_op jit(solution)/shard_map/pad,bd->pab/dot_general | solution.py:59
  122.8 3.3 %fusion.23 = (bf16[2,192,768]{2,1,0:T(8,128)(2,1)}, bf16[2,192,768]{2,1,0:T(8,128)(2,1)}, bf16[2,192,768]{2,1,0:T(8,128)(2,1)}) fusion(f32[2,4,192,768]{3,2,1,0:T(8,128)} %bitcast.78, s32[]{:T(128)S(6)} %select_n.85, s32[]{:T(128)S(6)} %select_n.87, s32[]{:T(128)S(6)} %select_n.89), kind=kLoop, calls=%fused_computation.26 | loop fusion | bytes 3538956 | tf_op jit(solution)/shard_map/convert_element_type | solution.py:41
  126.0 1.2 collective-permute-start.1
  127.2 1.5 collective-permute-start.2
  128.7 1.5 collective-permute-start.3
  130.2 11.7 %collective-permute-done.1 = bf16[2,192,768]{2,1,0:T(8,128)(2,1)S(1)} collective-permute-done((bf16[2,192,768]{2,1,0:T(8,128)(2,1)}, bf16[2,192,768]{2,1,0:T(8,128)(2,1)S(1)}, u32[]{:S(2)}, u32[]{:S(2)}) %collective-permute-start.1) | collective-permute-done | bytes 589856 | tf_op jit(solution)/shard_map/ppermute | solution.py:30
  141.9 0.0 collective-permute-done.2
  141.9 13.7 %collective-permute-done.3 = bf16[2,192,768]{2,1,0:T(8,128)(2,1)} collective-permute-done((bf16[2,192,768]{2,1,0:T(8,128)(2,1)}, bf16[2,192,768]{2,1,0:T(8,128)(2,1)}, u32[]{:S(2)}, u32[]{:S(2)}) %collective-permute-start.3) | collective-permute-done | bytes 589856 | tf_op jit(solution)/shard_map/ppermute | solution.py:30
  155.7 2.7 %fusion.14 = f32[2,192,768]{2,1,0:T(8,128)} fusion(bf16[2,192,768]{2,1,0:T(8,128)(2,1)} %collective-permute-done.3, bf16[2,192,768]{2,1,0:T(8,128)(2,1)S(1)} %collective-permute-done.2, bf16[2,192,768]{2,1,0:T(8,128)(2,1)S(1)} %collective-permute-done.1, f32[2,4,192,768]{3,2,1,0:T(8,128)} %bitcast.79, s32[]{:T(128)S(6)} %select_n.83), kind=kLoop, calls=%fused_computation.21 | loop fusion | flops 1769472 | bytes 4128772 | tf_op jit(solution)/shard_map/add | solution.py:45
  (3 shorter events, 0.0 us)
Async XLA Ops:
  6.5 84.4 %copy-start = (bf16[2,768,768]{2,1,0:T(8,128)(2,1)S(1)}, bf16[2,768,768]{2,1,0:T(8,128)(2,1)}, u32[]{:S(2)}) copy-start(bf16[2,768,768]{2,1,0:T(8,128)(2,1)} %param.3) | copy-start | bytes 7077892
  6.5 9.6 %copy-start.1 = (s32[4,4]{1,0:T(4,128)S(1)}, s32[4,4]{1,0:T(4,128)}, u32[]{:S(2)}) copy-start(s32[4,4]{1,0:T(4,128)} %param.5) | copy-start | bytes 196
  6.5 28.1 %all-to-all-start = ((bf16[32,24,768]{2,1,0:T(8,128)(2,1)}), bf16[32,24,768]{2,1,0:T(8,128)(2,1)S(1)}, u32[]{:S(2)}, u32[]{:S(2)}) async-start(bf16[32,24,768]{2,1,0:T(8,128)(2,1)} %bitcast.84), calls=%async_computation | async-start | bytes 2359296 | tf_op jit(solution)/shard_map/all_to_all | solution.py:16
  16.1 63.2 %all-gather.2.cloned.1.call-start = ((), (), s32[]{:S(2)}) async-start(), calls=%async_computation.1 | async-start | bytes 2506752 | tf_op jit(solution)/shard_map/all_gather | solution.py:18
  79.3 6.6 %collective-permute-start = (bf16[16,4,24,768]{3,2,0,1:T(8,128)(2,1)}, bf16[16,4,24,768]{3,2,0,1:T(8,128)(2,1)}, u32[]{:S(2)}, u32[]{:S(2)}) collective-permute-start(bf16[16,4,24,768]{3,2,0,1:T(8,128)(2,1)} %all-gather.2.cloned.1.call-done), channel_id=1, source_target_pairs={{0,4},{4,0},{1,5},{5,1},{2,6},{6,2},{3,7},{7,3},{8,12},{12,8},{9,1... | collective-permute-start | bytes 7077896 | tf_op jit(solution)/shard_map/ppermute | solution.py:20
  126.0 15.9 %collective-permute-start.1 = (bf16[2,192,768]{2,1,0:T(8,128)(2,1)}, bf16[2,192,768]{2,1,0:T(8,128)(2,1)S(1)}, u32[]{:S(2)}, u32[]{:S(2)}) collective-permute-start(bf16[2,192,768]{2,1,0:T(8,128)(2,1)} %get-tuple-element.5), channel_id=1, source_target_pairs={{0,1},{1,2},{2,3},{3,0},{4,5},{5,6},{6,7},{7,4},{8,9},{9,10},{10,1... | collective-permute-start | bytes 1769480 | tf_op jit(solution)/shard_map/ppermute | solution.py:30
  127.2 14.7 %collective-permute-start.2 = (bf16[2,192,768]{2,1,0:T(8,128)(2,1)}, bf16[2,192,768]{2,1,0:T(8,128)(2,1)S(1)}, u32[]{:S(2)}, u32[]{:S(2)}) collective-permute-start(bf16[2,192,768]{2,1,0:T(8,128)(2,1)} %get-tuple-element.6), channel_id=1, source_target_pairs={{0,3},{1,0},{2,1},{3,2},{4,7},{5,4},{6,5},{7,6},{8,11},{9,8},{10,9... | collective-permute-start | bytes 1769480 | tf_op jit(solution)/shard_map/ppermute | solution.py:30
  128.7 27.0 %collective-permute-start.3 = (bf16[2,192,768]{2,1,0:T(8,128)(2,1)}, bf16[2,192,768]{2,1,0:T(8,128)(2,1)}, u32[]{:S(2)}, u32[]{:S(2)}) collective-permute-start(bf16[2,192,768]{2,1,0:T(8,128)(2,1)} %get-tuple-element.7), channel_id=1, source_target_pairs={{0,2},{1,3},{2,0},{3,1},{4,6},{5,7},{6,4},{7,5},{8,10},{9,11},{10,... | collective-permute-start | bytes 1769480 | tf_op jit(solution)/shard_map/ppermute | solution.py:30
Sparse Core Ops, SparseCore 0:
  37.6 41.6 all-gather.1

commit v7 on v2

--- a/solution.py
+++ b/solution.py
@@ -6,6 +6,8 @@
 
 PAIR = ("z", "x", "core")
 CHIPS = ("z", "x")
+
+
 RING = 4
 
 
@@ -63,8 +65,27 @@
     inner = jnp.where(cq == 0, dz * nx + dx, dx * nz + dz)
     index = jnp.where(cq == core, 0, chips) + inner
     ordered = jnp.take(stacked, index, axis=0)
-    ordered = jnp.transpose(ordered, (0, 2, 1, 3))
-    return ordered.reshape(rows, slots, cols)
+    ordered = jnp.transpose(ordered, (1, 0, 2, 3))
+    return ordered.reshape(slots, rows, cols)
+
+
+def shifted(value, step, groups):
+    return lax.ppermute(value, "vgrp", [(g, (g + step) % groups) for g in range(groups)])
+
+
+def scatter_sum(total, vgrp, groups):
+    pairs, rows, cols = total.shape
+    block = rows // groups
+    blocks = total.reshape(pairs, groups, block, cols)
+
+    def pick(offset):
+        return lax.dynamic_index_in_dim(blocks, (vgrp + offset) % groups, 1, keepdims=False)
+
+    ahead = shifted(pick(1).astype(jnp.bfloat16), 1, groups)
+    behind = shifted(pick(-1).astype(jnp.bfloat16), -1, groups)
+    far = shifted(pick(2).astype(jnp.bfloat16), 2, groups)
+    near = ahead.astype(jnp.float32) + behind.astype(jnp.float32)
+    return pick(0) + near + far.astype(jnp.float32)
 
 
 def on_device(amplitudes, cholesky_vectors, owner_order, sizes):
@@ -72,43 +93,16 @@
     groups = lax.psum(1, "vgrp")
     owned_slots = lax.dynamic_index_in_dim(owner_order, vgrp, 0, keepdims=False)
     vectors = gather_slots(cholesky_vectors[0, 0], owned_slots, sizes)
-    rows, slots, cols = vectors.shape
-    block = rows // groups
-    flat = vectors.reshape(rows, slots * cols)
-
-    def partial(pair, index):
-        start = pl_multiple(index * block)
-        mine = lax.dynamic_slice_in_dim(flat, start, block, axis=0)
-        half = jnp.dot(
-            mine.reshape(block * slots, cols), amplitudes[pair], preferred_element_type=jnp.float32
+    total = jnp.zeros(amplitudes.shape, jnp.float32)
+    for slot in range(owned_slots.shape[0]):
+        vector = vectors[slot]
+        half_product = jnp.einsum(
+            "ac,pcd->pad", vector, amplitudes, preferred_element_type=jnp.float32
         ).astype(jnp.bfloat16)
-        return lax.dot_general(
-            half.reshape(block, slots * cols), flat, (((1,), (1,)), ((), ())),
-            preferred_element_type=jnp.float32,
+        total = total + jnp.einsum(
+            "pad,bd->pab", half_product, vector, preferred_element_type=jnp.float32
         )
-
-    outs = []
-    arrived = [None, None]
-    directions = (1, -1)
-    for step in range(RING):
-        sums = []
-        for pair, direction in enumerate(directions):
-            index = (vgrp - direction * (1 + step)) % groups
-            total = partial(pair, index)
-            if arrived[pair] is not None:
-                total = total + arrived[pair].astype(jnp.float32)
-            sums.append(total)
-        if step < RING - 1:
-            for pair, direction in enumerate(directions):
-                shift = [(g, (g + direction) % RING) for g in range(RING)]
-                arrived[pair] = lax.ppermute(sums[pair].astype(jnp.bfloat16), "vgrp", shift)
-        else:
-            outs = sums
-    return jnp.stack(outs, axis=0)
-
-
-def pl_multiple(value):
-    return value
+    return scatter_sum(total, vgrp, groups)
 
 
 def solution(mesh):
@@ -116,7 +110,7 @@
     cores = 2
     chips = pair // cores
     side = RING
-    assert chips == side * side and vgrp == RING
+    assert chips == side * side
     devices = mesh.devices.reshape(chips // side, side, cores, vgrp)
     fine = Mesh(devices, ("z", "x", "core", "vgrp"))
     sizes = (chips // side, side, cores)

time: 208 us -> 154 us (0.74); the launches traced: 205 us -> 154 us
  local copies, waits for them, and re-layouts: 52.9 us -> 11.8 us
  matrix products: 61.9 us -> 31.8 us
  waiting for transfers between devices: 48.3 us -> 66.6 us
  other arithmetic: 11 us -> 14.4 us
    reshape x16 -> x0, local copies, waits for them, and re-layouts: 39.6 us -> none  [the longest x8 20.2 us: partial(): half.reshape(block, slots * cols)]
    dot_general x16 -> x4, matrix products: 61.9 us -> 31.8 us  [on_device(): jnp.einsum('pad,bd->pab', half_product, vector, preferred_element_type=jn...]
    ppermute x6 -> x3, waiting for transfers between devices: 6.86 us -> 28.7 us  [shifted(): lax.ppermute(value, 'vgrp', [(g, (g + step) % groups) for g in range(grou...]
    ppermute x2, waiting for transfers between devices: 2.82 us -> 10.4 us  [ring_gather(): from_prev = lax.ppermute(piece, PAIR, ring_perm(sizes, stage, 1))]
    ppermute x2, waiting for transfers between devices: 7.56 us -> 0.01 us  [ring_gather(): from_next = lax.ppermute(piece, PAIR, ring_perm(sizes, stage, -1))]
    ppermute x2, waiting for transfers between devices: 3.56 us -> 0.01 us  [ring_gather(): far_high = lax.ppermute(from_next[half:], PAIR, ring_perm(sizes, stage, -1))]
    convert_element_type x0 -> x1, local copies, waits for them, and re-layouts: none -> 3.29 us  [scatter_sum(): ahead = shifted(pick(1).astype(jnp.bfloat16), 1, groups)]
    ppermute x6 -> x3, starting transfers between devices: 6.94 us -> 3.77 us  [shifted(): lax.ppermute(value, 'vgrp', [(g, (g + step) % groups) for g in range(grou...]
  transfers between devices with their start and end apart: 16 -> 13, of which waited for: 10 -> 8; matrix products, arithmetic and copies ran while one was open for 43% -> 1% of each run, Pallas kernels for 0% -> 0%
where the time goes in v7:
time: 154 us
  waiting for transfers between devices  66.6 us (43%)
  matrix products  31.8 us (21%)
  starting transfers between devices  28.7 us (19%)
  other arithmetic  14.4 us (9%)
  local copies, waits for them, and re-layouts  11.8 us (8%)
    dot_general x4, matrix products, on_device(): jnp.einsum('pad,bd->pab', half_product, vector, preferred_element_type=jn...  31.8 us
    ppermute x3, waiting for transfers between devices, shifted(): lax.ppermute(value, 'vgrp', [(g, (g + step) % groups) for g in range(grou...  28.7 us
    all_to_all x1, waiting for transfers between devices, gather_slots(): pieces = lax.all_to_all(pieces, PAIR, 0, 0, tiled=True)  18.5 us
    ppermute x2, waiting for transfers between devices, ring_gather(): from_prev = lax.ppermute(piece, PAIR, ring_perm(sizes, stage, 1))  10.4 us
    all_to_all x1, starting transfers between devices, gather_slots(): pieces = lax.all_to_all(pieces, PAIR, 0, 0, tiled=True)  9.55 us
    ppermute x2, starting transfers between devices, ring_gather(): far_high = lax.ppermute(from_next[half:], PAIR, ring_perm(sizes, stage, -1))  5.44 us
    gather x1, local copies, waits for them, and re-layouts, gather_slots(): ordered = jnp.take(stacked, index, axis=0)  5.35 us
    ppermute x2, starting transfers between devices, ring_gather(): from_next = lax.ppermute(piece, PAIR, ring_perm(sizes, stage, -1))  5.3 us
  transfers between devices with their start and end apart: 13, of which 8 were waited for; matrix products, arithmetic and copies ran while one was open for 1% of the time, Pallas kernels for 0%

profile of v7, /device:TPU:1, one launch (start us, length us, event | category | flops | bytes accessed | tf_op | source)
XLA Modules:
  0.0 153.6 jit_solution(18190450759552996005)
XLA Ops:
  0.0 9.6 %all-to-all-start = ((bf16[32,24,768]{2,1,0:T(8,128)(2,1)}), bf16[32,24,768]{2,1,0:T(8,128)(2,1)S(1)}, u32[]{:S(2)}, u32[]{:S(2)}) async-start(bf16[32,24,768]{2,1,0:T(8,128)(2,1)} %bitcast.94), calls=%async_computation | async-start | bytes 2359296 | tf_op jit(solution)/shard_map/all_to_all | solution.py:49
  9.6 18.5 %all-to-all-done = bf16[32,24,768]{2,1,0:T(8,128)(2,1)S(1)} async-done(((bf16[32,24,768]{2,1,0:T(8,128)(2,1)}), bf16[32,24,768]{2,1,0:T(8,128)(2,1)S(1)}, u32[]{:S(2)}, u32[]{:S(2)}) %all-to-all-start) | async-done | bytes 1179680 | tf_op jit(solution)/shard_map/all_to_all | solution.py:49
  28.1 1.2 gather_fusion
  29.3 1.0 broadcast_select_fusion
  30.4 2.7 %collective-permute-start = (bf16[4,24,768]{2,1,0:T(8,128)(2,1)S(1)}, bf16[4,24,768]{2,1,0:T(8,128)(2,1)S(1)}, u32[]{:S(2)}, u32[]{:S(2)}) collective-permute-start(bf16[4,24,768]{2,1,0:T(8,128)(2,1)S(1)} %broadcast_select_fusion), channel_id=1, source_target_pairs={{0,24},{4,100},{8,0},{12,108},{16,8},{20,116},{24,16},{28,124},{32... | collective-permute-start | bytes 442376 | tf_op jit(solution)/shard_map/ppermute | solution.py:35
  33.1 2.8 %collective-permute-done.1 = bf16[4,24,768]{2,1,0:T(8,128)(2,1)S(1)} collective-permute-done((bf16[4,24,768]{2,1,0:T(8,128)(2,1)S(1)}, bf16[4,24,768]{2,1,0:T(8,128)(2,1)S(1)}, u32[]{:S(2)}, u32[]{:S(2)}) %collective-permute-start.1) | collective-permute-done | bytes 147488 | tf_op jit(solution)/shard_map/ppermute | solution.py:34
  35.9 2.7 %collective-permute-start.3 = (bf16[2,24,768]{2,1,0:T(8,128)(2,1)S(1)}, bf16[2,24,768]{2,1,0:T(8,128)(2,1)S(1)}, u32[]{:S(2)}, u32[]{:S(2)}) collective-permute-start(bf16[2,24,768]{2,1,0:T(8,128)(2,1)S(1)} %slice.41), channel_id=1, source_target_pairs={{0,24},{4,100},{8,0},{12,108},{16,8},{20,116},{24,16},{28,124},{32... | collective-permute-start | bytes 221192 | tf_op jit(solution)/shard_map/ppermute | solution.py:37
  38.6 1.0 bitcast_select_fusion
  39.6 0.7 collective-permute-done.2
  40.4 0.1 collective-permute-start.5
  40.5 2.6 %collective-permute-start.4 = (bf16[4,4,24,768]{3,2,1,0:T(8,128)(2,1)S(1)}, bf16[4,4,24,768]{3,2,1,0:T(8,128)(2,1)S(1)}, u32[]{:S(2)}, u32[]{:S(2)}) collective-permute-start(bf16[4,4,24,768]{3,2,1,0:T(8,128)(2,1)S(1)} %get-tuple-element.13), channel_id=1, source_target_pairs={{0,96},{4,28},{8,104},{12,4},{16,112},{20,12},{24,120},{28,20},{32... | collective-permute-start | bytes 1769480 | tf_op jit(solution)/shard_map/ppermute | solution.py:35
  43.2 7.6 %collective-permute-done.5 = bf16[4,4,24,768]{3,2,1,0:T(8,128)(2,1)S(1)} collective-permute-done((bf16[4,4,24,768]{3,2,1,0:T(8,128)(2,1)S(1)}, bf16[4,4,24,768]{3,2,1,0:T(8,128)(2,1)S(1)}, u32[]{:S(2)}, u32[]{:S(2)}) %collective-permute-start.5) | collective-permute-done | bytes 589856 | tf_op jit(solution)/shard_map/ppermute | solution.py:34
  50.9 2.7 %collective-permute-start.7 = (bf16[2,4,24,768]{3,2,1,0:T(8,128)(2,1)S(1)}, bf16[2,4,24,768]{3,2,1,0:T(8,128)(2,1)S(1)}, u32[]{:S(2)}, u32[]{:S(2)}) collective-permute-start(bf16[2,4,24,768]{3,2,1,0:T(8,128)(2,1)S(1)} %slice.43), channel_id=1, source_target_pairs={{0,96},{4,28},{8,104},{12,4},{16,112},{20,12},{24,120},{28,20},{32... | collective-permute-start | bytes 884744 | tf_op jit(solution)/shard_map/ppermute | solution.py:37
  53.6 4.0 %collective-permute-done.6 = bf16[2,4,24,768]{3,2,1,0:T(8,128)(2,1)S(1)} collective-permute-done((bf16[2,4,24,768]{3,2,1,0:T(8,128)(2,1)S(1)}, bf16[2,4,24,768]{3,2,1,0:T(8,128)(2,1)S(1)}, u32[]{:S(2)}, u32[]{:S(2)}) %collective-permute-start.6) | collective-permute-done | bytes 294944 | tf_op jit(solution)/shard_map/ppermute | solution.py:36
  57.7 1.7 %pad_maximum_fusion.1 = bf16[4,4,4,24,768]{4,3,2,1,0:T(8,128)(2,1)} fusion(bf16[1,4,4,24,768]{4,3,2,1,0:T(8,128)(2,1)S(1)} %bitcast.88, bf16[1,4,4,24,768]{4,3,2,1,0:T(8,128)(2,1)S(1)} %maximum_bitcast_fusion, bf16[1,4,4,24,768]{4,3,2,1,0:T(8,128)(2,1)S(1)} %bitcast.89, bf16[1,4,4,24,768]{4,3,2,1,0:T(8,128)(2,1)S(1)} %get-tuple-element.12), kind=kLoop, calls=%fused_computation.5 | loop fusion | flops 3538944 | bytes 4718592 | tf_op jit(solution)/shard_map/stack | solution.py:39
  59.4 4.4 %collective-permute-start.8 = (bf16[4,4,4,24,768]{4,3,2,1,0:T(8,128)(2,1)}, bf16[4,4,4,24,768]{4,3,2,1,0:T(8,128)(2,1)}, u32[]{:S(2)}, u32[]{:S(2)}) collective-permute-start(bf16[4,4,4,24,768]{4,3,2,1,0:T(8,128)(2,1)} %pad_maximum_fusion.1), channel_id=1, source_target_pairs={{0,4},{4,0},{8,12},{12,8},{16,20},{20,16},{24,28},{28,24},{32,36},... | collective-permute-start | bytes 7077896 | tf_op jit(solution)/shard_map/ppermute | solution.py:54
  63.9 4.4 %collective-permute-done.8 = bf16[4,4,4,24,768]{4,3,2,1,0:T(8,128)(2,1)} collective-permute-done((bf16[4,4,4,24,768]{4,3,2,1,0:T(8,128)(2,1)}, bf16[4,4,4,24,768]{4,3,2,1,0:T(8,128)(2,1)}, u32[]{:S(2)}, u32[]{:S(2)}) %collective-permute-start.8) | collective-permute-done | bytes 2359328 | tf_op jit(solution)/shard_map/ppermute | solution.py:54
  68.3 4.9 %pad_maximum_fusion = bf16[32,4,24,768]{3,2,1,0:T(8,128)(2,1)} fusion(bf16[16,4,24,768]{3,2,1,0:T(8,128)(2,1)} %bitcast.13, bf16[16,4,24,768]{3,2,1,0:T(8,128)(2,1)} %bitcast.12), kind=kLoop, calls=%fused_computation.2 | loop fusion | flops 2359296 | bytes 9437184 | tf_op jit(solution)/shard_map/concatenate | solution.py:56
  73.2 5.3 %gather_fusion.1 = bf16[32,4,24,768]{3,2,1,0:T(8,128)(2,1)} fusion(bf16[32,4,24,768]{3,2,1,0:T(8,128)(2,1)} %pad_maximum_fusion, s32[1024]{0:T(1024)S(1)} %pad_clamp_fusion), kind=kCustom, calls=%fused_computation.1 | custom fusion | bytes 9437312 | tf_op jit(solution)/shard_map/jit(_take)/gather | solution.py:67
  78.6 2.9 %select_bitcast_fusion = bf16[4,32,24,768]{3,2,0,1:T(8,128)(2,1)S(1)} fusion(bf16[32,4,24,768]{3,2,1,0:T(8,128)(2,1)} %gather_fusion.1, pred[32]{0:T(512)(128)(4,1)S(1)} %compare_and_fusion.1), kind=kLoop, calls=%fused_computation.4 | loop fusion | flops 2359296 | bytes 9437216 | tf_op jit(solution)/shard_map/jit(_take)/select_n | solution.py:67
  81.4 1.9 %fusion.41 = (bf16[1,32,24,768]{3,2,0,1:T(8,128)(2,1)S(1)}, bf16[1,32,24,768]{3,2,0,1:T(8,128)(2,1)}, bf16[1,32,24,768]{3,2,0,1:T(8,128)(2,1)}, bf16[1,32,24,768]{3,2,0,1:T(8,128)(2,1)}) fusion(bf16[4,32,24,768]{3,2,0,1:T(8,128)(2,1)S(1)} %select_bitcast_fusion), kind=kLoop, calls=%fused_computation.93 | loop fusion | bytes 9437184 | tf_op jit(solution)/shard_map/slice | solution.py:98
  83.3 7.6 %fusion = f32[2,768,768]{2,1,0:T(8,128)} fusion(bf16[768,768,1]{1,0,2:T(8,128)(2,1)} %bitcast.93, bf16[2,768,768]{2,1,0:T(8,128)(2,1)S(1)} %copy-done), kind=kOutput, calls=%fused_computation.6 | convolution fusion | flops 3625058304 | bytes 8257536 | tf_op jit(solution)/shard_map/pad,bd->pab/dot_general | solution.py:102
  91.0 7.7 %fusion.2 = f32[2,768,768]{2,1,0:T(8,128)} fusion(bf16[768,768,1]{1,0,2:T(8,128)(2,1)} %bitcast.92, bf16[2,768,768]{2,1,0:T(8,128)(2,1)S(1)} %copy-done), kind=kOutput, calls=%fused_computation.8 | convolution fusion | flops 3625058304 | bytes 8257536 | tf_op jit(solution)/shard_map/pad,bd->pab/dot_general | solution.py:102
  98.6 7.7 %fusion.4 = f32[2,768,768]{2,1,0:T(8,128)} fusion(bf16[768,768,1]{1,0,2:T(8,128)(2,1)} %bitcast.91, bf16[2,768,768]{2,1,0:T(8,128)(2,1)S(1)} %copy-done), kind=kOutput, calls=%fused_computation.10 | convolution fusion | flops 3625058304 | bytes 8257536 | tf_op jit(solution)/shard_map/pad,bd->pab/dot_general | solution.py:102
  106.3 8.8 %add_add_fusion = f32[2,768,768]{2,1,0:T(8,128)} fusion(f32[2,768,768]{2,1,0:T(8,128)} %fusion, f32[2,768,768]{2,1,0:T(8,128)} %fusion.2, f32[2,768,768]{2,1,0:T(8,128)} %fusion.4, bf16[768,768,1]{1,0,2:T(8,128)(2,1)S(1)} %bitcast.90, bf16[2,768,768]{2,1,0:T(8,128)(2,1)S(1)} %copy-done), kind=kOutput, calls=%fused_computation.3 | convolution fusion | flops 3628597248 | bytes 22413312 | tf_op jit(solution)/shard_map/pad,bd->pab/dot_general | solution.py:102
  115.2 3.3 %fusion.23 = (bf16[2,192,768]{2,1,0:T(8,128)(2,1)}, bf16[2,192,768]{2,1,0:T(8,128)(2,1)}, bf16[2,192,768]{2,1,0:T(8,128)(2,1)}) fusion(f32[2,4,192,768]{3,2,1,0:T(8,128)} %bitcast.86, s32[]{:T(128)S(6)} %select_n.241, s32[]{:T(128)S(6)} %select_n.243, s32[]{:T(128)S(6)} %select_n.245), kind=kLoop, calls=%fused_computation.27 | loop fusion | bytes 3538956 | tf_op jit(solution)/shard_map/convert_element_type | solution.py:84
  118.4 2.7 %collective-permute-start.10 = (bf16[2,192,768]{2,1,0:T(8,128)(2,1)}, bf16[2,192,768]{2,1,0:T(8,128)(2,1)S(1)}, u32[]{:S(2)}, u32[]{:S(2)}) collective-permute-start(bf16[2,192,768]{2,1,0:T(8,128)(2,1)} %get-tuple-element.6), channel_id=1, source_target_pairs={{0,3},{1,0},{2,1},{3,2},{4,7},{5,4},{6,5},{7,6},{8,11},{9,8},{10,9... | collective-permute-start | bytes 1769480 | tf_op jit(solution)/shard_map/ppermute | solution.py:73
  121.2 0.4 collective-permute-start.11
  121.5 0.7 collective-permute-start.9
  122.2 24.1 %collective-permute-done.10 = bf16[2,192,768]{2,1,0:T(8,128)(2,1)S(1)} collective-permute-done((bf16[2,192,768]{2,1,0:T(8,128)(2,1)}, bf16[2,192,768]{2,1,0:T(8,128)(2,1)S(1)}, u32[]{:S(2)}, u32[]{:S(2)}) %collective-permute-start.10) | collective-permute-done | bytes 589856 | tf_op jit(solution)/shard_map/ppermute | solution.py:73
  146.3 4.6 %collective-permute-done.9 = bf16[2,192,768]{2,1,0:T(8,128)(2,1)} collective-permute-done((bf16[2,192,768]{2,1,0:T(8,128)(2,1)}, bf16[2,192,768]{2,1,0:T(8,128)(2,1)}, u32[]{:S(2)}, u32[]{:S(2)}) %collective-permute-start.9) | collective-permute-done | bytes 589856 | tf_op jit(solution)/shard_map/ppermute | solution.py:73
  150.9 2.7 %fusion.14 = f32[2,192,768]{2,1,0:T(8,128)} fusion(bf16[2,192,768]{2,1,0:T(8,128)(2,1)S(1)} %collective-permute-done.11, bf16[2,192,768]{2,1,0:T(8,128)(2,1)S(1)} %collective-permute-done.10, bf16[2,192,768]{2,1,0:T(8,128)(2,1)} %collective-permute-done.9, f32[2,4,192,768]{3,2,1,0:T(8,128)} %bitcast.87, s32[]{:T(128)S(6)} %select_n.239), kind=kLoop, calls=%fused_computation.22 | loop fusion | flops 1769472 | bytes 4128772 | tf_op jit(solution)/shard_map/add | solution.py:88
  (25 shorter events, 0.5 us)
Async XLA Ops:
  0.0 83.3 %copy-start = (bf16[2,768,768]{2,1,0:T(8,128)(2,1)S(1)}, bf16[2,768,768]{2,1,0:T(8,128)(2,1)}, u32[]{:S(2)}) copy-start(bf16[2,768,768]{2,1,0:T(8,128)(2,1)} %param.3) | copy-start | bytes 7077892
  0.0 9.6 %copy-start.1 = (s32[4,4]{1,0:T(4,128)S(1)}, s32[4,4]{1,0:T(4,128)}, u32[]{:S(2)}) copy-start(s32[4,4]{1,0:T(4,128)} %param.5) | copy-start | bytes 196
  0.0 28.1 %all-to-all-start = ((bf16[32,24,768]{2,1,0:T(8,128)(2,1)}), bf16[32,24,768]{2,1,0:T(8,128)(2,1)S(1)}, u32[]{:S(2)}, u32[]{:S(2)}) async-start(bf16[32,24,768]{2,1,0:T(8,128)(2,1)} %bitcast.94), calls=%async_computation | async-start | bytes 2359296 | tf_op jit(solution)/shard_map/all_to_all | solution.py:49
  30.3 5.6 %collective-permute-start.1 = (bf16[4,24,768]{2,1,0:T(8,128)(2,1)S(1)}, bf16[4,24,768]{2,1,0:T(8,128)(2,1)S(1)}, u32[]{:S(2)}, u32[]{:S(2)}) collective-permute-start(bf16[4,24,768]{2,1,0:T(8,128)(2,1)S(1)} %broadcast_select_fusion), channel_id=1, source_target_pairs={{0,8},{4,36},{8,16},{12,44},{16,24},{20,52},{24,0},{28,60},{32,40}... | collective-permute-start | bytes 442376 | tf_op jit(solution)/shard_map/ppermute | solution.py:34
  30.4 5.5 %collective-permute-start = (bf16[4,24,768]{2,1,0:T(8,128)(2,1)S(1)}, bf16[4,24,768]{2,1,0:T(8,128)(2,1)S(1)}, u32[]{:S(2)}, u32[]{:S(2)}) collective-permute-start(bf16[4,24,768]{2,1,0:T(8,128)(2,1)S(1)} %broadcast_select_fusion), channel_id=1, source_target_pairs={{0,24},{4,100},{8,0},{12,108},{16,8},{20,116},{24,16},{28,124},{32... | collective-permute-start | bytes 442376 | tf_op jit(solution)/shard_map/ppermute | solution.py:35
  35.9 4.4 %collective-permute-start.2 = (bf16[2,24,768]{2,1,0:T(8,128)(2,1)S(1)}, bf16[2,24,768]{2,1,0:T(8,128)(2,1)S(1)}, u32[]{:S(2)}, u32[]{:S(2)}) collective-permute-start(bf16[2,24,768]{2,1,0:T(8,128)(2,1)S(1)} %slice.40), channel_id=1, source_target_pairs={{0,8},{4,36},{8,16},{12,44},{16,24},{20,52},{24,0},{28,60},{32,40}... | collective-permute-start | bytes 221192 | tf_op jit(solution)/shard_map/ppermute | solution.py:36
  35.9 4.4 %collective-permute-start.3 = (bf16[2,24,768]{2,1,0:T(8,128)(2,1)S(1)}, bf16[2,24,768]{2,1,0:T(8,128)(2,1)S(1)}, u32[]{:S(2)}, u32[]{:S(2)}) collective-permute-start(bf16[2,24,768]{2,1,0:T(8,128)(2,1)S(1)} %slice.41), channel_id=1, source_target_pairs={{0,24},{4,100},{8,0},{12,108},{16,8},{20,116},{24,16},{28,124},{32... | collective-permute-start | bytes 221192 | tf_op jit(solution)/shard_map/ppermute | solution.py:37
  40.4 10.3 %collective-permute-start.5 = (bf16[4,4,24,768]{3,2,1,0:T(8,128)(2,1)S(1)}, bf16[4,4,24,768]{3,2,1,0:T(8,128)(2,1)S(1)}, u32[]{:S(2)}, u32[]{:S(2)}) collective-permute-start(bf16[4,4,24,768]{3,2,1,0:T(8,128)(2,1)S(1)} %get-tuple-element.13), channel_id=1, source_target_pairs={{0,32},{4,12},{8,40},{12,20},{16,48},{20,28},{24,56},{28,4},{32,64... | collective-permute-start | bytes 1769480 | tf_op jit(solution)/shard_map/ppermute | solution.py:34
  40.5 10.3 %collective-permute-start.4 = (bf16[4,4,24,768]{3,2,1,0:T(8,128)(2,1)S(1)}, bf16[4,4,24,768]{3,2,1,0:T(8,128)(2,1)S(1)}, u32[]{:S(2)}, u32[]{:S(2)}) collective-permute-start(bf16[4,4,24,768]{3,2,1,0:T(8,128)(2,1)S(1)} %get-tuple-element.13), channel_id=1, source_target_pairs={{0,96},{4,28},{8,104},{12,4},{16,112},{20,12},{24,120},{28,20},{32... | collective-permute-start | bytes 1769480 | tf_op jit(solution)/shard_map/ppermute | solution.py:35
  50.8 6.9 %collective-permute-start.6 = (bf16[2,4,24,768]{3,2,1,0:T(8,128)(2,1)S(1)}, bf16[2,4,24,768]{3,2,1,0:T(8,128)(2,1)S(1)}, u32[]{:S(2)}, u32[]{:S(2)}) collective-permute-start(bf16[2,4,24,768]{3,2,1,0:T(8,128)(2,1)S(1)} %slice.42), channel_id=1, source_target_pairs={{0,32},{4,12},{8,40},{12,20},{16,48},{20,28},{24,56},{28,4},{32,64... | collective-permute-start | bytes 884744 | tf_op jit(solution)/shard_map/ppermute | solution.py:36
  50.9 6.7 %collective-permute-start.7 = (bf16[2,4,24,768]{3,2,1,0:T(8,128)(2,1)S(1)}, bf16[2,4,24,768]{3,2,1,0:T(8,128)(2,1)S(1)}, u32[]{:S(2)}, u32[]{:S(2)}) collective-permute-start(bf16[2,4,24,768]{3,2,1,0:T(8,128)(2,1)S(1)} %slice.43), channel_id=1, source_target_pairs={{0,96},{4,28},{8,104},{12,4},{16,112},{20,12},{24,120},{28,20},{32... | collective-permute-start | bytes 884744 | tf_op jit(solution)/shard_map/ppermute | solution.py:37
  59.4 8.9 %collective-permute-start.8 = (bf16[4,4,4,24,768]{4,3,2,1,0:T(8,128)(2,1)}, bf16[4,4,4,24,768]{4,3,2,1,0:T(8,128)(2,1)}, u32[]{:S(2)}, u32[]{:S(2)}) collective-permute-start(bf16[4,4,4,24,768]{4,3,2,1,0:T(8,128)(2,1)} %pad_maximum_fusion.1), channel_id=1, source_target_pairs={{0,4},{4,0},{8,12},{12,8},{16,20},{20,16},{24,28},{28,24},{32,36},... | collective-permute-start | bytes 7077896 | tf_op jit(solution)/shard_map/ppermute | solution.py:54
  118.4 27.8 %collective-permute-start.10 = (bf16[2,192,768]{2,1,0:T(8,128)(2,1)}, bf16[2,192,768]{2,1,0:T(8,128)(2,1)S(1)}, u32[]{:S(2)}, u32[]{:S(2)}) collective-permute-start(bf16[2,192,768]{2,1,0:T(8,128)(2,1)} %get-tuple-element.6), channel_id=1, source_target_pairs={{0,3},{1,0},{2,1},{3,2},{4,7},{5,4},{6,5},{7,6},{8,11},{9,8},{10,9... | collective-permute-start | bytes 1769480 | tf_op jit(solution)/shard_map/ppermute | solution.py:73
  121.2 25.1 %collective-permute-start.11 = (bf16[2,192,768]{2,1,0:T(8,128)(2,1)}, bf16[2,192,768]{2,1,0:T(8,128)(2,1)S(1)}, u32[]{:S(2)}, u32[]{:S(2)}) collective-permute-start(bf16[2,192,768]{2,1,0:T(8,128)(2,1)} %get-tuple-element.7), channel_id=1, source_target_pairs={{0,2},{1,3},{2,0},{3,1},{4,6},{5,7},{6,4},{7,5},{8,10},{9,11},{10,... | collective-permute-start | bytes 1769480 | tf_op jit(solution)/shard_map/ppermute | solution.py:73
  121.5 29.4 %collective-permute-start.9 = (bf16[2,192,768]{2,1,0:T(8,128)(2,1)}, bf16[2,192,768]{2,1,0:T(8,128)(2,1)}, u32[]{:S(2)}, u32[]{:S(2)}) collective-permute-start(bf16[2,192,768]{2,1,0:T(8,128)(2,1)} %get-tuple-element.5), channel_id=1, source_target_pairs={{0,1},{1,2},{2,3},{3,0},{4,5},{5,6},{6,7},{7,4},{8,9},{9,10},{10,1... | collective-permute-start | bytes 1769480 | tf_op jit(solution)/shard_map/ppermute | solution.py:73

commit v8 on v7

--- a/solution.py
+++ b/solution.py
@@ -29,13 +29,16 @@
     return perm
 
 
-def ring_gather(piece, sizes, stage):
+def ring_gather(piece, sizes, stage, direct_far=False):
     half = piece.shape[0] // 2
     from_prev = lax.ppermute(piece, PAIR, ring_perm(sizes, stage, 1))
     from_next = lax.ppermute(piece, PAIR, ring_perm(sizes, stage, -1))
-    far_low = lax.ppermute(from_prev[:half], PAIR, ring_perm(sizes, stage, 1))
-    far_high = lax.ppermute(from_next[half:], PAIR, ring_perm(sizes, stage, -1))
-    far = jnp.concatenate([far_low, far_high], axis=0)
+    if direct_far:
+        far = lax.ppermute(piece, PAIR, ring_perm(sizes, stage, 2))
+    else:
+        far_low = lax.ppermute(from_prev[:half], PAIR, ring_perm(sizes, stage, 1))
+        far_high = lax.ppermute(from_next[half:], PAIR, ring_perm(sizes, stage, -1))
+        far = jnp.concatenate([far_low, far_high], axis=0)
     return jnp.stack([piece, from_next, far, from_prev], axis=0)
 
 
@@ -48,24 +51,26 @@
     pieces = own_vector.reshape(devices, piece, cols)
     pieces = lax.all_to_all(pieces, PAIR, 0, 0, tiled=True)
     picked = jnp.take(pieces, owned_slots, axis=0)
-    first = ring_gather(picked, sizes, 1)
+    first = ring_gather(picked, sizes, 1, direct_far=True)
     both = ring_gather(first, sizes, 2)
     swap = [(q, q ^ 1) for q in range(devices)]
     other = lax.ppermute(both, PAIR, swap)
     chips = nz * nx
-    stacked = jnp.concatenate(
-        [both.reshape((chips,) + both.shape[2:]), other.reshape((chips,) + both.shape[2:])], axis=0
-    )
     z = lax.axis_index("z")
     x = lax.axis_index("x")
     core = lax.axis_index("core")
-    q = jnp.arange(devices, dtype=jnp.int32)
-    zq, xq, cq = q // (nx * nc), (q // nc) % nx, q % nc
-    dz, dx = (zq - z) % nz, (xq - x) % nx
-    inner = jnp.where(cq == 0, dz * nx + dx, dx * nz + dz)
-    index = jnp.where(cq == core, 0, chips) + inner
-    ordered = jnp.take(stacked, index, axis=0)
-    ordered = jnp.transpose(ordered, (1, 0, 2, 3))
+    chip = jnp.arange(chips, dtype=jnp.int32)
+    dz, dx = (chip // nx - z) % nz, (chip % nx - x) % nx
+    x_first = dz * nx + dx
+    z_first = dx * nz + dz
+    mine = both.reshape((chips,) + both.shape[2:])
+    other = other.reshape((chips,) + both.shape[2:])
+    mine = jnp.take(mine, jnp.where(core == 0, x_first, z_first), axis=0)
+    other = jnp.take(other, jnp.where(core == 0, z_first, x_first), axis=0)
+    low = jnp.where(core == 0, mine, other)
+    high = jnp.where(core == 0, other, mine)
+    ordered = jnp.stack([low, high], axis=1)
+    ordered = jnp.transpose(ordered, (2, 0, 1, 3, 4))
     return ordered.reshape(slots, rows, cols)
 
 
@@ -83,7 +88,11 @@
 
     ahead = shifted(pick(1).astype(jnp.bfloat16), 1, groups)
     behind = shifted(pick(-1).astype(jnp.bfloat16), -1, groups)
-    far = shifted(pick(2).astype(jnp.bfloat16), 2, groups)
+    far = pick(2).astype(jnp.bfloat16)
+    half = block // 2
+    far_low = shifted(far[:, :half], 2, groups)
+    far_high = shifted(shifted(far[:, half:], 1, groups), 1, groups)
+    far = jnp.concatenate([far_low, far_high], axis=1)
     near = ahead.astype(jnp.float32) + behind.astype(jnp.float32)
     return pick(0) + near + far.astype(jnp.float32)
 

time: 154 us -> 156 us (1.013)
  local copies, waits for them, and re-layouts: 11.8 us -> 19.9 us
  other arithmetic: 14.4 us -> 9.87 us
  starting transfers between devices: 28.7 us -> 25.6 us
  matrix products: 31.8 us -> 34.5 us
    slice x1 -> x5, local copies, waits for them, and re-layouts: 1.87 us -> 7.03 us  [on_device(): vector = vectors[slot]]
    concatenate x1 -> x0, other arithmetic: 4.9 us -> none  [gather_slots(): jnp.concatenate([both.reshape((chips,) + both.shape[2:]), other.reshape((...]
    ppermute x1, waiting for transfers between devices: 4.44 us -> 0.65 us  [gather_slots(): other = lax.ppermute(both, PAIR, swap)]
    select_n x2 -> x0, other arithmetic: 2.88 us -> none  [gather_slots(): ordered = jnp.take(stacked, index, axis=0)]
    another operation x0 -> x1, other arithmetic: none -> 2.85 us  [gather_slots(): ordered = jnp.stack([low, high], axis=1)]
    ppermute x2 -> x1, starting transfers between devices: 5.44 us -> 2.72 us  [ring_gather(): far_high = lax.ppermute(from_next[half:], PAIR, ring_perm(sizes, stage, -1))]
    dot_general x4, matrix products: 31.8 us -> 34.5 us  [on_device(): jnp.einsum('pad,bd->pab', half_product, vector, preferred_element_type=jn...]
    ppermute x2, starting transfers between devices: 5.3 us -> 2.82 us  [ring_gather(): from_next = lax.ppermute(piece, PAIR, ring_perm(sizes, stage, -1))]
  transfers between devices with their start and end apart: 13 -> 14, of which waited for: 8 -> 10; matrix products, arithmetic and copies ran while one was open for 1% -> 3% of each run, Pallas kernels for 0% -> 0%
where the time goes in v8:
time: 156 us; the launch traced here: 155 us
  waiting for transfers between devices  65.5 us (42%)
  matrix products  34.5 us (22%)
  starting transfers between devices  25.6 us (16%)
  local copies, waits for them, and re-layouts  19.9 us (13%)
  other arithmetic  9.87 us (6%)
    dot_general x4, matrix products, on_device(): jnp.einsum('pad,bd->pab', half_product, vector, preferred_element_type=jn...  34.5 us
    ppermute x5, waiting for transfers between devices, shifted(): lax.ppermute(value, 'vgrp', [(g, (g + step) % groups) for g in range(grou...  29.5 us
    all_to_all x1, waiting for transfers between devices, gather_slots(): pieces = lax.all_to_all(pieces, PAIR, 0, 0, tiled=True)  18.5 us
    all_to_all x1, starting transfers between devices, gather_slots(): pieces = lax.all_to_all(pieces, PAIR, 0, 0, tiled=True)  9.55 us
    ppermute x2, waiting for transfers between devices, ring_gather(): from_prev = lax.ppermute(piece, PAIR, ring_perm(sizes, stage, 1))  9.14 us
    slice x5, local copies, waits for them, and re-layouts, on_device(): vector = vectors[slot]  7.03 us
    ppermute x5, starting transfers between devices, shifted(): lax.ppermute(value, 'vgrp', [(g, (g + step) % groups) for g in range(grou...  5.38 us
    ppermute x1, waiting for transfers between devices, ring_gather(): far_low = lax.ppermute(from_prev[:half], PAIR, ring_perm(sizes, stage, 1))  4.3 us
  transfers between devices with their start and end apart: 14, of which 10 were waited for; matrix products, arithmetic and copies ran while one was open for 3% of the time, Pallas kernels for 0%

profile of v8, /device:TPU:1, one launch (start us, length us, event | category | flops | bytes accessed | tf_op | source)
XLA Modules:
  0.0 155.4 jit_solution(3500041587249087596)
XLA Ops:
  0.0 9.6 %all-to-all-start = ((bf16[32,24,768]{2,1,0:T(8,128)(2,1)}), bf16[32,24,768]{2,1,0:T(8,128)(2,1)S(1)}, u32[]{:S(2)}, u32[]{:S(2)}) async-start(bf16[32,24,768]{2,1,0:T(8,128)(2,1)} %bitcast.91), calls=%async_computation | async-start | bytes 2359296 | tf_op jit(solution)/shard_map/all_to_all | solution.py:52
  9.6 18.5 %all-to-all-done = bf16[32,24,768]{2,1,0:T(8,128)(2,1)S(1)} async-done(((bf16[32,24,768]{2,1,0:T(8,128)(2,1)}), bf16[32,24,768]{2,1,0:T(8,128)(2,1)S(1)}, u32[]{:S(2)}, u32[]{:S(2)}) %all-to-all-start) | async-done | bytes 1179680 | tf_op jit(solution)/shard_map/all_to_all | solution.py:52
  28.1 1.2 gather_fusion
  33.3 1.4 collective-permute-done
  34.7 2.1 %collective-permute-done.1 = bf16[4,24,768]{2,1,0:T(8,128)(2,1)S(1)} collective-permute-done((bf16[4,24,768]{2,1,0:T(8,128)(2,1)S(1)}, bf16[4,24,768]{2,1,0:T(8,128)(2,1)S(1)}, u32[]{:S(2)}, u32[]{:S(2)}) %collective-permute-start.1) | collective-permute-done | bytes 147488 | tf_op jit(solution)/shard_map/ppermute | solution.py:37
  36.7 1.6 %collective-permute-done.2 = bf16[4,24,768]{2,1,0:T(8,128)(2,1)S(1)} collective-permute-done((bf16[4,24,768]{2,1,0:T(8,128)(2,1)S(1)}, bf16[4,24,768]{2,1,0:T(8,128)(2,1)S(1)}, u32[]{:S(2)}, u32[]{:S(2)}) %collective-permute-start.2) | collective-permute-done | bytes 147488 | tf_op jit(solution)/shard_map/ppermute | solution.py:34
  38.9 2.2 %collective-permute-start.3 = (bf16[4,4,24,768]{3,2,1,0:T(8,128)(2,1)S(1)}, bf16[4,4,24,768]{3,2,1,0:T(8,128)(2,1)S(1)}, u32[]{:S(2)}, u32[]{:S(2)}) collective-permute-start(bf16[4,4,24,768]{3,2,1,0:T(8,128)(2,1)S(1)} %get-tuple-element.22), channel_id=1, source_target_pairs={{0,96},{4,28},{8,104},{12,4},{16,112},{20,12},{24,120},{28,20},{32... | collective-permute-start | bytes 1769480 | tf_op jit(solution)/shard_map/ppermute | solution.py:35
  41.1 7.6 %collective-permute-done.4 = bf16[4,4,24,768]{3,2,1,0:T(8,128)(2,1)S(1)} collective-permute-done((bf16[4,4,24,768]{3,2,1,0:T(8,128)(2,1)S(1)}, bf16[4,4,24,768]{3,2,1,0:T(8,128)(2,1)S(1)}, u32[]{:S(2)}, u32[]{:S(2)}) %collective-permute-start.4) | collective-permute-done | bytes 589856 | tf_op jit(solution)/shard_map/ppermute | solution.py:34
  48.9 2.7 %collective-permute-start.6 = (bf16[2,4,24,768]{3,2,1,0:T(8,128)(2,1)S(1)}, bf16[2,4,24,768]{3,2,1,0:T(8,128)(2,1)S(1)}, u32[]{:S(2)}, u32[]{:S(2)}) collective-permute-start(bf16[2,4,24,768]{3,2,1,0:T(8,128)(2,1)S(1)} %slice.43), channel_id=1, source_target_pairs={{0,96},{4,28},{8,104},{12,4},{16,112},{20,12},{24,120},{28,20},{32... | collective-permute-start | bytes 884744 | tf_op jit(solution)/shard_map/ppermute | solution.py:40
  51.6 4.3 %collective-permute-done.5 = bf16[2,4,24,768]{3,2,1,0:T(8,128)(2,1)S(1)} collective-permute-done((bf16[2,4,24,768]{3,2,1,0:T(8,128)(2,1)S(1)}, bf16[2,4,24,768]{3,2,1,0:T(8,128)(2,1)S(1)}, u32[]{:S(2)}, u32[]{:S(2)}) %collective-permute-start.5) | collective-permute-done | bytes 294944 | tf_op jit(solution)/shard_map/ppermute | solution.py:39
  55.9 1.7 %pad_maximum_fusion = bf16[4,4,4,24,768]{4,3,2,1,0:T(8,128)(2,1)} fusion(bf16[1,4,4,24,768]{4,3,2,1,0:T(8,128)(2,1)S(1)} %bitcast.89, bf16[1,4,4,24,768]{4,3,2,1,0:T(8,128)(2,1)S(1)} %maximum_bitcast_fusion.1, bf16[1,4,4,24,768]{4,3,2,1,0:T(8,128)(2,1)S(1)} %bitcast.90, bf16[1,4,4,24,768]{4,3,2,1,0:T(8,128)(2,1)S(1)} %get-tuple-element.21), kind=kLoop, calls=%fused_computation.5 | loop fusion | flops 3538944 | bytes 4718592 | tf_op jit(solution)/shard_map/stack | solution.py:42
  57.7 3.1 %collective-permute-start.7 = (bf16[4,4,4,24,768]{4,3,2,1,0:T(8,128)(2,1)}, bf16[4,4,4,24,768]{4,3,2,1,0:T(8,128)(2,1)}, u32[]{:S(2)}, u32[]{:S(2)}) collective-permute-start(bf16[4,4,4,24,768]{4,3,2,1,0:T(8,128)(2,1)} %pad_maximum_fusion), channel_id=1, source_target_pairs={{0,4},{4,0},{8,12},{12,8},{16,20},{20,16},{24,28},{28,24},{32,36},... | collective-permute-start | bytes 7077896 | tf_op jit(solution)/shard_map/ppermute | solution.py:57
  60.8 3.8 %gather_fusion.1 = bf16[16,4,24,768]{3,2,1,0:T(8,128)(2,1)} fusion(bf16[16,4,24,768]{3,2,1,0:T(8,128)(2,1)} %bitcast.12, s32[1024]{0:T(1024)S(1)} %pad_clamp_fusion.1), kind=kCustom, calls=%fused_computation.clone | custom fusion | bytes 4718656 | tf_op jit(solution)/shard_map/jit(_take)/gather | solution.py:68
  65.3 3.8 %gather_fusion.2 = bf16[16,4,24,768]{3,2,1,0:T(8,128)(2,1)} fusion(bf16[16,4,24,768]{3,2,1,0:T(8,128)(2,1)} %bitcast.13, s32[1024]{0:T(1024)S(1)} %pad_clamp_fusion), kind=kCustom, calls=%fused_computation.1.clone | custom fusion | bytes 4718656 | tf_op jit(solution)/shard_map/jit(_take)/gather | solution.py:69
  69.1 2.9 %select_bitcast_fusion.1 = (bf16[16,1,4,24,768]{4,3,2,0,1:T(8,128)(2,1)S(1)}, bf16[16,1,4,24,768]{4,3,2,0,1:T(8,128)(2,1)S(1)}) fusion(pred[]{:T(512)S(6)} %eq.15, bf16[16,4,24,768]{3,2,1,0:T(8,128)(2,1)} %gather_fusion.1, pred[16]{0:T(512)(128)(4,1)S(1)} %get-tuple-element.23, bf16[16,4,24,768]{3,2,1,0:T(8,128)(2,1)} %gather_fusion.2, ...), kind=kLoop, calls=%fused_computation.19 | loop fusion | flops 4718592 | bytes 9437217 | tf_op jit(solution)/shard_map/stack | solution.py:72
  72.4 1.3 fusion.32
  73.7 1.1 copy.11
  74.8 1.1 copy.10
  76.0 7.7 %fusion = f32[2,768,768]{2,1,0:T(8,128)} fusion(bf16[768,768,1]{1,0,2:T(8,128)(2,1)} %bitcast.93, bf16[2,768,768]{2,1,0:T(8,128)(2,1)S(1)} %copy-done), kind=kOutput, calls=%fused_computation.6 | convolution fusion | flops 3625058304 | bytes 8257536 | tf_op jit(solution)/shard_map/pad,bd->pab/dot_general | solution.py:111
  83.7 7.8 %fusion.2 = f32[2,768,768]{2,1,0:T(8,128)} fusion(bf16[768,768,1]{1,0,2:T(8,128)(2,1)} %bitcast.94, bf16[2,768,768]{2,1,0:T(8,128)(2,1)S(1)} %copy-done), kind=kOutput, calls=%fused_computation.8 | convolution fusion | flops 3625058304 | bytes 8257536 | tf_op jit(solution)/shard_map/pad,bd->pab/dot_general | solution.py:111
  91.5 2.4 %copy.9 = bf16[1,16,2,24,768]{4,3,2,1,0:T(8,128)(2,1)} copy(bf16[1,16,2,24,768]{4,3,0,1,2:T(8,128)(2,1)} %get-tuple-element.18) | data formatting | bytes 2359296 | tf_op jit(solution)/shard_map/slice | solution.py:107
  93.8 7.7 %fusion.4 = f32[2,768,768]{2,1,0:T(8,128)} fusion(bf16[768,768,1]{1,0,2:T(8,128)(2,1)} %bitcast.95, bf16[2,768,768]{2,1,0:T(8,128)(2,1)S(1)} %copy-done), kind=kOutput, calls=%fused_computation.10 | convolution fusion | flops 3625058304 | bytes 8257536 | tf_op jit(solution)/shard_map/pad,bd->pab/dot_general | solution.py:111
  102.6 11.3 %add_add_fusion = f32[2,768,768]{2,1,0:T(8,128)} fusion(f32[2,768,768]{2,1,0:T(8,128)} %fusion, f32[2,768,768]{2,1,0:T(8,128)} %fusion.2, f32[2,768,768]{2,1,0:T(8,128)} %fusion.4, bf16[768,768,1]{1,0,2:T(8,128)(2,1)} %bitcast.92, bf16[2,768,768]{2,1,0:T(8,128)(2,1)S(1)} %copy-done), kind=kOutput, calls=%fused_computation.4 | convolution fusion | flops 3628597248 | bytes 22413312 | tf_op jit(solution)/shard_map/pad,bd->pab/dot_general | solution.py:111
  113.9 3.2 %fusion.25 = (bf16[2,192,768]{2,1,0:T(8,128)(2,1)S(1)}, bf16[2,192,768]{2,1,0:T(8,128)(2,1)}, bf16[2,192,768]{2,1,0:T(8,128)(2,1)}) fusion(f32[2,4,192,768]{3,2,1,0:T(8,128)} %bitcast.87, s32[]{:T(128)S(6)} %select_n.136, s32[]{:T(128)S(6)} %select_n.134, s32[]{:T(128)S(6)} %select_n.132), kind=kLoop, calls=%fused_computation.33 | loop fusion | bytes 3538956 | tf_op jit(solution)/shard_map/convert_element_type | solution.py:91
  117.9 1.3 collective-permute-start.11
  119.2 1.3 collective-permute-start.8
  120.5 1.4 collective-permute-start.9
  121.8 1.4 collective-permute-start.10
  123.2 4.2 %collective-permute-done.11 = bf16[2,96,768]{2,1,0:T(8,128)(2,1)} collective-permute-done((bf16[2,96,768]{2,1,0:T(8,128)(2,1)S(1)}, bf16[2,96,768]{2,1,0:T(8,128)(2,1)}, u32[]{:S(2)}, u32[]{:S(2)}) %collective-permute-start.11) | collective-permute-done | bytes 294944 | tf_op jit(solution)/shard_map/ppermute | solution.py:78
  127.5 20.1 %collective-permute-done.10 = bf16[2,96,768]{2,1,0:T(8,128)(2,1)} collective-permute-done((bf16[2,96,768]{2,1,0:T(8,128)(2,1)}, bf16[2,96,768]{2,1,0:T(8,128)(2,1)}, u32[]{:S(2)}, u32[]{:S(2)}) %collective-permute-start.10) | collective-permute-done | bytes 294944 | tf_op jit(solution)/shard_map/ppermute | solution.py:78
  147.6 5.1 %collective-permute-done.12 = bf16[2,96,768]{2,1,0:T(8,128)(2,1)} collective-permute-done((bf16[2,96,768]{2,1,0:T(8,128)(2,1)}, bf16[2,96,768]{2,1,0:T(8,128)(2,1)}, u32[]{:S(2)}, u32[]{:S(2)}) %collective-permute-start.12) | collective-permute-done | bytes 294944 | tf_op jit(solution)/shard_map/ppermute | solution.py:78
  152.8 2.6 %fusion.14 = f32[2,192,768]{2,1,0:T(8,128)} fusion(bf16[2,192,768]{2,1,0:T(8,128)(2,1)S(1)} %collective-permute-done.9, bf16[2,192,768]{2,1,0:T(8,128)(2,1)S(1)} %collective-permute-done.8, f32[2,4,192,768]{3,2,1,0:T(8,128)} %bitcast.88, s32[]{:T(128)S(6)} %select_n.130, bf16[2,96,768]{2,1,0:T(8,128)(2,1)} %collective-permute-done.12, ...), kind=kLoop, calls=%fused_computation.26 | loop fusion | flops 2654208 | bytes 4128772 | tf_op jit(solution)/shard_map/add | solution.py:97
  (30 shorter events, 7.8 us)
Async XLA Ops:
  0.0 76.0 %copy-start = (bf16[2,768,768]{2,1,0:T(8,128)(2,1)S(1)}, bf16[2,768,768]{2,1,0:T(8,128)(2,1)}, u32[]{:S(2)}) copy-start(bf16[2,768,768]{2,1,0:T(8,128)(2,1)} %param.5) | copy-start | bytes 7077892
  0.0 9.6 %copy-start.1 = (s32[4,4]{1,0:T(4,128)S(1)}, s32[4,4]{1,0:T(4,128)}, u32[]{:S(2)}) copy-start(s32[4,4]{1,0:T(4,128)} %param.7) | copy-start | bytes 196
  0.0 28.1 %all-to-all-start = ((bf16[32,24,768]{2,1,0:T(8,128)(2,1)}), bf16[32,24,768]{2,1,0:T(8,128)(2,1)S(1)}, u32[]{:S(2)}, u32[]{:S(2)}) async-start(bf16[32,24,768]{2,1,0:T(8,128)(2,1)} %bitcast.91), calls=%async_computation | async-start | bytes 2359296 | tf_op jit(solution)/shard_map/all_to_all | solution.py:52
  30.3 4.4 %collective-permute-start = (bf16[4,24,768]{2,1,0:T(8,128)(2,1)S(1)}, bf16[4,24,768]{2,1,0:T(8,128)(2,1)S(1)}, u32[]{:S(2)}, u32[]{:S(2)}) collective-permute-start(bf16[4,24,768]{2,1,0:T(8,128)(2,1)S(1)} %broadcast_select_fusion.2), channel_id=1, source_target_pairs={{0,24},{4,100},{8,0},{12,108},{16,8},{20,116},{24,16},{28,124},{32... | collective-permute-start | bytes 442376 | tf_op jit(solution)/shard_map/ppermute | solution.py:35
  30.9 5.8 %collective-permute-start.1 = (bf16[4,24,768]{2,1,0:T(8,128)(2,1)S(1)}, bf16[4,24,768]{2,1,0:T(8,128)(2,1)S(1)}, u32[]{:S(2)}, u32[]{:S(2)}) collective-permute-start(bf16[4,24,768]{2,1,0:T(8,128)(2,1)S(1)} %broadcast_select_fusion.2), channel_id=1, source_target_pairs={{0,16},{4,68},{8,24},{12,76},{16,0},{20,84},{24,8},{28,92},{32,48}... | collective-permute-start | bytes 442376 | tf_op jit(solution)/shard_map/ppermute | solution.py:37
  32.0 6.3 %collective-permute-start.2 = (bf16[4,24,768]{2,1,0:T(8,128)(2,1)S(1)}, bf16[4,24,768]{2,1,0:T(8,128)(2,1)S(1)}, u32[]{:S(2)}, u32[]{:S(2)}) collective-permute-start(bf16[4,24,768]{2,1,0:T(8,128)(2,1)S(1)} %broadcast_select_fusion.2), channel_id=1, source_target_pairs={{0,8},{4,36},{8,16},{12,44},{16,24},{20,52},{24,0},{28,60},{32,40}... | collective-permute-start | bytes 442376 | tf_op jit(solution)/shard_map/ppermute | solution.py:34
  38.4 10.3 %collective-permute-start.4 = (bf16[4,4,24,768]{3,2,1,0:T(8,128)(2,1)S(1)}, bf16[4,4,24,768]{3,2,1,0:T(8,128)(2,1)S(1)}, u32[]{:S(2)}, u32[]{:S(2)}) collective-permute-start(bf16[4,4,24,768]{3,2,1,0:T(8,128)(2,1)S(1)} %get-tuple-element.22), channel_id=1, source_target_pairs={{0,32},{4,12},{8,40},{12,20},{16,48},{20,28},{24,56},{28,4},{32,64... | collective-permute-start | bytes 1769480 | tf_op jit(solution)/shard_map/ppermute | solution.py:34
  38.9 9.9 %collective-permute-start.3 = (bf16[4,4,24,768]{3,2,1,0:T(8,128)(2,1)S(1)}, bf16[4,4,24,768]{3,2,1,0:T(8,128)(2,1)S(1)}, u32[]{:S(2)}, u32[]{:S(2)}) collective-permute-start(bf16[4,4,24,768]{3,2,1,0:T(8,128)(2,1)S(1)} %get-tuple-element.22), channel_id=1, source_target_pairs={{0,96},{4,28},{8,104},{12,4},{16,112},{20,12},{24,120},{28,20},{32... | collective-permute-start | bytes 1769480 | tf_op jit(solution)/shard_map/ppermute | solution.py:35
  48.7 7.1 %collective-permute-start.5 = (bf16[2,4,24,768]{3,2,1,0:T(8,128)(2,1)S(1)}, bf16[2,4,24,768]{3,2,1,0:T(8,128)(2,1)S(1)}, u32[]{:S(2)}, u32[]{:S(2)}) collective-permute-start(bf16[2,4,24,768]{3,2,1,0:T(8,128)(2,1)S(1)} %slice.42), channel_id=1, source_target_pairs={{0,32},{4,12},{8,40},{12,20},{16,48},{20,28},{24,56},{28,4},{32,64... | collective-permute-start | bytes 884744 | tf_op jit(solution)/shard_map/ppermute | solution.py:39
  48.9 7.0 %collective-permute-start.6 = (bf16[2,4,24,768]{3,2,1,0:T(8,128)(2,1)S(1)}, bf16[2,4,24,768]{3,2,1,0:T(8,128)(2,1)S(1)}, u32[]{:S(2)}, u32[]{:S(2)}) collective-permute-start(bf16[2,4,24,768]{3,2,1,0:T(8,128)(2,1)S(1)} %slice.43), channel_id=1, source_target_pairs={{0,96},{4,28},{8,104},{12,4},{16,112},{20,12},{24,120},{28,20},{32... | collective-permute-start | bytes 884744 | tf_op jit(solution)/shard_map/ppermute | solution.py:40
  57.7 7.6 %collective-permute-start.7 = (bf16[4,4,4,24,768]{4,3,2,1,0:T(8,128)(2,1)}, bf16[4,4,4,24,768]{4,3,2,1,0:T(8,128)(2,1)}, u32[]{:S(2)}, u32[]{:S(2)}) collective-permute-start(bf16[4,4,4,24,768]{4,3,2,1,0:T(8,128)(2,1)} %pad_maximum_fusion), channel_id=1, source_target_pairs={{0,4},{4,0},{8,12},{12,8},{16,20},{20,16},{24,28},{28,24},{32,36},... | collective-permute-start | bytes 7077896 | tf_op jit(solution)/shard_map/ppermute | solution.py:57
  117.9 9.6 %collective-permute-start.11 = (bf16[2,96,768]{2,1,0:T(8,128)(2,1)S(1)}, bf16[2,96,768]{2,1,0:T(8,128)(2,1)}, u32[]{:S(2)}, u32[]{:S(2)}) collective-permute-start(bf16[2,96,768]{2,1,0:T(8,128)(2,1)S(1)} %get-tuple-element.20), channel_id=1, source_target_pairs={{0,1},{1,2},{2,3},{3,0},{4,5},{5,6},{6,7},{7,4},{8,9},{9,10},{10,1... | collective-permute-start | bytes 884744 | tf_op jit(solution)/shard_map/ppermute | solution.py:78
  119.2 28.5 %collective-permute-start.8 = (bf16[2,192,768]{2,1,0:T(8,128)(2,1)}, bf16[2,192,768]{2,1,0:T(8,128)(2,1)S(1)}, u32[]{:S(2)}, u32[]{:S(2)}) collective-permute-start(bf16[2,192,768]{2,1,0:T(8,128)(2,1)} %get-tuple-element.14), channel_id=1, source_target_pairs={{0,1},{1,2},{2,3},{3,0},{4,5},{5,6},{6,7},{7,4},{8,9},{9,10},{10,1... | collective-permute-start | bytes 1769480 | tf_op jit(solution)/shard_map/ppermute | solution.py:78
  120.5 27.2 %collective-permute-start.9 = (bf16[2,192,768]{2,1,0:T(8,128)(2,1)}, bf16[2,192,768]{2,1,0:T(8,128)(2,1)S(1)}, u32[]{:S(2)}, u32[]{:S(2)}) collective-permute-start(bf16[2,192,768]{2,1,0:T(8,128)(2,1)} %get-tuple-element.13), channel_id=1, source_target_pairs={{0,3},{1,0},{2,1},{3,2},{4,7},{5,4},{6,5},{7,6},{8,11},{9,8},{10,9... | collective-permute-start | bytes 1769480 | tf_op jit(solution)/shard_map/ppermute | solution.py:78
  121.8 25.8 %collective-permute-start.10 = (bf16[2,96,768]{2,1,0:T(8,128)(2,1)}, bf16[2,96,768]{2,1,0:T(8,128)(2,1)}, u32[]{:S(2)}, u32[]{:S(2)}) collective-permute-start(bf16[2,96,768]{2,1,0:T(8,128)(2,1)} %get-tuple-element.19), channel_id=1, source_target_pairs={{0,2},{1,3},{2,0},{3,1},{4,6},{5,7},{6,4},{7,5},{8,10},{9,11},{10,... | collective-permute-start | bytes 884744 | tf_op jit(solution)/shard_map/ppermute | solution.py:78
  127.5 25.3 %collective-permute-start.12 = (bf16[2,96,768]{2,1,0:T(8,128)(2,1)}, bf16[2,96,768]{2,1,0:T(8,128)(2,1)}, u32[]{:S(2)}, u32[]{:S(2)}) collective-permute-start(bf16[2,96,768]{2,1,0:T(8,128)(2,1)} %collective-permute-done.11), channel_id=1, source_target_pairs={{0,1},{1,2},{2,3},{3,0},{4,5},{5,6},{6,7},{7,4},{8,9},{9,10},{10,1... | collective-permute-start | bytes 884744 | tf_op jit(solution)/shard_map/ppermute | solution.py:78

commit v9 on v7

--- a/solution.py
+++ b/solution.py
@@ -29,13 +29,16 @@
     return perm
 
 
-def ring_gather(piece, sizes, stage):
+def ring_gather(piece, sizes, stage, direct_far=False):
     half = piece.shape[0] // 2
     from_prev = lax.ppermute(piece, PAIR, ring_perm(sizes, stage, 1))
     from_next = lax.ppermute(piece, PAIR, ring_perm(sizes, stage, -1))
-    far_low = lax.ppermute(from_prev[:half], PAIR, ring_perm(sizes, stage, 1))
-    far_high = lax.ppermute(from_next[half:], PAIR, ring_perm(sizes, stage, -1))
-    far = jnp.concatenate([far_low, far_high], axis=0)
+    if direct_far:
+        far = lax.ppermute(piece, PAIR, ring_perm(sizes, stage, 2))
+    else:
+        far_low = lax.ppermute(from_prev[:half], PAIR, ring_perm(sizes, stage, 1))
+        far_high = lax.ppermute(from_next[half:], PAIR, ring_perm(sizes, stage, -1))
+        far = jnp.concatenate([far_low, far_high], axis=0)
     return jnp.stack([piece, from_next, far, from_prev], axis=0)
 
 
@@ -48,7 +51,7 @@
     pieces = own_vector.reshape(devices, piece, cols)
     pieces = lax.all_to_all(pieces, PAIR, 0, 0, tiled=True)
     picked = jnp.take(pieces, owned_slots, axis=0)
-    first = ring_gather(picked, sizes, 1)
+    first = ring_gather(picked, sizes, 1, direct_far=True)
     both = ring_gather(first, sizes, 2)
     swap = [(q, q ^ 1) for q in range(devices)]
     other = lax.ppermute(both, PAIR, swap)

time: 154 us -> 148 us (0.961)
  starting transfers between devices: 28.7 us -> 25.8 us
  waiting for transfers between devices: 66.6 us -> 63.8 us
    ppermute x3, waiting for transfers between devices: 28.7 us -> 24 us  [shifted(): lax.ppermute(value, 'vgrp', [(g, (g + step) % groups) for g in range(grou...]
    ppermute x2 -> x1, starting transfers between devices: 5.44 us -> 2.72 us  [ring_gather(): far_high = lax.ppermute(from_next[half:], PAIR, ring_perm(sizes, stage, -1))]
    ppermute x2, starting transfers between devices: 5.3 us -> 2.82 us  [ring_gather(): from_next = lax.ppermute(piece, PAIR, ring_perm(sizes, stage, -1))]
    ppermute x0 -> x1, waiting for transfers between devices: none -> 2.05 us  [ring_gather(): far = lax.ppermute(piece, PAIR, ring_perm(sizes, stage, 2))]
    ppermute x3, starting transfers between devices: 3.77 us -> 5.59 us  [shifted(): lax.ppermute(value, 'vgrp', [(g, (g + step) % groups) for g in range(grou...]
    ppermute x2 -> x1, waiting for transfers between devices: 4.67 us -> 4.3 us  [ring_gather(): far_low = lax.ppermute(from_prev[:half], PAIR, ring_perm(sizes, stage, 1))]
  transfers between devices with their start and end apart: 13 -> 12, of which waited for: 8 -> 9; matrix products, arithmetic and copies ran while one was open for 1% -> 1% of each run, Pallas kernels for 0% -> 0%
where the time goes in v9:
time: 148 us
  waiting for transfers between devices  63.8 us (43%)
  matrix products  31.8 us (21%)
  starting transfers between devices  25.8 us (17%)
  other arithmetic  14.4 us (10%)
  local copies, waits for them, and re-layouts  11.8 us (8%)
    dot_general x4, matrix products, on_device(): jnp.einsum('pad,bd->pab', half_product, vector, preferred_element_type=jn...  31.8 us
    ppermute x3, waiting for transfers between devices, shifted(): lax.ppermute(value, 'vgrp', [(g, (g + step) % groups) for g in range(grou...  24 us
    all_to_all x1, waiting for transfers between devices, gather_slots(): pieces = lax.all_to_all(pieces, PAIR, 0, 0, tiled=True)  18.5 us
    all_to_all x1, starting transfers between devices, gather_slots(): pieces = lax.all_to_all(pieces, PAIR, 0, 0, tiled=True)  9.55 us
    ppermute x2, waiting for transfers between devices, ring_gather(): from_prev = lax.ppermute(piece, PAIR, ring_perm(sizes, stage, 1))  9.14 us
    ppermute x3, starting transfers between devices, shifted(): lax.ppermute(value, 'vgrp', [(g, (g + step) % groups) for g in range(grou...  5.59 us
    gather x1, local copies, waits for them, and re-layouts, gather_slots(): ordered = jnp.take(stacked, index, axis=0)  5.35 us
    concatenate x1, other arithmetic, gather_slots(): jnp.concatenate([both.reshape((chips,) + both.shape[2:]), other.reshape((...  4.91 us
  transfers between devices with their start and end apart: 12, of which 9 were waited for; matrix products, arithmetic and copies ran while one was open for 1% of the time, Pallas kernels for 0%

profile of v9, /device:TPU:1, one launch (start us, length us, event | category | flops | bytes accessed | tf_op | source)
XLA Modules:
  0.0 147.7 jit_solution(17024600319862689084)
XLA Ops:
  0.0 9.6 %all-to-all-start = ((bf16[32,24,768]{2,1,0:T(8,128)(2,1)}), bf16[32,24,768]{2,1,0:T(8,128)(2,1)S(1)}, u32[]{:S(2)}, u32[]{:S(2)}) async-start(bf16[32,24,768]{2,1,0:T(8,128)(2,1)} %bitcast.93), calls=%async_computation | async-start | bytes 2359296 | tf_op jit(solution)/shard_map/all_to_all | solution.py:52
  9.6 18.5 %all-to-all-done = bf16[32,24,768]{2,1,0:T(8,128)(2,1)S(1)} async-done(((bf16[32,24,768]{2,1,0:T(8,128)(2,1)}), bf16[32,24,768]{2,1,0:T(8,128)(2,1)S(1)}, u32[]{:S(2)}, u32[]{:S(2)}) %all-to-all-start) | async-done | bytes 1179680 | tf_op jit(solution)/shard_map/all_to_all | solution.py:52
  28.1 1.2 gather_fusion
  29.3 1.0 broadcast_select_fusion
  30.3 0.6 collective-permute-start
  30.9 1.1 collective-permute-start.1
  32.3 1.0 bitcast_select_fusion
  33.3 1.4 collective-permute-done
  34.7 2.1 %collective-permute-done.1 = bf16[4,24,768]{2,1,0:T(8,128)(2,1)S(1)} collective-permute-done((bf16[4,24,768]{2,1,0:T(8,128)(2,1)S(1)}, bf16[4,24,768]{2,1,0:T(8,128)(2,1)S(1)}, u32[]{:S(2)}, u32[]{:S(2)}) %collective-permute-start.1) | collective-permute-done | bytes 147488 | tf_op jit(solution)/shard_map/ppermute | solution.py:37
  36.7 1.6 %collective-permute-done.2 = bf16[4,24,768]{2,1,0:T(8,128)(2,1)S(1)} collective-permute-done((bf16[4,24,768]{2,1,0:T(8,128)(2,1)S(1)}, bf16[4,24,768]{2,1,0:T(8,128)(2,1)S(1)}, u32[]{:S(2)}, u32[]{:S(2)}) %collective-permute-start.2) | collective-permute-done | bytes 147488 | tf_op jit(solution)/shard_map/ppermute | solution.py:34
  38.4 0.5 collective-permute-start.4
  38.9 2.2 %collective-permute-start.3 = (bf16[4,4,24,768]{3,2,1,0:T(8,128)(2,1)S(1)}, bf16[4,4,24,768]{3,2,1,0:T(8,128)(2,1)S(1)}, u32[]{:S(2)}, u32[]{:S(2)}) collective-permute-start(bf16[4,4,24,768]{3,2,1,0:T(8,128)(2,1)S(1)} %get-tuple-element.13), channel_id=1, source_target_pairs={{0,96},{4,28},{8,104},{12,4},{16,112},{20,12},{24,120},{28,20},{32... | collective-permute-start | bytes 1769480 | tf_op jit(solution)/shard_map/ppermute | solution.py:35
  41.1 7.6 %collective-permute-done.4 = bf16[4,4,24,768]{3,2,1,0:T(8,128)(2,1)S(1)} collective-permute-done((bf16[4,4,24,768]{3,2,1,0:T(8,128)(2,1)S(1)}, bf16[4,4,24,768]{3,2,1,0:T(8,128)(2,1)S(1)}, u32[]{:S(2)}, u32[]{:S(2)}) %collective-permute-start.4) | collective-permute-done | bytes 589856 | tf_op jit(solution)/shard_map/ppermute | solution.py:34
  48.9 2.7 %collective-permute-start.6 = (bf16[2,4,24,768]{3,2,1,0:T(8,128)(2,1)S(1)}, bf16[2,4,24,768]{3,2,1,0:T(8,128)(2,1)S(1)}, u32[]{:S(2)}, u32[]{:S(2)}) collective-permute-start(bf16[2,4,24,768]{3,2,1,0:T(8,128)(2,1)S(1)} %slice.33), channel_id=1, source_target_pairs={{0,96},{4,28},{8,104},{12,4},{16,112},{20,12},{24,120},{28,20},{32... | collective-permute-start | bytes 884744 | tf_op jit(solution)/shard_map/ppermute | solution.py:40
  51.6 4.3 %collective-permute-done.5 = bf16[2,4,24,768]{3,2,1,0:T(8,128)(2,1)S(1)} collective-permute-done((bf16[2,4,24,768]{3,2,1,0:T(8,128)(2,1)S(1)}, bf16[2,4,24,768]{3,2,1,0:T(8,128)(2,1)S(1)}, u32[]{:S(2)}, u32[]{:S(2)}) %collective-permute-start.5) | collective-permute-done | bytes 294944 | tf_op jit(solution)/shard_map/ppermute | solution.py:39
  55.9 1.7 %pad_maximum_fusion.1 = bf16[4,4,4,24,768]{4,3,2,1,0:T(8,128)(2,1)} fusion(bf16[1,4,4,24,768]{4,3,2,1,0:T(8,128)(2,1)S(1)} %bitcast.87, bf16[1,4,4,24,768]{4,3,2,1,0:T(8,128)(2,1)S(1)} %maximum_bitcast_fusion, bf16[1,4,4,24,768]{4,3,2,1,0:T(8,128)(2,1)S(1)} %bitcast.88, bf16[1,4,4,24,768]{4,3,2,1,0:T(8,128)(2,1)S(1)} %get-tuple-element.12), kind=kLoop, calls=%fused_computation.5 | loop fusion | flops 3538944 | bytes 4718592 | tf_op jit(solution)/shard_map/stack | solution.py:42
  57.7 3.1 %collective-permute-start.7 = (bf16[4,4,4,24,768]{4,3,2,1,0:T(8,128)(2,1)}, bf16[4,4,4,24,768]{4,3,2,1,0:T(8,128)(2,1)}, u32[]{:S(2)}, u32[]{:S(2)}) collective-permute-start(bf16[4,4,4,24,768]{4,3,2,1,0:T(8,128)(2,1)} %pad_maximum_fusion.1), channel_id=1, source_target_pairs={{0,4},{4,0},{8,12},{12,8},{16,20},{20,16},{24,28},{28,24},{32,36},... | collective-permute-start | bytes 7077896 | tf_op jit(solution)/shard_map/ppermute | solution.py:57
  60.9 4.4 %collective-permute-done.7 = bf16[4,4,4,24,768]{4,3,2,1,0:T(8,128)(2,1)} collective-permute-done((bf16[4,4,4,24,768]{4,3,2,1,0:T(8,128)(2,1)}, bf16[4,4,4,24,768]{4,3,2,1,0:T(8,128)(2,1)}, u32[]{:S(2)}, u32[]{:S(2)}) %collective-permute-start.7) | collective-permute-done | bytes 2359328 | tf_op jit(solution)/shard_map/ppermute | solution.py:57
  65.3 4.9 %pad_maximum_fusion = bf16[32,4,24,768]{3,2,1,0:T(8,128)(2,1)} fusion(bf16[16,4,24,768]{3,2,1,0:T(8,128)(2,1)} %bitcast.13, bf16[16,4,24,768]{3,2,1,0:T(8,128)(2,1)} %bitcast.12), kind=kLoop, calls=%fused_computation.2 | loop fusion | flops 2359296 | bytes 9437184 | tf_op jit(solution)/shard_map/concatenate | solution.py:59
  70.2 5.4 %gather_fusion.1 = bf16[32,4,24,768]{3,2,1,0:T(8,128)(2,1)} fusion(bf16[32,4,24,768]{3,2,1,0:T(8,128)(2,1)} %pad_maximum_fusion, s32[1024]{0:T(1024)S(1)} %pad_clamp_fusion), kind=kCustom, calls=%fused_computation.1 | custom fusion | bytes 9437312 | tf_op jit(solution)/shard_map/jit(_take)/gather | solution.py:70
  75.6 2.9 %select_bitcast_fusion = bf16[4,32,24,768]{3,2,0,1:T(8,128)(2,1)S(1)} fusion(bf16[32,4,24,768]{3,2,1,0:T(8,128)(2,1)} %gather_fusion.1, pred[32]{0:T(512)(128)(4,1)S(1)} %compare_and_fusion.1), kind=kLoop, calls=%fused_computation.4 | loop fusion | flops 2359296 | bytes 9437216 | tf_op jit(solution)/shard_map/jit(_take)/select_n | solution.py:70
  78.4 1.9 %fusion.41 = (bf16[1,32,24,768]{3,2,0,1:T(8,128)(2,1)S(1)}, bf16[1,32,24,768]{3,2,0,1:T(8,128)(2,1)}, bf16[1,32,24,768]{3,2,0,1:T(8,128)(2,1)}, bf16[1,32,24,768]{3,2,0,1:T(8,128)(2,1)}) fusion(bf16[4,32,24,768]{3,2,0,1:T(8,128)(2,1)S(1)} %select_bitcast_fusion), kind=kLoop, calls=%fused_computation.92 | loop fusion | bytes 9437184 | tf_op jit(solution)/shard_map/slice | solution.py:101
  80.3 7.6 %fusion = f32[2,768,768]{2,1,0:T(8,128)} fusion(bf16[768,768,1]{1,0,2:T(8,128)(2,1)} %bitcast.92, bf16[2,768,768]{2,1,0:T(8,128)(2,1)S(1)} %copy-done), kind=kOutput, calls=%fused_computation.6 | convolution fusion | flops 3625058304 | bytes 8257536 | tf_op jit(solution)/shard_map/pad,bd->pab/dot_general | solution.py:105
  87.9 7.6 %fusion.2 = f32[2,768,768]{2,1,0:T(8,128)} fusion(bf16[768,768,1]{1,0,2:T(8,128)(2,1)} %bitcast.91, bf16[2,768,768]{2,1,0:T(8,128)(2,1)S(1)} %copy-done), kind=kOutput, calls=%fused_computation.8 | convolution fusion | flops 3625058304 | bytes 8257536 | tf_op jit(solution)/shard_map/pad,bd->pab/dot_general | solution.py:105
  95.6 7.7 %fusion.4 = f32[2,768,768]{2,1,0:T(8,128)} fusion(bf16[768,768,1]{1,0,2:T(8,128)(2,1)} %bitcast.90, bf16[2,768,768]{2,1,0:T(8,128)(2,1)S(1)} %copy-done), kind=kOutput, calls=%fused_computation.10 | convolution fusion | flops 3625058304 | bytes 8257536 | tf_op jit(solution)/shard_map/pad,bd->pab/dot_general | solution.py:105
  103.3 8.8 %add_add_fusion = f32[2,768,768]{2,1,0:T(8,128)} fusion(f32[2,768,768]{2,1,0:T(8,128)} %fusion, f32[2,768,768]{2,1,0:T(8,128)} %fusion.2, f32[2,768,768]{2,1,0:T(8,128)} %fusion.4, bf16[768,768,1]{1,0,2:T(8,128)(2,1)S(1)} %bitcast.89, bf16[2,768,768]{2,1,0:T(8,128)(2,1)S(1)} %copy-done), kind=kOutput, calls=%fused_computation.3 | convolution fusion | flops 3628597248 | bytes 22413312 | tf_op jit(solution)/shard_map/pad,bd->pab/dot_general | solution.py:105
  112.1 3.3 %fusion.23 = (bf16[2,192,768]{2,1,0:T(8,128)(2,1)}, bf16[2,192,768]{2,1,0:T(8,128)(2,1)}, bf16[2,192,768]{2,1,0:T(8,128)(2,1)}) fusion(f32[2,4,192,768]{3,2,1,0:T(8,128)} %bitcast.85, s32[]{:T(128)S(6)} %select_n.241, s32[]{:T(128)S(6)} %select_n.243, s32[]{:T(128)S(6)} %select_n.245), kind=kLoop, calls=%fused_computation.27 | loop fusion | bytes 3538956 | tf_op jit(solution)/shard_map/convert_element_type | solution.py:87
  115.4 2.9 %collective-permute-start.10 = (bf16[2,192,768]{2,1,0:T(8,128)(2,1)}, bf16[2,192,768]{2,1,0:T(8,128)(2,1)S(1)}, u32[]{:S(2)}, u32[]{:S(2)}) collective-permute-start(bf16[2,192,768]{2,1,0:T(8,128)(2,1)} %get-tuple-element.7), channel_id=1, source_target_pairs={{0,2},{1,3},{2,0},{3,1},{4,6},{5,7},{6,4},{7,5},{8,10},{9,11},{10,... | collective-permute-start | bytes 1769480 | tf_op jit(solution)/shard_map/ppermute | solution.py:76
  118.7 2.3 %collective-permute-start.9 = (bf16[2,192,768]{2,1,0:T(8,128)(2,1)}, bf16[2,192,768]{2,1,0:T(8,128)(2,1)}, u32[]{:S(2)}, u32[]{:S(2)}) collective-permute-start(bf16[2,192,768]{2,1,0:T(8,128)(2,1)} %get-tuple-element.6), channel_id=1, source_target_pairs={{0,3},{1,0},{2,1},{3,2},{4,7},{5,4},{6,5},{7,6},{8,11},{9,8},{10,9... | collective-permute-start | bytes 1769480 | tf_op jit(solution)/shard_map/ppermute | solution.py:76
  121.0 10.7 %collective-permute-done.10 = bf16[2,192,768]{2,1,0:T(8,128)(2,1)S(1)} collective-permute-done((bf16[2,192,768]{2,1,0:T(8,128)(2,1)}, bf16[2,192,768]{2,1,0:T(8,128)(2,1)S(1)}, u32[]{:S(2)}, u32[]{:S(2)}) %collective-permute-start.10) | collective-permute-done | bytes 589856 | tf_op jit(solution)/shard_map/ppermute | solution.py:76
  131.6 13.3 %collective-permute-done.8 = bf16[2,192,768]{2,1,0:T(8,128)(2,1)S(1)} collective-permute-done((bf16[2,192,768]{2,1,0:T(8,128)(2,1)}, bf16[2,192,768]{2,1,0:T(8,128)(2,1)S(1)}, u32[]{:S(2)}, u32[]{:S(2)}) %collective-permute-start.8) | collective-permute-done | bytes 589856 | tf_op jit(solution)/shard_map/ppermute | solution.py:76
  145.0 2.7 %fusion.14 = f32[2,192,768]{2,1,0:T(8,128)} fusion(bf16[2,192,768]{2,1,0:T(8,128)(2,1)S(1)} %collective-permute-done.10, bf16[2,192,768]{2,1,0:T(8,128)(2,1)} %collective-permute-done.9, bf16[2,192,768]{2,1,0:T(8,128)(2,1)S(1)} %collective-permute-done.8, f32[2,4,192,768]{3,2,1,0:T(8,128)} %bitcast.86, s32[]{:T(128)S(6)} %select_n.239), kind=kLoop, calls=%fused_computation.22 | loop fusion | flops 1769472 | bytes 4128772 | tf_op jit(solution)/shard_map/add | solution.py:91
  (20 shorter events, 1.1 us)
Async XLA Ops:
  0.0 80.3 %copy-start = (bf16[2,768,768]{2,1,0:T(8,128)(2,1)S(1)}, bf16[2,768,768]{2,1,0:T(8,128)(2,1)}, u32[]{:S(2)}) copy-start(bf16[2,768,768]{2,1,0:T(8,128)(2,1)} %param.3) | copy-start | bytes 7077892
  0.0 9.6 %copy-start.1 = (s32[4,4]{1,0:T(4,128)S(1)}, s32[4,4]{1,0:T(4,128)}, u32[]{:S(2)}) copy-start(s32[4,4]{1,0:T(4,128)} %param.5) | copy-start | bytes 196
  0.0 28.1 %all-to-all-start = ((bf16[32,24,768]{2,1,0:T(8,128)(2,1)}), bf16[32,24,768]{2,1,0:T(8,128)(2,1)S(1)}, u32[]{:S(2)}, u32[]{:S(2)}) async-start(bf16[32,24,768]{2,1,0:T(8,128)(2,1)} %bitcast.93), calls=%async_computation | async-start | bytes 2359296 | tf_op jit(solution)/shard_map/all_to_all | solution.py:52
  30.3 4.4 %collective-permute-start = (bf16[4,24,768]{2,1,0:T(8,128)(2,1)S(1)}, bf16[4,24,768]{2,1,0:T(8,128)(2,1)S(1)}, u32[]{:S(2)}, u32[]{:S(2)}) collective-permute-start(bf16[4,24,768]{2,1,0:T(8,128)(2,1)S(1)} %broadcast_select_fusion), channel_id=1, source_target_pairs={{0,24},{4,100},{8,0},{12,108},{16,8},{20,116},{24,16},{28,124},{32... | collective-permute-start | bytes 442376 | tf_op jit(solution)/shard_map/ppermute | solution.py:35
  30.9 5.8 %collective-permute-start.1 = (bf16[4,24,768]{2,1,0:T(8,128)(2,1)S(1)}, bf16[4,24,768]{2,1,0:T(8,128)(2,1)S(1)}, u32[]{:S(2)}, u32[]{:S(2)}) collective-permute-start(bf16[4,24,768]{2,1,0:T(8,128)(2,1)S(1)} %broadcast_select_fusion), channel_id=1, source_target_pairs={{0,16},{4,68},{8,24},{12,76},{16,0},{20,84},{24,8},{28,92},{32,48}... | collective-permute-start | bytes 442376 | tf_op jit(solution)/shard_map/ppermute | solution.py:37
  32.0 6.3 %collective-permute-start.2 = (bf16[4,24,768]{2,1,0:T(8,128)(2,1)S(1)}, bf16[4,24,768]{2,1,0:T(8,128)(2,1)S(1)}, u32[]{:S(2)}, u32[]{:S(2)}) collective-permute-start(bf16[4,24,768]{2,1,0:T(8,128)(2,1)S(1)} %broadcast_select_fusion), channel_id=1, source_target_pairs={{0,8},{4,36},{8,16},{12,44},{16,24},{20,52},{24,0},{28,60},{32,40}... | collective-permute-start | bytes 442376 | tf_op jit(solution)/shard_map/ppermute | solution.py:34
  38.4 10.3 %collective-permute-start.4 = (bf16[4,4,24,768]{3,2,1,0:T(8,128)(2,1)S(1)}, bf16[4,4,24,768]{3,2,1,0:T(8,128)(2,1)S(1)}, u32[]{:S(2)}, u32[]{:S(2)}) collective-permute-start(bf16[4,4,24,768]{3,2,1,0:T(8,128)(2,1)S(1)} %get-tuple-element.13), channel_id=1, source_target_pairs={{0,32},{4,12},{8,40},{12,20},{16,48},{20,28},{24,56},{28,4},{32,64... | collective-permute-start | bytes 1769480 | tf_op jit(solution)/shard_map/ppermute | solution.py:34
  38.9 9.9 %collective-permute-start.3 = (bf16[4,4,24,768]{3,2,1,0:T(8,128)(2,1)S(1)}, bf16[4,4,24,768]{3,2,1,0:T(8,128)(2,1)S(1)}, u32[]{:S(2)}, u32[]{:S(2)}) collective-permute-start(bf16[4,4,24,768]{3,2,1,0:T(8,128)(2,1)S(1)} %get-tuple-element.13), channel_id=1, source_target_pairs={{0,96},{4,28},{8,104},{12,4},{16,112},{20,12},{24,120},{28,20},{32... | collective-permute-start | bytes 1769480 | tf_op jit(solution)/shard_map/ppermute | solution.py:35
  48.7 7.1 %collective-permute-start.5 = (bf16[2,4,24,768]{3,2,1,0:T(8,128)(2,1)S(1)}, bf16[2,4,24,768]{3,2,1,0:T(8,128)(2,1)S(1)}, u32[]{:S(2)}, u32[]{:S(2)}) collective-permute-start(bf16[2,4,24,768]{3,2,1,0:T(8,128)(2,1)S(1)} %slice.32), channel_id=1, source_target_pairs={{0,32},{4,12},{8,40},{12,20},{16,48},{20,28},{24,56},{28,4},{32,64... | collective-permute-start | bytes 884744 | tf_op jit(solution)/shard_map/ppermute | solution.py:39
  48.9 7.0 %collective-permute-start.6 = (bf16[2,4,24,768]{3,2,1,0:T(8,128)(2,1)S(1)}, bf16[2,4,24,768]{3,2,1,0:T(8,128)(2,1)S(1)}, u32[]{:S(2)}, u32[]{:S(2)}) collective-permute-start(bf16[2,4,24,768]{3,2,1,0:T(8,128)(2,1)S(1)} %slice.33), channel_id=1, source_target_pairs={{0,96},{4,28},{8,104},{12,4},{16,112},{20,12},{24,120},{28,20},{32... | collective-permute-start | bytes 884744 | tf_op jit(solution)/shard_map/ppermute | solution.py:40
  57.7 7.6 %collective-permute-start.7 = (bf16[4,4,4,24,768]{4,3,2,1,0:T(8,128)(2,1)}, bf16[4,4,4,24,768]{4,3,2,1,0:T(8,128)(2,1)}, u32[]{:S(2)}, u32[]{:S(2)}) collective-permute-start(bf16[4,4,4,24,768]{4,3,2,1,0:T(8,128)(2,1)} %pad_maximum_fusion.1), channel_id=1, source_target_pairs={{0,4},{4,0},{8,12},{12,8},{16,20},{20,16},{24,28},{28,24},{32,36},... | collective-permute-start | bytes 7077896 | tf_op jit(solution)/shard_map/ppermute | solution.py:57
  115.4 16.3 %collective-permute-start.10 = (bf16[2,192,768]{2,1,0:T(8,128)(2,1)}, bf16[2,192,768]{2,1,0:T(8,128)(2,1)S(1)}, u32[]{:S(2)}, u32[]{:S(2)}) collective-permute-start(bf16[2,192,768]{2,1,0:T(8,128)(2,1)} %get-tuple-element.7), channel_id=1, source_target_pairs={{0,2},{1,3},{2,0},{3,1},{4,6},{5,7},{6,4},{7,5},{8,10},{9,11},{10,... | collective-permute-start | bytes 1769480 | tf_op jit(solution)/shard_map/ppermute | solution.py:76
  118.3 26.7 %collective-permute-start.8 = (bf16[2,192,768]{2,1,0:T(8,128)(2,1)}, bf16[2,192,768]{2,1,0:T(8,128)(2,1)S(1)}, u32[]{:S(2)}, u32[]{:S(2)}) collective-permute-start(bf16[2,192,768]{2,1,0:T(8,128)(2,1)} %get-tuple-element.5), channel_id=1, source_target_pairs={{0,1},{1,2},{2,3},{3,0},{4,5},{5,6},{6,7},{7,4},{8,9},{9,10},{10,1... | collective-permute-start | bytes 1769480 | tf_op jit(solution)/shard_map/ppermute | solution.py:76
  118.7 26.3 %collective-permute-start.9 = (bf16[2,192,768]{2,1,0:T(8,128)(2,1)}, bf16[2,192,768]{2,1,0:T(8,128)(2,1)}, u32[]{:S(2)}, u32[]{:S(2)}) collective-permute-start(bf16[2,192,768]{2,1,0:T(8,128)(2,1)} %get-tuple-element.6), channel_id=1, source_target_pairs={{0,3},{1,0},{2,1},{3,2},{4,7},{5,4},{6,5},{7,6},{8,11},{9,8},{10,9... | collective-permute-start | bytes 1769480 | tf_op jit(solution)/shard_map/ppermute | solution.py:76

commit v10 on v9

--- a/solution.py
+++ b/solution.py
@@ -4,8 +4,8 @@
 from jax.sharding import Mesh
 from jax.sharding import PartitionSpec as P
 
+
 PAIR = ("z", "x", "core")
-CHIPS = ("z", "x")
 
 
 RING = 4
@@ -76,7 +76,7 @@
     return lax.ppermute(value, "vgrp", [(g, (g + step) % groups) for g in range(groups)])
 
 
-def scatter_sum(total, vgrp, groups):
+def prepare(total, vgrp, groups):
     pairs, rows, cols = total.shape
     block = rows // groups
     blocks = total.reshape(pairs, groups, block, cols)
@@ -84,11 +84,31 @@
     def pick(offset):
         return lax.dynamic_index_in_dim(blocks, (vgrp + offset) % groups, 1, keepdims=False)
 
-    ahead = shifted(pick(1).astype(jnp.bfloat16), 1, groups)
-    behind = shifted(pick(-1).astype(jnp.bfloat16), -1, groups)
-    far = shifted(pick(2).astype(jnp.bfloat16), 2, groups)
+    owed = tuple(pick(offset).astype(jnp.bfloat16) for offset in (1, -1, 2))
+    return pick(0), owed
+
+
+def exchange(own, owed, groups):
+    ahead, behind, far = owed
+    half = far.shape[1] // 2
+    ahead = shifted(ahead, 1, groups)
+    behind = shifted(behind, -1, groups)
+    far_low = shifted(far[:, :half], 2, groups)
+    far_high = shifted(far[:, half:], 1, groups)
+    far_high = shifted(far_high, 1, groups)
+    far = jnp.concatenate([far_low, far_high], axis=1)
     near = ahead.astype(jnp.float32) + behind.astype(jnp.float32)
-    return pick(0) + near + far.astype(jnp.float32)
+    return own + near + far.astype(jnp.float32)
+
+
+def columns(halves, vectors, lo, hi):
+    total = None
+    for slot, half_product in enumerate(halves):
+        term = jnp.einsum(
+            "pad,bd->pab", half_product, vectors[slot, lo:hi], preferred_element_type=jnp.float32
+        )
+        total = term if total is None else total + term
+    return total
 
 
 def on_device(amplitudes, cholesky_vectors, owner_order, sizes):
@@ -96,16 +116,19 @@
     groups = lax.psum(1, "vgrp")
     owned_slots = lax.dynamic_index_in_dim(owner_order, vgrp, 0, keepdims=False)
     vectors = gather_slots(cholesky_vectors[0, 0], owned_slots, sizes)
-    total = jnp.zeros(amplitudes.shape, jnp.float32)
-    for slot in range(owned_slots.shape[0]):
-        vector = vectors[slot]
-        half_product = jnp.einsum(
-            "ac,pcd->pad", vector, amplitudes, preferred_element_type=jnp.float32
+    halves = tuple(
+        jnp.einsum(
+            "ac,pcd->pad", vectors[slot], amplitudes, preferred_element_type=jnp.float32
         ).astype(jnp.bfloat16)
-        total = total + jnp.einsum(
-            "pad,bd->pab", half_product, vector, preferred_element_type=jnp.float32
-        )
-    return scatter_sum(total, vgrp, groups)
+        for slot in range(vectors.shape[0])
+    )
+    split = vectors.shape[1] // 2
+    own_a, owed_a = prepare(columns(halves, vectors, 0, split), vgrp, groups)
+    halves, owed_a = lax.optimization_barrier((halves, owed_a))
+    out_a = exchange(own_a, owed_a, groups)
+    own_b, owed_b = prepare(columns(halves, vectors, split, None), vgrp, groups)
+    out_b = exchange(own_b, owed_b, groups)
+    return jnp.concatenate([out_a, out_b], axis=2)
 
 
 def solution(mesh):

time: 148 us -> 145 us (0.980)
  matrix products: 31.8 us -> 19.7 us
  waiting for transfers between devices: 63.8 us -> 67.4 us
  starting transfers between devices: 25.8 us -> 28.9 us
    dot_general x4 -> x12, matrix products: 31.8 us -> 19.7 us  [the longest x8 11.7 us: columns(): jnp.einsum('pad,bd->pab', half_product, vectors[slot, lo:hi], preferred_e...]
    ppermute x2, waiting for transfers between devices: 1.37 us -> 8.14 us  [ring_gather(): from_next = lax.ppermute(piece, PAIR, ring_perm(sizes, stage, -1))]
    ppermute x2, waiting for transfers between devices: 9.14 us -> 2.95 us  [ring_gather(): from_prev = lax.ppermute(piece, PAIR, ring_perm(sizes, stage, 1))]
    ppermute x3 -> x10, starting transfers between devices: 5.59 us -> 9.19 us  [shifted(): lax.ppermute(value, 'vgrp', [(g, (g + step) % groups) for g in range(grou...]
    ppermute x1, waiting for transfers between devices: 0.01 us -> 3.56 us  [ring_gather(): far_high = lax.ppermute(from_next[half:], PAIR, ring_perm(sizes, stage, -1))]
    ppermute x3 -> x10, waiting for transfers between devices: 24 us -> 26.4 us  [shifted(): lax.ppermute(value, 'vgrp', [(g, (g + step) % groups) for g in range(grou...]
    ppermute x1, waiting for transfers between devices: 2.05 us -> 0.01 us  [ring_gather(): far = lax.ppermute(piece, PAIR, ring_perm(sizes, stage, 2))]
    convert_element_type x1 -> x2, local copies, waits for them, and re-layouts: 3.27 us -> 2.31 us  [prepare(): owed = tuple((pick(offset).astype(jnp.bfloat16) for offset in (1, -1, 2)))]
  transfers between devices with their start and end apart: 12 -> 19, of which waited for: 9 -> 13; matrix products, arithmetic and copies ran while one was open for 1% -> 2% of each run, Pallas kernels for 0% -> 0%
where the time goes in v10:
time: 145 us; the launch traced here: 143 us
  waiting for transfers between devices  67.4 us (46%)
  starting transfers between devices  28.9 us (20%)
  matrix products  19.7 us (14%)
  other arithmetic  15.4 us (11%)
  local copies, waits for them, and re-layouts  11.7 us (8%)
    ppermute x10, waiting for transfers between devices, shifted(): lax.ppermute(value, 'vgrp', [(g, (g + step) % groups) for g in range(grou...  26.4 us
    all_to_all x1, waiting for transfers between devices, gather_slots(): pieces = lax.all_to_all(pieces, PAIR, 0, 0, tiled=True)  18.5 us
    dot_general x8, matrix products, columns(): jnp.einsum('pad,bd->pab', half_product, vectors[slot, lo:hi], preferred_e...  11.7 us
    all_to_all x1, starting transfers between devices, gather_slots(): pieces = lax.all_to_all(pieces, PAIR, 0, 0, tiled=True)  9.55 us
    ppermute x10, starting transfers between devices, shifted(): lax.ppermute(value, 'vgrp', [(g, (g + step) % groups) for g in range(grou...  9.19 us
    ppermute x2, waiting for transfers between devices, ring_gather(): from_next = lax.ppermute(piece, PAIR, ring_perm(sizes, stage, -1))  8.14 us
    dot_general x4, matrix products, on_device(): jnp.einsum('ac,pcd->pad', vectors[slot], amplitudes, preferred_element_ty...  8.01 us
    gather x1, local copies, waits for them, and re-layouts, gather_slots(): ordered = jnp.take(stacked, index, axis=0)  5.35 us
  transfers between devices with their start and end apart: 19, of which 13 were waited for; matrix products, arithmetic and copies ran while one was open for 2% of the time, Pallas kernels for 0%

profile of v10, /device:TPU:1, one launch (start us, length us, event | category | flops | bytes accessed | tf_op | source)
XLA Modules:
  0.0 143.5 jit_solution(13044312847355367480)
XLA Ops:
  0.0 9.6 %all-to-all-start = ((bf16[32,24,768]{2,1,0:T(8,128)(2,1)}), bf16[32,24,768]{2,1,0:T(8,128)(2,1)S(1)}, u32[]{:S(2)}, u32[]{:S(2)}) async-start(bf16[32,24,768]{2,1,0:T(8,128)(2,1)} %bitcast.157), calls=%async_computation | async-start | bytes 2359296 | tf_op jit(solution)/shard_map/all_to_all | solution.py:52
  9.6 18.5 %all-to-all-done = bf16[32,24,768]{2,1,0:T(8,128)(2,1)S(1)} async-done(((bf16[32,24,768]{2,1,0:T(8,128)(2,1)}), bf16[32,24,768]{2,1,0:T(8,128)(2,1)S(1)}, u32[]{:S(2)}, u32[]{:S(2)}) %all-to-all-start) | async-done | bytes 1179680 | tf_op jit(solution)/shard_map/all_to_all | solution.py:52
  30.4 1.7 %collective-permute-start.1 = (bf16[4,24,768]{2,1,0:T(8,128)(2,1)S(1)}, bf16[4,24,768]{2,1,0:T(8,128)(2,1)S(1)}, u32[]{:S(2)}, u32[]{:S(2)}) collective-permute-start(bf16[4,24,768]{2,1,0:T(8,128)(2,1)S(1)} %broadcast_select_fusion), channel_id=1, source_target_pairs={{0,16},{4,68},{8,24},{12,76},{16,0},{20,84},{24,8},{28,92},{32,48}... | collective-permute-start | bytes 442376 | tf_op jit(solution)/shard_map/ppermute | solution.py:37
  34.5 2.9 %collective-permute-done.2 = bf16[4,24,768]{2,1,0:T(8,128)(2,1)S(1)} collective-permute-done((bf16[4,24,768]{2,1,0:T(8,128)(2,1)S(1)}, bf16[4,24,768]{2,1,0:T(8,128)(2,1)S(1)}, u32[]{:S(2)}, u32[]{:S(2)}) %collective-permute-start.2) | collective-permute-done | bytes 147488 | tf_op jit(solution)/shard_map/ppermute | solution.py:34
  38.1 1.4 collective-permute-start.3
  39.7 7.6 %collective-permute-done.3 = bf16[4,4,24,768]{3,2,1,0:T(8,128)(2,1)S(1)} collective-permute-done((bf16[4,4,24,768]{3,2,1,0:T(8,128)(2,1)S(1)}, bf16[4,4,24,768]{3,2,1,0:T(8,128)(2,1)S(1)}, u32[]{:S(2)}, u32[]{:S(2)}) %collective-permute-start.3) | collective-permute-done | bytes 589856 | tf_op jit(solution)/shard_map/ppermute | solution.py:35
  47.3 2.6 %collective-permute-start.6 = (bf16[2,4,24,768]{3,2,1,0:T(8,128)(2,1)S(1)}, bf16[2,4,24,768]{3,2,1,0:T(8,128)(2,1)S(1)}, u32[]{:S(2)}, u32[]{:S(2)}) collective-permute-start(bf16[2,4,24,768]{3,2,1,0:T(8,128)(2,1)S(1)} %slice.81), channel_id=1, source_target_pairs={{0,96},{4,28},{8,104},{12,4},{16,112},{20,12},{24,120},{28,20},{32... | collective-permute-start | bytes 884744 | tf_op jit(solution)/shard_map/ppermute | solution.py:40
  50.0 3.6 %collective-permute-done.6 = bf16[2,4,24,768]{3,2,1,0:T(8,128)(2,1)S(1)} collective-permute-done((bf16[2,4,24,768]{3,2,1,0:T(8,128)(2,1)S(1)}, bf16[2,4,24,768]{3,2,1,0:T(8,128)(2,1)S(1)}, u32[]{:S(2)}, u32[]{:S(2)}) %collective-permute-start.6) | collective-permute-done | bytes 294944 | tf_op jit(solution)/shard_map/ppermute | solution.py:40
  53.6 3.5 %collective-permute-done.5 = bf16[2,4,24,768]{3,2,1,0:T(8,128)(2,1)S(1)} collective-permute-done((bf16[2,4,24,768]{3,2,1,0:T(8,128)(2,1)S(1)}, bf16[2,4,24,768]{3,2,1,0:T(8,128)(2,1)S(1)}, u32[]{:S(2)}, u32[]{:S(2)}) %collective-permute-start.5) | collective-permute-done | bytes 294944 | tf_op jit(solution)/shard_map/ppermute | solution.py:39
  57.1 1.7 %pad_maximum_fusion.1 = bf16[4,4,4,24,768]{4,3,2,1,0:T(8,128)(2,1)} fusion(bf16[1,4,4,24,768]{4,3,2,1,0:T(8,128)(2,1)S(1)} %bitcast.152, bf16[1,4,4,24,768]{4,3,2,1,0:T(8,128)(2,1)S(1)} %maximum_bitcast_fusion, bf16[1,4,4,24,768]{4,3,2,1,0:T(8,128)(2,1)S(1)} %bitcast.151, bf16[1,4,4,24,768]{4,3,2,1,0:T(8,128)(2,1)S(1)} %get-tuple-element.29), kind=kLoop, calls=%fused_computation.4 | loop fusion | flops 3538944 | bytes 4718592 | tf_op jit(solution)/shard_map/stack | solution.py:42
  58.9 2.7 %collective-permute-start.7 = (bf16[4,4,4,24,768]{4,3,2,1,0:T(8,128)(2,1)}, bf16[4,4,4,24,768]{4,3,2,1,0:T(8,128)(2,1)}, u32[]{:S(2)}, u32[]{:S(2)}) collective-permute-start(bf16[4,4,4,24,768]{4,3,2,1,0:T(8,128)(2,1)} %pad_maximum_fusion.1), channel_id=1, source_target_pairs={{0,4},{4,0},{8,12},{12,8},{16,20},{20,16},{24,28},{28,24},{32,36},... | collective-permute-start | bytes 7077896 | tf_op jit(solution)/shard_map/ppermute | solution.py:57
  61.6 4.4 %collective-permute-done.7 = bf16[4,4,4,24,768]{4,3,2,1,0:T(8,128)(2,1)} collective-permute-done((bf16[4,4,4,24,768]{4,3,2,1,0:T(8,128)(2,1)}, bf16[4,4,4,24,768]{4,3,2,1,0:T(8,128)(2,1)}, u32[]{:S(2)}, u32[]{:S(2)}) %collective-permute-start.7) | collective-permute-done | bytes 2359328 | tf_op jit(solution)/shard_map/ppermute | solution.py:57
  66.1 4.9 %pad_maximum_fusion = bf16[32,4,24,768]{3,2,1,0:T(8,128)(2,1)} fusion(bf16[16,4,24,768]{3,2,1,0:T(8,128)(2,1)} %bitcast.13, bf16[16,4,24,768]{3,2,1,0:T(8,128)(2,1)} %bitcast.12), kind=kLoop, calls=%fused_computation.2 | loop fusion | flops 2359296 | bytes 9437184 | tf_op jit(solution)/shard_map/concatenate | solution.py:59
  71.0 5.4 %gather_fusion.1 = bf16[32,4,24,768]{3,2,1,0:T(8,128)(2,1)} fusion(bf16[32,4,24,768]{3,2,1,0:T(8,128)(2,1)} %pad_maximum_fusion, s32[1024]{0:T(1024)S(1)} %pad_clamp_fusion), kind=kCustom, calls=%fused_computation.1 | custom fusion | bytes 9437312 | tf_op jit(solution)/shard_map/jit(_take)/gather | solution.py:70
  76.4 2.9 %select_bitcast_fusion = bf16[4,32,24,768]{3,2,0,1:T(8,128)(2,1)S(1)} fusion(bf16[32,4,24,768]{3,2,1,0:T(8,128)(2,1)} %gather_fusion.1, pred[32]{0:T(512)(128)(4,1)S(1)} %compare_and_fusion.1), kind=kLoop, calls=%fused_computation.3 | loop fusion | flops 2359296 | bytes 9437216 | tf_op jit(solution)/shard_map/jit(_take)/select_n | solution.py:70
  79.9 2.0 %convert_bitcast_fusion.3 = bf16[2,768,768]{2,1,0:T(8,128)(2,1)S(1)} fusion(bf16[768,768,1]{1,0,2:T(8,128)(2,1)S(1)} %bitcast.156, bf16[2,768,768]{2,1,0:T(8,128)(2,1)S(1)} %copy-done), kind=kOutput, calls=%fused_computation.10 | convolution fusion | flops 1813118976 | bytes 5898240 | tf_op jit(solution)/shard_map/ac,pcd->pad/dot_general | solution.py:120
  81.9 2.0 %convert_bitcast_fusion.2 = bf16[2,768,768]{2,1,0:T(8,128)(2,1)S(1)} fusion(bf16[768,768,1]{1,0,2:T(8,128)(2,1)S(1)} %bitcast.155, bf16[2,768,768]{2,1,0:T(8,128)(2,1)S(1)} %copy-done), kind=kOutput, calls=%fused_computation.9 | convolution fusion | flops 1813118976 | bytes 5898240 | tf_op jit(solution)/shard_map/ac,pcd->pad/dot_general | solution.py:120
  83.9 2.0 %convert_bitcast_fusion.1 = bf16[2,768,768]{2,1,0:T(8,128)(2,1)S(1)} fusion(bf16[768,768,1]{1,0,2:T(8,128)(2,1)S(1)} %bitcast.154, bf16[2,768,768]{2,1,0:T(8,128)(2,1)S(1)} %copy-done), kind=kOutput, calls=%fused_computation.8 | convolution fusion | flops 1813118976 | bytes 5898240 | tf_op jit(solution)/shard_map/ac,pcd->pad/dot_general | solution.py:120
  85.9 2.0 %convert_bitcast_fusion = bf16[2,768,768]{2,1,0:T(8,128)(2,1)S(1)} fusion(bf16[768,768,1]{1,0,2:T(8,128)(2,1)S(1)} %bitcast.153, bf16[2,768,768]{2,1,0:T(8,128)(2,1)S(1)} %copy-done), kind=kOutput, calls=%fused_computation.6 | convolution fusion | flops 1813118976 | bytes 5898240 | tf_op jit(solution)/shard_map/ac,pcd->pad/dot_general | solution.py:120
  92.2 1.6 %add_add_fusion.1 = f32[2,768,384]{2,1,0:T(8,128)S(1)} fusion(f32[2,768,384]{2,1,0:T(8,128)S(1)} %fusion.3, f32[2,768,384]{2,1,0:T(8,128)S(1)} %fusion.5, f32[2,768,384]{2,1,0:T(8,128)S(1)} %fusion.4, bf16[2,768,768]{2,1,0:T(8,128)(2,1)S(1)} %convert_bitcast_fusion, bf16[4,768,768]{2,1,0:T(8,128)(2,1)S(1)} %bitcast.142), kind=kOutput, calls=%fused_computation.7 | convolution fusion | flops 907739136 | bytes 12386304 | tf_op jit(solution)/shard_map/pad,bd->pab/dot_general | solution.py:107
  98.0 1.4 fusion.1
  99.4 1.6 %add_add_fusion = f32[2,768,384]{2,1,0:T(8,128)S(1)} fusion(f32[2,768,384]{2,1,0:T(8,128)S(1)} %fusion, f32[2,768,384]{2,1,0:T(8,128)S(1)} %fusion.2, f32[2,768,384]{2,1,0:T(8,128)S(1)} %fusion.1, bf16[2,768,768]{2,1,0:T(8,128)(2,1)S(1)} %convert_bitcast_fusion, bf16[4,768,768]{2,1,0:T(8,128)(2,1)S(1)} %bitcast.146), kind=kOutput, calls=%fused_computation.5 | convolution fusion | flops 907739136 | bytes 12386304 | tf_op jit(solution)/shard_map/pad,bd->pab/dot_general | solution.py:107
  101.1 1.4 %copy-done.3 = f32[2,768,384]{2,1,0:T(8,128)} copy-done((f32[2,768,384]{2,1,0:T(8,128)}, f32[2,768,384]{2,1,0:T(8,128)S(1)}, u32[]{:S(2)}) %copy-start.3) | copy-done | bytes 2359320
  103.4 2.7 %collective-permute-start.14 = (bf16[2,192,384]{2,1,0:T(8,128)(2,1)}, bf16[2,192,384]{2,1,0:T(8,128)(2,1)S(1)}, u32[]{:S(2)}, u32[]{:S(2)}) collective-permute-start(bf16[2,192,384]{2,1,0:T(8,128)(2,1)} %get-tuple-element.24), channel_id=1, source_target_pairs={{0,3},{1,0},{2,1},{3,2},{4,7},{5,4},{6,5},{7,6},{8,11},{9,8},{10,9... | collective-permute-start | bytes 884744 | tf_op jit(solution)/shard_map/ppermute | solution.py:76
  106.3 3.8 %collective-permute-start.15 = (bf16[2,96,384]{2,1,0:T(8,128)(2,1)S(1)}, bf16[2,96,384]{2,1,0:T(8,128)(2,1)S(1)}, u32[]{:S(2)}, u32[]{:S(2)}) collective-permute-start(bf16[2,96,384]{2,1,0:T(8,128)(2,1)S(1)} %get-tuple-element.33), channel_id=1, source_target_pairs={{0,2},{1,3},{2,0},{3,1},{4,6},{5,7},{6,4},{7,5},{8,10},{9,11},{10,... | collective-permute-start | bytes 442376 | tf_op jit(solution)/shard_map/ppermute | solution.py:76
  110.8 8.8 %collective-permute-done.16 = bf16[2,96,384]{2,1,0:T(8,128)(2,1)S(1)} collective-permute-done((bf16[2,96,384]{2,1,0:T(8,128)(2,1)S(1)}, bf16[2,96,384]{2,1,0:T(8,128)(2,1)S(1)}, u32[]{:S(2)}, u32[]{:S(2)}) %collective-permute-start.16) | collective-permute-done | bytes 147488 | tf_op jit(solution)/shard_map/ppermute | solution.py:76
  120.8 1.6 %collective-permute-start.9 = (bf16[2,192,384]{2,1,0:T(8,128)(2,1)}, bf16[2,192,384]{2,1,0:T(8,128)(2,1)S(1)}, u32[]{:S(2)}, u32[]{:S(2)}) collective-permute-start(bf16[2,192,384]{2,1,0:T(8,128)(2,1)} %get-tuple-element.13), channel_id=1, source_target_pairs={{0,3},{1,0},{2,1},{3,2},{4,7},{5,4},{6,5},{7,6},{8,11},{9,8},{10,9... | collective-permute-start | bytes 884744 | tf_op jit(solution)/shard_map/ppermute | solution.py:76
  122.3 2.7 %collective-permute-done.11 = bf16[2,96,384]{2,1,0:T(8,128)(2,1)} collective-permute-done((bf16[2,96,384]{2,1,0:T(8,128)(2,1)S(1)}, bf16[2,96,384]{2,1,0:T(8,128)(2,1)}, u32[]{:S(2)}, u32[]{:S(2)}) %collective-permute-start.11) | collective-permute-done | bytes 147488 | tf_op jit(solution)/shard_map/ppermute | solution.py:76
  125.1 2.3 %collective-permute-done.17 = bf16[2,96,384]{2,1,0:T(8,128)(2,1)S(1)} collective-permute-done((bf16[2,96,384]{2,1,0:T(8,128)(2,1)S(1)}, bf16[2,96,384]{2,1,0:T(8,128)(2,1)S(1)}, u32[]{:S(2)}, u32[]{:S(2)}) %collective-permute-start.17) | collective-permute-done | bytes 147488 | tf_op jit(solution)/shard_map/ppermute | solution.py:76
  128.4 1.4 fusion.6
  129.8 5.3 %collective-permute-done.10 = bf16[2,96,384]{2,1,0:T(8,128)(2,1)S(1)} collective-permute-done((bf16[2,96,384]{2,1,0:T(8,128)(2,1)}, bf16[2,96,384]{2,1,0:T(8,128)(2,1)S(1)}, u32[]{:S(2)}, u32[]{:S(2)}) %collective-permute-start.10) | collective-permute-done | bytes 147488 | tf_op jit(solution)/shard_map/ppermute | solution.py:76
  135.1 6.1 %collective-permute-done.12 = bf16[2,96,384]{2,1,0:T(8,128)(2,1)S(1)} collective-permute-done((bf16[2,96,384]{2,1,0:T(8,128)(2,1)}, bf16[2,96,384]{2,1,0:T(8,128)(2,1)S(1)}, u32[]{:S(2)}, u32[]{:S(2)}) %collective-permute-start.12) | collective-permute-done | bytes 147488 | tf_op jit(solution)/shard_map/ppermute | solution.py:76
  (58 shorter events, 20.9 us)
Async XLA Ops:
  0.0 79.9 %copy-start = (bf16[2,768,768]{2,1,0:T(8,128)(2,1)S(1)}, bf16[2,768,768]{2,1,0:T(8,128)(2,1)}, u32[]{:S(2)}) copy-start(bf16[2,768,768]{2,1,0:T(8,128)(2,1)} %param.3) | copy-start | bytes 7077892
  0.0 9.6 %copy-start.6 = (s32[4,4]{1,0:T(4,128)S(1)}, s32[4,4]{1,0:T(4,128)}, u32[]{:S(2)}) copy-start(s32[4,4]{1,0:T(4,128)} %param.5) | copy-start | bytes 196
  0.0 28.1 %all-to-all-start = ((bf16[32,24,768]{2,1,0:T(8,128)(2,1)}), bf16[32,24,768]{2,1,0:T(8,128)(2,1)S(1)}, u32[]{:S(2)}, u32[]{:S(2)}) async-start(bf16[32,24,768]{2,1,0:T(8,128)(2,1)} %bitcast.157), calls=%async_computation | async-start | bytes 2359296 | tf_op jit(solution)/shard_map/all_to_all | solution.py:52
  30.3 7.1 %collective-permute-start.2 = (bf16[4,24,768]{2,1,0:T(8,128)(2,1)S(1)}, bf16[4,24,768]{2,1,0:T(8,128)(2,1)S(1)}, u32[]{:S(2)}, u32[]{:S(2)}) collective-permute-start(bf16[4,24,768]{2,1,0:T(8,128)(2,1)S(1)} %broadcast_select_fusion), channel_id=1, source_target_pairs={{0,8},{4,36},{8,16},{12,44},{16,24},{20,52},{24,0},{28,60},{32,40}... | collective-permute-start | bytes 442376 | tf_op jit(solution)/shard_map/ppermute | solution.py:34
  30.4 7.1 %collective-permute-start.1 = (bf16[4,24,768]{2,1,0:T(8,128)(2,1)S(1)}, bf16[4,24,768]{2,1,0:T(8,128)(2,1)S(1)}, u32[]{:S(2)}, u32[]{:S(2)}) collective-permute-start(bf16[4,24,768]{2,1,0:T(8,128)(2,1)S(1)} %broadcast_select_fusion), channel_id=1, source_target_pairs={{0,16},{4,68},{8,24},{12,76},{16,0},{20,84},{24,8},{28,92},{32,48}... | collective-permute-start | bytes 442376 | tf_op jit(solution)/shard_map/ppermute | solution.py:37
  32.1 5.9 %collective-permute-start = (bf16[4,24,768]{2,1,0:T(8,128)(2,1)S(1)}, bf16[4,24,768]{2,1,0:T(8,128)(2,1)S(1)}, u32[]{:S(2)}, u32[]{:S(2)}) collective-permute-start(bf16[4,24,768]{2,1,0:T(8,128)(2,1)S(1)} %broadcast_select_fusion), channel_id=1, source_target_pairs={{0,24},{4,100},{8,0},{12,108},{16,8},{20,116},{24,16},{28,124},{32... | collective-permute-start | bytes 442376 | tf_op jit(solution)/shard_map/ppermute | solution.py:35
  38.1 9.1 %collective-permute-start.3 = (bf16[4,4,24,768]{3,2,1,0:T(8,128)(2,1)S(1)}, bf16[4,4,24,768]{3,2,1,0:T(8,128)(2,1)S(1)}, u32[]{:S(2)}, u32[]{:S(2)}) collective-permute-start(bf16[4,4,24,768]{3,2,1,0:T(8,128)(2,1)S(1)} %get-tuple-element.30), channel_id=1, source_target_pairs={{0,96},{4,28},{8,104},{12,4},{16,112},{20,12},{24,120},{28,20},{32... | collective-permute-start | bytes 1769480 | tf_op jit(solution)/shard_map/ppermute | solution.py:35
  39.6 10.3 %collective-permute-start.4 = (bf16[4,4,24,768]{3,2,1,0:T(8,128)(2,1)S(1)}, bf16[4,4,24,768]{3,2,1,0:T(8,128)(2,1)S(1)}, u32[]{:S(2)}, u32[]{:S(2)}) collective-permute-start(bf16[4,4,24,768]{3,2,1,0:T(8,128)(2,1)S(1)} %get-tuple-element.30), channel_id=1, source_target_pairs={{0,32},{4,12},{8,40},{12,20},{16,48},{20,28},{24,56},{28,4},{32,64... | collective-permute-start | bytes 1769480 | tf_op jit(solution)/shard_map/ppermute | solution.py:34
  47.3 6.3 %collective-permute-start.6 = (bf16[2,4,24,768]{3,2,1,0:T(8,128)(2,1)S(1)}, bf16[2,4,24,768]{3,2,1,0:T(8,128)(2,1)S(1)}, u32[]{:S(2)}, u32[]{:S(2)}) collective-permute-start(bf16[2,4,24,768]{3,2,1,0:T(8,128)(2,1)S(1)} %slice.81), channel_id=1, source_target_pairs={{0,96},{4,28},{8,104},{12,4},{16,112},{20,12},{24,120},{28,20},{32... | collective-permute-start | bytes 884744 | tf_op jit(solution)/shard_map/ppermute | solution.py:40
  49.9 7.1 %collective-permute-start.5 = (bf16[2,4,24,768]{3,2,1,0:T(8,128)(2,1)S(1)}, bf16[2,4,24,768]{3,2,1,0:T(8,128)(2,1)S(1)}, u32[]{:S(2)}, u32[]{:S(2)}) collective-permute-start(bf16[2,4,24,768]{3,2,1,0:T(8,128)(2,1)S(1)} %slice.80), channel_id=1, source_target_pairs={{0,32},{4,12},{8,40},{12,20},{16,48},{20,28},{24,56},{28,4},{32,64... | collective-permute-start | bytes 884744 | tf_op jit(solution)/shard_map/ppermute | solution.py:39
  58.9 7.2 %collective-permute-start.7 = (bf16[4,4,4,24,768]{4,3,2,1,0:T(8,128)(2,1)}, bf16[4,4,4,24,768]{4,3,2,1,0:T(8,128)(2,1)}, u32[]{:S(2)}, u32[]{:S(2)}) collective-permute-start(bf16[4,4,4,24,768]{4,3,2,1,0:T(8,128)(2,1)} %pad_maximum_fusion.1), channel_id=1, source_target_pairs={{0,4},{4,0},{8,12},{12,8},{16,20},{20,16},{24,28},{28,24},{32,36},... | collective-permute-start | bytes 7077896 | tf_op jit(solution)/shard_map/ppermute | solution.py:57
  93.8 2.8 %copy-start.2 = (f32[2,768,384]{2,1,0:T(8,128)}, f32[2,768,384]{2,1,0:T(8,128)S(1)}, u32[]{:S(2)}) copy-start(f32[2,768,384]{2,1,0:T(8,128)S(1)} %add_add_fusion.1) | copy-start | bytes 7077892
  101.1 1.4 %copy-start.3 = (f32[2,768,384]{2,1,0:T(8,128)}, f32[2,768,384]{2,1,0:T(8,128)S(1)}, u32[]{:S(2)}) copy-start(f32[2,768,384]{2,1,0:T(8,128)S(1)} %add_add_fusion) | copy-start | bytes 7077892
  103.4 24.0 %collective-permute-start.14 = (bf16[2,192,384]{2,1,0:T(8,128)(2,1)}, bf16[2,192,384]{2,1,0:T(8,128)(2,1)S(1)}, u32[]{:S(2)}, u32[]{:S(2)}) collective-permute-start(bf16[2,192,384]{2,1,0:T(8,128)(2,1)} %get-tuple-element.24), channel_id=1, source_target_pairs={{0,3},{1,0},{2,1},{3,2},{4,7},{5,4},{6,5},{7,6},{8,11},{9,8},{10,9... | collective-permute-start | bytes 884744 | tf_op jit(solution)/shard_map/ppermute | solution.py:76
  106.2 22.2 %collective-permute-start.13 = (bf16[2,192,384]{2,1,0:T(8,128)(2,1)}, bf16[2,192,384]{2,1,0:T(8,128)(2,1)S(1)}, u32[]{:S(2)}, u32[]{:S(2)}) collective-permute-start(bf16[2,192,384]{2,1,0:T(8,128)(2,1)} %get-tuple-element.25), channel_id=1, source_target_pairs={{0,1},{1,2},{2,3},{3,0},{4,5},{5,6},{6,7},{7,4},{8,9},{9,10},{10,1... | collective-permute-start | bytes 884744 | tf_op jit(solution)/shard_map/ppermute | solution.py:76
  106.2 13.5 %collective-permute-start.16 = (bf16[2,96,384]{2,1,0:T(8,128)(2,1)S(1)}, bf16[2,96,384]{2,1,0:T(8,128)(2,1)S(1)}, u32[]{:S(2)}, u32[]{:S(2)}) collective-permute-start(bf16[2,96,384]{2,1,0:T(8,128)(2,1)S(1)} %get-tuple-element.34), channel_id=1, source_target_pairs={{0,1},{1,2},{2,3},{3,0},{4,5},{5,6},{6,7},{7,4},{8,9},{9,10},{10,1... | collective-permute-start | bytes 442376 | tf_op jit(solution)/shard_map/ppermute | solution.py:76
  106.3 14.5 %collective-permute-start.15 = (bf16[2,96,384]{2,1,0:T(8,128)(2,1)S(1)}, bf16[2,96,384]{2,1,0:T(8,128)(2,1)S(1)}, u32[]{:S(2)}, u32[]{:S(2)}) collective-permute-start(bf16[2,96,384]{2,1,0:T(8,128)(2,1)S(1)} %get-tuple-element.33), channel_id=1, source_target_pairs={{0,2},{1,3},{2,0},{3,1},{4,6},{5,7},{6,4},{7,5},{8,10},{9,11},{10,... | collective-permute-start | bytes 442376 | tf_op jit(solution)/shard_map/ppermute | solution.py:76
  110.8 14.3 %collective-permute-start.11 = (bf16[2,96,384]{2,1,0:T(8,128)(2,1)S(1)}, bf16[2,96,384]{2,1,0:T(8,128)(2,1)}, u32[]{:S(2)}, u32[]{:S(2)}) collective-permute-start(bf16[2,96,384]{2,1,0:T(8,128)(2,1)S(1)} %get-tuple-element.32), channel_id=1, source_target_pairs={{0,1},{1,2},{2,3},{3,0},{4,5},{5,6},{6,7},{7,4},{8,9},{9,10},{10,1... | collective-permute-start | bytes 442376 | tf_op jit(solution)/shard_map/ppermute | solution.py:76
  119.7 7.7 %collective-permute-start.17 = (bf16[2,96,384]{2,1,0:T(8,128)(2,1)S(1)}, bf16[2,96,384]{2,1,0:T(8,128)(2,1)S(1)}, u32[]{:S(2)}, u32[]{:S(2)}) collective-permute-start(bf16[2,96,384]{2,1,0:T(8,128)(2,1)S(1)} %collective-permute-done.16), channel_id=1, source_target_pairs={{0,1},{1,2},{2,3},{3,0},{4,5},{5,6},{6,7},{7,4},{8,9},{9,10},{10,1... | collective-permute-start | bytes 442376 | tf_op jit(solution)/shard_map/ppermute | solution.py:76
  120.8 7.6 %copy-start.4 = (bf16[2,96,384]{2,1,0:T(8,128)(2,1)}, bf16[2,96,384]{2,1,0:T(8,128)(2,1)S(1)}, u32[]{:S(2)}) copy-start(bf16[2,96,384]{2,1,0:T(8,128)(2,1)S(1)} %collective-permute-done.15) | copy-start | bytes 442372
  120.8 20.4 %collective-permute-start.9 = (bf16[2,192,384]{2,1,0:T(8,128)(2,1)}, bf16[2,192,384]{2,1,0:T(8,128)(2,1)S(1)}, u32[]{:S(2)}, u32[]{:S(2)}) collective-permute-start(bf16[2,192,384]{2,1,0:T(8,128)(2,1)} %get-tuple-element.13), channel_id=1, source_target_pairs={{0,3},{1,0},{2,1},{3,2},{4,7},{5,4},{6,5},{7,6},{8,11},{9,8},{10,9... | collective-permute-start | bytes 884744 | tf_op jit(solution)/shard_map/ppermute | solution.py:76
  125.1 16.1 %collective-permute-start.8 = (bf16[2,192,384]{2,1,0:T(8,128)(2,1)}, bf16[2,192,384]{2,1,0:T(8,128)(2,1)S(1)}, u32[]{:S(2)}, u32[]{:S(2)}) collective-permute-start(bf16[2,192,384]{2,1,0:T(8,128)(2,1)} %get-tuple-element.12), channel_id=1, source_target_pairs={{0,1},{1,2},{2,3},{3,0},{4,5},{5,6},{6,7},{7,4},{8,9},{9,10},{10,1... | collective-permute-start | bytes 884744 | tf_op jit(solution)/shard_map/ppermute | solution.py:76
  127.4 1.0 copy-start.5
  127.4 7.7 %collective-permute-start.10 = (bf16[2,96,384]{2,1,0:T(8,128)(2,1)}, bf16[2,96,384]{2,1,0:T(8,128)(2,1)S(1)}, u32[]{:S(2)}, u32[]{:S(2)}) collective-permute-start(bf16[2,96,384]{2,1,0:T(8,128)(2,1)} %get-tuple-element.31), channel_id=1, source_target_pairs={{0,2},{1,3},{2,0},{3,1},{4,6},{5,7},{6,4},{7,5},{8,10},{9,11},{10,... | collective-permute-start | bytes 442376 | tf_op jit(solution)/shard_map/ppermute | solution.py:76
  127.4 13.8 %collective-permute-start.12 = (bf16[2,96,384]{2,1,0:T(8,128)(2,1)}, bf16[2,96,384]{2,1,0:T(8,128)(2,1)S(1)}, u32[]{:S(2)}, u32[]{:S(2)}) collective-permute-start(bf16[2,96,384]{2,1,0:T(8,128)(2,1)} %collective-permute-done.11), channel_id=1, source_target_pairs={{0,1},{1,2},{2,3},{3,0},{4,5},{5,6},{6,7},{7,4},{8,9},{9,10},{10,1... | collective-permute-start | bytes 442376 | tf_op jit(solution)/shard_map/ppermute | solution.py:76
  128.4 15.1 %copy-start.1 = (bf16[2,768,768]{2,1,0:T(8,128)(2,1)S(1)}, bf16[2,768,768]{2,1,0:T(8,128)(2,1)}, u32[]{:S(2)}) copy-start(bf16[2,768,768]{2,1,0:T(8,128)(2,1)} %param.3) | copy-start | bytes 7077892

commit v11 on v10

--- a/solution.py
+++ b/solution.py
@@ -84,21 +84,19 @@
     def pick(offset):
         return lax.dynamic_index_in_dim(blocks, (vgrp + offset) % groups, 1, keepdims=False)
 
-    owed = tuple(pick(offset).astype(jnp.bfloat16) for offset in (1, -1, 2))
-    return pick(0), owed
+    return pick(0), (pick(1), pick(-1), pick(2).astype(jnp.bfloat16))
 
 
 def exchange(own, owed, groups):
     ahead, behind, far = owed
     half = far.shape[1] // 2
-    ahead = shifted(ahead, 1, groups)
-    behind = shifted(behind, -1, groups)
-    far_low = shifted(far[:, :half], 2, groups)
-    far_high = shifted(far[:, half:], 1, groups)
-    far_high = shifted(far_high, 1, groups)
-    far = jnp.concatenate([far_low, far_high], axis=1)
-    near = ahead.astype(jnp.float32) + behind.astype(jnp.float32)
-    return own + near + far.astype(jnp.float32)
+    far_up = shifted(far[:, :half], 1, groups)
+    far_down = shifted(far[:, half:], -1, groups)
+    ahead = jnp.concatenate([ahead[:, :half] + far_up.astype(jnp.float32), ahead[:, half:]], axis=1)
+    behind = jnp.concatenate([behind[:, :half], behind[:, half:] + far_down.astype(jnp.float32)], axis=1)
+    ahead = shifted(ahead.astype(jnp.bfloat16), 1, groups)
+    behind = shifted(behind.astype(jnp.bfloat16), -1, groups)
+    return own + ahead.astype(jnp.float32) + behind.astype(jnp.float32)
 
 
 def columns(halves, vectors, lo, hi):

time: 145 us -> 128 us (0.88)
  waiting for transfers between devices: 67.4 us -> 51.2 us
  local copies, waits for them, and re-layouts: 11.7 us -> 7.89 us
  starting transfers between devices: 28.9 us -> 31.5 us
    ppermute x10 -> x8, waiting for transfers between devices: 26.4 us -> 10.1 us  [shifted(): lax.ppermute(value, 'vgrp', [(g, (g + step) % groups) for g in range(grou...]
    ppermute x10 -> x8, starting transfers between devices: 9.19 us -> 11.8 us  [shifted(): lax.ppermute(value, 'vgrp', [(g, (g + step) % groups) for g in range(grou...]
    convert_element_type x2, local copies, waits for them, and re-layouts: 2.31 us -> 0.31 us  [prepare(): return (pick(0), (pick(1), pick(-1), pick(2).astype(jnp.bfloat16)))]
  transfers between devices with their start and end apart: 19 -> 17, of which waited for: 13 -> 11; matrix products, arithmetic and copies ran while one was open for 2% -> 2% of each run, Pallas kernels for 0% -> 0%
where the time goes in v11:
time: 128 us; the launch traced here: 126 us
  waiting for transfers between devices  51.2 us (40%)
  starting transfers between devices  31.5 us (25%)
  matrix products  19.7 us (15%)
  other arithmetic  15.8 us (12%)
  local copies, waits for them, and re-layouts  7.89 us (6%)
    all_to_all x1, waiting for transfers between devices, gather_slots(): pieces = lax.all_to_all(pieces, PAIR, 0, 0, tiled=True)  18.5 us
    ppermute x8, starting transfers between devices, shifted(): lax.ppermute(value, 'vgrp', [(g, (g + step) % groups) for g in range(grou...  11.8 us
    dot_general x8, matrix products, columns(): jnp.einsum('pad,bd->pab', half_product, vectors[slot, lo:hi], preferred_e...  11.7 us
    ppermute x8, waiting for transfers between devices, shifted(): lax.ppermute(value, 'vgrp', [(g, (g + step) % groups) for g in range(grou...  10.1 us
    all_to_all x1, starting transfers between devices, gather_slots(): pieces = lax.all_to_all(pieces, PAIR, 0, 0, tiled=True)  9.55 us
    ppermute x2, waiting for transfers between devices, ring_gather(): from_next = lax.ppermute(piece, PAIR, ring_perm(sizes, stage, -1))  8.14 us
    dot_general x4, matrix products, on_device(): jnp.einsum('ac,pcd->pad', vectors[slot], amplitudes, preferred_element_ty...  8.01 us
    gather x1, local copies, waits for them, and re-layouts, gather_slots(): ordered = jnp.take(stacked, index, axis=0)  5.37 us
  transfers between devices with their start and end apart: 17, of which 11 were waited for; matrix products, arithmetic and copies ran while one was open for 2% of the time, Pallas kernels for 0%

profile of v11, /device:TPU:1, one launch (start us, length us, event | category | flops | bytes accessed | tf_op | source)
XLA Modules:
  0.0 126.5 jit_solution(10232045022911723100)
XLA Ops:
  0.0 9.6 %all-to-all-start = ((bf16[32,24,768]{2,1,0:T(8,128)(2,1)}), bf16[32,24,768]{2,1,0:T(8,128)(2,1)S(1)}, u32[]{:S(2)}, u32[]{:S(2)}) async-start(bf16[32,24,768]{2,1,0:T(8,128)(2,1)} %bitcast.143), calls=%async_computation | async-start | bytes 2359296 | tf_op jit(solution)/shard_map/all_to_all | solution.py:52
  9.6 18.5 %all-to-all-done = bf16[32,24,768]{2,1,0:T(8,128)(2,1)S(1)} async-done(((bf16[32,24,768]{2,1,0:T(8,128)(2,1)}), bf16[32,24,768]{2,1,0:T(8,128)(2,1)S(1)}, u32[]{:S(2)}, u32[]{:S(2)}) %all-to-all-start) | async-done | bytes 1179680 | tf_op jit(solution)/shard_map/all_to_all | solution.py:52
  30.4 1.7 %collective-permute-start.1 = (bf16[4,24,768]{2,1,0:T(8,128)(2,1)S(1)}, bf16[4,24,768]{2,1,0:T(8,128)(2,1)S(1)}, u32[]{:S(2)}, u32[]{:S(2)}) collective-permute-start(bf16[4,24,768]{2,1,0:T(8,128)(2,1)S(1)} %broadcast_select_fusion), channel_id=1, source_target_pairs={{0,16},{4,68},{8,24},{12,76},{16,0},{20,84},{24,8},{28,92},{32,48}... | collective-permute-start | bytes 442376 | tf_op jit(solution)/shard_map/ppermute | solution.py:37
  34.5 2.9 %collective-permute-done.2 = bf16[4,24,768]{2,1,0:T(8,128)(2,1)S(1)} collective-permute-done((bf16[4,24,768]{2,1,0:T(8,128)(2,1)S(1)}, bf16[4,24,768]{2,1,0:T(8,128)(2,1)S(1)}, u32[]{:S(2)}, u32[]{:S(2)}) %collective-permute-start.2) | collective-permute-done | bytes 147488 | tf_op jit(solution)/shard_map/ppermute | solution.py:34
  38.1 1.4 %collective-permute-start.3 = (bf16[4,4,24,768]{3,2,1,0:T(8,128)(2,1)S(1)}, bf16[4,4,24,768]{3,2,1,0:T(8,128)(2,1)S(1)}, u32[]{:S(2)}, u32[]{:S(2)}) collective-permute-start(bf16[4,4,24,768]{3,2,1,0:T(8,128)(2,1)S(1)} %get-tuple-element.28), channel_id=1, source_target_pairs={{0,96},{4,28},{8,104},{12,4},{16,112},{20,12},{24,120},{28,20},{32... | collective-permute-start | bytes 1769480 | tf_op jit(solution)/shard_map/ppermute | solution.py:35
  39.7 7.6 %collective-permute-done.3 = bf16[4,4,24,768]{3,2,1,0:T(8,128)(2,1)S(1)} collective-permute-done((bf16[4,4,24,768]{3,2,1,0:T(8,128)(2,1)S(1)}, bf16[4,4,24,768]{3,2,1,0:T(8,128)(2,1)S(1)}, u32[]{:S(2)}, u32[]{:S(2)}) %collective-permute-start.3) | collective-permute-done | bytes 589856 | tf_op jit(solution)/shard_map/ppermute | solution.py:35
  47.3 2.6 %collective-permute-start.6 = (bf16[2,4,24,768]{3,2,1,0:T(8,128)(2,1)S(1)}, bf16[2,4,24,768]{3,2,1,0:T(8,128)(2,1)S(1)}, u32[]{:S(2)}, u32[]{:S(2)}) collective-permute-start(bf16[2,4,24,768]{3,2,1,0:T(8,128)(2,1)S(1)} %slice.117), channel_id=1, source_target_pairs={{0,96},{4,28},{8,104},{12,4},{16,112},{20,12},{24,120},{28,20},{32... | collective-permute-start | bytes 884744 | tf_op jit(solution)/shard_map/ppermute | solution.py:40
  50.0 3.6 %collective-permute-done.6 = bf16[2,4,24,768]{3,2,1,0:T(8,128)(2,1)S(1)} collective-permute-done((bf16[2,4,24,768]{3,2,1,0:T(8,128)(2,1)S(1)}, bf16[2,4,24,768]{3,2,1,0:T(8,128)(2,1)S(1)}, u32[]{:S(2)}, u32[]{:S(2)}) %collective-permute-start.6) | collective-permute-done | bytes 294944 | tf_op jit(solution)/shard_map/ppermute | solution.py:40
  53.6 3.5 %collective-permute-done.5 = bf16[2,4,24,768]{3,2,1,0:T(8,128)(2,1)S(1)} collective-permute-done((bf16[2,4,24,768]{3,2,1,0:T(8,128)(2,1)S(1)}, bf16[2,4,24,768]{3,2,1,0:T(8,128)(2,1)S(1)}, u32[]{:S(2)}, u32[]{:S(2)}) %collective-permute-start.5) | collective-permute-done | bytes 294944 | tf_op jit(solution)/shard_map/ppermute | solution.py:39
  57.1 1.7 %pad_maximum_fusion.1 = bf16[4,4,4,24,768]{4,3,2,1,0:T(8,128)(2,1)} fusion(bf16[1,4,4,24,768]{4,3,2,1,0:T(8,128)(2,1)S(1)} %bitcast.138, bf16[1,4,4,24,768]{4,3,2,1,0:T(8,128)(2,1)S(1)} %maximum_bitcast_fusion, bf16[1,4,4,24,768]{4,3,2,1,0:T(8,128)(2,1)S(1)} %bitcast.137, bf16[1,4,4,24,768]{4,3,2,1,0:T(8,128)(2,1)S(1)} %get-tuple-element.27), kind=kLoop, calls=%fused_computation.4 | loop fusion | flops 3538944 | bytes 4718592 | tf_op jit(solution)/shard_map/stack | solution.py:42
  58.9 2.7 %collective-permute-start.7 = (bf16[4,4,4,24,768]{4,3,2,1,0:T(8,128)(2,1)}, bf16[4,4,4,24,768]{4,3,2,1,0:T(8,128)(2,1)}, u32[]{:S(2)}, u32[]{:S(2)}) collective-permute-start(bf16[4,4,4,24,768]{4,3,2,1,0:T(8,128)(2,1)} %pad_maximum_fusion.1), channel_id=1, source_target_pairs={{0,4},{4,0},{8,12},{12,8},{16,20},{20,16},{24,28},{28,24},{32,36},... | collective-permute-start | bytes 7077896 | tf_op jit(solution)/shard_map/ppermute | solution.py:57
  61.6 4.4 %collective-permute-done.7 = bf16[4,4,4,24,768]{4,3,2,1,0:T(8,128)(2,1)} collective-permute-done((bf16[4,4,4,24,768]{4,3,2,1,0:T(8,128)(2,1)}, bf16[4,4,4,24,768]{4,3,2,1,0:T(8,128)(2,1)}, u32[]{:S(2)}, u32[]{:S(2)}) %collective-permute-start.7) | collective-permute-done | bytes 2359328 | tf_op jit(solution)/shard_map/ppermute | solution.py:57
  66.1 4.9 %pad_maximum_fusion = bf16[32,4,24,768]{3,2,1,0:T(8,128)(2,1)} fusion(bf16[16,4,24,768]{3,2,1,0:T(8,128)(2,1)} %bitcast.13, bf16[16,4,24,768]{3,2,1,0:T(8,128)(2,1)} %bitcast.12), kind=kLoop, calls=%fused_computation.2 | loop fusion | flops 2359296 | bytes 9437184 | tf_op jit(solution)/shard_map/concatenate | solution.py:59
  71.0 5.4 %gather_fusion.1 = bf16[32,4,24,768]{3,2,1,0:T(8,128)(2,1)} fusion(bf16[32,4,24,768]{3,2,1,0:T(8,128)(2,1)} %pad_maximum_fusion, s32[1024]{0:T(1024)S(1)} %pad_clamp_fusion), kind=kCustom, calls=%fused_computation.1 | custom fusion | bytes 9437312 | tf_op jit(solution)/shard_map/jit(_take)/gather | solution.py:70
  76.4 2.9 %select_bitcast_fusion = bf16[4,32,24,768]{3,2,0,1:T(8,128)(2,1)S(1)} fusion(bf16[32,4,24,768]{3,2,1,0:T(8,128)(2,1)} %gather_fusion.1, pred[32]{0:T(512)(128)(4,1)S(1)} %compare_and_fusion.1), kind=kLoop, calls=%fused_computation.3 | loop fusion | flops 2359296 | bytes 9437216 | tf_op jit(solution)/shard_map/jit(_take)/select_n | solution.py:70
  79.9 2.0 %convert_bitcast_fusion.3 = bf16[2,768,768]{2,1,0:T(8,128)(2,1)S(1)} fusion(bf16[768,768,1]{1,0,2:T(8,128)(2,1)S(1)} %bitcast.142, bf16[2,768,768]{2,1,0:T(8,128)(2,1)S(1)} %copy-done), kind=kOutput, calls=%fused_computation.10 | convolution fusion | flops 1813118976 | bytes 5898240 | tf_op jit(solution)/shard_map/ac,pcd->pad/dot_general | solution.py:118
  81.9 2.0 %convert_bitcast_fusion.2 = bf16[2,768,768]{2,1,0:T(8,128)(2,1)S(1)} fusion(bf16[768,768,1]{1,0,2:T(8,128)(2,1)S(1)} %bitcast.141, bf16[2,768,768]{2,1,0:T(8,128)(2,1)S(1)} %copy-done), kind=kOutput, calls=%fused_computation.9 | convolution fusion | flops 1813118976 | bytes 5898240 | tf_op jit(solution)/shard_map/ac,pcd->pad/dot_general | solution.py:118
  83.9 2.0 %convert_bitcast_fusion.1 = bf16[2,768,768]{2,1,0:T(8,128)(2,1)S(1)} fusion(bf16[768,768,1]{1,0,2:T(8,128)(2,1)S(1)} %bitcast.140, bf16[2,768,768]{2,1,0:T(8,128)(2,1)S(1)} %copy-done), kind=kOutput, calls=%fused_computation.8 | convolution fusion | flops 1813118976 | bytes 5898240 | tf_op jit(solution)/shard_map/ac,pcd->pad/dot_general | solution.py:118
  85.9 2.0 %convert_bitcast_fusion = bf16[2,768,768]{2,1,0:T(8,128)(2,1)S(1)} fusion(bf16[768,768,1]{1,0,2:T(8,128)(2,1)S(1)} %bitcast.139, bf16[2,768,768]{2,1,0:T(8,128)(2,1)S(1)} %copy-done), kind=kOutput, calls=%fused_computation.6 | convolution fusion | flops 1813118976 | bytes 5898240 | tf_op jit(solution)/shard_map/ac,pcd->pad/dot_general | solution.py:118
  87.9 1.4 %fusion.3 = f32[2,768,384]{2,1,0:T(8,128)S(1)} fusion(bf16[2,768,768]{2,1,0:T(8,128)(2,1)S(1)} %convert_bitcast_fusion.1, bf16[4,768,768]{2,1,0:T(8,128)(2,1)S(1)} %bitcast.129), kind=kOutput, calls=%fused_computation.21 | convolution fusion | flops 905969664 | bytes 5308416 | tf_op jit(solution)/shard_map/pad,bd->pab/dot_general | solution.py:105
  92.2 1.6 %add_add_fusion.1 = f32[2,768,384]{2,1,0:T(8,128)S(1)} fusion(f32[2,768,384]{2,1,0:T(8,128)S(1)} %fusion.3, f32[2,768,384]{2,1,0:T(8,128)S(1)} %fusion.5, f32[2,768,384]{2,1,0:T(8,128)S(1)} %fusion.4, bf16[2,768,768]{2,1,0:T(8,128)(2,1)S(1)} %convert_bitcast_fusion, bf16[4,768,768]{2,1,0:T(8,128)(2,1)S(1)} %bitcast.132), kind=kOutput, calls=%fused_computation.7 | convolution fusion | flops 907739136 | bytes 12386304 | tf_op jit(solution)/shard_map/pad,bd->pab/dot_general | solution.py:105
  94.2 1.4 %fusion = f32[2,768,384]{2,1,0:T(8,128)S(1)} fusion(bf16[2,768,768]{2,1,0:T(8,128)(2,1)S(1)} %convert_bitcast_fusion.1, bf16[4,768,768]{2,1,0:T(8,128)(2,1)S(1)} %bitcast.133), kind=kOutput, calls=%fused_computation.14 | convolution fusion | flops 905969664 | bytes 5308416 | tf_op jit(solution)/shard_map/pad,bd->pab/dot_general | solution.py:105
  97.0 1.4 %fusion.1 = f32[2,768,384]{2,1,0:T(8,128)S(1)} fusion(bf16[2,768,768]{2,1,0:T(8,128)(2,1)S(1)} %convert_bitcast_fusion.2, bf16[4,768,768]{2,1,0:T(8,128)(2,1)S(1)} %bitcast.135), kind=kOutput, calls=%fused_computation.16 | convolution fusion | flops 905969664 | bytes 5308416 | tf_op jit(solution)/shard_map/pad,bd->pab/dot_general | solution.py:105
  98.4 1.6 %add_add_fusion = f32[2,768,384]{2,1,0:T(8,128)S(1)} fusion(f32[2,768,384]{2,1,0:T(8,128)S(1)} %fusion, f32[2,768,384]{2,1,0:T(8,128)S(1)} %fusion.2, f32[2,768,384]{2,1,0:T(8,128)S(1)} %fusion.1, bf16[2,768,768]{2,1,0:T(8,128)(2,1)S(1)} %convert_bitcast_fusion, bf16[4,768,768]{2,1,0:T(8,128)(2,1)S(1)} %bitcast.136), kind=kOutput, calls=%fused_computation.5 | convolution fusion | flops 907739136 | bytes 12386304 | tf_op jit(solution)/shard_map/pad,bd->pab/dot_general | solution.py:105
  100.3 2.8 %collective-permute-start.14 = (bf16[2,96,384]{2,1,0:T(8,128)(2,1)S(1)}, bf16[2,96,384]{2,1,0:T(8,128)(2,1)S(1)}, u32[]{:S(2)}, u32[]{:S(2)}) collective-permute-start(bf16[2,96,384]{2,1,0:T(8,128)(2,1)S(1)} %get-tuple-element.32), channel_id=1, source_target_pairs={{0,3},{1,0},{2,1},{3,2},{4,7},{5,4},{6,5},{7,6},{8,11},{9,8},{10,9... | collective-permute-start | bytes 442376 | tf_op jit(solution)/shard_map/ppermute | solution.py:76
  103.2 2.7 %collective-permute-start.10 = (bf16[2,96,384]{2,1,0:T(8,128)(2,1)S(1)}, bf16[2,96,384]{2,1,0:T(8,128)(2,1)S(1)}, u32[]{:S(2)}, u32[]{:S(2)}) collective-permute-start(bf16[2,96,384]{2,1,0:T(8,128)(2,1)S(1)} %get-tuple-element.30), channel_id=1, source_target_pairs={{0,3},{1,0},{2,1},{3,2},{4,7},{5,4},{6,5},{7,6},{8,11},{9,8},{10,9... | collective-permute-start | bytes 442376 | tf_op jit(solution)/shard_map/ppermute | solution.py:76
  106.2 3.3 %collective-permute-start.15 = (bf16[2,192,384]{2,1,0:T(8,128)(2,1)S(1)}, bf16[2,192,384]{2,1,0:T(8,128)(2,1)S(1)}, u32[]{:S(2)}, u32[]{:S(2)}) collective-permute-start(bf16[2,192,384]{2,1,0:T(8,128)(2,1)S(1)} %pad_maximum_fusion.7), channel_id=1, source_target_pairs={{0,3},{1,0},{2,1},{3,2},{4,7},{5,4},{6,5},{7,6},{8,11},{9,8},{10,9... | collective-permute-start | bytes 884744 | tf_op jit(solution)/shard_map/ppermute | solution.py:76
  109.7 2.7 %collective-permute-start.11 = (bf16[2,192,384]{2,1,0:T(8,128)(2,1)S(1)}, bf16[2,192,384]{2,1,0:T(8,128)(2,1)}, u32[]{:S(2)}, u32[]{:S(2)}) collective-permute-start(bf16[2,192,384]{2,1,0:T(8,128)(2,1)S(1)} %pad_maximum_fusion.5), channel_id=1, source_target_pairs={{0,3},{1,0},{2,1},{3,2},{4,7},{5,4},{6,5},{7,6},{8,11},{9,8},{10,9... | collective-permute-start | bytes 884744 | tf_op jit(solution)/shard_map/ppermute | solution.py:76
  112.6 1.7 %collective-permute-done.15 = bf16[2,192,384]{2,1,0:T(8,128)(2,1)S(1)} collective-permute-done((bf16[2,192,384]{2,1,0:T(8,128)(2,1)S(1)}, bf16[2,192,384]{2,1,0:T(8,128)(2,1)S(1)}, u32[]{:S(2)}, u32[]{:S(2)}) %collective-permute-start.15) | collective-permute-done | bytes 294944 | tf_op jit(solution)/shard_map/ppermute | solution.py:76
  114.3 3.3 %collective-permute-done.13 = bf16[2,192,384]{2,1,0:T(8,128)(2,1)S(1)} collective-permute-done((bf16[2,192,384]{2,1,0:T(8,128)(2,1)S(1)}, bf16[2,192,384]{2,1,0:T(8,128)(2,1)S(1)}, u32[]{:S(2)}, u32[]{:S(2)}) %collective-permute-start.13) | collective-permute-done | bytes 294944 | tf_op jit(solution)/shard_map/ppermute | solution.py:76
  118.9 1.8 %collective-permute-done.11 = bf16[2,192,384]{2,1,0:T(8,128)(2,1)} collective-permute-done((bf16[2,192,384]{2,1,0:T(8,128)(2,1)S(1)}, bf16[2,192,384]{2,1,0:T(8,128)(2,1)}, u32[]{:S(2)}, u32[]{:S(2)}) %collective-permute-start.11) | collective-permute-done | bytes 294944 | tf_op jit(solution)/shard_map/ppermute | solution.py:76
  120.8 3.3 %collective-permute-done.9 = bf16[2,192,384]{2,1,0:T(8,128)(2,1)} collective-permute-done((bf16[2,192,384]{2,1,0:T(8,128)(2,1)S(1)}, bf16[2,192,384]{2,1,0:T(8,128)(2,1)}, u32[]{:S(2)}, u32[]{:S(2)}) %collective-permute-start.9) | collective-permute-done | bytes 294944 | tf_op jit(solution)/shard_map/ppermute | solution.py:76
  (64 shorter events, 15.5 us)
Async XLA Ops:
  0.0 79.9 %copy-start = (bf16[2,768,768]{2,1,0:T(8,128)(2,1)S(1)}, bf16[2,768,768]{2,1,0:T(8,128)(2,1)}, u32[]{:S(2)}) copy-start(bf16[2,768,768]{2,1,0:T(8,128)(2,1)} %param.3) | copy-start | bytes 7077892
  0.0 9.6 %copy-start.4 = (s32[4,4]{1,0:T(4,128)S(1)}, s32[4,4]{1,0:T(4,128)}, u32[]{:S(2)}) copy-start(s32[4,4]{1,0:T(4,128)} %param.5) | copy-start | bytes 196
  0.0 28.1 %all-to-all-start = ((bf16[32,24,768]{2,1,0:T(8,128)(2,1)}), bf16[32,24,768]{2,1,0:T(8,128)(2,1)S(1)}, u32[]{:S(2)}, u32[]{:S(2)}) async-start(bf16[32,24,768]{2,1,0:T(8,128)(2,1)} %bitcast.143), calls=%async_computation | async-start | bytes 2359296 | tf_op jit(solution)/shard_map/all_to_all | solution.py:52
  30.3 7.1 %collective-permute-start.2 = (bf16[4,24,768]{2,1,0:T(8,128)(2,1)S(1)}, bf16[4,24,768]{2,1,0:T(8,128)(2,1)S(1)}, u32[]{:S(2)}, u32[]{:S(2)}) collective-permute-start(bf16[4,24,768]{2,1,0:T(8,128)(2,1)S(1)} %broadcast_select_fusion), channel_id=1, source_target_pairs={{0,8},{4,36},{8,16},{12,44},{16,24},{20,52},{24,0},{28,60},{32,40}... | collective-permute-start | bytes 442376 | tf_op jit(solution)/shard_map/ppermute | solution.py:34
  30.4 7.1 %collective-permute-start.1 = (bf16[4,24,768]{2,1,0:T(8,128)(2,1)S(1)}, bf16[4,24,768]{2,1,0:T(8,128)(2,1)S(1)}, u32[]{:S(2)}, u32[]{:S(2)}) collective-permute-start(bf16[4,24,768]{2,1,0:T(8,128)(2,1)S(1)} %broadcast_select_fusion), channel_id=1, source_target_pairs={{0,16},{4,68},{8,24},{12,76},{16,0},{20,84},{24,8},{28,92},{32,48}... | collective-permute-start | bytes 442376 | tf_op jit(solution)/shard_map/ppermute | solution.py:37
  32.1 5.9 %collective-permute-start = (bf16[4,24,768]{2,1,0:T(8,128)(2,1)S(1)}, bf16[4,24,768]{2,1,0:T(8,128)(2,1)S(1)}, u32[]{:S(2)}, u32[]{:S(2)}) collective-permute-start(bf16[4,24,768]{2,1,0:T(8,128)(2,1)S(1)} %broadcast_select_fusion), channel_id=1, source_target_pairs={{0,24},{4,100},{8,0},{12,108},{16,8},{20,116},{24,16},{28,124},{32... | collective-permute-start | bytes 442376 | tf_op jit(solution)/shard_map/ppermute | solution.py:35
  38.1 9.1 %collective-permute-start.3 = (bf16[4,4,24,768]{3,2,1,0:T(8,128)(2,1)S(1)}, bf16[4,4,24,768]{3,2,1,0:T(8,128)(2,1)S(1)}, u32[]{:S(2)}, u32[]{:S(2)}) collective-permute-start(bf16[4,4,24,768]{3,2,1,0:T(8,128)(2,1)S(1)} %get-tuple-element.28), channel_id=1, source_target_pairs={{0,96},{4,28},{8,104},{12,4},{16,112},{20,12},{24,120},{28,20},{32... | collective-permute-start | bytes 1769480 | tf_op jit(solution)/shard_map/ppermute | solution.py:35
  39.6 10.3 %collective-permute-start.4 = (bf16[4,4,24,768]{3,2,1,0:T(8,128)(2,1)S(1)}, bf16[4,4,24,768]{3,2,1,0:T(8,128)(2,1)S(1)}, u32[]{:S(2)}, u32[]{:S(2)}) collective-permute-start(bf16[4,4,24,768]{3,2,1,0:T(8,128)(2,1)S(1)} %get-tuple-element.28), channel_id=1, source_target_pairs={{0,32},{4,12},{8,40},{12,20},{16,48},{20,28},{24,56},{28,4},{32,64... | collective-permute-start | bytes 1769480 | tf_op jit(solution)/shard_map/ppermute | solution.py:34
  47.3 6.3 %collective-permute-start.6 = (bf16[2,4,24,768]{3,2,1,0:T(8,128)(2,1)S(1)}, bf16[2,4,24,768]{3,2,1,0:T(8,128)(2,1)S(1)}, u32[]{:S(2)}, u32[]{:S(2)}) collective-permute-start(bf16[2,4,24,768]{3,2,1,0:T(8,128)(2,1)S(1)} %slice.117), channel_id=1, source_target_pairs={{0,96},{4,28},{8,104},{12,4},{16,112},{20,12},{24,120},{28,20},{32... | collective-permute-start | bytes 884744 | tf_op jit(solution)/shard_map/ppermute | solution.py:40
  49.9 7.1 %collective-permute-start.5 = (bf16[2,4,24,768]{3,2,1,0:T(8,128)(2,1)S(1)}, bf16[2,4,24,768]{3,2,1,0:T(8,128)(2,1)S(1)}, u32[]{:S(2)}, u32[]{:S(2)}) collective-permute-start(bf16[2,4,24,768]{3,2,1,0:T(8,128)(2,1)S(1)} %slice.116), channel_id=1, source_target_pairs={{0,32},{4,12},{8,40},{12,20},{16,48},{20,28},{24,56},{28,4},{32,64... | collective-permute-start | bytes 884744 | tf_op jit(solution)/shard_map/ppermute | solution.py:39
  58.9 7.2 %collective-permute-start.7 = (bf16[4,4,4,24,768]{4,3,2,1,0:T(8,128)(2,1)}, bf16[4,4,4,24,768]{4,3,2,1,0:T(8,128)(2,1)}, u32[]{:S(2)}, u32[]{:S(2)}) collective-permute-start(bf16[4,4,4,24,768]{4,3,2,1,0:T(8,128)(2,1)} %pad_maximum_fusion.1), channel_id=1, source_target_pairs={{0,4},{4,0},{8,12},{12,8},{16,20},{20,16},{24,28},{28,24},{32,36},... | collective-permute-start | bytes 7077896 | tf_op jit(solution)/shard_map/ppermute | solution.py:57
  93.8 1.8 %copy-start.2 = (f32[2,768,384]{2,1,0:T(8,128)}, f32[2,768,384]{2,1,0:T(8,128)S(1)}, u32[]{:S(2)}) copy-start(f32[2,768,384]{2,1,0:T(8,128)S(1)} %add_add_fusion.1) | copy-start | bytes 7077892
  100.1 3.2 %copy-start.3 = (f32[2,768,384]{2,1,0:T(8,128)}, f32[2,768,384]{2,1,0:T(8,128)S(1)}, u32[]{:S(2)}) copy-start(f32[2,768,384]{2,1,0:T(8,128)S(1)} %add_add_fusion) | copy-start | bytes 7077892
  100.3 5.8 %collective-permute-start.14 = (bf16[2,96,384]{2,1,0:T(8,128)(2,1)S(1)}, bf16[2,96,384]{2,1,0:T(8,128)(2,1)S(1)}, u32[]{:S(2)}, u32[]{:S(2)}) collective-permute-start(bf16[2,96,384]{2,1,0:T(8,128)(2,1)S(1)} %get-tuple-element.32), channel_id=1, source_target_pairs={{0,3},{1,0},{2,1},{3,2},{4,7},{5,4},{6,5},{7,6},{8,11},{9,8},{10,9... | collective-permute-start | bytes 442376 | tf_op jit(solution)/shard_map/ppermute | solution.py:76
  103.1 6.3 %collective-permute-start.12 = (bf16[2,96,384]{2,1,0:T(8,128)(2,1)S(1)}, bf16[2,96,384]{2,1,0:T(8,128)(2,1)S(1)}, u32[]{:S(2)}, u32[]{:S(2)}) collective-permute-start(bf16[2,96,384]{2,1,0:T(8,128)(2,1)S(1)} %get-tuple-element.31), channel_id=1, source_target_pairs={{0,1},{1,2},{2,3},{3,0},{4,5},{5,6},{6,7},{7,4},{8,9},{9,10},{10,1... | collective-permute-start | bytes 442376 | tf_op jit(solution)/shard_map/ppermute | solution.py:76
  103.2 6.4 %collective-permute-start.10 = (bf16[2,96,384]{2,1,0:T(8,128)(2,1)S(1)}, bf16[2,96,384]{2,1,0:T(8,128)(2,1)S(1)}, u32[]{:S(2)}, u32[]{:S(2)}) collective-permute-start(bf16[2,96,384]{2,1,0:T(8,128)(2,1)S(1)} %get-tuple-element.30), channel_id=1, source_target_pairs={{0,3},{1,0},{2,1},{3,2},{4,7},{5,4},{6,5},{7,6},{8,11},{9,8},{10,9... | collective-permute-start | bytes 442376 | tf_op jit(solution)/shard_map/ppermute | solution.py:76
  106.0 6.4 %collective-permute-start.8 = (bf16[2,96,384]{2,1,0:T(8,128)(2,1)S(1)}, bf16[2,96,384]{2,1,0:T(8,128)(2,1)S(1)}, u32[]{:S(2)}, u32[]{:S(2)}) collective-permute-start(bf16[2,96,384]{2,1,0:T(8,128)(2,1)S(1)} %get-tuple-element.29), channel_id=1, source_target_pairs={{0,1},{1,2},{2,3},{3,0},{4,5},{5,6},{6,7},{7,4},{8,9},{9,10},{10,1... | collective-permute-start | bytes 442376 | tf_op jit(solution)/shard_map/ppermute | solution.py:76
  106.2 8.1 %collective-permute-start.15 = (bf16[2,192,384]{2,1,0:T(8,128)(2,1)S(1)}, bf16[2,192,384]{2,1,0:T(8,128)(2,1)S(1)}, u32[]{:S(2)}, u32[]{:S(2)}) collective-permute-start(bf16[2,192,384]{2,1,0:T(8,128)(2,1)S(1)} %pad_maximum_fusion.7), channel_id=1, source_target_pairs={{0,3},{1,0},{2,1},{3,2},{4,7},{5,4},{6,5},{7,6},{8,11},{9,8},{10,9... | collective-permute-start | bytes 884744 | tf_op jit(solution)/shard_map/ppermute | solution.py:76
  109.5 8.1 %collective-permute-start.13 = (bf16[2,192,384]{2,1,0:T(8,128)(2,1)S(1)}, bf16[2,192,384]{2,1,0:T(8,128)(2,1)S(1)}, u32[]{:S(2)}, u32[]{:S(2)}) collective-permute-start(bf16[2,192,384]{2,1,0:T(8,128)(2,1)S(1)} %pad_maximum_fusion.6), channel_id=1, source_target_pairs={{0,1},{1,2},{2,3},{3,0},{4,5},{5,6},{6,7},{7,4},{8,9},{9,10},{10,1... | collective-permute-start | bytes 884744 | tf_op jit(solution)/shard_map/ppermute | solution.py:76
  109.7 11.0 %collective-permute-start.11 = (bf16[2,192,384]{2,1,0:T(8,128)(2,1)S(1)}, bf16[2,192,384]{2,1,0:T(8,128)(2,1)}, u32[]{:S(2)}, u32[]{:S(2)}) collective-permute-start(bf16[2,192,384]{2,1,0:T(8,128)(2,1)S(1)} %pad_maximum_fusion.5), channel_id=1, source_target_pairs={{0,3},{1,0},{2,1},{3,2},{4,7},{5,4},{6,5},{7,6},{8,11},{9,8},{10,9... | collective-permute-start | bytes 884744 | tf_op jit(solution)/shard_map/ppermute | solution.py:76
  112.5 11.5 %collective-permute-start.9 = (bf16[2,192,384]{2,1,0:T(8,128)(2,1)S(1)}, bf16[2,192,384]{2,1,0:T(8,128)(2,1)}, u32[]{:S(2)}, u32[]{:S(2)}) collective-permute-start(bf16[2,192,384]{2,1,0:T(8,128)(2,1)S(1)} %pad_maximum_fusion.4), channel_id=1, source_target_pairs={{0,1},{1,2},{2,3},{3,0},{4,5},{5,6},{6,7},{7,4},{8,9},{9,10},{10,1... | collective-permute-start | bytes 884744 | tf_op jit(solution)/shard_map/ppermute | solution.py:76
  117.6 8.9 %copy-start.1 = (bf16[2,768,768]{2,1,0:T(8,128)(2,1)S(1)}, bf16[2,768,768]{2,1,0:T(8,128)(2,1)}, u32[]{:S(2)}) copy-start(bf16[2,768,768]{2,1,0:T(8,128)(2,1)} %param.3) | copy-start | bytes 7077892

commit v12 on v10

--- a/solution.py
+++ b/solution.py
@@ -50,7 +50,7 @@
     slots = owned_slots.shape[0]
     pieces = own_vector.reshape(devices, piece, cols)
     pieces = lax.all_to_all(pieces, PAIR, 0, 0, tiled=True)
-    picked = jnp.take(pieces, owned_slots, axis=0)
+    picked = pieces.at[owned_slots].get(mode="promise_in_bounds")
     first = ring_gather(picked, sizes, 1, direct_far=True)
     both = ring_gather(first, sizes, 2)
     swap = [(q, q ^ 1) for q in range(devices)]
@@ -67,7 +67,7 @@
     dz, dx = (zq - z) % nz, (xq - x) % nx
     inner = jnp.where(cq == 0, dz * nx + dx, dx * nz + dz)
     index = jnp.where(cq == core, 0, chips) + inner
-    ordered = jnp.take(stacked, index, axis=0)
+    ordered = stacked.at[index].get(mode="promise_in_bounds")
     ordered = jnp.transpose(ordered, (1, 0, 2, 3))
     return ordered.reshape(slots, rows, cols)
 
@@ -90,13 +90,9 @@
 
 def exchange(own, owed, groups):
     ahead, behind, far = owed
-    half = far.shape[1] // 2
     ahead = shifted(ahead, 1, groups)
     behind = shifted(behind, -1, groups)
-    far_low = shifted(far[:, :half], 2, groups)
-    far_high = shifted(far[:, half:], 1, groups)
-    far_high = shifted(far_high, 1, groups)
-    far = jnp.concatenate([far_low, far_high], axis=1)
+    far = shifted(far, 2, groups)
     near = ahead.astype(jnp.float32) + behind.astype(jnp.float32)
     return own + near + far.astype(jnp.float32)
 

time: 145 us -> 136 us (0.938)
  waiting for transfers between devices: 67.4 us -> 61.2 us
  other arithmetic: 15.4 us -> 12.2 us
  local copies, waits for them, and re-layouts: 11.7 us -> 14.1 us
    ppermute x10 -> x6, waiting for transfers between devices: 26.4 us -> 19.6 us  [shifted(): lax.ppermute(value, 'vgrp', [(g, (g + step) % groups) for g in range(grou...]
    select_n x5 -> x2, other arithmetic: 4.87 us -> 0.72 us  [the longest x1 0.69 us: gather_slots(): picked = pieces.at[owned_slots].get(mode='promise_in_bounds')]
    slice x1, local copies, waits for them, and re-layouts: 0.31 us -> 2.8 us  [on_device(): vectors[slot]]
    ppermute x10 -> x6, starting transfers between devices: 9.19 us -> 8.48 us  [shifted(): lax.ppermute(value, 'vgrp', [(g, (g + step) % groups) for g in range(grou...]
  transfers between devices with their start and end apart: 19 -> 15, of which waited for: 13 -> 13; matrix products, arithmetic and copies ran while one was open for 2% -> 2% of each run, Pallas kernels for 0% -> 0%
where the time goes in v12:
time: 136 us
  waiting for transfers between devices  61.2 us (45%)
  starting transfers between devices  28.1 us (21%)
  matrix products  19.9 us (15%)
  local copies, waits for them, and re-layouts  14.1 us (10%)
  other arithmetic  12.2 us (9%)
    ppermute x6, waiting for transfers between devices, shifted(): lax.ppermute(value, 'vgrp', [(g, (g + step) % groups) for g in range(grou...  19.6 us
    all_to_all x1, waiting for transfers between devices, gather_slots(): pieces = lax.all_to_all(pieces, PAIR, 0, 0, tiled=True)  17.8 us
    dot_general x8, matrix products, columns(): jnp.einsum('pad,bd->pab', half_product, vectors[slot, lo:hi], preferred_e...  11.9 us
    all_to_all x1, starting transfers between devices, gather_slots(): pieces = lax.all_to_all(pieces, PAIR, 0, 0, tiled=True)  9.55 us
    ppermute x6, starting transfers between devices, shifted(): lax.ppermute(value, 'vgrp', [(g, (g + step) % groups) for g in range(grou...  8.48 us
    ppermute x2, waiting for transfers between devices, ring_gather(): from_next = lax.ppermute(piece, PAIR, ring_perm(sizes, stage, -1))  8.14 us
    dot_general x4, matrix products, on_device(): jnp.einsum('ac,pcd->pad', vectors[slot], amplitudes, preferred_element_ty...  8.01 us
    gather x1, local copies, waits for them, and re-layouts, gather_slots(): ordered = stacked.at[index].get(mode='promise_in_bounds')  5.38 us
  transfers between devices with their start and end apart: 15, of which 13 were waited for; matrix products, arithmetic and copies ran while one was open for 2% of the time, Pallas kernels for 0%

profile of v12, /device:TPU:1, one launch (start us, length us, event | category | flops | bytes accessed | tf_op | source)
XLA Modules:
  0.0 135.8 jit_solution(9380846568324397379)
XLA Ops:
  0.0 9.6 %all-to-all-start = ((bf16[32,24,768]{2,1,0:T(8,128)(2,1)}), bf16[32,24,768]{2,1,0:T(8,128)(2,1)S(1)}, u32[]{:S(2)}, u32[]{:S(2)}) async-start(bf16[32,24,768]{2,1,0:T(8,128)(2,1)} %bitcast.161), calls=%async_computation | async-start | bytes 2359296 | tf_op jit(solution)/shard_map/all_to_all | solution.py:52
  10.3 17.8 %all-to-all-done = bf16[32,24,768]{2,1,0:T(8,128)(2,1)S(1)} async-done(((bf16[32,24,768]{2,1,0:T(8,128)(2,1)}), bf16[32,24,768]{2,1,0:T(8,128)(2,1)S(1)}, u32[]{:S(2)}, u32[]{:S(2)}) %all-to-all-start) | async-done | bytes 1179680 | tf_op jit(solution)/shard_map/all_to_all | solution.py:52
  29.3 1.7 %collective-permute-start.1 = (bf16[4,24,768]{2,1,0:T(8,128)(2,1)}, bf16[4,24,768]{2,1,0:T(8,128)(2,1)S(1)}, u32[]{:S(2)}, u32[]{:S(2)}) collective-permute-start(bf16[4,24,768]{2,1,0:T(8,128)(2,1)} %gather_fusion), channel_id=1, source_target_pairs={{0,16},{4,68},{8,24},{12,76},{16,0},{20,84},{24,8},{28,92},{32,48}... | collective-permute-start | bytes 442376 | tf_op jit(solution)/shard_map/ppermute | solution.py:37
  32.4 4.2 %collective-permute-done.2 = bf16[4,24,768]{2,1,0:T(8,128)(2,1)S(1)} collective-permute-done((bf16[4,24,768]{2,1,0:T(8,128)(2,1)}, bf16[4,24,768]{2,1,0:T(8,128)(2,1)S(1)}, u32[]{:S(2)}, u32[]{:S(2)}) %collective-permute-start.2) | collective-permute-done | bytes 147488 | tf_op jit(solution)/shard_map/ppermute | solution.py:34
  38.2 1.4 %collective-permute-start.3 = (bf16[4,4,24,768]{3,2,1,0:T(8,128)(2,1)S(1)}, bf16[4,4,24,768]{3,2,1,0:T(8,128)(2,1)S(1)}, u32[]{:S(2)}, u32[]{:S(2)}) collective-permute-start(bf16[4,4,24,768]{3,2,1,0:T(8,128)(2,1)S(1)} %get-tuple-element.30), channel_id=1, source_target_pairs={{0,96},{4,28},{8,104},{12,4},{16,112},{20,12},{24,120},{28,20},{32... | collective-permute-start | bytes 1769480 | tf_op jit(solution)/shard_map/ppermute | solution.py:35
  39.7 7.6 %collective-permute-done.3 = bf16[4,4,24,768]{3,2,1,0:T(8,128)(2,1)S(1)} collective-permute-done((bf16[4,4,24,768]{3,2,1,0:T(8,128)(2,1)S(1)}, bf16[4,4,24,768]{3,2,1,0:T(8,128)(2,1)S(1)}, u32[]{:S(2)}, u32[]{:S(2)}) %collective-permute-start.3) | collective-permute-done | bytes 589856 | tf_op jit(solution)/shard_map/ppermute | solution.py:35
  47.3 2.6 %collective-permute-start.6 = (bf16[2,4,24,768]{3,2,1,0:T(8,128)(2,1)S(1)}, bf16[2,4,24,768]{3,2,1,0:T(8,128)(2,1)S(1)}, u32[]{:S(2)}, u32[]{:S(2)}) collective-permute-start(bf16[2,4,24,768]{3,2,1,0:T(8,128)(2,1)S(1)} %slice.65), channel_id=1, source_target_pairs={{0,96},{4,28},{8,104},{12,4},{16,112},{20,12},{24,120},{28,20},{32... | collective-permute-start | bytes 884744 | tf_op jit(solution)/shard_map/ppermute | solution.py:40
  50.1 3.6 %collective-permute-done.6 = bf16[2,4,24,768]{3,2,1,0:T(8,128)(2,1)S(1)} collective-permute-done((bf16[2,4,24,768]{3,2,1,0:T(8,128)(2,1)S(1)}, bf16[2,4,24,768]{3,2,1,0:T(8,128)(2,1)S(1)}, u32[]{:S(2)}, u32[]{:S(2)}) %collective-permute-start.6) | collective-permute-done | bytes 294944 | tf_op jit(solution)/shard_map/ppermute | solution.py:40
  53.6 3.5 %collective-permute-done.5 = bf16[2,4,24,768]{3,2,1,0:T(8,128)(2,1)S(1)} collective-permute-done((bf16[2,4,24,768]{3,2,1,0:T(8,128)(2,1)S(1)}, bf16[2,4,24,768]{3,2,1,0:T(8,128)(2,1)S(1)}, u32[]{:S(2)}, u32[]{:S(2)}) %collective-permute-start.5) | collective-permute-done | bytes 294944 | tf_op jit(solution)/shard_map/ppermute | solution.py:39
  57.2 1.7 %pad_maximum_fusion.1 = bf16[4,4,4,24,768]{4,3,2,1,0:T(8,128)(2,1)} fusion(bf16[1,4,4,24,768]{4,3,2,1,0:T(8,128)(2,1)S(1)} %bitcast.156, bf16[1,4,4,24,768]{4,3,2,1,0:T(8,128)(2,1)S(1)} %maximum_bitcast_fusion, bf16[1,4,4,24,768]{4,3,2,1,0:T(8,128)(2,1)S(1)} %bitcast.155, bf16[1,4,4,24,768]{4,3,2,1,0:T(8,128)(2,1)S(1)} %get-tuple-element.29), kind=kLoop, calls=%fused_computation.3 | loop fusion | flops 3538944 | bytes 4718592 | tf_op jit(solution)/shard_map/stack | solution.py:42
  58.9 2.7 %collective-permute-start.7 = (bf16[4,4,4,24,768]{4,3,2,1,0:T(8,128)(2,1)}, bf16[4,4,4,24,768]{4,3,2,1,0:T(8,128)(2,1)}, u32[]{:S(2)}, u32[]{:S(2)}) collective-permute-start(bf16[4,4,4,24,768]{4,3,2,1,0:T(8,128)(2,1)} %pad_maximum_fusion.1), channel_id=1, source_target_pairs={{0,4},{4,0},{8,12},{12,8},{16,20},{20,16},{24,28},{28,24},{32,36},... | collective-permute-start | bytes 7077896 | tf_op jit(solution)/shard_map/ppermute | solution.py:57
  61.7 4.5 %collective-permute-done.7 = bf16[4,4,4,24,768]{4,3,2,1,0:T(8,128)(2,1)} collective-permute-done((bf16[4,4,4,24,768]{4,3,2,1,0:T(8,128)(2,1)}, bf16[4,4,4,24,768]{4,3,2,1,0:T(8,128)(2,1)}, u32[]{:S(2)}, u32[]{:S(2)}) %collective-permute-start.7) | collective-permute-done | bytes 2359328 | tf_op jit(solution)/shard_map/ppermute | solution.py:57
  66.1 4.9 %pad_maximum_fusion = bf16[32,4,24,768]{3,2,1,0:T(8,128)(2,1)} fusion(bf16[16,4,24,768]{3,2,1,0:T(8,128)(2,1)} %bitcast.12, bf16[16,4,24,768]{3,2,1,0:T(8,128)(2,1)} %bitcast.11), kind=kLoop, calls=%fused_computation.2 | loop fusion | flops 2359296 | bytes 9437184 | tf_op jit(solution)/shard_map/concatenate | solution.py:59
  71.0 5.4 %gather_fusion.1 = bf16[32,4,24,768]{3,2,1,0:T(8,128)(2,1)} fusion(bf16[32,4,24,768]{3,2,1,0:T(8,128)(2,1)} %pad_maximum_fusion, s32[1024]{0:T(1024)S(1)} %pad_clamp_fusion), kind=kCustom, calls=%fused_computation.1 | custom fusion | bytes 9437312 | tf_op jit(solution)/shard_map/gather | solution.py:70
  76.4 2.8 %fusion.24 = (bf16[1,32,24,768]{3,2,0,1:T(8,128)(2,1)S(1)}, bf16[1,32,24,768]{3,2,0,1:T(8,128)(2,1)S(1)}, bf16[1,32,24,768]{3,2,0,1:T(8,128)(2,1)S(1)}, bf16[1,32,24,768]{3,2,0,1:T(8,128)(2,1)S(1)}) fusion(bf16[4,32,24,768]{3,2,0,1:T(8,128)(2,1)} %bitcast.139), kind=kLoop, calls=%fused_computation.75 | loop fusion | bytes 9437184 | tf_op jit(solution)/shard_map/slice | solution.py:117
  80.5 2.0 %convert_bitcast_fusion.3 = bf16[2,768,768]{2,1,0:T(8,128)(2,1)S(1)} fusion(bf16[768,768,1]{1,0,2:T(8,128)(2,1)S(1)} %bitcast.160, bf16[2,768,768]{2,1,0:T(8,128)(2,1)S(1)} %copy-done), kind=kOutput, calls=%fused_computation.9 | convolution fusion | flops 1813118976 | bytes 5898240 | tf_op jit(solution)/shard_map/ac,pcd->pad/dot_general | solution.py:116
  82.5 2.0 %convert_bitcast_fusion.2 = bf16[2,768,768]{2,1,0:T(8,128)(2,1)S(1)} fusion(bf16[768,768,1]{1,0,2:T(8,128)(2,1)S(1)} %bitcast.159, bf16[2,768,768]{2,1,0:T(8,128)(2,1)S(1)} %copy-done), kind=kOutput, calls=%fused_computation.8 | convolution fusion | flops 1813118976 | bytes 5898240 | tf_op jit(solution)/shard_map/ac,pcd->pad/dot_general | solution.py:116
  84.5 2.0 %convert_bitcast_fusion.1 = bf16[2,768,768]{2,1,0:T(8,128)(2,1)S(1)} fusion(bf16[768,768,1]{1,0,2:T(8,128)(2,1)S(1)} %bitcast.158, bf16[2,768,768]{2,1,0:T(8,128)(2,1)S(1)} %copy-done), kind=kOutput, calls=%fused_computation.7 | convolution fusion | flops 1813118976 | bytes 5898240 | tf_op jit(solution)/shard_map/ac,pcd->pad/dot_general | solution.py:116
  86.5 2.0 %convert_bitcast_fusion = bf16[2,768,768]{2,1,0:T(8,128)(2,1)S(1)} fusion(bf16[768,768,1]{1,0,2:T(8,128)(2,1)S(1)} %bitcast.157, bf16[2,768,768]{2,1,0:T(8,128)(2,1)S(1)} %copy-done), kind=kOutput, calls=%fused_computation.5 | convolution fusion | flops 1813118976 | bytes 5898240 | tf_op jit(solution)/shard_map/ac,pcd->pad/dot_general | solution.py:116
  88.5 1.4 %fusion.3 = f32[2,768,384]{2,1,0:T(8,128)S(1)} fusion(bf16[2,768,768]{2,1,0:T(8,128)(2,1)S(1)} %convert_bitcast_fusion.1, bf16[4,768,768]{2,1,0:T(8,128)(2,1)S(1)} %bitcast.143), kind=kOutput, calls=%fused_computation.20 | convolution fusion | flops 905969664 | bytes 5308416 | tf_op jit(solution)/shard_map/pad,bd->pab/dot_general | solution.py:103
  92.8 1.6 %add_add_fusion.1 = f32[2,768,384]{2,1,0:T(8,128)S(1)} fusion(f32[2,768,384]{2,1,0:T(8,128)S(1)} %fusion.3, f32[2,768,384]{2,1,0:T(8,128)S(1)} %fusion.5, f32[2,768,384]{2,1,0:T(8,128)S(1)} %fusion.4, bf16[2,768,768]{2,1,0:T(8,128)(2,1)S(1)} %convert_bitcast_fusion, bf16[4,768,768]{2,1,0:T(8,128)(2,1)S(1)} %bitcast.146), kind=kOutput, calls=%fused_computation.6 | convolution fusion | flops 907739136 | bytes 12386304 | tf_op jit(solution)/shard_map/pad,bd->pab/dot_general | solution.py:103
  95.4 1.6 %fusion = f32[2,768,384]{2,1,0:T(8,128)S(1)} fusion(bf16[2,768,768]{2,1,0:T(8,128)(2,1)S(1)} %convert_bitcast_fusion.1, bf16[4,768,768]{2,1,0:T(8,128)(2,1)S(1)} %bitcast.147), kind=kOutput, calls=%fused_computation.13 | convolution fusion | flops 905969664 | bytes 5308416 | tf_op jit(solution)/shard_map/pad,bd->pab/dot_general | solution.py:103
  97.1 1.4 %fusion.2 = f32[2,768,384]{2,1,0:T(8,128)S(1)} fusion(bf16[2,768,768]{2,1,0:T(8,128)(2,1)S(1)} %convert_bitcast_fusion.3, bf16[4,768,768]{2,1,0:T(8,128)(2,1)S(1)} %bitcast.148), kind=kOutput, calls=%fused_computation.17 | convolution fusion | flops 905969664 | bytes 5308416 | tf_op jit(solution)/shard_map/pad,bd->pab/dot_general | solution.py:103
  99.9 1.6 %add_add_fusion = f32[2,768,384]{2,1,0:T(8,128)S(1)} fusion(f32[2,768,384]{2,1,0:T(8,128)S(1)} %fusion, f32[2,768,384]{2,1,0:T(8,128)S(1)} %fusion.2, f32[2,768,384]{2,1,0:T(8,128)S(1)} %fusion.1, bf16[2,768,768]{2,1,0:T(8,128)(2,1)S(1)} %convert_bitcast_fusion, bf16[4,768,768]{2,1,0:T(8,128)(2,1)S(1)} %bitcast.150), kind=kOutput, calls=%fused_computation.4 | convolution fusion | flops 907739136 | bytes 12386304 | tf_op jit(solution)/shard_map/pad,bd->pab/dot_general | solution.py:103
  101.6 1.4 %copy-done.3 = f32[2,768,384]{2,1,0:T(8,128)} copy-done((f32[2,768,384]{2,1,0:T(8,128)}, f32[2,768,384]{2,1,0:T(8,128)S(1)}, u32[]{:S(2)}) %copy-start.3) | copy-done | bytes 2359320
  103.9 2.9 %collective-permute-start.13 = (bf16[2,192,384]{2,1,0:T(8,128)(2,1)S(1)}, bf16[2,192,384]{2,1,0:T(8,128)(2,1)S(1)}, u32[]{:S(2)}, u32[]{:S(2)}) collective-permute-start(bf16[2,192,384]{2,1,0:T(8,128)(2,1)S(1)} %get-tuple-element.25), channel_id=1, source_target_pairs={{0,2},{1,3},{2,0},{3,1},{4,6},{5,7},{6,4},{7,5},{8,10},{9,11},{10,... | collective-permute-start | bytes 884744 | tf_op jit(solution)/shard_map/ppermute | solution.py:76
  109.0 2.1 %collective-permute-start.9 = (bf16[2,192,384]{2,1,0:T(8,128)(2,1)}, bf16[2,192,384]{2,1,0:T(8,128)(2,1)S(1)}, u32[]{:S(2)}, u32[]{:S(2)}) collective-permute-start(bf16[2,192,384]{2,1,0:T(8,128)(2,1)} %get-tuple-element.13), channel_id=1, source_target_pairs={{0,3},{1,0},{2,1},{3,2},{4,7},{5,4},{6,5},{7,6},{8,11},{9,8},{10,9... | collective-permute-start | bytes 884744 | tf_op jit(solution)/shard_map/ppermute | solution.py:76
  111.1 2.6 %collective-permute-done.13 = bf16[2,192,384]{2,1,0:T(8,128)(2,1)S(1)} collective-permute-done((bf16[2,192,384]{2,1,0:T(8,128)(2,1)S(1)}, bf16[2,192,384]{2,1,0:T(8,128)(2,1)S(1)}, u32[]{:S(2)}, u32[]{:S(2)}) %collective-permute-start.13) | collective-permute-done | bytes 294944 | tf_op jit(solution)/shard_map/ppermute | solution.py:76
  114.9 5.5 %collective-permute-done.12 = bf16[2,192,384]{2,1,0:T(8,128)(2,1)S(1)} collective-permute-done((bf16[2,192,384]{2,1,0:T(8,128)(2,1)}, bf16[2,192,384]{2,1,0:T(8,128)(2,1)S(1)}, u32[]{:S(2)}, u32[]{:S(2)}) %collective-permute-start.12) | collective-permute-done | bytes 294944 | tf_op jit(solution)/shard_map/ppermute | solution.py:76
  121.5 1.4 %fusion.6 = f32[2,192,384]{2,1,0:T(8,128)S(1)} fusion(bf16[2,192,384]{2,1,0:T(8,128)(2,1)S(1)} %collective-permute-done.13, bf16[2,192,384]{2,1,0:T(8,128)(2,1)S(1)} %collective-permute-done.12, bf16[2,192,384]{2,1,0:T(8,128)(2,1)} %collective-permute-done.11, f32[2,4,192,384]{3,2,1,0:T(8,128)} %bitcast.154, s32[]{:T(128)S(6)} %select_n.171), kind=kLoop, calls=%fused_computation.34 | loop fusion | flops 884736 | bytes 2064388 | tf_op jit(solution)/shard_map/add | solution.py:97
  122.9 3.4 %collective-permute-done.10 = bf16[2,192,384]{2,1,0:T(8,128)(2,1)S(1)} collective-permute-done((bf16[2,192,384]{2,1,0:T(8,128)(2,1)}, bf16[2,192,384]{2,1,0:T(8,128)(2,1)S(1)}, u32[]{:S(2)}, u32[]{:S(2)}) %collective-permute-start.10) | collective-permute-done | bytes 294944 | tf_op jit(solution)/shard_map/ppermute | solution.py:76
  126.3 6.8 %collective-permute-done.9 = bf16[2,192,384]{2,1,0:T(8,128)(2,1)S(1)} collective-permute-done((bf16[2,192,384]{2,1,0:T(8,128)(2,1)}, bf16[2,192,384]{2,1,0:T(8,128)(2,1)S(1)}, u32[]{:S(2)}, u32[]{:S(2)}) %collective-permute-start.9) | collective-permute-done | bytes 294944 | tf_op jit(solution)/shard_map/ppermute | solution.py:76
  (42 shorter events, 19.9 us)
Async XLA Ops:
  0.0 80.5 %copy-start = (bf16[2,768,768]{2,1,0:T(8,128)(2,1)S(1)}, bf16[2,768,768]{2,1,0:T(8,128)(2,1)}, u32[]{:S(2)}) copy-start(bf16[2,768,768]{2,1,0:T(8,128)(2,1)} %param.3) | copy-start | bytes 7077892
  0.0 28.1 %all-to-all-start = ((bf16[32,24,768]{2,1,0:T(8,128)(2,1)}), bf16[32,24,768]{2,1,0:T(8,128)(2,1)S(1)}, u32[]{:S(2)}, u32[]{:S(2)}) async-start(bf16[32,24,768]{2,1,0:T(8,128)(2,1)} %bitcast.161), calls=%async_computation | async-start | bytes 2359296 | tf_op jit(solution)/shard_map/all_to_all | solution.py:52
  29.3 7.3 %collective-permute-start.2 = (bf16[4,24,768]{2,1,0:T(8,128)(2,1)}, bf16[4,24,768]{2,1,0:T(8,128)(2,1)S(1)}, u32[]{:S(2)}, u32[]{:S(2)}) collective-permute-start(bf16[4,24,768]{2,1,0:T(8,128)(2,1)} %gather_fusion), channel_id=1, source_target_pairs={{0,8},{4,36},{8,16},{12,44},{16,24},{20,52},{24,0},{28,60},{32,40}... | collective-permute-start | bytes 442376 | tf_op jit(solution)/shard_map/ppermute | solution.py:34
  29.3 7.3 %collective-permute-start.1 = (bf16[4,24,768]{2,1,0:T(8,128)(2,1)}, bf16[4,24,768]{2,1,0:T(8,128)(2,1)S(1)}, u32[]{:S(2)}, u32[]{:S(2)}) collective-permute-start(bf16[4,24,768]{2,1,0:T(8,128)(2,1)} %gather_fusion), channel_id=1, source_target_pairs={{0,16},{4,68},{8,24},{12,76},{16,0},{20,84},{24,8},{28,92},{32,48}... | collective-permute-start | bytes 442376 | tf_op jit(solution)/shard_map/ppermute | solution.py:37
  31.0 6.1 %collective-permute-start = (bf16[4,24,768]{2,1,0:T(8,128)(2,1)}, bf16[4,24,768]{2,1,0:T(8,128)(2,1)S(1)}, u32[]{:S(2)}, u32[]{:S(2)}) collective-permute-start(bf16[4,24,768]{2,1,0:T(8,128)(2,1)} %gather_fusion), channel_id=1, source_target_pairs={{0,24},{4,100},{8,0},{12,108},{16,8},{20,116},{24,16},{28,124},{32... | collective-permute-start | bytes 442376 | tf_op jit(solution)/shard_map/ppermute | solution.py:35
  38.2 9.1 %collective-permute-start.3 = (bf16[4,4,24,768]{3,2,1,0:T(8,128)(2,1)S(1)}, bf16[4,4,24,768]{3,2,1,0:T(8,128)(2,1)S(1)}, u32[]{:S(2)}, u32[]{:S(2)}) collective-permute-start(bf16[4,4,24,768]{3,2,1,0:T(8,128)(2,1)S(1)} %get-tuple-element.30), channel_id=1, source_target_pairs={{0,96},{4,28},{8,104},{12,4},{16,112},{20,12},{24,120},{28,20},{32... | collective-permute-start | bytes 1769480 | tf_op jit(solution)/shard_map/ppermute | solution.py:35
  39.6 10.3 %collective-permute-start.4 = (bf16[4,4,24,768]{3,2,1,0:T(8,128)(2,1)S(1)}, bf16[4,4,24,768]{3,2,1,0:T(8,128)(2,1)S(1)}, u32[]{:S(2)}, u32[]{:S(2)}) collective-permute-start(bf16[4,4,24,768]{3,2,1,0:T(8,128)(2,1)S(1)} %get-tuple-element.30), channel_id=1, source_target_pairs={{0,32},{4,12},{8,40},{12,20},{16,48},{20,28},{24,56},{28,4},{32,64... | collective-permute-start | bytes 1769480 | tf_op jit(solution)/shard_map/ppermute | solution.py:34
  47.3 6.3 %collective-permute-start.6 = (bf16[2,4,24,768]{3,2,1,0:T(8,128)(2,1)S(1)}, bf16[2,4,24,768]{3,2,1,0:T(8,128)(2,1)S(1)}, u32[]{:S(2)}, u32[]{:S(2)}) collective-permute-start(bf16[2,4,24,768]{3,2,1,0:T(8,128)(2,1)S(1)} %slice.65), channel_id=1, source_target_pairs={{0,96},{4,28},{8,104},{12,4},{16,112},{20,12},{24,120},{28,20},{32... | collective-permute-start | bytes 884744 | tf_op jit(solution)/shard_map/ppermute | solution.py:40
  50.0 7.1 %collective-permute-start.5 = (bf16[2,4,24,768]{3,2,1,0:T(8,128)(2,1)S(1)}, bf16[2,4,24,768]{3,2,1,0:T(8,128)(2,1)S(1)}, u32[]{:S(2)}, u32[]{:S(2)}) collective-permute-start(bf16[2,4,24,768]{3,2,1,0:T(8,128)(2,1)S(1)} %slice.64), channel_id=1, source_target_pairs={{0,32},{4,12},{8,40},{12,20},{16,48},{20,28},{24,56},{28,4},{32,64... | collective-permute-start | bytes 884744 | tf_op jit(solution)/shard_map/ppermute | solution.py:39
  58.9 7.2 %collective-permute-start.7 = (bf16[4,4,4,24,768]{4,3,2,1,0:T(8,128)(2,1)}, bf16[4,4,4,24,768]{4,3,2,1,0:T(8,128)(2,1)}, u32[]{:S(2)}, u32[]{:S(2)}) collective-permute-start(bf16[4,4,4,24,768]{4,3,2,1,0:T(8,128)(2,1)} %pad_maximum_fusion.1), channel_id=1, source_target_pairs={{0,4},{4,0},{8,12},{12,8},{16,20},{20,16},{24,28},{28,24},{32,36},... | collective-permute-start | bytes 7077896 | tf_op jit(solution)/shard_map/ppermute | solution.py:57
  76.4 3.6 %slice-start = ((s8[4718592]{0:T(1024)(128)(4,1)}), s8[4194304]{0:T(1024)(128)(4,1)S(1)}, s32[]{:S(2)}) async-start(s8[4718592]{0:T(1024)(128)(4,1)} %bitcast.140), calls=%async_computation.1 | async-start | bytes 8388608
  76.4 3.7 %slice-start.1 = ((s8[4718592]{0:T(1024)(128)(4,1)}), s8[524288]{0:T(1024)(128)(4,1)S(1)}, s32[]{:S(2)}) async-start(s8[4718592]{0:T(1024)(128)(4,1)} %bitcast.140), calls=%async_computation.2 | async-start | bytes 1048576
  94.4 2.7 %copy-start.2 = (f32[2,768,384]{2,1,0:T(8,128)}, f32[2,768,384]{2,1,0:T(8,128)S(1)}, u32[]{:S(2)}) copy-start(f32[2,768,384]{2,1,0:T(8,128)S(1)} %add_add_fusion.1) | copy-start | bytes 7077892
  101.5 1.4 %copy-start.3 = (f32[2,768,384]{2,1,0:T(8,128)}, f32[2,768,384]{2,1,0:T(8,128)S(1)}, u32[]{:S(2)}) copy-start(f32[2,768,384]{2,1,0:T(8,128)S(1)} %add_add_fusion) | copy-start | bytes 7077892
  103.9 9.7 %collective-permute-start.13 = (bf16[2,192,384]{2,1,0:T(8,128)(2,1)S(1)}, bf16[2,192,384]{2,1,0:T(8,128)(2,1)S(1)}, u32[]{:S(2)}, u32[]{:S(2)}) collective-permute-start(bf16[2,192,384]{2,1,0:T(8,128)(2,1)S(1)} %get-tuple-element.25), channel_id=1, source_target_pairs={{0,2},{1,3},{2,0},{3,1},{4,6},{5,7},{6,4},{7,5},{8,10},{9,11},{10,... | collective-permute-start | bytes 884744 | tf_op jit(solution)/shard_map/ppermute | solution.py:76
  106.8 13.6 %collective-permute-start.12 = (bf16[2,192,384]{2,1,0:T(8,128)(2,1)}, bf16[2,192,384]{2,1,0:T(8,128)(2,1)S(1)}, u32[]{:S(2)}, u32[]{:S(2)}) collective-permute-start(bf16[2,192,384]{2,1,0:T(8,128)(2,1)} %get-tuple-element.24), channel_id=1, source_target_pairs={{0,3},{1,0},{2,1},{3,2},{4,7},{5,4},{6,5},{7,6},{8,11},{9,8},{10,9... | collective-permute-start | bytes 884744 | tf_op jit(solution)/shard_map/ppermute | solution.py:76
  107.6 13.9 %collective-permute-start.11 = (bf16[2,192,384]{2,1,0:T(8,128)(2,1)}, bf16[2,192,384]{2,1,0:T(8,128)(2,1)}, u32[]{:S(2)}, u32[]{:S(2)}) collective-permute-start(bf16[2,192,384]{2,1,0:T(8,128)(2,1)} %get-tuple-element.23), channel_id=1, source_target_pairs={{0,1},{1,2},{2,3},{3,0},{4,5},{5,6},{6,7},{7,4},{8,9},{9,10},{10,1... | collective-permute-start | bytes 884744 | tf_op jit(solution)/shard_map/ppermute | solution.py:76
  108.3 18.0 %collective-permute-start.10 = (bf16[2,192,384]{2,1,0:T(8,128)(2,1)}, bf16[2,192,384]{2,1,0:T(8,128)(2,1)S(1)}, u32[]{:S(2)}, u32[]{:S(2)}) collective-permute-start(bf16[2,192,384]{2,1,0:T(8,128)(2,1)} %get-tuple-element.14), channel_id=1, source_target_pairs={{0,2},{1,3},{2,0},{3,1},{4,6},{5,7},{6,4},{7,5},{8,10},{9,11},{10,... | collective-permute-start | bytes 884744 | tf_op jit(solution)/shard_map/ppermute | solution.py:76
  109.0 24.1 %collective-permute-start.9 = (bf16[2,192,384]{2,1,0:T(8,128)(2,1)}, bf16[2,192,384]{2,1,0:T(8,128)(2,1)S(1)}, u32[]{:S(2)}, u32[]{:S(2)}) collective-permute-start(bf16[2,192,384]{2,1,0:T(8,128)(2,1)} %get-tuple-element.13), channel_id=1, source_target_pairs={{0,3},{1,0},{2,1},{3,2},{4,7},{5,4},{6,5},{7,6},{8,11},{9,8},{10,9... | collective-permute-start | bytes 884744 | tf_op jit(solution)/shard_map/ppermute | solution.py:76
  113.6 19.8 %collective-permute-start.8 = (bf16[2,192,384]{2,1,0:T(8,128)(2,1)}, bf16[2,192,384]{2,1,0:T(8,128)(2,1)}, u32[]{:S(2)}, u32[]{:S(2)}) collective-permute-start(bf16[2,192,384]{2,1,0:T(8,128)(2,1)} %get-tuple-element.12), channel_id=1, source_target_pairs={{0,1},{1,2},{2,3},{3,0},{4,5},{5,6},{6,7},{7,4},{8,9},{9,10},{10,1... | collective-permute-start | bytes 884744 | tf_op jit(solution)/shard_map/ppermute | solution.py:76
  121.5 14.3 %copy-start.1 = (bf16[2,768,768]{2,1,0:T(8,128)(2,1)S(1)}, bf16[2,768,768]{2,1,0:T(8,128)(2,1)}, u32[]{:S(2)}) copy-start(bf16[2,768,768]{2,1,0:T(8,128)(2,1)} %param.3) | copy-start | bytes 7077892

commit v13 on v12

--- a/solution.py
+++ b/solution.py
@@ -9,6 +9,7 @@
 
 
 RING = 4
+CHUNKS = 6
 
 
 def ring_axis(stage, core):
@@ -118,13 +119,15 @@
         ).astype(jnp.bfloat16)
         for slot in range(vectors.shape[0])
     )
-    split = vectors.shape[1] // 2
-    own_a, owed_a = prepare(columns(halves, vectors, 0, split), vgrp, groups)
-    halves, owed_a = lax.optimization_barrier((halves, owed_a))
-    out_a = exchange(own_a, owed_a, groups)
-    own_b, owed_b = prepare(columns(halves, vectors, split, None), vgrp, groups)
-    out_b = exchange(own_b, owed_b, groups)
-    return jnp.concatenate([out_a, out_b], axis=2)
+    width = vectors.shape[1] // CHUNKS
+    outs = []
+    for chunk in range(CHUNKS):
+        cut = columns(halves, vectors, chunk * width, (chunk + 1) * width)
+        own, owed = prepare(cut, vgrp, groups)
+        if chunk < CHUNKS - 1:
+            halves, owed = lax.optimization_barrier((halves, owed))
+        outs.append(exchange(own, owed, groups))
+    return jnp.concatenate(outs, axis=2)
 
 
 def solution(mesh):

time: 136 us -> 142 us (1.044)
  the two profiles are of different devices: /device:TPU:1 before, /device:TPU:0 now
where the time goes in v13:
time: 142 us
  waiting for transfers between devices  52.5 us (37%)
  starting transfers between devices  41.4 us (29%)
  matrix products  27.4 us (19%)
  local copies, waits for them, and re-layouts  10.9 us (8%)
  other arithmetic  9.41 us (7%)
    ppermute x18, starting transfers between devices, shifted(): lax.ppermute(value, 'vgrp', [(g, (g + step) % groups) for g in range(grou...  25.5 us
    dot_general x24, matrix products, columns(): jnp.einsum('pad,bd->pab', half_product, vectors[slot, lo:hi], preferred_e...  19.3 us
    all_to_all x1, waiting for transfers between devices, gather_slots(): pieces = lax.all_to_all(pieces, PAIR, 0, 0, tiled=True)  18 us
    all_to_all x1, starting transfers between devices, gather_slots(): pieces = lax.all_to_all(pieces, PAIR, 0, 0, tiled=True)  8.41 us
    dot_general x4, matrix products, on_device(): jnp.einsum('ac,pcd->pad', vectors[slot], amplitudes, preferred_element_ty...  8.01 us
    ppermute x2, waiting for transfers between devices, ring_gather(): from_next = lax.ppermute(piece, PAIR, ring_perm(sizes, stage, -1))  7.86 us
    ppermute x18, waiting for transfers between devices, shifted(): lax.ppermute(value, 'vgrp', [(g, (g + step) % groups) for g in range(grou...  7.51 us
    gather x1, local copies, waits for them, and re-layouts, gather_slots(): ordered = stacked.at[index].get(mode='promise_in_bounds')  5.35 us
  transfers between devices with their start and end apart: 27, of which 14 were waited for; matrix products, arithmetic and copies ran while one was open for 12% of the time, Pallas kernels for 0%

profile of v13, /device:TPU:0, one launch (start us, length us, event | category | flops | bytes accessed | tf_op | source)
XLA Modules:
  0.0 142.0 jit_solution(10909593332139060357)
XLA Ops:
  0.0 8.4 %all-to-all-start = ((bf16[32,24,768]{2,1,0:T(8,128)(2,1)}), bf16[32,24,768]{2,1,0:T(8,128)(2,1)S(1)}, u32[]{:S(2)}, u32[]{:S(2)}) async-start(bf16[32,24,768]{2,1,0:T(8,128)(2,1)} %bitcast.367), calls=%async_computation | async-start | bytes 2359296 | tf_op jit(solution)/shard_map/all_to_all | solution.py:53
  9.1 18.0 %all-to-all-done = bf16[32,24,768]{2,1,0:T(8,128)(2,1)S(1)} async-done(((bf16[32,24,768]{2,1,0:T(8,128)(2,1)}), bf16[32,24,768]{2,1,0:T(8,128)(2,1)S(1)}, u32[]{:S(2)}, u32[]{:S(2)}) %all-to-all-start) | async-done | bytes 1179680 | tf_op jit(solution)/shard_map/all_to_all | solution.py:53
  28.3 1.3 collective-permute-start.1
  29.6 1.9 %collective-permute-start = (bf16[4,24,768]{2,1,0:T(8,128)(2,1)}, bf16[4,24,768]{2,1,0:T(8,128)(2,1)S(1)}, u32[]{:S(2)}, u32[]{:S(2)}) collective-permute-start(bf16[4,24,768]{2,1,0:T(8,128)(2,1)} %gather_fusion), channel_id=1, source_target_pairs={{0,24},{4,100},{8,0},{12,108},{16,8},{20,116},{24,16},{28,124},{32... | collective-permute-start | bytes 442376 | tf_op jit(solution)/shard_map/ppermute | solution.py:36
  31.6 3.6 %collective-permute-done.1 = bf16[4,24,768]{2,1,0:T(8,128)(2,1)S(1)} collective-permute-done((bf16[4,24,768]{2,1,0:T(8,128)(2,1)}, bf16[4,24,768]{2,1,0:T(8,128)(2,1)S(1)}, u32[]{:S(2)}, u32[]{:S(2)}) %collective-permute-start.1) | collective-permute-done | bytes 147488 | tf_op jit(solution)/shard_map/ppermute | solution.py:38
  35.2 2.9 %collective-permute-done.2 = bf16[4,24,768]{2,1,0:T(8,128)(2,1)S(1)} collective-permute-done((bf16[4,24,768]{2,1,0:T(8,128)(2,1)}, bf16[4,24,768]{2,1,0:T(8,128)(2,1)S(1)}, u32[]{:S(2)}, u32[]{:S(2)}) %collective-permute-start.2) | collective-permute-done | bytes 147488 | tf_op jit(solution)/shard_map/ppermute | solution.py:35
  39.9 1.2 collective-permute-start.4
  41.2 7.9 %collective-permute-done.3 = bf16[4,4,24,768]{3,2,1,0:T(8,128)(2,1)S(1)} collective-permute-done((bf16[4,4,24,768]{3,2,1,0:T(8,128)(2,1)S(1)}, bf16[4,4,24,768]{3,2,1,0:T(8,128)(2,1)S(1)}, u32[]{:S(2)}, u32[]{:S(2)}) %collective-permute-start.3) | collective-permute-done | bytes 589856 | tf_op jit(solution)/shard_map/ppermute | solution.py:36
  49.0 2.1 %collective-permute-start.6 = (bf16[2,4,24,768]{3,2,1,0:T(8,128)(2,1)S(1)}, bf16[2,4,24,768]{3,2,1,0:T(8,128)(2,1)S(1)}, u32[]{:S(2)}, u32[]{:S(2)}) collective-permute-start(bf16[2,4,24,768]{3,2,1,0:T(8,128)(2,1)S(1)} %slice.129), channel_id=1, source_target_pairs={{0,96},{4,28},{8,104},{12,4},{16,112},{20,12},{24,120},{28,20},{32... | collective-permute-start | bytes 884744 | tf_op jit(solution)/shard_map/ppermute | solution.py:41
  51.2 4.6 %collective-permute-done.6 = bf16[2,4,24,768]{3,2,1,0:T(8,128)(2,1)S(1)} collective-permute-done((bf16[2,4,24,768]{3,2,1,0:T(8,128)(2,1)S(1)}, bf16[2,4,24,768]{3,2,1,0:T(8,128)(2,1)S(1)}, u32[]{:S(2)}, u32[]{:S(2)}) %collective-permute-start.6) | collective-permute-done | bytes 294944 | tf_op jit(solution)/shard_map/ppermute | solution.py:41
  55.8 3.3 %collective-permute-done.5 = bf16[2,4,24,768]{3,2,1,0:T(8,128)(2,1)S(1)} collective-permute-done((bf16[2,4,24,768]{3,2,1,0:T(8,128)(2,1)S(1)}, bf16[2,4,24,768]{3,2,1,0:T(8,128)(2,1)S(1)}, u32[]{:S(2)}, u32[]{:S(2)}) %collective-permute-start.5) | collective-permute-done | bytes 294944 | tf_op jit(solution)/shard_map/ppermute | solution.py:40
  59.2 1.7 %pad_maximum_fusion.1 = bf16[4,4,4,24,768]{4,3,2,1,0:T(8,128)(2,1)} fusion(bf16[1,4,4,24,768]{4,3,2,1,0:T(8,128)(2,1)S(1)} %bitcast.362, bf16[1,4,4,24,768]{4,3,2,1,0:T(8,128)(2,1)S(1)} %maximum_bitcast_fusion, bf16[1,4,4,24,768]{4,3,2,1,0:T(8,128)(2,1)S(1)} %bitcast.361, bf16[1,4,4,24,768]{4,3,2,1,0:T(8,128)(2,1)S(1)} %get-tuple-element.97), kind=kLoop, calls=%fused_computation.3 | loop fusion | flops 3538944 | bytes 4718592 | tf_op jit(solution)/shard_map/stack | solution.py:43
  61.0 4.8 %collective-permute-done.7 = bf16[4,4,4,24,768]{4,3,2,1,0:T(8,128)(2,1)} collective-permute-done((bf16[4,4,4,24,768]{4,3,2,1,0:T(8,128)(2,1)}, bf16[4,4,4,24,768]{4,3,2,1,0:T(8,128)(2,1)}, u32[]{:S(2)}, u32[]{:S(2)}) %collective-permute-start.7) | collective-permute-done | bytes 2359328 | tf_op jit(solution)/shard_map/ppermute | solution.py:58
  65.8 4.9 %pad_maximum_fusion = bf16[32,4,24,768]{3,2,1,0:T(8,128)(2,1)} fusion(bf16[16,4,24,768]{3,2,1,0:T(8,128)(2,1)} %bitcast.12, bf16[16,4,24,768]{3,2,1,0:T(8,128)(2,1)} %bitcast.11), kind=kLoop, calls=%fused_computation.2 | loop fusion | flops 2359296 | bytes 9437184 | tf_op jit(solution)/shard_map/concatenate | solution.py:60
  70.7 5.3 %gather_fusion.1 = bf16[32,4,24,768]{3,2,1,0:T(8,128)(2,1)} fusion(bf16[32,4,24,768]{3,2,1,0:T(8,128)(2,1)} %pad_maximum_fusion, s32[1024]{0:T(1024)S(1)} %pad_clamp_fusion), kind=kCustom, calls=%fused_computation.1 | custom fusion | bytes 9437312 | tf_op jit(solution)/shard_map/gather | solution.py:71
  76.1 2.8 %copy.22 = bf16[4,32,24,768]{3,2,1,0:T(8,128)(2,1)S(1)} copy(bf16[4,32,24,768]{3,2,0,1:T(8,128)(2,1)} %bitcast.321) | data formatting | bytes 9437184 | tf_op jit(solution)/shard_map/transpose | solution.py:72
  80.1 2.0 %convert_bitcast_fusion.1 = bf16[2,768,768]{2,1,0:T(8,128)(2,1)S(1)} fusion(bf16[768,768,1]{1,0,2:T(8,128)(2,1)S(1)} %bitcast.366, bf16[2,768,768]{2,1,0:T(8,128)(2,1)S(1)} %copy-done), kind=kOutput, calls=%fused_computation.5 | convolution fusion | flops 1813118976 | bytes 5898240 | tf_op jit(solution)/shard_map/ac,pcd->pad/dot_general | solution.py:117
  82.2 2.0 %convert_bitcast_fusion = bf16[2,768,768]{2,1,0:T(8,128)(2,1)S(1)} fusion(bf16[768,768,1]{1,0,2:T(8,128)(2,1)S(1)} %bitcast.365, bf16[2,768,768]{2,1,0:T(8,128)(2,1)S(1)} %copy-done), kind=kOutput, calls=%fused_computation.4 | convolution fusion | flops 1813118976 | bytes 5898240 | tf_op jit(solution)/shard_map/ac,pcd->pad/dot_general | solution.py:117
  84.2 2.0 %convert_bitcast_fusion.2 = bf16[2,768,768]{2,1,0:T(8,128)(2,1)S(1)} fusion(bf16[768,768,1]{1,0,2:T(8,128)(2,1)S(1)} %bitcast.364, bf16[2,768,768]{2,1,0:T(8,128)(2,1)S(1)} %copy-done), kind=kOutput, calls=%fused_computation.6 | convolution fusion | flops 1813118976 | bytes 5898240 | tf_op jit(solution)/shard_map/ac,pcd->pad/dot_general | solution.py:117
  86.2 2.0 %convert_bitcast_fusion.3 = bf16[2,768,768]{2,1,0:T(8,128)(2,1)S(1)} fusion(bf16[768,768,1]{1,0,2:T(8,128)(2,1)S(1)} %bitcast.363, bf16[2,768,768]{2,1,0:T(8,128)(2,1)S(1)} %copy-done), kind=kOutput, calls=%fused_computation.7 | convolution fusion | flops 1813118976 | bytes 5898240 | tf_op jit(solution)/shard_map/ac,pcd->pad/dot_general | solution.py:117
  91.5 1.6 %collective-permute-start.8 = (bf16[2,192,128]{2,1,0:T(8,128)(2,1)S(1)}, bf16[2,192,128]{2,1,0:T(8,128)(2,1)S(1)}, u32[]{:S(2)}, u32[]{:S(2)}) collective-permute-start(bf16[2,192,128]{2,1,0:T(8,128)(2,1)S(1)} %get-tuple-element.40), channel_id=1, source_target_pairs={{0,1},{1,2},{2,3},{3,0},{4,5},{5,6},{6,7},{7,4},{8,9},{9,10},{10,1... | collective-permute-start | bytes 294920 | tf_op jit(solution)/shard_map/ppermute | solution.py:77
  93.1 1.7 %collective-permute-start.9 = (bf16[2,192,128]{2,1,0:T(8,128)(2,1)S(1)}, bf16[2,192,128]{2,1,0:T(8,128)(2,1)S(1)}, u32[]{:S(2)}, u32[]{:S(2)}) collective-permute-start(bf16[2,192,128]{2,1,0:T(8,128)(2,1)S(1)} %get-tuple-element.41), channel_id=1, source_target_pairs={{0,3},{1,0},{2,1},{3,2},{4,7},{5,4},{6,5},{7,6},{8,11},{9,8},{10,9... | collective-permute-start | bytes 294920 | tf_op jit(solution)/shard_map/ppermute | solution.py:77
  94.8 2.0 %collective-permute-start.10 = (bf16[2,192,128]{2,1,0:T(8,128)(2,1)S(1)}, bf16[2,192,128]{2,1,0:T(8,128)(2,1)S(1)}, u32[]{:S(2)}, u32[]{:S(2)}) collective-permute-start(bf16[2,192,128]{2,1,0:T(8,128)(2,1)S(1)} %get-tuple-element.42), channel_id=1, source_target_pairs={{0,2},{1,3},{2,0},{3,1},{4,6},{5,7},{6,4},{7,5},{8,10},{9,11},{10,... | collective-permute-start | bytes 294920 | tf_op jit(solution)/shard_map/ppermute | solution.py:77
  100.8 2.6 %collective-permute-start.12 = (bf16[2,192,128]{2,1,0:T(8,128)(2,1)S(1)}, bf16[2,192,128]{2,1,0:T(8,128)(2,1)S(1)}, u32[]{:S(2)}, u32[]{:S(2)}) collective-permute-start(bf16[2,192,128]{2,1,0:T(8,128)(2,1)S(1)} %get-tuple-element.48), channel_id=1, source_target_pairs={{0,3},{1,0},{2,1},{3,2},{4,7},{5,4},{6,5},{7,6},{8,11},{9,8},{10,9... | collective-permute-start | bytes 294920 | tf_op jit(solution)/shard_map/ppermute | solution.py:77
  117.5 2.7 %collective-permute-start.15 = (bf16[2,192,128]{2,1,0:T(8,128)(2,1)S(1)}, bf16[2,192,128]{2,1,0:T(8,128)(2,1)S(1)}, u32[]{:S(2)}, u32[]{:S(2)}) collective-permute-start(bf16[2,192,128]{2,1,0:T(8,128)(2,1)S(1)} %get-tuple-element.55), channel_id=1, source_target_pairs={{0,3},{1,0},{2,1},{3,2},{4,7},{5,4},{6,5},{7,6},{8,11},{9,8},{10,9... | collective-permute-start | bytes 294920 | tf_op jit(solution)/shard_map/ppermute | solution.py:77
  120.3 2.3 %collective-permute-start.16 = (bf16[2,192,128]{2,1,0:T(8,128)(2,1)S(1)}, bf16[2,192,128]{2,1,0:T(8,128)(2,1)S(1)}, u32[]{:S(2)}, u32[]{:S(2)}) collective-permute-start(bf16[2,192,128]{2,1,0:T(8,128)(2,1)S(1)} %get-tuple-element.56), channel_id=1, source_target_pairs={{0,2},{1,3},{2,0},{3,1},{4,6},{5,7},{6,4},{7,5},{8,10},{9,11},{10,... | collective-permute-start | bytes 294920 | tf_op jit(solution)/shard_map/ppermute | solution.py:77
  122.9 3.0 %collective-permute-start.18 = (bf16[2,192,128]{2,1,0:T(8,128)(2,1)S(1)}, bf16[2,192,128]{2,1,0:T(8,128)(2,1)S(1)}, u32[]{:S(2)}, u32[]{:S(2)}) collective-permute-start(bf16[2,192,128]{2,1,0:T(8,128)(2,1)S(1)} %get-tuple-element.62), channel_id=1, source_target_pairs={{0,3},{1,0},{2,1},{3,2},{4,7},{5,4},{6,5},{7,6},{8,11},{9,8},{10,9... | collective-permute-start | bytes 294920 | tf_op jit(solution)/shard_map/ppermute | solution.py:77
  127.0 2.6 %collective-permute-start.21 = (bf16[2,192,128]{2,1,0:T(8,128)(2,1)S(1)}, bf16[2,192,128]{2,1,0:T(8,128)(2,1)S(1)}, u32[]{:S(2)}, u32[]{:S(2)}) collective-permute-start(bf16[2,192,128]{2,1,0:T(8,128)(2,1)S(1)} %get-tuple-element.69), channel_id=1, source_target_pairs={{0,3},{1,0},{2,1},{3,2},{4,7},{5,4},{6,5},{7,6},{8,11},{9,8},{10,9... | collective-permute-start | bytes 294920 | tf_op jit(solution)/shard_map/ppermute | solution.py:77
  130.2 1.5 %collective-permute-start.22 = (bf16[2,192,128]{2,1,0:T(8,128)(2,1)S(1)}, bf16[2,192,128]{2,1,0:T(8,128)(2,1)S(1)}, u32[]{:S(2)}, u32[]{:S(2)}) collective-permute-start(bf16[2,192,128]{2,1,0:T(8,128)(2,1)S(1)} %get-tuple-element.70), channel_id=1, source_target_pairs={{0,2},{1,3},{2,0},{3,1},{4,6},{5,7},{6,4},{7,5},{8,10},{9,11},{10,... | collective-permute-start | bytes 294920 | tf_op jit(solution)/shard_map/ppermute | solution.py:77
  131.8 1.4 %collective-permute-done.19 = bf16[2,192,128]{2,1,0:T(8,128)(2,1)S(1)} collective-permute-done((bf16[2,192,128]{2,1,0:T(8,128)(2,1)S(1)}, bf16[2,192,128]{2,1,0:T(8,128)(2,1)S(1)}, u32[]{:S(2)}, u32[]{:S(2)}) %collective-permute-start.19) | collective-permute-done | bytes 98336 | tf_op jit(solution)/shard_map/ppermute | solution.py:77
  133.2 1.8 %collective-permute-start.24 = (bf16[2,192,128]{2,1,0:T(8,128)(2,1)S(1)}, bf16[2,192,128]{2,1,0:T(8,128)(2,1)S(1)}, u32[]{:S(2)}, u32[]{:S(2)}) collective-permute-start(bf16[2,192,128]{2,1,0:T(8,128)(2,1)S(1)} %get-tuple-element.80), channel_id=1, source_target_pairs={{0,3},{1,0},{2,1},{3,2},{4,7},{5,4},{6,5},{7,6},{8,11},{9,8},{10,9... | collective-permute-start | bytes 294920 | tf_op jit(solution)/shard_map/ppermute | solution.py:77
  137.8 3.4 %collective-permute-done.25 = bf16[2,192,128]{2,1,0:T(8,128)(2,1)S(1)} collective-permute-done((bf16[2,192,128]{2,1,0:T(8,128)(2,1)S(1)}, bf16[2,192,128]{2,1,0:T(8,128)(2,1)S(1)}, u32[]{:S(2)}, u32[]{:S(2)}) %collective-permute-start.25) | collective-permute-done | bytes 98336 | tf_op jit(solution)/shard_map/ppermute | solution.py:77
  (85 shorter events, 32.3 us)
Async XLA Ops:
  0.0 80.1 %copy-start = (bf16[2,768,768]{2,1,0:T(8,128)(2,1)S(1)}, bf16[2,768,768]{2,1,0:T(8,128)(2,1)}, u32[]{:S(2)}) copy-start(bf16[2,768,768]{2,1,0:T(8,128)(2,1)} %param.3) | copy-start | bytes 7077892
  0.0 27.1 %all-to-all-start = ((bf16[32,24,768]{2,1,0:T(8,128)(2,1)}), bf16[32,24,768]{2,1,0:T(8,128)(2,1)S(1)}, u32[]{:S(2)}, u32[]{:S(2)}) async-start(bf16[32,24,768]{2,1,0:T(8,128)(2,1)} %bitcast.367), calls=%async_computation | async-start | bytes 2359296 | tf_op jit(solution)/shard_map/all_to_all | solution.py:53
  28.3 6.9 %collective-permute-start.1 = (bf16[4,24,768]{2,1,0:T(8,128)(2,1)}, bf16[4,24,768]{2,1,0:T(8,128)(2,1)S(1)}, u32[]{:S(2)}, u32[]{:S(2)}) collective-permute-start(bf16[4,24,768]{2,1,0:T(8,128)(2,1)} %gather_fusion), channel_id=1, source_target_pairs={{0,16},{4,68},{8,24},{12,76},{16,0},{20,84},{24,8},{28,92},{32,48}... | collective-permute-start | bytes 442376 | tf_op jit(solution)/shard_map/ppermute | solution.py:38
  29.6 5.6 %collective-permute-start = (bf16[4,24,768]{2,1,0:T(8,128)(2,1)}, bf16[4,24,768]{2,1,0:T(8,128)(2,1)S(1)}, u32[]{:S(2)}, u32[]{:S(2)}) collective-permute-start(bf16[4,24,768]{2,1,0:T(8,128)(2,1)} %gather_fusion), channel_id=1, source_target_pairs={{0,24},{4,100},{8,0},{12,108},{16,8},{20,116},{24,16},{28,124},{32... | collective-permute-start | bytes 442376 | tf_op jit(solution)/shard_map/ppermute | solution.py:36
  31.5 6.6 %collective-permute-start.2 = (bf16[4,24,768]{2,1,0:T(8,128)(2,1)}, bf16[4,24,768]{2,1,0:T(8,128)(2,1)S(1)}, u32[]{:S(2)}, u32[]{:S(2)}) collective-permute-start(bf16[4,24,768]{2,1,0:T(8,128)(2,1)} %gather_fusion), channel_id=1, source_target_pairs={{0,8},{4,36},{8,16},{12,44},{16,24},{20,52},{24,0},{28,60},{32,40}... | collective-permute-start | bytes 442376 | tf_op jit(solution)/shard_map/ppermute | solution.py:35
  39.1 10.0 %collective-permute-start.3 = (bf16[4,4,24,768]{3,2,1,0:T(8,128)(2,1)S(1)}, bf16[4,4,24,768]{3,2,1,0:T(8,128)(2,1)S(1)}, u32[]{:S(2)}, u32[]{:S(2)}) collective-permute-start(bf16[4,4,24,768]{3,2,1,0:T(8,128)(2,1)S(1)} %get-tuple-element.98), channel_id=1, source_target_pairs={{0,96},{4,28},{8,104},{12,4},{16,112},{20,12},{24,120},{28,20},{32... | collective-permute-start | bytes 1769480 | tf_op jit(solution)/shard_map/ppermute | solution.py:36
  39.9 11.2 %collective-permute-start.4 = (bf16[4,4,24,768]{3,2,1,0:T(8,128)(2,1)S(1)}, bf16[4,4,24,768]{3,2,1,0:T(8,128)(2,1)S(1)}, u32[]{:S(2)}, u32[]{:S(2)}) collective-permute-start(bf16[4,4,24,768]{3,2,1,0:T(8,128)(2,1)S(1)} %get-tuple-element.98), channel_id=1, source_target_pairs={{0,32},{4,12},{8,40},{12,20},{16,48},{20,28},{24,56},{28,4},{32,64... | collective-permute-start | bytes 1769480 | tf_op jit(solution)/shard_map/ppermute | solution.py:35
  49.0 6.8 %collective-permute-start.6 = (bf16[2,4,24,768]{3,2,1,0:T(8,128)(2,1)S(1)}, bf16[2,4,24,768]{3,2,1,0:T(8,128)(2,1)S(1)}, u32[]{:S(2)}, u32[]{:S(2)}) collective-permute-start(bf16[2,4,24,768]{3,2,1,0:T(8,128)(2,1)S(1)} %slice.129), channel_id=1, source_target_pairs={{0,96},{4,28},{8,104},{12,4},{16,112},{20,12},{24,120},{28,20},{32... | collective-permute-start | bytes 884744 | tf_op jit(solution)/shard_map/ppermute | solution.py:41
  51.2 8.0 %collective-permute-start.5 = (bf16[2,4,24,768]{3,2,1,0:T(8,128)(2,1)S(1)}, bf16[2,4,24,768]{3,2,1,0:T(8,128)(2,1)S(1)}, u32[]{:S(2)}, u32[]{:S(2)}) collective-permute-start(bf16[2,4,24,768]{3,2,1,0:T(8,128)(2,1)S(1)} %slice.128), channel_id=1, source_target_pairs={{0,32},{4,12},{8,40},{12,20},{16,48},{20,28},{24,56},{28,4},{32,64... | collective-permute-start | bytes 884744 | tf_op jit(solution)/shard_map/ppermute | solution.py:40
  60.9 4.9 %collective-permute-start.7 = (bf16[4,4,4,24,768]{4,3,2,1,0:T(8,128)(2,1)}, bf16[4,4,4,24,768]{4,3,2,1,0:T(8,128)(2,1)}, u32[]{:S(2)}, u32[]{:S(2)}) collective-permute-start(bf16[4,4,4,24,768]{4,3,2,1,0:T(8,128)(2,1)} %pad_maximum_fusion.1), channel_id=1, source_target_pairs={{0,4},{4,0},{8,12},{12,8},{16,20},{20,16},{24,28},{28,24},{32,36},... | collective-permute-start | bytes 7077896 | tf_op jit(solution)/shard_map/ppermute | solution.py:58
  76.1 3.6 %slice-start = ((s8[4718592]{0:T(1024)(128)(4,1)}), s8[4194304]{0:T(1024)(128)(4,1)S(1)}, s32[]{:S(2)}) async-start(s8[4718592]{0:T(1024)(128)(4,1)} %bitcast.322), calls=%async_computation.1 | async-start | bytes 8388608
  76.1 3.7 %slice-start.1 = ((s8[4718592]{0:T(1024)(128)(4,1)}), s8[524288]{0:T(1024)(128)(4,1)S(1)}, s32[]{:S(2)}) async-start(s8[4718592]{0:T(1024)(128)(4,1)} %bitcast.322), calls=%async_computation.2 | async-start | bytes 1048576
  91.5 25.1 %collective-permute-start.8 = (bf16[2,192,128]{2,1,0:T(8,128)(2,1)S(1)}, bf16[2,192,128]{2,1,0:T(8,128)(2,1)S(1)}, u32[]{:S(2)}, u32[]{:S(2)}) collective-permute-start(bf16[2,192,128]{2,1,0:T(8,128)(2,1)S(1)} %get-tuple-element.40), channel_id=1, source_target_pairs={{0,1},{1,2},{2,3},{3,0},{4,5},{5,6},{6,7},{7,4},{8,9},{9,10},{10,1... | collective-permute-start | bytes 294920 | tf_op jit(solution)/shard_map/ppermute | solution.py:77
  93.1 23.9 %collective-permute-start.9 = (bf16[2,192,128]{2,1,0:T(8,128)(2,1)S(1)}, bf16[2,192,128]{2,1,0:T(8,128)(2,1)S(1)}, u32[]{:S(2)}, u32[]{:S(2)}) collective-permute-start(bf16[2,192,128]{2,1,0:T(8,128)(2,1)S(1)} %get-tuple-element.41), channel_id=1, source_target_pairs={{0,3},{1,0},{2,1},{3,2},{4,7},{5,4},{6,5},{7,6},{8,11},{9,8},{10,9... | collective-permute-start | bytes 294920 | tf_op jit(solution)/shard_map/ppermute | solution.py:77
  94.8 22.7 %collective-permute-start.10 = (bf16[2,192,128]{2,1,0:T(8,128)(2,1)S(1)}, bf16[2,192,128]{2,1,0:T(8,128)(2,1)S(1)}, u32[]{:S(2)}, u32[]{:S(2)}) collective-permute-start(bf16[2,192,128]{2,1,0:T(8,128)(2,1)S(1)} %get-tuple-element.42), channel_id=1, source_target_pairs={{0,2},{1,3},{2,0},{3,1},{4,6},{5,7},{6,4},{7,5},{8,10},{9,11},{10,... | collective-permute-start | bytes 294920 | tf_op jit(solution)/shard_map/ppermute | solution.py:77
  100.1 20.2 %collective-permute-start.11 = (bf16[2,192,128]{2,1,0:T(8,128)(2,1)S(1)}, bf16[2,192,128]{2,1,0:T(8,128)(2,1)S(1)}, u32[]{:S(2)}, u32[]{:S(2)}) collective-permute-start(bf16[2,192,128]{2,1,0:T(8,128)(2,1)S(1)} %get-tuple-element.47), channel_id=1, source_target_pairs={{0,1},{1,2},{2,3},{3,0},{4,5},{5,6},{6,7},{7,4},{8,9},{9,10},{10,1... | collective-permute-start | bytes 294920 | tf_op jit(solution)/shard_map/ppermute | solution.py:77
  100.8 21.8 %collective-permute-start.12 = (bf16[2,192,128]{2,1,0:T(8,128)(2,1)S(1)}, bf16[2,192,128]{2,1,0:T(8,128)(2,1)S(1)}, u32[]{:S(2)}, u32[]{:S(2)}) collective-permute-start(bf16[2,192,128]{2,1,0:T(8,128)(2,1)S(1)} %get-tuple-element.48), channel_id=1, source_target_pairs={{0,3},{1,0},{2,1},{3,2},{4,7},{5,4},{6,5},{7,6},{8,11},{9,8},{10,9... | collective-permute-start | bytes 294920 | tf_op jit(solution)/shard_map/ppermute | solution.py:77
  116.6 6.3 %collective-permute-start.13 = (bf16[2,192,128]{2,1,0:T(8,128)(2,1)S(1)}, bf16[2,192,128]{2,1,0:T(8,128)(2,1)S(1)}, u32[]{:S(2)}, u32[]{:S(2)}) collective-permute-start(bf16[2,192,128]{2,1,0:T(8,128)(2,1)S(1)} %get-tuple-element.49), channel_id=1, source_target_pairs={{0,2},{1,3},{2,0},{3,1},{4,6},{5,7},{6,4},{7,5},{8,10},{9,11},{10,... | collective-permute-start | bytes 294920 | tf_op jit(solution)/shard_map/ppermute | solution.py:77
  117.0 8.9 %collective-permute-start.14 = (bf16[2,192,128]{2,1,0:T(8,128)(2,1)S(1)}, bf16[2,192,128]{2,1,0:T(8,128)(2,1)S(1)}, u32[]{:S(2)}, u32[]{:S(2)}) collective-permute-start(bf16[2,192,128]{2,1,0:T(8,128)(2,1)S(1)} %get-tuple-element.54), channel_id=1, source_target_pairs={{0,1},{1,2},{2,3},{3,0},{4,5},{5,6},{6,7},{7,4},{8,9},{9,10},{10,1... | collective-permute-start | bytes 294920 | tf_op jit(solution)/shard_map/ppermute | solution.py:77
  117.5 8.8 %collective-permute-start.15 = (bf16[2,192,128]{2,1,0:T(8,128)(2,1)S(1)}, bf16[2,192,128]{2,1,0:T(8,128)(2,1)S(1)}, u32[]{:S(2)}, u32[]{:S(2)}) collective-permute-start(bf16[2,192,128]{2,1,0:T(8,128)(2,1)S(1)} %get-tuple-element.55), channel_id=1, source_target_pairs={{0,3},{1,0},{2,1},{3,2},{4,7},{5,4},{6,5},{7,6},{8,11},{9,8},{10,9... | collective-permute-start | bytes 294920 | tf_op jit(solution)/shard_map/ppermute | solution.py:77
  120.3 6.7 %collective-permute-start.16 = (bf16[2,192,128]{2,1,0:T(8,128)(2,1)S(1)}, bf16[2,192,128]{2,1,0:T(8,128)(2,1)S(1)}, u32[]{:S(2)}, u32[]{:S(2)}) collective-permute-start(bf16[2,192,128]{2,1,0:T(8,128)(2,1)S(1)} %get-tuple-element.56), channel_id=1, source_target_pairs={{0,2},{1,3},{2,0},{3,1},{4,6},{5,7},{6,4},{7,5},{8,10},{9,11},{10,... | collective-permute-start | bytes 294920 | tf_op jit(solution)/shard_map/ppermute | solution.py:77
  122.6 7.6 %collective-permute-start.17 = (bf16[2,192,128]{2,1,0:T(8,128)(2,1)S(1)}, bf16[2,192,128]{2,1,0:T(8,128)(2,1)S(1)}, u32[]{:S(2)}, u32[]{:S(2)}) collective-permute-start(bf16[2,192,128]{2,1,0:T(8,128)(2,1)S(1)} %get-tuple-element.61), channel_id=1, source_target_pairs={{0,1},{1,2},{2,3},{3,0},{4,5},{5,6},{6,7},{7,4},{8,9},{9,10},{10,1... | collective-permute-start | bytes 294920 | tf_op jit(solution)/shard_map/ppermute | solution.py:77
  122.9 8.8 %collective-permute-start.18 = (bf16[2,192,128]{2,1,0:T(8,128)(2,1)S(1)}, bf16[2,192,128]{2,1,0:T(8,128)(2,1)S(1)}, u32[]{:S(2)}, u32[]{:S(2)}) collective-permute-start(bf16[2,192,128]{2,1,0:T(8,128)(2,1)S(1)} %get-tuple-element.62), channel_id=1, source_target_pairs={{0,3},{1,0},{2,1},{3,2},{4,7},{5,4},{6,5},{7,6},{8,11},{9,8},{10,9... | collective-permute-start | bytes 294920 | tf_op jit(solution)/shard_map/ppermute | solution.py:77
  125.9 7.2 %collective-permute-start.19 = (bf16[2,192,128]{2,1,0:T(8,128)(2,1)S(1)}, bf16[2,192,128]{2,1,0:T(8,128)(2,1)S(1)}, u32[]{:S(2)}, u32[]{:S(2)}) collective-permute-start(bf16[2,192,128]{2,1,0:T(8,128)(2,1)S(1)} %get-tuple-element.63), channel_id=1, source_target_pairs={{0,2},{1,3},{2,0},{3,1},{4,6},{5,7},{6,4},{7,5},{8,10},{9,11},{10,... | collective-permute-start | bytes 294920 | tf_op jit(solution)/shard_map/ppermute | solution.py:77
  126.4 8.7 %collective-permute-start.20 = (bf16[2,192,128]{2,1,0:T(8,128)(2,1)S(1)}, bf16[2,192,128]{2,1,0:T(8,128)(2,1)S(1)}, u32[]{:S(2)}, u32[]{:S(2)}) collective-permute-start(bf16[2,192,128]{2,1,0:T(8,128)(2,1)S(1)} %get-tuple-element.68), channel_id=1, source_target_pairs={{0,1},{1,2},{2,3},{3,0},{4,5},{5,6},{6,7},{7,4},{8,9},{9,10},{10,1... | collective-permute-start | bytes 294920 | tf_op jit(solution)/shard_map/ppermute | solution.py:77
  127.0 9.1 %collective-permute-start.21 = (bf16[2,192,128]{2,1,0:T(8,128)(2,1)S(1)}, bf16[2,192,128]{2,1,0:T(8,128)(2,1)S(1)}, u32[]{:S(2)}, u32[]{:S(2)}) collective-permute-start(bf16[2,192,128]{2,1,0:T(8,128)(2,1)S(1)} %get-tuple-element.69), channel_id=1, source_target_pairs={{0,3},{1,0},{2,1},{3,2},{4,7},{5,4},{6,5},{7,6},{8,11},{9,8},{10,9... | collective-permute-start | bytes 294920 | tf_op jit(solution)/shard_map/ppermute | solution.py:77
  130.2 6.5 %collective-permute-start.22 = (bf16[2,192,128]{2,1,0:T(8,128)(2,1)S(1)}, bf16[2,192,128]{2,1,0:T(8,128)(2,1)S(1)}, u32[]{:S(2)}, u32[]{:S(2)}) collective-permute-start(bf16[2,192,128]{2,1,0:T(8,128)(2,1)S(1)} %get-tuple-element.70), channel_id=1, source_target_pairs={{0,2},{1,3},{2,0},{3,1},{4,6},{5,7},{6,4},{7,5},{8,10},{9,11},{10,... | collective-permute-start | bytes 294920 | tf_op jit(solution)/shard_map/ppermute | solution.py:77
  131.8 6.0 %collective-permute-start.23 = (bf16[2,192,128]{2,1,0:T(8,128)(2,1)S(1)}, bf16[2,192,128]{2,1,0:T(8,128)(2,1)S(1)}, u32[]{:S(2)}, u32[]{:S(2)}) collective-permute-start(bf16[2,192,128]{2,1,0:T(8,128)(2,1)S(1)} %get-tuple-element.79), channel_id=1, source_target_pairs={{0,1},{1,2},{2,3},{3,0},{4,5},{5,6},{6,7},{7,4},{8,9},{9,10},{10,1... | collective-permute-start | bytes 294920 | tf_op jit(solution)/shard_map/ppermute | solution.py:77
  133.2 4.6 %collective-permute-start.24 = (bf16[2,192,128]{2,1,0:T(8,128)(2,1)S(1)}, bf16[2,192,128]{2,1,0:T(8,128)(2,1)S(1)}, u32[]{:S(2)}, u32[]{:S(2)}) collective-permute-start(bf16[2,192,128]{2,1,0:T(8,128)(2,1)S(1)} %get-tuple-element.80), channel_id=1, source_target_pairs={{0,3},{1,0},{2,1},{3,2},{4,7},{5,4},{6,5},{7,6},{8,11},{9,8},{10,9... | collective-permute-start | bytes 294920 | tf_op jit(solution)/shard_map/ppermute | solution.py:77
  135.1 6.2 %collective-permute-start.25 = (bf16[2,192,128]{2,1,0:T(8,128)(2,1)S(1)}, bf16[2,192,128]{2,1,0:T(8,128)(2,1)S(1)}, u32[]{:S(2)}, u32[]{:S(2)}) collective-permute-start(bf16[2,192,128]{2,1,0:T(8,128)(2,1)S(1)} %get-tuple-element.81), channel_id=1, source_target_pairs={{0,2},{1,3},{2,0},{3,1},{4,6},{5,7},{6,4},{7,5},{8,10},{9,11},{10,... | collective-permute-start | bytes 294920 | tf_op jit(solution)/shard_map/ppermute | solution.py:77
  136.8 4.5 %copy-start.1 = (f32[2,192,768]{2,1,0:T(8,128)}, f32[2,192,768]{2,1,0:T(8,128)S(1)}, u32[]{:S(2)}) copy-start(f32[2,192,768]{2,1,0:T(8,128)S(1)} %fusion.9) | copy-start | bytes 3538948

commit v14 on v13

--- a/solution.py
+++ b/solution.py
@@ -9,7 +9,7 @@
 
 
 RING = 4
-CHUNKS = 6
+CHUNKS = 3
 
 
 def ring_axis(stage, core):
@@ -85,17 +85,19 @@
     def pick(offset):
         return lax.dynamic_index_in_dim(blocks, (vgrp + offset) % groups, 1, keepdims=False)
 
-    owed = tuple(pick(offset).astype(jnp.bfloat16) for offset in (1, -1, 2))
-    return pick(0), owed
+    return pick(0), (pick(1), pick(-1), pick(2).astype(jnp.bfloat16))
 
 
 def exchange(own, owed, groups):
     ahead, behind, far = owed
-    ahead = shifted(ahead, 1, groups)
-    behind = shifted(behind, -1, groups)
-    far = shifted(far, 2, groups)
-    near = ahead.astype(jnp.float32) + behind.astype(jnp.float32)
-    return own + near + far.astype(jnp.float32)
+    half = far.shape[1] // 2
+    far_up = shifted(far[:, :half], 1, groups)
+    far_down = shifted(far[:, half:], -1, groups)
+    ahead = jnp.concatenate([ahead[:, :half] + far_up.astype(jnp.float32), ahead[:, half:]], axis=1)
+    behind = jnp.concatenate([behind[:, :half], behind[:, half:] + far_down.astype(jnp.float32)], axis=1)
+    ahead = shifted(ahead.astype(jnp.bfloat16), 1, groups)
+    behind = shifted(behind.astype(jnp.bfloat16), -1, groups)
+    return own + ahead.astype(jnp.float32) + behind.astype(jnp.float32)
 
 
 def columns(halves, vectors, lo, hi):

time: 142 us -> 126 us (0.89)
  the two profiles are of different devices: /device:TPU:0 before, /device:TPU:1 now
where the time goes in v14:
time: 126 us; the launch traced here: 125 us
  waiting for transfers between devices  50.9 us (40%)
  starting transfers between devices  34.5 us (27%)
  matrix products  18.1 us (14%)
  local copies, waits for them, and re-layouts  11.1 us (9%)
  other arithmetic  9.98 us (8%)
    all_to_all x1, waiting for transfers between devices, gather_slots(): pieces = lax.all_to_all(pieces, PAIR, 0, 0, tiled=True)  17.8 us
    ppermute x12, starting transfers between devices, shifted(): lax.ppermute(value, 'vgrp', [(g, (g + step) % groups) for g in range(grou...  14.2 us
    dot_general x12, matrix products, columns(): jnp.einsum('pad,bd->pab', half_product, vectors[slot, lo:hi], preferred_e...  10.1 us
    all_to_all x1, starting transfers between devices, gather_slots(): pieces = lax.all_to_all(pieces, PAIR, 0, 0, tiled=True)  9.55 us
    ppermute x12, waiting for transfers between devices, shifted(): lax.ppermute(value, 'vgrp', [(g, (g + step) % groups) for g in range(grou...  9.25 us
    dot_general x4, matrix products, on_device(): jnp.einsum('ac,pcd->pad', vectors[slot], amplitudes, preferred_element_ty...  8.01 us
    ppermute x2, waiting for transfers between devices, ring_gather(): from_next = lax.ppermute(piece, PAIR, ring_perm(sizes, stage, -1))  7.2 us
    gather x1, local copies, waits for them, and re-layouts, gather_slots(): ordered = stacked.at[index].get(mode='promise_in_bounds')  5.38 us
  transfers between devices with their start and end apart: 21, of which 11 were waited for; matrix products, arithmetic and copies ran while one was open for 4% of the time, Pallas kernels for 0%

profile of v14, /device:TPU:1, one launch (start us, length us, event | category | flops | bytes accessed | tf_op | source)
XLA Modules:
  0.0 125.0 jit_solution(7131946763782808373)
XLA Ops:
  0.0 9.6 %all-to-all-start = ((bf16[32,24,768]{2,1,0:T(8,128)(2,1)}), bf16[32,24,768]{2,1,0:T(8,128)(2,1)S(1)}, u32[]{:S(2)}, u32[]{:S(2)}) async-start(bf16[32,24,768]{2,1,0:T(8,128)(2,1)} %bitcast.187), calls=%async_computation | async-start | bytes 2359296 | tf_op jit(solution)/shard_map/all_to_all | solution.py:53
  10.3 17.8 %all-to-all-done = bf16[32,24,768]{2,1,0:T(8,128)(2,1)S(1)} async-done(((bf16[32,24,768]{2,1,0:T(8,128)(2,1)}), bf16[32,24,768]{2,1,0:T(8,128)(2,1)S(1)}, u32[]{:S(2)}, u32[]{:S(2)}) %all-to-all-start) | async-done | bytes 1179680 | tf_op jit(solution)/shard_map/all_to_all | solution.py:53
  28.1 1.2 gather_fusion
  30.4 1.2 collective-permute-start
  31.8 3.5 %collective-permute-done.1 = bf16[4,24,768]{2,1,0:T(8,128)(2,1)S(1)} collective-permute-done((bf16[4,24,768]{2,1,0:T(8,128)(2,1)}, bf16[4,24,768]{2,1,0:T(8,128)(2,1)S(1)}, u32[]{:S(2)}, u32[]{:S(2)}) %collective-permute-start.1) | collective-permute-done | bytes 147488 | tf_op jit(solution)/shard_map/ppermute | solution.py:38
  35.3 1.6 %collective-permute-done.2 = bf16[4,24,768]{2,1,0:T(8,128)(2,1)S(1)} collective-permute-done((bf16[4,24,768]{2,1,0:T(8,128)(2,1)}, bf16[4,24,768]{2,1,0:T(8,128)(2,1)S(1)}, u32[]{:S(2)}, u32[]{:S(2)}) %collective-permute-start.2) | collective-permute-done | bytes 147488 | tf_op jit(solution)/shard_map/ppermute | solution.py:35
  38.0 1.9 %collective-permute-start.3 = (bf16[4,4,24,768]{3,2,1,0:T(8,128)(2,1)S(1)}, bf16[4,4,24,768]{3,2,1,0:T(8,128)(2,1)S(1)}, u32[]{:S(2)}, u32[]{:S(2)}) collective-permute-start(bf16[4,4,24,768]{3,2,1,0:T(8,128)(2,1)S(1)} %get-tuple-element.44), channel_id=1, source_target_pairs={{0,96},{4,28},{8,104},{12,4},{16,112},{20,12},{24,120},{28,20},{32... | collective-permute-start | bytes 1769480 | tf_op jit(solution)/shard_map/ppermute | solution.py:36
  39.9 7.2 %collective-permute-done.3 = bf16[4,4,24,768]{3,2,1,0:T(8,128)(2,1)S(1)} collective-permute-done((bf16[4,4,24,768]{3,2,1,0:T(8,128)(2,1)S(1)}, bf16[4,4,24,768]{3,2,1,0:T(8,128)(2,1)S(1)}, u32[]{:S(2)}, u32[]{:S(2)}) %collective-permute-start.3) | collective-permute-done | bytes 589856 | tf_op jit(solution)/shard_map/ppermute | solution.py:36
  47.1 3.1 %collective-permute-start.6 = (bf16[2,4,24,768]{3,2,1,0:T(8,128)(2,1)S(1)}, bf16[2,4,24,768]{3,2,1,0:T(8,128)(2,1)S(1)}, u32[]{:S(2)}, u32[]{:S(2)}) collective-permute-start(bf16[2,4,24,768]{3,2,1,0:T(8,128)(2,1)S(1)} %slice.159), channel_id=1, source_target_pairs={{0,96},{4,28},{8,104},{12,4},{16,112},{20,12},{24,120},{28,20},{32... | collective-permute-start | bytes 884744 | tf_op jit(solution)/shard_map/ppermute | solution.py:41
  50.3 3.6 %collective-permute-done.6 = bf16[2,4,24,768]{3,2,1,0:T(8,128)(2,1)S(1)} collective-permute-done((bf16[2,4,24,768]{3,2,1,0:T(8,128)(2,1)S(1)}, bf16[2,4,24,768]{3,2,1,0:T(8,128)(2,1)S(1)}, u32[]{:S(2)}, u32[]{:S(2)}) %collective-permute-start.6) | collective-permute-done | bytes 294944 | tf_op jit(solution)/shard_map/ppermute | solution.py:41
  53.8 3.5 %collective-permute-done.5 = bf16[2,4,24,768]{3,2,1,0:T(8,128)(2,1)S(1)} collective-permute-done((bf16[2,4,24,768]{3,2,1,0:T(8,128)(2,1)S(1)}, bf16[2,4,24,768]{3,2,1,0:T(8,128)(2,1)S(1)}, u32[]{:S(2)}, u32[]{:S(2)}) %collective-permute-start.5) | collective-permute-done | bytes 294944 | tf_op jit(solution)/shard_map/ppermute | solution.py:40
  57.4 1.7 %pad_maximum_fusion.1 = bf16[4,4,4,24,768]{4,3,2,1,0:T(8,128)(2,1)} fusion(bf16[1,4,4,24,768]{4,3,2,1,0:T(8,128)(2,1)S(1)} %bitcast.182, bf16[1,4,4,24,768]{4,3,2,1,0:T(8,128)(2,1)S(1)} %maximum_bitcast_fusion, bf16[1,4,4,24,768]{4,3,2,1,0:T(8,128)(2,1)S(1)} %bitcast.181, bf16[1,4,4,24,768]{4,3,2,1,0:T(8,128)(2,1)S(1)} %get-tuple-element.43), kind=kLoop, calls=%fused_computation.3 | loop fusion | flops 3538944 | bytes 4718592 | tf_op jit(solution)/shard_map/stack | solution.py:43
  59.2 3.2 %collective-permute-start.7 = (bf16[4,4,4,24,768]{4,3,2,1,0:T(8,128)(2,1)}, bf16[4,4,4,24,768]{4,3,2,1,0:T(8,128)(2,1)}, u32[]{:S(2)}, u32[]{:S(2)}) collective-permute-start(bf16[4,4,4,24,768]{4,3,2,1,0:T(8,128)(2,1)} %pad_maximum_fusion.1), channel_id=1, source_target_pairs={{0,4},{4,0},{8,12},{12,8},{16,20},{20,16},{24,28},{28,24},{32,36},... | collective-permute-start | bytes 7077896 | tf_op jit(solution)/shard_map/ppermute | solution.py:58
  62.4 4.5 %collective-permute-done.7 = bf16[4,4,4,24,768]{4,3,2,1,0:T(8,128)(2,1)} collective-permute-done((bf16[4,4,4,24,768]{4,3,2,1,0:T(8,128)(2,1)}, bf16[4,4,4,24,768]{4,3,2,1,0:T(8,128)(2,1)}, u32[]{:S(2)}, u32[]{:S(2)}) %collective-permute-start.7) | collective-permute-done | bytes 2359328 | tf_op jit(solution)/shard_map/ppermute | solution.py:58
  66.8 4.9 %pad_maximum_fusion = bf16[32,4,24,768]{3,2,1,0:T(8,128)(2,1)} fusion(bf16[16,4,24,768]{3,2,1,0:T(8,128)(2,1)} %bitcast.12, bf16[16,4,24,768]{3,2,1,0:T(8,128)(2,1)} %bitcast.11), kind=kLoop, calls=%fused_computation.2 | loop fusion | flops 2359296 | bytes 9437184 | tf_op jit(solution)/shard_map/concatenate | solution.py:60
  71.8 5.4 %gather_fusion.1 = bf16[32,4,24,768]{3,2,1,0:T(8,128)(2,1)} fusion(bf16[32,4,24,768]{3,2,1,0:T(8,128)(2,1)} %pad_maximum_fusion, s32[1024]{0:T(1024)S(1)} %pad_clamp_fusion), kind=kCustom, calls=%fused_computation.1 | custom fusion | bytes 9437312 | tf_op jit(solution)/shard_map/gather | solution.py:71
  77.1 2.8 %copy.7 = bf16[4,32,24,768]{3,2,1,0:T(8,128)(2,1)S(1)} copy(bf16[4,32,24,768]{3,2,0,1:T(8,128)(2,1)} %bitcast.156) | data formatting | bytes 9437184 | tf_op jit(solution)/shard_map/transpose | solution.py:72
  81.2 2.0 %convert_bitcast_fusion.1 = bf16[2,768,768]{2,1,0:T(8,128)(2,1)S(1)} fusion(bf16[768,768,1]{1,0,2:T(8,128)(2,1)S(1)} %bitcast.186, bf16[2,768,768]{2,1,0:T(8,128)(2,1)S(1)} %copy-done), kind=kOutput, calls=%fused_computation.5 | convolution fusion | flops 1813118976 | bytes 5898240 | tf_op jit(solution)/shard_map/ac,pcd->pad/dot_general | solution.py:119
  83.2 2.0 %convert_bitcast_fusion = bf16[2,768,768]{2,1,0:T(8,128)(2,1)S(1)} fusion(bf16[768,768,1]{1,0,2:T(8,128)(2,1)S(1)} %bitcast.185, bf16[2,768,768]{2,1,0:T(8,128)(2,1)S(1)} %copy-done), kind=kOutput, calls=%fused_computation.4 | convolution fusion | flops 1813118976 | bytes 5898240 | tf_op jit(solution)/shard_map/ac,pcd->pad/dot_general | solution.py:119
  85.2 2.0 %convert_bitcast_fusion.2 = bf16[2,768,768]{2,1,0:T(8,128)(2,1)S(1)} fusion(bf16[768,768,1]{1,0,2:T(8,128)(2,1)S(1)} %bitcast.184, bf16[2,768,768]{2,1,0:T(8,128)(2,1)S(1)} %copy-done), kind=kOutput, calls=%fused_computation.6 | convolution fusion | flops 1813118976 | bytes 5898240 | tf_op jit(solution)/shard_map/ac,pcd->pad/dot_general | solution.py:119
  87.2 2.0 %convert_bitcast_fusion.3 = bf16[2,768,768]{2,1,0:T(8,128)(2,1)S(1)} fusion(bf16[768,768,1]{1,0,2:T(8,128)(2,1)S(1)} %bitcast.183, bf16[2,768,768]{2,1,0:T(8,128)(2,1)S(1)} %copy-done), kind=kOutput, calls=%fused_computation.7 | convolution fusion | flops 1813118976 | bytes 5898240 | tf_op jit(solution)/shard_map/ac,pcd->pad/dot_general | solution.py:119
  96.4 1.4 %collective-permute-start.8 = (bf16[2,96,256]{2,1,0:T(8,128)(2,1)S(1)}, bf16[2,96,256]{2,1,0:T(8,128)(2,1)S(1)}, u32[]{:S(2)}, u32[]{:S(2)}) collective-permute-start(bf16[2,96,256]{2,1,0:T(8,128)(2,1)S(1)} %get-tuple-element.45), channel_id=1, source_target_pairs={{0,1},{1,2},{2,3},{3,0},{4,5},{5,6},{6,7},{7,4},{8,9},{9,10},{10,1... | collective-permute-start | bytes 294920 | tf_op jit(solution)/shard_map/ppermute | solution.py:77
  97.7 1.5 %collective-permute-start.10 = (bf16[2,96,256]{2,1,0:T(8,128)(2,1)S(1)}, bf16[2,96,256]{2,1,0:T(8,128)(2,1)S(1)}, u32[]{:S(2)}, u32[]{:S(2)}) collective-permute-start(bf16[2,96,256]{2,1,0:T(8,128)(2,1)S(1)} %get-tuple-element.46), channel_id=1, source_target_pairs={{0,3},{1,0},{2,1},{3,2},{4,7},{5,4},{6,5},{7,6},{8,11},{9,8},{10,9... | collective-permute-start | bytes 294920 | tf_op jit(solution)/shard_map/ppermute | solution.py:77
  99.4 2.7 %collective-permute-start.14 = (bf16[2,96,256]{2,1,0:T(8,128)(2,1)S(1)}, bf16[2,96,256]{2,1,0:T(8,128)(2,1)S(1)}, u32[]{:S(2)}, u32[]{:S(2)}) collective-permute-start(bf16[2,96,256]{2,1,0:T(8,128)(2,1)S(1)} %get-tuple-element.48), channel_id=1, source_target_pairs={{0,3},{1,0},{2,1},{3,2},{4,7},{5,4},{6,5},{7,6},{8,11},{9,8},{10,9... | collective-permute-start | bytes 294920 | tf_op jit(solution)/shard_map/ppermute | solution.py:77
  105.6 2.7 %collective-permute-start.18 = (bf16[2,96,256]{2,1,0:T(8,128)(2,1)S(1)}, bf16[2,96,256]{2,1,0:T(8,128)(2,1)S(1)}, u32[]{:S(2)}, u32[]{:S(2)}) collective-permute-start(bf16[2,96,256]{2,1,0:T(8,128)(2,1)S(1)} %get-tuple-element.50), channel_id=1, source_target_pairs={{0,3},{1,0},{2,1},{3,2},{4,7},{5,4},{6,5},{7,6},{8,11},{9,8},{10,9... | collective-permute-start | bytes 294920 | tf_op jit(solution)/shard_map/ppermute | solution.py:77
  108.5 1.5 %collective-permute-start.9 = (bf16[2,192,256]{2,1,0:T(8,128)(2,1)S(1)}, bf16[2,192,256]{2,1,0:T(8,128)(2,1)S(1)}, u32[]{:S(2)}, u32[]{:S(2)}) collective-permute-start(bf16[2,192,256]{2,1,0:T(8,128)(2,1)S(1)} %pad_maximum_fusion.4), channel_id=1, source_target_pairs={{0,1},{1,2},{2,3},{3,0},{4,5},{5,6},{6,7},{7,4},{8,9},{9,10},{10,1... | collective-permute-start | bytes 589832 | tf_op jit(solution)/shard_map/ppermute | solution.py:77
  110.1 1.3 %collective-permute-start.15 = (bf16[2,192,256]{2,1,0:T(8,128)(2,1)S(1)}, bf16[2,192,256]{2,1,0:T(8,128)(2,1)S(1)}, u32[]{:S(2)}, u32[]{:S(2)}) collective-permute-start(bf16[2,192,256]{2,1,0:T(8,128)(2,1)S(1)} %pad_maximum_fusion.7), channel_id=1, source_target_pairs={{0,3},{1,0},{2,1},{3,2},{4,7},{5,4},{6,5},{7,6},{8,11},{9,8},{10,9... | collective-permute-start | bytes 589832 | tf_op jit(solution)/shard_map/ppermute | solution.py:77
  111.8 2.5 %collective-permute-start.19 = (bf16[2,192,256]{2,1,0:T(8,128)(2,1)S(1)}, bf16[2,192,256]{2,1,0:T(8,128)(2,1)S(1)}, u32[]{:S(2)}, u32[]{:S(2)}) collective-permute-start(bf16[2,192,256]{2,1,0:T(8,128)(2,1)S(1)} %pad_maximum_fusion.9), channel_id=1, source_target_pairs={{0,3},{1,0},{2,1},{3,2},{4,7},{5,4},{6,5},{7,6},{8,11},{9,8},{10,9... | collective-permute-start | bytes 589832 | tf_op jit(solution)/shard_map/ppermute | solution.py:77
  114.6 2.8 %collective-permute-done.15 = bf16[2,192,256]{2,1,0:T(8,128)(2,1)S(1)} collective-permute-done((bf16[2,192,256]{2,1,0:T(8,128)(2,1)S(1)}, bf16[2,192,256]{2,1,0:T(8,128)(2,1)S(1)}, u32[]{:S(2)}, u32[]{:S(2)}) %collective-permute-start.15) | collective-permute-done | bytes 196640 | tf_op jit(solution)/shard_map/ppermute | solution.py:77
  117.4 2.3 %collective-permute-done.13 = bf16[2,192,256]{2,1,0:T(8,128)(2,1)S(1)} collective-permute-done((bf16[2,192,256]{2,1,0:T(8,128)(2,1)S(1)}, bf16[2,192,256]{2,1,0:T(8,128)(2,1)S(1)}, u32[]{:S(2)}, u32[]{:S(2)}) %collective-permute-start.13) | collective-permute-done | bytes 196640 | tf_op jit(solution)/shard_map/ppermute | solution.py:77
  119.7 1.9 %collective-permute-done.19 = bf16[2,192,256]{2,1,0:T(8,128)(2,1)S(1)} collective-permute-done((bf16[2,192,256]{2,1,0:T(8,128)(2,1)S(1)}, bf16[2,192,256]{2,1,0:T(8,128)(2,1)S(1)}, u32[]{:S(2)}, u32[]{:S(2)}) %collective-permute-start.19) | collective-permute-done | bytes 196640 | tf_op jit(solution)/shard_map/ppermute | solution.py:77
  121.6 2.3 %collective-permute-done.17 = bf16[2,192,256]{2,1,0:T(8,128)(2,1)S(1)} collective-permute-done((bf16[2,192,256]{2,1,0:T(8,128)(2,1)S(1)}, bf16[2,192,256]{2,1,0:T(8,128)(2,1)S(1)}, u32[]{:S(2)}, u32[]{:S(2)}) %collective-permute-start.17) | collective-permute-done | bytes 196640 | tf_op jit(solution)/shard_map/ppermute | solution.py:77
  (80 shorter events, 17.1 us)
Async XLA Ops:
  0.0 81.2 %copy-start = (bf16[2,768,768]{2,1,0:T(8,128)(2,1)S(1)}, bf16[2,768,768]{2,1,0:T(8,128)(2,1)}, u32[]{:S(2)}) copy-start(bf16[2,768,768]{2,1,0:T(8,128)(2,1)} %param.3) | copy-start | bytes 7077892
  0.0 28.1 %all-to-all-start = ((bf16[32,24,768]{2,1,0:T(8,128)(2,1)}), bf16[32,24,768]{2,1,0:T(8,128)(2,1)S(1)}, u32[]{:S(2)}, u32[]{:S(2)}) async-start(bf16[32,24,768]{2,1,0:T(8,128)(2,1)} %bitcast.187), calls=%async_computation | async-start | bytes 2359296 | tf_op jit(solution)/shard_map/all_to_all | solution.py:53
  29.3 6.0 %collective-permute-start.1 = (bf16[4,24,768]{2,1,0:T(8,128)(2,1)}, bf16[4,24,768]{2,1,0:T(8,128)(2,1)S(1)}, u32[]{:S(2)}, u32[]{:S(2)}) collective-permute-start(bf16[4,24,768]{2,1,0:T(8,128)(2,1)} %gather_fusion), channel_id=1, source_target_pairs={{0,16},{4,68},{8,24},{12,76},{16,0},{20,84},{24,8},{28,92},{32,48}... | collective-permute-start | bytes 442376 | tf_op jit(solution)/shard_map/ppermute | solution.py:38
  30.4 4.9 %collective-permute-start = (bf16[4,24,768]{2,1,0:T(8,128)(2,1)}, bf16[4,24,768]{2,1,0:T(8,128)(2,1)S(1)}, u32[]{:S(2)}, u32[]{:S(2)}) collective-permute-start(bf16[4,24,768]{2,1,0:T(8,128)(2,1)} %gather_fusion), channel_id=1, source_target_pairs={{0,24},{4,100},{8,0},{12,108},{16,8},{20,116},{24,16},{28,124},{32... | collective-permute-start | bytes 442376 | tf_op jit(solution)/shard_map/ppermute | solution.py:36
  31.5 5.4 %collective-permute-start.2 = (bf16[4,24,768]{2,1,0:T(8,128)(2,1)}, bf16[4,24,768]{2,1,0:T(8,128)(2,1)S(1)}, u32[]{:S(2)}, u32[]{:S(2)}) collective-permute-start(bf16[4,24,768]{2,1,0:T(8,128)(2,1)} %gather_fusion), channel_id=1, source_target_pairs={{0,8},{4,36},{8,16},{12,44},{16,24},{20,52},{24,0},{28,60},{32,40}... | collective-permute-start | bytes 442376 | tf_op jit(solution)/shard_map/ppermute | solution.py:35
  38.0 9.1 %collective-permute-start.3 = (bf16[4,4,24,768]{3,2,1,0:T(8,128)(2,1)S(1)}, bf16[4,4,24,768]{3,2,1,0:T(8,128)(2,1)S(1)}, u32[]{:S(2)}, u32[]{:S(2)}) collective-permute-start(bf16[4,4,24,768]{3,2,1,0:T(8,128)(2,1)S(1)} %get-tuple-element.44), channel_id=1, source_target_pairs={{0,96},{4,28},{8,104},{12,4},{16,112},{20,12},{24,120},{28,20},{32... | collective-permute-start | bytes 1769480 | tf_op jit(solution)/shard_map/ppermute | solution.py:36
  39.8 10.3 %collective-permute-start.4 = (bf16[4,4,24,768]{3,2,1,0:T(8,128)(2,1)S(1)}, bf16[4,4,24,768]{3,2,1,0:T(8,128)(2,1)S(1)}, u32[]{:S(2)}, u32[]{:S(2)}) collective-permute-start(bf16[4,4,24,768]{3,2,1,0:T(8,128)(2,1)S(1)} %get-tuple-element.44), channel_id=1, source_target_pairs={{0,32},{4,12},{8,40},{12,20},{16,48},{20,28},{24,56},{28,4},{32,64... | collective-permute-start | bytes 1769480 | tf_op jit(solution)/shard_map/ppermute | solution.py:35
  47.1 6.8 %collective-permute-start.6 = (bf16[2,4,24,768]{3,2,1,0:T(8,128)(2,1)S(1)}, bf16[2,4,24,768]{3,2,1,0:T(8,128)(2,1)S(1)}, u32[]{:S(2)}, u32[]{:S(2)}) collective-permute-start(bf16[2,4,24,768]{3,2,1,0:T(8,128)(2,1)S(1)} %slice.159), channel_id=1, source_target_pairs={{0,96},{4,28},{8,104},{12,4},{16,112},{20,12},{24,120},{28,20},{32... | collective-permute-start | bytes 884744 | tf_op jit(solution)/shard_map/ppermute | solution.py:41
  50.2 7.1 %collective-permute-start.5 = (bf16[2,4,24,768]{3,2,1,0:T(8,128)(2,1)S(1)}, bf16[2,4,24,768]{3,2,1,0:T(8,128)(2,1)S(1)}, u32[]{:S(2)}, u32[]{:S(2)}) collective-permute-start(bf16[2,4,24,768]{3,2,1,0:T(8,128)(2,1)S(1)} %slice.158), channel_id=1, source_target_pairs={{0,32},{4,12},{8,40},{12,20},{16,48},{20,28},{24,56},{28,4},{32,64... | collective-permute-start | bytes 884744 | tf_op jit(solution)/shard_map/ppermute | solution.py:40
  59.2 7.7 %collective-permute-start.7 = (bf16[4,4,4,24,768]{4,3,2,1,0:T(8,128)(2,1)}, bf16[4,4,4,24,768]{4,3,2,1,0:T(8,128)(2,1)}, u32[]{:S(2)}, u32[]{:S(2)}) collective-permute-start(bf16[4,4,4,24,768]{4,3,2,1,0:T(8,128)(2,1)} %pad_maximum_fusion.1), channel_id=1, source_target_pairs={{0,4},{4,0},{8,12},{12,8},{16,20},{20,16},{24,28},{28,24},{32,36},... | collective-permute-start | bytes 7077896 | tf_op jit(solution)/shard_map/ppermute | solution.py:58
  77.1 3.6 %slice-start = ((s8[4718592]{0:T(1024)(128)(4,1)}), s8[4194304]{0:T(1024)(128)(4,1)S(1)}, s32[]{:S(2)}) async-start(s8[4718592]{0:T(1024)(128)(4,1)} %bitcast.157), calls=%async_computation.1 | async-start | bytes 8388608
  77.1 3.7 %slice-start.1 = ((s8[4718592]{0:T(1024)(128)(4,1)}), s8[524288]{0:T(1024)(128)(4,1)S(1)}, s32[]{:S(2)}) async-start(s8[4718592]{0:T(1024)(128)(4,1)} %bitcast.157), calls=%async_computation.2 | async-start | bytes 1048576
  96.4 12.0 %collective-permute-start.8 = (bf16[2,96,256]{2,1,0:T(8,128)(2,1)S(1)}, bf16[2,96,256]{2,1,0:T(8,128)(2,1)S(1)}, u32[]{:S(2)}, u32[]{:S(2)}) collective-permute-start(bf16[2,96,256]{2,1,0:T(8,128)(2,1)S(1)} %get-tuple-element.45), channel_id=1, source_target_pairs={{0,1},{1,2},{2,3},{3,0},{4,5},{5,6},{6,7},{7,4},{8,9},{9,10},{10,1... | collective-permute-start | bytes 294920 | tf_op jit(solution)/shard_map/ppermute | solution.py:77
  97.7 7.8 %collective-permute-start.10 = (bf16[2,96,256]{2,1,0:T(8,128)(2,1)S(1)}, bf16[2,96,256]{2,1,0:T(8,128)(2,1)S(1)}, u32[]{:S(2)}, u32[]{:S(2)}) collective-permute-start(bf16[2,96,256]{2,1,0:T(8,128)(2,1)S(1)} %get-tuple-element.46), channel_id=1, source_target_pairs={{0,3},{1,0},{2,1},{3,2},{4,7},{5,4},{6,5},{7,6},{8,11},{9,8},{10,9... | collective-permute-start | bytes 294920 | tf_op jit(solution)/shard_map/ppermute | solution.py:77
  99.3 10.8 %collective-permute-start.12 = (bf16[2,96,256]{2,1,0:T(8,128)(2,1)S(1)}, bf16[2,96,256]{2,1,0:T(8,128)(2,1)S(1)}, u32[]{:S(2)}, u32[]{:S(2)}) collective-permute-start(bf16[2,96,256]{2,1,0:T(8,128)(2,1)S(1)} %get-tuple-element.47), channel_id=1, source_target_pairs={{0,1},{1,2},{2,3},{3,0},{4,5},{5,6},{6,7},{7,4},{8,9},{9,10},{10,1... | collective-permute-start | bytes 294920 | tf_op jit(solution)/shard_map/ppermute | solution.py:77
  99.4 9.1 %collective-permute-start.14 = (bf16[2,96,256]{2,1,0:T(8,128)(2,1)S(1)}, bf16[2,96,256]{2,1,0:T(8,128)(2,1)S(1)}, u32[]{:S(2)}, u32[]{:S(2)}) collective-permute-start(bf16[2,96,256]{2,1,0:T(8,128)(2,1)S(1)} %get-tuple-element.48), channel_id=1, source_target_pairs={{0,3},{1,0},{2,1},{3,2},{4,7},{5,4},{6,5},{7,6},{8,11},{9,8},{10,9... | collective-permute-start | bytes 294920 | tf_op jit(solution)/shard_map/ppermute | solution.py:77
  105.4 6.4 %collective-permute-start.16 = (bf16[2,96,256]{2,1,0:T(8,128)(2,1)S(1)}, bf16[2,96,256]{2,1,0:T(8,128)(2,1)S(1)}, u32[]{:S(2)}, u32[]{:S(2)}) collective-permute-start(bf16[2,96,256]{2,1,0:T(8,128)(2,1)S(1)} %get-tuple-element.49), channel_id=1, source_target_pairs={{0,1},{1,2},{2,3},{3,0},{4,5},{5,6},{6,7},{7,4},{8,9},{9,10},{10,1... | collective-permute-start | bytes 294920 | tf_op jit(solution)/shard_map/ppermute | solution.py:77
  105.6 5.8 %collective-permute-start.18 = (bf16[2,96,256]{2,1,0:T(8,128)(2,1)S(1)}, bf16[2,96,256]{2,1,0:T(8,128)(2,1)S(1)}, u32[]{:S(2)}, u32[]{:S(2)}) collective-permute-start(bf16[2,96,256]{2,1,0:T(8,128)(2,1)S(1)} %get-tuple-element.50), channel_id=1, source_target_pairs={{0,3},{1,0},{2,1},{3,2},{4,7},{5,4},{6,5},{7,6},{8,11},{9,8},{10,9... | collective-permute-start | bytes 294920 | tf_op jit(solution)/shard_map/ppermute | solution.py:77
  108.4 6.0 %collective-permute-start.11 = (bf16[2,192,256]{2,1,0:T(8,128)(2,1)S(1)}, bf16[2,192,256]{2,1,0:T(8,128)(2,1)S(1)}, u32[]{:S(2)}, u32[]{:S(2)}) collective-permute-start(bf16[2,192,256]{2,1,0:T(8,128)(2,1)S(1)} %pad_maximum_fusion.5), channel_id=1, source_target_pairs={{0,3},{1,0},{2,1},{3,2},{4,7},{5,4},{6,5},{7,6},{8,11},{9,8},{10,9... | collective-permute-start | bytes 589832 | tf_op jit(solution)/shard_map/ppermute | solution.py:77
  108.5 6.0 %collective-permute-start.9 = (bf16[2,192,256]{2,1,0:T(8,128)(2,1)S(1)}, bf16[2,192,256]{2,1,0:T(8,128)(2,1)S(1)}, u32[]{:S(2)}, u32[]{:S(2)}) collective-permute-start(bf16[2,192,256]{2,1,0:T(8,128)(2,1)S(1)} %pad_maximum_fusion.4), channel_id=1, source_target_pairs={{0,1},{1,2},{2,3},{3,0},{4,5},{5,6},{6,7},{7,4},{8,9},{9,10},{10,1... | collective-permute-start | bytes 589832 | tf_op jit(solution)/shard_map/ppermute | solution.py:77
  110.1 7.3 %collective-permute-start.15 = (bf16[2,192,256]{2,1,0:T(8,128)(2,1)S(1)}, bf16[2,192,256]{2,1,0:T(8,128)(2,1)S(1)}, u32[]{:S(2)}, u32[]{:S(2)}) collective-permute-start(bf16[2,192,256]{2,1,0:T(8,128)(2,1)S(1)} %pad_maximum_fusion.7), channel_id=1, source_target_pairs={{0,3},{1,0},{2,1},{3,2},{4,7},{5,4},{6,5},{7,6},{8,11},{9,8},{10,9... | collective-permute-start | bytes 589832 | tf_op jit(solution)/shard_map/ppermute | solution.py:77
  111.5 8.2 %collective-permute-start.13 = (bf16[2,192,256]{2,1,0:T(8,128)(2,1)S(1)}, bf16[2,192,256]{2,1,0:T(8,128)(2,1)S(1)}, u32[]{:S(2)}, u32[]{:S(2)}) collective-permute-start(bf16[2,192,256]{2,1,0:T(8,128)(2,1)S(1)} %pad_maximum_fusion.6), channel_id=1, source_target_pairs={{0,1},{1,2},{2,3},{3,0},{4,5},{5,6},{6,7},{7,4},{8,9},{9,10},{10,1... | collective-permute-start | bytes 589832 | tf_op jit(solution)/shard_map/ppermute | solution.py:77
  111.8 9.8 %collective-permute-start.19 = (bf16[2,192,256]{2,1,0:T(8,128)(2,1)S(1)}, bf16[2,192,256]{2,1,0:T(8,128)(2,1)S(1)}, u32[]{:S(2)}, u32[]{:S(2)}) collective-permute-start(bf16[2,192,256]{2,1,0:T(8,128)(2,1)S(1)} %pad_maximum_fusion.9), channel_id=1, source_target_pairs={{0,3},{1,0},{2,1},{3,2},{4,7},{5,4},{6,5},{7,6},{8,11},{9,8},{10,9... | collective-permute-start | bytes 589832 | tf_op jit(solution)/shard_map/ppermute | solution.py:77
  114.4 9.5 %collective-permute-start.17 = (bf16[2,192,256]{2,1,0:T(8,128)(2,1)S(1)}, bf16[2,192,256]{2,1,0:T(8,128)(2,1)S(1)}, u32[]{:S(2)}, u32[]{:S(2)}) collective-permute-start(bf16[2,192,256]{2,1,0:T(8,128)(2,1)S(1)} %pad_maximum_fusion.8), channel_id=1, source_target_pairs={{0,1},{1,2},{2,3},{3,0},{4,5},{5,6},{6,7},{7,4},{8,9},{9,10},{10,1... | collective-permute-start | bytes 589832 | tf_op jit(solution)/shard_map/ppermute | solution.py:77
  114.5 10.5 %copy-start.1 = (bf16[2,768,768]{2,1,0:T(8,128)(2,1)S(1)}, bf16[2,768,768]{2,1,0:T(8,128)(2,1)}, u32[]{:S(2)}) copy-start(bf16[2,768,768]{2,1,0:T(8,128)(2,1)} %param.3) | copy-start | bytes 7077892

commit v15 on v13

--- a/solution.py
+++ b/solution.py
@@ -9,7 +9,7 @@
 
 
 RING = 4
-CHUNKS = 6
+CHUNKS = 3
 
 
 def ring_axis(stage, core):
@@ -68,9 +68,10 @@
     dz, dx = (zq - z) % nz, (xq - x) % nx
     inner = jnp.where(cq == 0, dz * nx + dx, dx * nz + dz)
     index = jnp.where(cq == core, 0, chips) + inner
-    ordered = stacked.at[index].get(mode="promise_in_bounds")
-    ordered = jnp.transpose(ordered, (1, 0, 2, 3))
-    return ordered.reshape(slots, rows, cols)
+    return tuple(
+        stacked[:, slot].at[index].get(mode="promise_in_bounds").reshape(rows, cols)
+        for slot in range(slots)
+    )
 
 
 def shifted(value, step, groups):
@@ -102,7 +103,7 @@
     total = None
     for slot, half_product in enumerate(halves):
         term = jnp.einsum(
-            "pad,bd->pab", half_product, vectors[slot, lo:hi], preferred_element_type=jnp.float32
+            "pad,bd->pab", half_product, vectors[slot][lo:hi], preferred_element_type=jnp.float32
         )
         total = term if total is None else total + term
     return total
@@ -115,11 +116,11 @@
     vectors = gather_slots(cholesky_vectors[0, 0], owned_slots, sizes)
     halves = tuple(
         jnp.einsum(
-            "ac,pcd->pad", vectors[slot], amplitudes, preferred_element_type=jnp.float32
+            "ac,pcd->pad", vector, amplitudes, preferred_element_type=jnp.float32
         ).astype(jnp.bfloat16)
-        for slot in range(vectors.shape[0])
+        for vector in vectors
     )
-    width = vectors.shape[1] // CHUNKS
+    width = vectors[0].shape[0] // CHUNKS
     outs = []
     for chunk in range(CHUNKS):
         cut = columns(halves, vectors, chunk * width, (chunk + 1) * width)

time: 142 us -> 126 us (0.89)
  the two profiles are of different devices: /device:TPU:0 before, /device:TPU:1 now
where the time goes in v15:
time: 126 us; the launch traced here: 124 us
  waiting for transfers between devices  51.9 us (41%)
  starting transfers between devices  31.5 us (25%)
  matrix products  19.1 us (15%)
  local copies, waits for them, and re-layouts  12.1 us (10%)
  other arithmetic  8.8 us (7%)
    all_to_all x1, waiting for transfers between devices, gather_slots(): pieces = lax.all_to_all(pieces, PAIR, 0, 0, tiled=True)  17.8 us
    ppermute x9, starting transfers between devices, shifted(): lax.ppermute(value, 'vgrp', [(g, (g + step) % groups) for g in range(grou...  11.2 us
    gather x4, local copies, waits for them, and re-layouts, gather_slots(): stacked[:, slot].at[index].get(mode='promise_in_bounds').reshape(rows, cols)  10.7 us
    ppermute x9, waiting for transfers between devices, shifted(): lax.ppermute(value, 'vgrp', [(g, (g + step) % groups) for g in range(grou...  10.3 us
    dot_general x12, matrix products, columns(): jnp.einsum('pad,bd->pab', half_product, vectors[slot][lo:hi], preferred_e...  9.71 us
    all_to_all x1, starting transfers between devices, gather_slots(): pieces = lax.all_to_all(pieces, PAIR, 0, 0, tiled=True)  9.55 us
    dot_general x4, matrix products, on_device(): jnp.einsum('ac,pcd->pad', vector, amplitudes, preferred_element_type=jnp....  9.35 us
    ppermute x2, waiting for transfers between devices, ring_gather(): from_next = lax.ppermute(piece, PAIR, ring_perm(sizes, stage, -1))  7.2 us
  transfers between devices with their start and end apart: 18, of which 11 were waited for; matrix products, arithmetic and copies ran while one was open for 6% of the time, Pallas kernels for 0%

profile of v15, /device:TPU:1, one launch (start us, length us, event | category | flops | bytes accessed | tf_op | source)
XLA Modules:
  0.0 123.8 jit_solution(3178910564839284452)
XLA Ops:
  0.0 9.6 %all-to-all-start = ((bf16[32,24,768]{2,1,0:T(8,128)(2,1)}), bf16[32,24,768]{2,1,0:T(8,128)(2,1)S(1)}, u32[]{:S(2)}, u32[]{:S(2)}) async-start(bf16[32,24,768]{2,1,0:T(8,128)(2,1)} %bitcast.198), calls=%async_computation | async-start | bytes 2359296 | tf_op jit(solution)/shard_map/all_to_all | solution.py:53
  10.3 17.8 %all-to-all-done = bf16[32,24,768]{2,1,0:T(8,128)(2,1)S(1)} async-done(((bf16[32,24,768]{2,1,0:T(8,128)(2,1)}), bf16[32,24,768]{2,1,0:T(8,128)(2,1)S(1)}, u32[]{:S(2)}, u32[]{:S(2)}) %all-to-all-start) | async-done | bytes 1179680 | tf_op jit(solution)/shard_map/all_to_all | solution.py:53
  28.1 1.2 gather_fusion
  29.3 1.1 collective-permute-start.1
  30.4 1.2 collective-permute-start
  31.8 3.5 %collective-permute-done.1 = bf16[4,24,768]{2,1,0:T(8,128)(2,1)S(1)} collective-permute-done((bf16[4,24,768]{2,1,0:T(8,128)(2,1)}, bf16[4,24,768]{2,1,0:T(8,128)(2,1)S(1)}, u32[]{:S(2)}, u32[]{:S(2)}) %collective-permute-start.1) | collective-permute-done | bytes 147488 | tf_op jit(solution)/shard_map/ppermute | solution.py:38
  35.3 1.6 %collective-permute-done.2 = bf16[4,24,768]{2,1,0:T(8,128)(2,1)S(1)} collective-permute-done((bf16[4,24,768]{2,1,0:T(8,128)(2,1)}, bf16[4,24,768]{2,1,0:T(8,128)(2,1)S(1)}, u32[]{:S(2)}, u32[]{:S(2)}) %collective-permute-start.2) | collective-permute-done | bytes 147488 | tf_op jit(solution)/shard_map/ppermute | solution.py:35
  38.0 1.9 %collective-permute-start.3 = (bf16[4,4,24,768]{3,2,1,0:T(8,128)(2,1)S(1)}, bf16[4,4,24,768]{3,2,1,0:T(8,128)(2,1)S(1)}, u32[]{:S(2)}, u32[]{:S(2)}) collective-permute-start(bf16[4,4,24,768]{3,2,1,0:T(8,128)(2,1)S(1)} %get-tuple-element.47), channel_id=1, source_target_pairs={{0,96},{4,28},{8,104},{12,4},{16,112},{20,12},{24,120},{28,20},{32... | collective-permute-start | bytes 1769480 | tf_op jit(solution)/shard_map/ppermute | solution.py:36
  39.9 7.2 %collective-permute-done.3 = bf16[4,4,24,768]{3,2,1,0:T(8,128)(2,1)S(1)} collective-permute-done((bf16[4,4,24,768]{3,2,1,0:T(8,128)(2,1)S(1)}, bf16[4,4,24,768]{3,2,1,0:T(8,128)(2,1)S(1)}, u32[]{:S(2)}, u32[]{:S(2)}) %collective-permute-start.3) | collective-permute-done | bytes 589856 | tf_op jit(solution)/shard_map/ppermute | solution.py:36
  47.1 3.1 %collective-permute-start.6 = (bf16[2,4,24,768]{3,2,1,0:T(8,128)(2,1)S(1)}, bf16[2,4,24,768]{3,2,1,0:T(8,128)(2,1)S(1)}, u32[]{:S(2)}, u32[]{:S(2)}) collective-permute-start(bf16[2,4,24,768]{3,2,1,0:T(8,128)(2,1)S(1)} %slice.83), channel_id=1, source_target_pairs={{0,96},{4,28},{8,104},{12,4},{16,112},{20,12},{24,120},{28,20},{32... | collective-permute-start | bytes 884744 | tf_op jit(solution)/shard_map/ppermute | solution.py:41
  50.3 3.6 %collective-permute-done.6 = bf16[2,4,24,768]{3,2,1,0:T(8,128)(2,1)S(1)} collective-permute-done((bf16[2,4,24,768]{3,2,1,0:T(8,128)(2,1)S(1)}, bf16[2,4,24,768]{3,2,1,0:T(8,128)(2,1)S(1)}, u32[]{:S(2)}, u32[]{:S(2)}) %collective-permute-start.6) | collective-permute-done | bytes 294944 | tf_op jit(solution)/shard_map/ppermute | solution.py:41
  53.8 3.5 %collective-permute-done.5 = bf16[2,4,24,768]{3,2,1,0:T(8,128)(2,1)S(1)} collective-permute-done((bf16[2,4,24,768]{3,2,1,0:T(8,128)(2,1)S(1)}, bf16[2,4,24,768]{3,2,1,0:T(8,128)(2,1)S(1)}, u32[]{:S(2)}, u32[]{:S(2)}) %collective-permute-start.5) | collective-permute-done | bytes 294944 | tf_op jit(solution)/shard_map/ppermute | solution.py:40
  57.4 1.7 %pad_maximum_fusion = bf16[4,4,4,24,768]{4,3,2,1,0:T(8,128)(2,1)} fusion(bf16[1,4,4,24,768]{4,3,2,1,0:T(8,128)(2,1)S(1)} %bitcast.197, bf16[1,4,4,24,768]{4,3,2,1,0:T(8,128)(2,1)S(1)} %maximum_bitcast_fusion, bf16[1,4,4,24,768]{4,3,2,1,0:T(8,128)(2,1)S(1)} %bitcast.196, bf16[1,4,4,24,768]{4,3,2,1,0:T(8,128)(2,1)S(1)} %get-tuple-element.46), kind=kLoop, calls=%fused_computation.11 | loop fusion | flops 3538944 | bytes 4718592 | tf_op jit(solution)/shard_map/stack | solution.py:43
  59.1 3.2 %collective-permute-start.7 = (bf16[4,4,4,24,768]{4,3,2,1,0:T(8,128)(2,1)}, bf16[4,4,4,24,768]{4,3,2,1,0:T(8,128)(2,1)}, u32[]{:S(2)}, u32[]{:S(2)}) collective-permute-start(bf16[4,4,4,24,768]{4,3,2,1,0:T(8,128)(2,1)} %pad_maximum_fusion), channel_id=1, source_target_pairs={{0,4},{4,0},{8,12},{12,8},{16,20},{20,16},{24,28},{28,24},{32,36},... | collective-permute-start | bytes 7077896 | tf_op jit(solution)/shard_map/ppermute | solution.py:58
  62.4 4.5 %collective-permute-done.7 = bf16[4,4,4,24,768]{4,3,2,1,0:T(8,128)(2,1)} collective-permute-done((bf16[4,4,4,24,768]{4,3,2,1,0:T(8,128)(2,1)}, bf16[4,4,4,24,768]{4,3,2,1,0:T(8,128)(2,1)}, u32[]{:S(2)}, u32[]{:S(2)}) %collective-permute-start.7) | collective-permute-done | bytes 2359328 | tf_op jit(solution)/shard_map/ppermute | solution.py:58
  66.8 3.9 %fusion.6 = (bf16[32,24,768]{2,1,0:T(8,128)(2,1)}, bf16[32,24,768]{2,1,0:T(8,128)(2,1)}, bf16[32,24,768]{2,1,0:T(8,128)(2,1)}, bf16[32,24,768]{2,1,0:T(8,128)(2,1)}) fusion(bf16[16,4,24,768]{3,2,1,0:T(8,128)(2,1)} %bitcast.12, bf16[16,4,24,768]{3,2,1,0:T(8,128)(2,1)} %bitcast.11), kind=kLoop, calls=%fused_computation.26 | loop fusion | flops 2359296 | bytes 9437184 | tf_op jit(solution)/shard_map/squeeze | solution.py:72
  70.8 1.9 %gather_fusion.4 = bf16[32,24,768]{2,1,0:T(8,128)(2,1)S(1)} fusion(bf16[32,24,768]{2,1,0:T(8,128)(2,1)} %get-tuple-element.33, s32[1024]{0:T(1024)S(1)} %pad_clamp_fusion), kind=kCustom, calls=%fused_computation.4 | custom fusion | bytes 2359424 | tf_op jit(solution)/shard_map/gather | solution.py:72
  72.7 2.9 %gather_fusion.1 = bf16[32,24,768]{2,1,0:T(8,128)(2,1)} fusion(bf16[32,24,768]{2,1,0:T(8,128)(2,1)} %get-tuple-element.34, s32[1024]{0:T(1024)S(1)} %pad_clamp_fusion), kind=kCustom, calls=%fused_computation.1 | custom fusion | bytes 2359424 | tf_op jit(solution)/shard_map/gather | solution.py:72
  75.6 2.9 %gather_fusion.2 = bf16[32,24,768]{2,1,0:T(8,128)(2,1)} fusion(bf16[32,24,768]{2,1,0:T(8,128)(2,1)} %get-tuple-element.35, s32[1024]{0:T(1024)S(1)} %pad_clamp_fusion), kind=kCustom, calls=%fused_computation.2 | custom fusion | bytes 2359424 | tf_op jit(solution)/shard_map/gather | solution.py:72
  78.5 2.9 %gather_fusion.3 = bf16[32,24,768]{2,1,0:T(8,128)(2,1)} fusion(bf16[32,24,768]{2,1,0:T(8,128)(2,1)} %get-tuple-element.36, s32[1024]{0:T(1024)S(1)} %pad_clamp_fusion), kind=kCustom, calls=%fused_computation.3 | custom fusion | bytes 2359424 | tf_op jit(solution)/shard_map/gather | solution.py:72
  81.4 3.4 %convert_bitcast_fusion.2 = bf16[2,768,768]{2,1,0:T(8,128)(2,1)S(1)} fusion(bf16[768,768,1]{1,0,2:T(8,128)(2,1)} %bitcast.178, bf16[2,768,768]{2,1,0:T(8,128)(2,1)S(1)} %copy-done), kind=kOutput, calls=%fused_computation.14 | convolution fusion | flops 1813118976 | bytes 5898240 | tf_op jit(solution)/shard_map/ac,pcd->pad/dot_general | solution.py:118
  84.8 2.0 %convert_bitcast_fusion.1 = bf16[2,768,768]{2,1,0:T(8,128)(2,1)S(1)} fusion(bf16[768,768,1]{1,0,2:T(8,128)(2,1)S(1)} %bitcast.182, bf16[2,768,768]{2,1,0:T(8,128)(2,1)S(1)} %copy-done), kind=kOutput, calls=%fused_computation.13 | convolution fusion | flops 1813118976 | bytes 5898240 | tf_op jit(solution)/shard_map/ac,pcd->pad/dot_general | solution.py:118
  86.8 2.0 %convert_bitcast_fusion.3 = bf16[2,768,768]{2,1,0:T(8,128)(2,1)S(1)} fusion(bf16[768,768,1]{1,0,2:T(8,128)(2,1)S(1)} %bitcast.186, bf16[2,768,768]{2,1,0:T(8,128)(2,1)S(1)} %copy-done), kind=kOutput, calls=%fused_computation.15 | convolution fusion | flops 1813118976 | bytes 5898240 | tf_op jit(solution)/shard_map/ac,pcd->pad/dot_general | solution.py:118
  88.8 2.0 %convert_bitcast_fusion = bf16[2,768,768]{2,1,0:T(8,128)(2,1)S(1)} fusion(bf16[768,768,1]{1,0,2:T(8,128)(2,1)S(1)} %bitcast.174, bf16[2,768,768]{2,1,0:T(8,128)(2,1)S(1)} %copy-done), kind=kOutput, calls=%fused_computation.12 | convolution fusion | flops 1813118976 | bytes 5898240 | tf_op jit(solution)/shard_map/ac,pcd->pad/dot_general | solution.py:118
  94.2 1.4 %collective-permute-start.8 = (bf16[2,192,256]{2,1,0:T(8,128)(2,1)S(1)}, bf16[2,192,256]{2,1,0:T(8,128)(2,1)S(1)}, u32[]{:S(2)}, u32[]{:S(2)}) collective-permute-start(bf16[2,192,256]{2,1,0:T(8,128)(2,1)S(1)} %get-tuple-element.19), channel_id=1, source_target_pairs={{0,1},{1,2},{2,3},{3,0},{4,5},{5,6},{6,7},{7,4},{8,9},{9,10},{10,1... | collective-permute-start | bytes 589832 | tf_op jit(solution)/shard_map/ppermute | solution.py:78
  95.6 1.5 %collective-permute-start.9 = (bf16[2,192,256]{2,1,0:T(8,128)(2,1)S(1)}, bf16[2,192,256]{2,1,0:T(8,128)(2,1)S(1)}, u32[]{:S(2)}, u32[]{:S(2)}) collective-permute-start(bf16[2,192,256]{2,1,0:T(8,128)(2,1)S(1)} %get-tuple-element.20), channel_id=1, source_target_pairs={{0,3},{1,0},{2,1},{3,2},{4,7},{5,4},{6,5},{7,6},{8,11},{9,8},{10,9... | collective-permute-start | bytes 589832 | tf_op jit(solution)/shard_map/ppermute | solution.py:78
  97.1 1.6 %collective-permute-start.10 = (bf16[2,192,256]{2,1,0:T(8,128)(2,1)S(1)}, bf16[2,192,256]{2,1,0:T(8,128)(2,1)S(1)}, u32[]{:S(2)}, u32[]{:S(2)}) collective-permute-start(bf16[2,192,256]{2,1,0:T(8,128)(2,1)S(1)} %get-tuple-element.21), channel_id=1, source_target_pairs={{0,2},{1,3},{2,0},{3,1},{4,6},{5,7},{6,4},{7,5},{8,10},{9,11},{10,... | collective-permute-start | bytes 589832 | tf_op jit(solution)/shard_map/ppermute | solution.py:78
  102.5 2.3 %collective-permute-start.12 = (bf16[2,192,256]{2,1,0:T(8,128)(2,1)S(1)}, bf16[2,192,256]{2,1,0:T(8,128)(2,1)S(1)}, u32[]{:S(2)}, u32[]{:S(2)}) collective-permute-start(bf16[2,192,256]{2,1,0:T(8,128)(2,1)S(1)} %get-tuple-element.27), channel_id=1, source_target_pairs={{0,3},{1,0},{2,1},{3,2},{4,7},{5,4},{6,5},{7,6},{8,11},{9,8},{10,9... | collective-permute-start | bytes 589832 | tf_op jit(solution)/shard_map/ppermute | solution.py:78
  108.8 2.3 %collective-permute-start.15 = (bf16[2,192,256]{2,1,0:T(8,128)(2,1)S(1)}, bf16[2,192,256]{2,1,0:T(8,128)(2,1)S(1)}, u32[]{:S(2)}, u32[]{:S(2)}) collective-permute-start(bf16[2,192,256]{2,1,0:T(8,128)(2,1)S(1)} %get-tuple-element.38), channel_id=1, source_target_pairs={{0,3},{1,0},{2,1},{3,2},{4,7},{5,4},{6,5},{7,6},{8,11},{9,8},{10,9... | collective-permute-start | bytes 589832 | tf_op jit(solution)/shard_map/ppermute | solution.py:78
  112.8 1.5 %collective-permute-done.13 = bf16[2,192,256]{2,1,0:T(8,128)(2,1)S(1)} collective-permute-done((bf16[2,192,256]{2,1,0:T(8,128)(2,1)S(1)}, bf16[2,192,256]{2,1,0:T(8,128)(2,1)S(1)}, u32[]{:S(2)}, u32[]{:S(2)}) %collective-permute-start.13) | collective-permute-done | bytes 196640 | tf_op jit(solution)/shard_map/ppermute | solution.py:78
  114.4 7.9 %collective-permute-done.14 = bf16[2,192,256]{2,1,0:T(8,128)(2,1)S(1)} collective-permute-done((bf16[2,192,256]{2,1,0:T(8,128)(2,1)S(1)}, bf16[2,192,256]{2,1,0:T(8,128)(2,1)S(1)}, u32[]{:S(2)}, u32[]{:S(2)}) %collective-permute-start.14) | collective-permute-done | bytes 196640 | tf_op jit(solution)/shard_map/ppermute | solution.py:78
  122.7 1.1 pad_maximum_fusion.2
  (50 shorter events, 15.5 us)
Async XLA Ops:
  0.0 81.4 %copy-start = (bf16[2,768,768]{2,1,0:T(8,128)(2,1)S(1)}, bf16[2,768,768]{2,1,0:T(8,128)(2,1)}, u32[]{:S(2)}) copy-start(bf16[2,768,768]{2,1,0:T(8,128)(2,1)} %param.3) | copy-start | bytes 7077892
  0.0 28.1 %all-to-all-start = ((bf16[32,24,768]{2,1,0:T(8,128)(2,1)}), bf16[32,24,768]{2,1,0:T(8,128)(2,1)S(1)}, u32[]{:S(2)}, u32[]{:S(2)}) async-start(bf16[32,24,768]{2,1,0:T(8,128)(2,1)} %bitcast.198), calls=%async_computation | async-start | bytes 2359296 | tf_op jit(solution)/shard_map/all_to_all | solution.py:53
  29.3 6.0 %collective-permute-start.1 = (bf16[4,24,768]{2,1,0:T(8,128)(2,1)}, bf16[4,24,768]{2,1,0:T(8,128)(2,1)S(1)}, u32[]{:S(2)}, u32[]{:S(2)}) collective-permute-start(bf16[4,24,768]{2,1,0:T(8,128)(2,1)} %gather_fusion), channel_id=1, source_target_pairs={{0,16},{4,68},{8,24},{12,76},{16,0},{20,84},{24,8},{28,92},{32,48}... | collective-permute-start | bytes 442376 | tf_op jit(solution)/shard_map/ppermute | solution.py:38
  30.4 4.9 %collective-permute-start = (bf16[4,24,768]{2,1,0:T(8,128)(2,1)}, bf16[4,24,768]{2,1,0:T(8,128)(2,1)S(1)}, u32[]{:S(2)}, u32[]{:S(2)}) collective-permute-start(bf16[4,24,768]{2,1,0:T(8,128)(2,1)} %gather_fusion), channel_id=1, source_target_pairs={{0,24},{4,100},{8,0},{12,108},{16,8},{20,116},{24,16},{28,124},{32... | collective-permute-start | bytes 442376 | tf_op jit(solution)/shard_map/ppermute | solution.py:36
  31.5 5.4 %collective-permute-start.2 = (bf16[4,24,768]{2,1,0:T(8,128)(2,1)}, bf16[4,24,768]{2,1,0:T(8,128)(2,1)S(1)}, u32[]{:S(2)}, u32[]{:S(2)}) collective-permute-start(bf16[4,24,768]{2,1,0:T(8,128)(2,1)} %gather_fusion), channel_id=1, source_target_pairs={{0,8},{4,36},{8,16},{12,44},{16,24},{20,52},{24,0},{28,60},{32,40}... | collective-permute-start | bytes 442376 | tf_op jit(solution)/shard_map/ppermute | solution.py:35
  38.0 9.1 %collective-permute-start.3 = (bf16[4,4,24,768]{3,2,1,0:T(8,128)(2,1)S(1)}, bf16[4,4,24,768]{3,2,1,0:T(8,128)(2,1)S(1)}, u32[]{:S(2)}, u32[]{:S(2)}) collective-permute-start(bf16[4,4,24,768]{3,2,1,0:T(8,128)(2,1)S(1)} %get-tuple-element.47), channel_id=1, source_target_pairs={{0,96},{4,28},{8,104},{12,4},{16,112},{20,12},{24,120},{28,20},{32... | collective-permute-start | bytes 1769480 | tf_op jit(solution)/shard_map/ppermute | solution.py:36
  39.8 10.3 %collective-permute-start.4 = (bf16[4,4,24,768]{3,2,1,0:T(8,128)(2,1)S(1)}, bf16[4,4,24,768]{3,2,1,0:T(8,128)(2,1)S(1)}, u32[]{:S(2)}, u32[]{:S(2)}) collective-permute-start(bf16[4,4,24,768]{3,2,1,0:T(8,128)(2,1)S(1)} %get-tuple-element.47), channel_id=1, source_target_pairs={{0,32},{4,12},{8,40},{12,20},{16,48},{20,28},{24,56},{28,4},{32,64... | collective-permute-start | bytes 1769480 | tf_op jit(solution)/shard_map/ppermute | solution.py:35
  47.1 6.8 %collective-permute-start.6 = (bf16[2,4,24,768]{3,2,1,0:T(8,128)(2,1)S(1)}, bf16[2,4,24,768]{3,2,1,0:T(8,128)(2,1)S(1)}, u32[]{:S(2)}, u32[]{:S(2)}) collective-permute-start(bf16[2,4,24,768]{3,2,1,0:T(8,128)(2,1)S(1)} %slice.83), channel_id=1, source_target_pairs={{0,96},{4,28},{8,104},{12,4},{16,112},{20,12},{24,120},{28,20},{32... | collective-permute-start | bytes 884744 | tf_op jit(solution)/shard_map/ppermute | solution.py:41
  50.2 7.1 %collective-permute-start.5 = (bf16[2,4,24,768]{3,2,1,0:T(8,128)(2,1)S(1)}, bf16[2,4,24,768]{3,2,1,0:T(8,128)(2,1)S(1)}, u32[]{:S(2)}, u32[]{:S(2)}) collective-permute-start(bf16[2,4,24,768]{3,2,1,0:T(8,128)(2,1)S(1)} %slice.82), channel_id=1, source_target_pairs={{0,32},{4,12},{8,40},{12,20},{16,48},{20,28},{24,56},{28,4},{32,64... | collective-permute-start | bytes 884744 | tf_op jit(solution)/shard_map/ppermute | solution.py:40
  59.1 7.7 %collective-permute-start.7 = (bf16[4,4,4,24,768]{4,3,2,1,0:T(8,128)(2,1)}, bf16[4,4,4,24,768]{4,3,2,1,0:T(8,128)(2,1)}, u32[]{:S(2)}, u32[]{:S(2)}) collective-permute-start(bf16[4,4,4,24,768]{4,3,2,1,0:T(8,128)(2,1)} %pad_maximum_fusion), channel_id=1, source_target_pairs={{0,4},{4,0},{8,12},{12,8},{16,20},{20,16},{24,28},{28,24},{32,36},... | collective-permute-start | bytes 7077896 | tf_op jit(solution)/shard_map/ppermute | solution.py:58
  81.4 3.4 %copy-start.2 = (bf16[32,24,768]{2,1,0:T(8,128)(2,1)S(1)}, bf16[32,24,768]{2,1,0:T(8,128)(2,1)}, u32[]{:S(2)}) copy-start(bf16[32,24,768]{2,1,0:T(8,128)(2,1)} %gather_fusion.3) | copy-start | bytes 3538948
  84.8 2.0 %copy-start.3 = (bf16[32,24,768]{2,1,0:T(8,128)(2,1)S(1)}, bf16[32,24,768]{2,1,0:T(8,128)(2,1)}, u32[]{:S(2)}) copy-start(bf16[32,24,768]{2,1,0:T(8,128)(2,1)} %gather_fusion.1) | copy-start | bytes 3538948
  88.8 2.0 %copy-start.1 = (bf16[32,24,768]{2,1,0:T(8,128)(2,1)S(1)}, bf16[32,24,768]{2,1,0:T(8,128)(2,1)}, u32[]{:S(2)}) copy-start(bf16[32,24,768]{2,1,0:T(8,128)(2,1)} %gather_fusion.2) | copy-start | bytes 3538948
  94.2 13.9 %collective-permute-start.8 = (bf16[2,192,256]{2,1,0:T(8,128)(2,1)S(1)}, bf16[2,192,256]{2,1,0:T(8,128)(2,1)S(1)}, u32[]{:S(2)}, u32[]{:S(2)}) collective-permute-start(bf16[2,192,256]{2,1,0:T(8,128)(2,1)S(1)} %get-tuple-element.19), channel_id=1, source_target_pairs={{0,1},{1,2},{2,3},{3,0},{4,5},{5,6},{6,7},{7,4},{8,9},{9,10},{10,1... | collective-permute-start | bytes 589832 | tf_op jit(solution)/shard_map/ppermute | solution.py:78
  95.6 12.8 %collective-permute-start.9 = (bf16[2,192,256]{2,1,0:T(8,128)(2,1)S(1)}, bf16[2,192,256]{2,1,0:T(8,128)(2,1)S(1)}, u32[]{:S(2)}, u32[]{:S(2)}) collective-permute-start(bf16[2,192,256]{2,1,0:T(8,128)(2,1)S(1)} %get-tuple-element.20), channel_id=1, source_target_pairs={{0,3},{1,0},{2,1},{3,2},{4,7},{5,4},{6,5},{7,6},{8,11},{9,8},{10,9... | collective-permute-start | bytes 589832 | tf_op jit(solution)/shard_map/ppermute | solution.py:78
  97.1 11.7 %collective-permute-start.10 = (bf16[2,192,256]{2,1,0:T(8,128)(2,1)S(1)}, bf16[2,192,256]{2,1,0:T(8,128)(2,1)S(1)}, u32[]{:S(2)}, u32[]{:S(2)}) collective-permute-start(bf16[2,192,256]{2,1,0:T(8,128)(2,1)S(1)} %get-tuple-element.21), channel_id=1, source_target_pairs={{0,2},{1,3},{2,0},{3,1},{4,6},{5,7},{6,4},{7,5},{8,10},{9,11},{10,... | collective-permute-start | bytes 589832 | tf_op jit(solution)/shard_map/ppermute | solution.py:78
  102.0 9.7 %collective-permute-start.11 = (bf16[2,192,256]{2,1,0:T(8,128)(2,1)S(1)}, bf16[2,192,256]{2,1,0:T(8,128)(2,1)S(1)}, u32[]{:S(2)}, u32[]{:S(2)}) collective-permute-start(bf16[2,192,256]{2,1,0:T(8,128)(2,1)S(1)} %get-tuple-element.26), channel_id=1, source_target_pairs={{0,1},{1,2},{2,3},{3,0},{4,5},{5,6},{6,7},{7,4},{8,9},{9,10},{10,1... | collective-permute-start | bytes 589832 | tf_op jit(solution)/shard_map/ppermute | solution.py:78
  102.5 10.3 %collective-permute-start.12 = (bf16[2,192,256]{2,1,0:T(8,128)(2,1)S(1)}, bf16[2,192,256]{2,1,0:T(8,128)(2,1)S(1)}, u32[]{:S(2)}, u32[]{:S(2)}) collective-permute-start(bf16[2,192,256]{2,1,0:T(8,128)(2,1)S(1)} %get-tuple-element.27), channel_id=1, source_target_pairs={{0,3},{1,0},{2,1},{3,2},{4,7},{5,4},{6,5},{7,6},{8,11},{9,8},{10,9... | collective-permute-start | bytes 589832 | tf_op jit(solution)/shard_map/ppermute | solution.py:78
  108.1 6.2 %collective-permute-start.13 = (bf16[2,192,256]{2,1,0:T(8,128)(2,1)S(1)}, bf16[2,192,256]{2,1,0:T(8,128)(2,1)S(1)}, u32[]{:S(2)}, u32[]{:S(2)}) collective-permute-start(bf16[2,192,256]{2,1,0:T(8,128)(2,1)S(1)} %get-tuple-element.28), channel_id=1, source_target_pairs={{0,2},{1,3},{2,0},{3,1},{4,6},{5,7},{6,4},{7,5},{8,10},{9,11},{10,... | collective-permute-start | bytes 589832 | tf_op jit(solution)/shard_map/ppermute | solution.py:78
  108.4 13.9 %collective-permute-start.14 = (bf16[2,192,256]{2,1,0:T(8,128)(2,1)S(1)}, bf16[2,192,256]{2,1,0:T(8,128)(2,1)S(1)}, u32[]{:S(2)}, u32[]{:S(2)}) collective-permute-start(bf16[2,192,256]{2,1,0:T(8,128)(2,1)S(1)} %get-tuple-element.37), channel_id=1, source_target_pairs={{0,1},{1,2},{2,3},{3,0},{4,5},{5,6},{6,7},{7,4},{8,9},{9,10},{10,1... | collective-permute-start | bytes 589832 | tf_op jit(solution)/shard_map/ppermute | solution.py:78
  108.8 13.5 %collective-permute-start.15 = (bf16[2,192,256]{2,1,0:T(8,128)(2,1)S(1)}, bf16[2,192,256]{2,1,0:T(8,128)(2,1)S(1)}, u32[]{:S(2)}, u32[]{:S(2)}) collective-permute-start(bf16[2,192,256]{2,1,0:T(8,128)(2,1)S(1)} %get-tuple-element.38), channel_id=1, source_target_pairs={{0,3},{1,0},{2,1},{3,2},{4,7},{5,4},{6,5},{7,6},{8,11},{9,8},{10,9... | collective-permute-start | bytes 589832 | tf_op jit(solution)/shard_map/ppermute | solution.py:78
  111.7 10.8 %collective-permute-start.16 = (bf16[2,192,256]{2,1,0:T(8,128)(2,1)S(1)}, bf16[2,192,256]{2,1,0:T(8,128)(2,1)S(1)}, u32[]{:S(2)}, u32[]{:S(2)}) collective-permute-start(bf16[2,192,256]{2,1,0:T(8,128)(2,1)S(1)} %get-tuple-element.39), channel_id=1, source_target_pairs={{0,2},{1,3},{2,0},{3,1},{4,6},{5,7},{6,4},{7,5},{8,10},{9,11},{10,... | collective-permute-start | bytes 589832 | tf_op jit(solution)/shard_map/ppermute | solution.py:78

commit v16 on v13

--- a/solution.py
+++ b/solution.py
@@ -9,7 +9,7 @@
 
 
 RING = 4
-CHUNKS = 6
+CHUNKS = (1, 2, 3)
 
 
 def ring_axis(stage, core):
@@ -119,12 +119,15 @@
         ).astype(jnp.bfloat16)
         for slot in range(vectors.shape[0])
     )
-    width = vectors.shape[1] // CHUNKS
+    unit = vectors.shape[1] // sum(CHUNKS)
+    edges = [0]
+    for share in CHUNKS:
+        edges.append(edges[-1] + share * unit)
     outs = []
-    for chunk in range(CHUNKS):
-        cut = columns(halves, vectors, chunk * width, (chunk + 1) * width)
+    for chunk in range(len(CHUNKS)):
+        cut = columns(halves, vectors, edges[chunk], edges[chunk + 1])
         own, owed = prepare(cut, vgrp, groups)
-        if chunk < CHUNKS - 1:
+        if chunk < len(CHUNKS) - 1:
             halves, owed = lax.optimization_barrier((halves, owed))
         outs.append(exchange(own, owed, groups))
     return jnp.concatenate(outs, axis=2)

time: 142 us -> 131 us (0.923)
  the two profiles are of different devices: /device:TPU:0 before, /device:TPU:1 now
where the time goes in v16:
time: 131 us; the launch traced here: 129 us
  waiting for transfers between devices  56 us (43%)
  starting transfers between devices  32.1 us (25%)
  matrix products  20.2 us (15%)
  local copies, waits for them, and re-layouts  10.9 us (8%)
  other arithmetic  9.84 us (8%)
    all_to_all x1, waiting for transfers between devices, gather_slots(): pieces = lax.all_to_all(pieces, PAIR, 0, 0, tiled=True)  17.8 us
    ppermute x9, waiting for transfers between devices, shifted(): lax.ppermute(value, 'vgrp', [(g, (g + step) % groups) for g in range(grou...  14.3 us
    dot_general x12, matrix products, columns(): jnp.einsum('pad,bd->pab', half_product, vectors[slot, lo:hi], preferred_e...  12.2 us
    ppermute x9, starting transfers between devices, shifted(): lax.ppermute(value, 'vgrp', [(g, (g + step) % groups) for g in range(grou...  11.7 us
    all_to_all x1, starting transfers between devices, gather_slots(): pieces = lax.all_to_all(pieces, PAIR, 0, 0, tiled=True)  9.55 us
    dot_general x4, matrix products, on_device(): jnp.einsum('ac,pcd->pad', vectors[slot], amplitudes, preferred_element_ty...  8.01 us
    ppermute x2, waiting for transfers between devices, ring_gather(): from_next = lax.ppermute(piece, PAIR, ring_perm(sizes, stage, -1))  7.2 us
    gather x1, local copies, waits for them, and re-layouts, gather_slots(): ordered = stacked.at[index].get(mode='promise_in_bounds')  5.37 us
  transfers between devices with their start and end apart: 18, of which 10 were waited for; matrix products, arithmetic and copies ran while one was open for 8% of the time, Pallas kernels for 0%

profile of v16, /device:TPU:1, one launch (start us, length us, event | category | flops | bytes accessed | tf_op | source)
XLA Modules:
  0.0 129.2 jit_solution(18296090342456391261)
XLA Ops:
  0.0 9.6 %all-to-all-start = ((bf16[32,24,768]{2,1,0:T(8,128)(2,1)}), bf16[32,24,768]{2,1,0:T(8,128)(2,1)S(1)}, u32[]{:S(2)}, u32[]{:S(2)}) async-start(bf16[32,24,768]{2,1,0:T(8,128)(2,1)} %bitcast.208), calls=%async_computation | async-start | bytes 2359296 | tf_op jit(solution)/shard_map/all_to_all | solution.py:53
  10.3 17.8 %all-to-all-done = bf16[32,24,768]{2,1,0:T(8,128)(2,1)S(1)} async-done(((bf16[32,24,768]{2,1,0:T(8,128)(2,1)}), bf16[32,24,768]{2,1,0:T(8,128)(2,1)S(1)}, u32[]{:S(2)}, u32[]{:S(2)}) %all-to-all-start) | async-done | bytes 1179680 | tf_op jit(solution)/shard_map/all_to_all | solution.py:53
  31.8 3.5 %collective-permute-done.1 = bf16[4,24,768]{2,1,0:T(8,128)(2,1)S(1)} collective-permute-done((bf16[4,24,768]{2,1,0:T(8,128)(2,1)}, bf16[4,24,768]{2,1,0:T(8,128)(2,1)S(1)}, u32[]{:S(2)}, u32[]{:S(2)}) %collective-permute-start.1) | collective-permute-done | bytes 147488 | tf_op jit(solution)/shard_map/ppermute | solution.py:38
  35.3 1.6 %collective-permute-done.2 = bf16[4,24,768]{2,1,0:T(8,128)(2,1)S(1)} collective-permute-done((bf16[4,24,768]{2,1,0:T(8,128)(2,1)}, bf16[4,24,768]{2,1,0:T(8,128)(2,1)S(1)}, u32[]{:S(2)}, u32[]{:S(2)}) %collective-permute-start.2) | collective-permute-done | bytes 147488 | tf_op jit(solution)/shard_map/ppermute | solution.py:35
  38.0 1.9 %collective-permute-start.3 = (bf16[4,4,24,768]{3,2,1,0:T(8,128)(2,1)S(1)}, bf16[4,4,24,768]{3,2,1,0:T(8,128)(2,1)S(1)}, u32[]{:S(2)}, u32[]{:S(2)}) collective-permute-start(bf16[4,4,24,768]{3,2,1,0:T(8,128)(2,1)S(1)} %get-tuple-element.47), channel_id=1, source_target_pairs={{0,96},{4,28},{8,104},{12,4},{16,112},{20,12},{24,120},{28,20},{32... | collective-permute-start | bytes 1769480 | tf_op jit(solution)/shard_map/ppermute | solution.py:36
  39.9 7.2 %collective-permute-done.3 = bf16[4,4,24,768]{3,2,1,0:T(8,128)(2,1)S(1)} collective-permute-done((bf16[4,4,24,768]{3,2,1,0:T(8,128)(2,1)S(1)}, bf16[4,4,24,768]{3,2,1,0:T(8,128)(2,1)S(1)}, u32[]{:S(2)}, u32[]{:S(2)}) %collective-permute-start.3) | collective-permute-done | bytes 589856 | tf_op jit(solution)/shard_map/ppermute | solution.py:36
  47.1 3.1 %collective-permute-start.6 = (bf16[2,4,24,768]{3,2,1,0:T(8,128)(2,1)S(1)}, bf16[2,4,24,768]{3,2,1,0:T(8,128)(2,1)S(1)}, u32[]{:S(2)}, u32[]{:S(2)}) collective-permute-start(bf16[2,4,24,768]{3,2,1,0:T(8,128)(2,1)S(1)} %slice.81), channel_id=1, source_target_pairs={{0,96},{4,28},{8,104},{12,4},{16,112},{20,12},{24,120},{28,20},{32... | collective-permute-start | bytes 884744 | tf_op jit(solution)/shard_map/ppermute | solution.py:41
  50.3 3.6 %collective-permute-done.6 = bf16[2,4,24,768]{3,2,1,0:T(8,128)(2,1)S(1)} collective-permute-done((bf16[2,4,24,768]{3,2,1,0:T(8,128)(2,1)S(1)}, bf16[2,4,24,768]{3,2,1,0:T(8,128)(2,1)S(1)}, u32[]{:S(2)}, u32[]{:S(2)}) %collective-permute-start.6) | collective-permute-done | bytes 294944 | tf_op jit(solution)/shard_map/ppermute | solution.py:41
  53.8 3.5 %collective-permute-done.5 = bf16[2,4,24,768]{3,2,1,0:T(8,128)(2,1)S(1)} collective-permute-done((bf16[2,4,24,768]{3,2,1,0:T(8,128)(2,1)S(1)}, bf16[2,4,24,768]{3,2,1,0:T(8,128)(2,1)S(1)}, u32[]{:S(2)}, u32[]{:S(2)}) %collective-permute-start.5) | collective-permute-done | bytes 294944 | tf_op jit(solution)/shard_map/ppermute | solution.py:40
  57.4 1.7 %pad_maximum_fusion.1 = bf16[4,4,4,24,768]{4,3,2,1,0:T(8,128)(2,1)} fusion(bf16[1,4,4,24,768]{4,3,2,1,0:T(8,128)(2,1)S(1)} %bitcast.203, bf16[1,4,4,24,768]{4,3,2,1,0:T(8,128)(2,1)S(1)} %maximum_bitcast_fusion, bf16[1,4,4,24,768]{4,3,2,1,0:T(8,128)(2,1)S(1)} %bitcast.202, bf16[1,4,4,24,768]{4,3,2,1,0:T(8,128)(2,1)S(1)} %get-tuple-element.46), kind=kLoop, calls=%fused_computation.3 | loop fusion | flops 3538944 | bytes 4718592 | tf_op jit(solution)/shard_map/stack | solution.py:43
  59.2 3.2 %collective-permute-start.7 = (bf16[4,4,4,24,768]{4,3,2,1,0:T(8,128)(2,1)}, bf16[4,4,4,24,768]{4,3,2,1,0:T(8,128)(2,1)}, u32[]{:S(2)}, u32[]{:S(2)}) collective-permute-start(bf16[4,4,4,24,768]{4,3,2,1,0:T(8,128)(2,1)} %pad_maximum_fusion.1), channel_id=1, source_target_pairs={{0,4},{4,0},{8,12},{12,8},{16,20},{20,16},{24,28},{28,24},{32,36},... | collective-permute-start | bytes 7077896 | tf_op jit(solution)/shard_map/ppermute | solution.py:58
  62.4 4.5 %collective-permute-done.7 = bf16[4,4,4,24,768]{4,3,2,1,0:T(8,128)(2,1)} collective-permute-done((bf16[4,4,4,24,768]{4,3,2,1,0:T(8,128)(2,1)}, bf16[4,4,4,24,768]{4,3,2,1,0:T(8,128)(2,1)}, u32[]{:S(2)}, u32[]{:S(2)}) %collective-permute-start.7) | collective-permute-done | bytes 2359328 | tf_op jit(solution)/shard_map/ppermute | solution.py:58
  66.8 4.9 %pad_maximum_fusion = bf16[32,4,24,768]{3,2,1,0:T(8,128)(2,1)} fusion(bf16[16,4,24,768]{3,2,1,0:T(8,128)(2,1)} %bitcast.12, bf16[16,4,24,768]{3,2,1,0:T(8,128)(2,1)} %bitcast.11), kind=kLoop, calls=%fused_computation.2 | loop fusion | flops 2359296 | bytes 9437184 | tf_op jit(solution)/shard_map/concatenate | solution.py:60
  71.8 5.4 %gather_fusion.1 = bf16[32,4,24,768]{3,2,1,0:T(8,128)(2,1)} fusion(bf16[32,4,24,768]{3,2,1,0:T(8,128)(2,1)} %pad_maximum_fusion, s32[1024]{0:T(1024)S(1)} %pad_clamp_fusion), kind=kCustom, calls=%fused_computation.1 | custom fusion | bytes 9437312 | tf_op jit(solution)/shard_map/gather | solution.py:71
  77.1 2.8 %copy.13 = bf16[4,32,24,768]{3,2,1,0:T(8,128)(2,1)S(1)} copy(bf16[4,32,24,768]{3,2,0,1:T(8,128)(2,1)} %bitcast.180) | data formatting | bytes 9437184 | tf_op jit(solution)/shard_map/transpose | solution.py:72
  81.2 2.0 %convert_bitcast_fusion.1 = bf16[2,768,768]{2,1,0:T(8,128)(2,1)S(1)} fusion(bf16[768,768,1]{1,0,2:T(8,128)(2,1)S(1)} %bitcast.207, bf16[2,768,768]{2,1,0:T(8,128)(2,1)S(1)} %copy-done), kind=kOutput, calls=%fused_computation.6 | convolution fusion | flops 1813118976 | bytes 5898240 | tf_op jit(solution)/shard_map/ac,pcd->pad/dot_general | solution.py:117
  83.2 2.0 %convert_bitcast_fusion = bf16[2,768,768]{2,1,0:T(8,128)(2,1)S(1)} fusion(bf16[768,768,1]{1,0,2:T(8,128)(2,1)S(1)} %bitcast.206, bf16[2,768,768]{2,1,0:T(8,128)(2,1)S(1)} %copy-done), kind=kOutput, calls=%fused_computation.5 | convolution fusion | flops 1813118976 | bytes 5898240 | tf_op jit(solution)/shard_map/ac,pcd->pad/dot_general | solution.py:117
  85.2 2.0 %convert_bitcast_fusion.2 = bf16[2,768,768]{2,1,0:T(8,128)(2,1)S(1)} fusion(bf16[768,768,1]{1,0,2:T(8,128)(2,1)S(1)} %bitcast.205, bf16[2,768,768]{2,1,0:T(8,128)(2,1)S(1)} %copy-done), kind=kOutput, calls=%fused_computation.7 | convolution fusion | flops 1813118976 | bytes 5898240 | tf_op jit(solution)/shard_map/ac,pcd->pad/dot_general | solution.py:117
  87.2 2.0 %convert_bitcast_fusion.3 = bf16[2,768,768]{2,1,0:T(8,128)(2,1)S(1)} fusion(bf16[768,768,1]{1,0,2:T(8,128)(2,1)S(1)} %bitcast.204, bf16[2,768,768]{2,1,0:T(8,128)(2,1)S(1)} %copy-done), kind=kOutput, calls=%fused_computation.8 | convolution fusion | flops 1813118976 | bytes 5898240 | tf_op jit(solution)/shard_map/ac,pcd->pad/dot_general | solution.py:117
  92.4 1.4 %collective-permute-start.8 = (bf16[2,192,128]{2,1,0:T(8,128)(2,1)S(1)}, bf16[2,192,128]{2,1,0:T(8,128)(2,1)S(1)}, u32[]{:S(2)}, u32[]{:S(2)}) collective-permute-start(bf16[2,192,128]{2,1,0:T(8,128)(2,1)S(1)} %get-tuple-element.19), channel_id=1, source_target_pairs={{0,1},{1,2},{2,3},{3,0},{4,5},{5,6},{6,7},{7,4},{8,9},{9,10},{10,1... | collective-permute-start | bytes 294920 | tf_op jit(solution)/shard_map/ppermute | solution.py:77
  93.8 1.5 %collective-permute-start.9 = (bf16[2,192,128]{2,1,0:T(8,128)(2,1)S(1)}, bf16[2,192,128]{2,1,0:T(8,128)(2,1)S(1)}, u32[]{:S(2)}, u32[]{:S(2)}) collective-permute-start(bf16[2,192,128]{2,1,0:T(8,128)(2,1)S(1)} %get-tuple-element.20), channel_id=1, source_target_pairs={{0,3},{1,0},{2,1},{3,2},{4,7},{5,4},{6,5},{7,6},{8,11},{9,8},{10,9... | collective-permute-start | bytes 294920 | tf_op jit(solution)/shard_map/ppermute | solution.py:77
  95.3 1.6 %collective-permute-start.10 = (bf16[2,192,128]{2,1,0:T(8,128)(2,1)S(1)}, bf16[2,192,128]{2,1,0:T(8,128)(2,1)S(1)}, u32[]{:S(2)}, u32[]{:S(2)}) collective-permute-start(bf16[2,192,128]{2,1,0:T(8,128)(2,1)S(1)} %get-tuple-element.21), channel_id=1, source_target_pairs={{0,2},{1,3},{2,0},{3,1},{4,6},{5,7},{6,4},{7,5},{8,10},{9,11},{10,... | collective-permute-start | bytes 294920 | tf_op jit(solution)/shard_map/ppermute | solution.py:77
  100.8 2.3 %collective-permute-start.12 = (bf16[2,192,256]{2,1,0:T(8,128)(2,1)S(1)}, bf16[2,192,256]{2,1,0:T(8,128)(2,1)S(1)}, u32[]{:S(2)}, u32[]{:S(2)}) collective-permute-start(bf16[2,192,256]{2,1,0:T(8,128)(2,1)S(1)} %get-tuple-element.27), channel_id=1, source_target_pairs={{0,3},{1,0},{2,1},{3,2},{4,7},{5,4},{6,5},{7,6},{8,11},{9,8},{10,9... | collective-permute-start | bytes 589832 | tf_op jit(solution)/shard_map/ppermute | solution.py:77
  103.1 1.4 %fusion.2 = f32[2,768,384]{2,1,0:T(8,128)S(1)} fusion(bf16[2,768,768]{2,1,0:T(8,128)(2,1)S(1)} %convert_bitcast_fusion.3, bf16[4,768,768]{2,1,0:T(8,128)(2,1)S(1)} %bitcast.192), kind=kOutput, calls=%fused_computation.20 | convolution fusion | flops 905969664 | bytes 5308416 | tf_op jit(solution)/shard_map/pad,bd->pab/dot_general | solution.py:104
  104.5 1.4 %fusion.1 = f32[2,768,384]{2,1,0:T(8,128)S(1)} fusion(bf16[2,768,768]{2,1,0:T(8,128)(2,1)S(1)} %convert_bitcast_fusion.2, bf16[4,768,768]{2,1,0:T(8,128)(2,1)S(1)} %bitcast.193), kind=kOutput, calls=%fused_computation.18 | convolution fusion | flops 905969664 | bytes 5308416 | tf_op jit(solution)/shard_map/pad,bd->pab/dot_general | solution.py:104
  105.9 1.4 %fusion = f32[2,768,384]{2,1,0:T(8,128)S(1)} fusion(bf16[2,768,768]{2,1,0:T(8,128)(2,1)S(1)} %convert_bitcast_fusion.1, bf16[4,768,768]{2,1,0:T(8,128)(2,1)S(1)} %bitcast.194), kind=kOutput, calls=%fused_computation.16 | convolution fusion | flops 905969664 | bytes 5308416 | tf_op jit(solution)/shard_map/pad,bd->pab/dot_general | solution.py:104
  107.3 1.5 %add_add_fusion = f32[2,768,384]{2,1,0:T(8,128)S(1)} fusion(f32[2,768,384]{2,1,0:T(8,128)S(1)} %fusion, f32[2,768,384]{2,1,0:T(8,128)S(1)} %fusion.2, f32[2,768,384]{2,1,0:T(8,128)S(1)} %fusion.1, bf16[2,768,768]{2,1,0:T(8,128)(2,1)S(1)} %convert_bitcast_fusion, bf16[4,768,768]{2,1,0:T(8,128)(2,1)S(1)} %bitcast.195), kind=kOutput, calls=%fused_computation.4 | convolution fusion | flops 907739136 | bytes 12386304 | tf_op jit(solution)/shard_map/pad,bd->pab/dot_general | solution.py:104
  109.6 2.3 %collective-permute-start.15 = (bf16[2,192,384]{2,1,0:T(8,128)(2,1)S(1)}, bf16[2,192,384]{2,1,0:T(8,128)(2,1)S(1)}, u32[]{:S(2)}, u32[]{:S(2)}) collective-permute-start(bf16[2,192,384]{2,1,0:T(8,128)(2,1)S(1)} %get-tuple-element.38), channel_id=1, source_target_pairs={{0,3},{1,0},{2,1},{3,2},{4,7},{5,4},{6,5},{7,6},{8,11},{9,8},{10,9... | collective-permute-start | bytes 884744 | tf_op jit(solution)/shard_map/ppermute | solution.py:77
  111.9 1.6 %collective-permute-start.16 = (bf16[2,192,384]{2,1,0:T(8,128)(2,1)S(1)}, bf16[2,192,384]{2,1,0:T(8,128)(2,1)S(1)}, u32[]{:S(2)}, u32[]{:S(2)}) collective-permute-start(bf16[2,192,384]{2,1,0:T(8,128)(2,1)S(1)} %get-tuple-element.39), channel_id=1, source_target_pairs={{0,2},{1,3},{2,0},{3,1},{4,6},{5,7},{6,4},{7,5},{8,10},{9,11},{10,... | collective-permute-start | bytes 884744 | tf_op jit(solution)/shard_map/ppermute | solution.py:77
  113.5 1.6 %collective-permute-done.13 = bf16[2,192,256]{2,1,0:T(8,128)(2,1)S(1)} collective-permute-done((bf16[2,192,256]{2,1,0:T(8,128)(2,1)S(1)}, bf16[2,192,256]{2,1,0:T(8,128)(2,1)S(1)}, u32[]{:S(2)}, u32[]{:S(2)}) %collective-permute-start.13) | collective-permute-done | bytes 196640 | tf_op jit(solution)/shard_map/ppermute | solution.py:77
  115.2 10.0 %collective-permute-done.14 = bf16[2,192,384]{2,1,0:T(8,128)(2,1)S(1)} collective-permute-done((bf16[2,192,384]{2,1,0:T(8,128)(2,1)S(1)}, bf16[2,192,384]{2,1,0:T(8,128)(2,1)S(1)}, u32[]{:S(2)}, u32[]{:S(2)}) %collective-permute-start.14) | collective-permute-done | bytes 294944 | tf_op jit(solution)/shard_map/ppermute | solution.py:77
  125.2 2.7 %collective-permute-done.16 = bf16[2,192,384]{2,1,0:T(8,128)(2,1)S(1)} collective-permute-done((bf16[2,192,384]{2,1,0:T(8,128)(2,1)S(1)}, bf16[2,192,384]{2,1,0:T(8,128)(2,1)S(1)}, u32[]{:S(2)}, u32[]{:S(2)}) %collective-permute-start.16) | collective-permute-done | bytes 294944 | tf_op jit(solution)/shard_map/ppermute | solution.py:77
  (50 shorter events, 16.1 us)
Async XLA Ops:
  0.0 81.2 %copy-start = (bf16[2,768,768]{2,1,0:T(8,128)(2,1)S(1)}, bf16[2,768,768]{2,1,0:T(8,128)(2,1)}, u32[]{:S(2)}) copy-start(bf16[2,768,768]{2,1,0:T(8,128)(2,1)} %param.3) | copy-start | bytes 7077892
  0.0 28.1 %all-to-all-start = ((bf16[32,24,768]{2,1,0:T(8,128)(2,1)}), bf16[32,24,768]{2,1,0:T(8,128)(2,1)S(1)}, u32[]{:S(2)}, u32[]{:S(2)}) async-start(bf16[32,24,768]{2,1,0:T(8,128)(2,1)} %bitcast.208), calls=%async_computation | async-start | bytes 2359296 | tf_op jit(solution)/shard_map/all_to_all | solution.py:53
  29.3 6.0 %collective-permute-start.1 = (bf16[4,24,768]{2,1,0:T(8,128)(2,1)}, bf16[4,24,768]{2,1,0:T(8,128)(2,1)S(1)}, u32[]{:S(2)}, u32[]{:S(2)}) collective-permute-start(bf16[4,24,768]{2,1,0:T(8,128)(2,1)} %gather_fusion), channel_id=1, source_target_pairs={{0,16},{4,68},{8,24},{12,76},{16,0},{20,84},{24,8},{28,92},{32,48}... | collective-permute-start | bytes 442376 | tf_op jit(solution)/shard_map/ppermute | solution.py:38
  30.4 4.9 %collective-permute-start = (bf16[4,24,768]{2,1,0:T(8,128)(2,1)}, bf16[4,24,768]{2,1,0:T(8,128)(2,1)S(1)}, u32[]{:S(2)}, u32[]{:S(2)}) collective-permute-start(bf16[4,24,768]{2,1,0:T(8,128)(2,1)} %gather_fusion), channel_id=1, source_target_pairs={{0,24},{4,100},{8,0},{12,108},{16,8},{20,116},{24,16},{28,124},{32... | collective-permute-start | bytes 442376 | tf_op jit(solution)/shard_map/ppermute | solution.py:36
  31.5 5.4 %collective-permute-start.2 = (bf16[4,24,768]{2,1,0:T(8,128)(2,1)}, bf16[4,24,768]{2,1,0:T(8,128)(2,1)S(1)}, u32[]{:S(2)}, u32[]{:S(2)}) collective-permute-start(bf16[4,24,768]{2,1,0:T(8,128)(2,1)} %gather_fusion), channel_id=1, source_target_pairs={{0,8},{4,36},{8,16},{12,44},{16,24},{20,52},{24,0},{28,60},{32,40}... | collective-permute-start | bytes 442376 | tf_op jit(solution)/shard_map/ppermute | solution.py:35
  38.0 9.1 %collective-permute-start.3 = (bf16[4,4,24,768]{3,2,1,0:T(8,128)(2,1)S(1)}, bf16[4,4,24,768]{3,2,1,0:T(8,128)(2,1)S(1)}, u32[]{:S(2)}, u32[]{:S(2)}) collective-permute-start(bf16[4,4,24,768]{3,2,1,0:T(8,128)(2,1)S(1)} %get-tuple-element.47), channel_id=1, source_target_pairs={{0,96},{4,28},{8,104},{12,4},{16,112},{20,12},{24,120},{28,20},{32... | collective-permute-start | bytes 1769480 | tf_op jit(solution)/shard_map/ppermute | solution.py:36
  39.8 10.3 %collective-permute-start.4 = (bf16[4,4,24,768]{3,2,1,0:T(8,128)(2,1)S(1)}, bf16[4,4,24,768]{3,2,1,0:T(8,128)(2,1)S(1)}, u32[]{:S(2)}, u32[]{:S(2)}) collective-permute-start(bf16[4,4,24,768]{3,2,1,0:T(8,128)(2,1)S(1)} %get-tuple-element.47), channel_id=1, source_target_pairs={{0,32},{4,12},{8,40},{12,20},{16,48},{20,28},{24,56},{28,4},{32,64... | collective-permute-start | bytes 1769480 | tf_op jit(solution)/shard_map/ppermute | solution.py:35
  47.1 6.8 %collective-permute-start.6 = (bf16[2,4,24,768]{3,2,1,0:T(8,128)(2,1)S(1)}, bf16[2,4,24,768]{3,2,1,0:T(8,128)(2,1)S(1)}, u32[]{:S(2)}, u32[]{:S(2)}) collective-permute-start(bf16[2,4,24,768]{3,2,1,0:T(8,128)(2,1)S(1)} %slice.81), channel_id=1, source_target_pairs={{0,96},{4,28},{8,104},{12,4},{16,112},{20,12},{24,120},{28,20},{32... | collective-permute-start | bytes 884744 | tf_op jit(solution)/shard_map/ppermute | solution.py:41
  50.2 7.1 %collective-permute-start.5 = (bf16[2,4,24,768]{3,2,1,0:T(8,128)(2,1)S(1)}, bf16[2,4,24,768]{3,2,1,0:T(8,128)(2,1)S(1)}, u32[]{:S(2)}, u32[]{:S(2)}) collective-permute-start(bf16[2,4,24,768]{3,2,1,0:T(8,128)(2,1)S(1)} %slice.80), channel_id=1, source_target_pairs={{0,32},{4,12},{8,40},{12,20},{16,48},{20,28},{24,56},{28,4},{32,64... | collective-permute-start | bytes 884744 | tf_op jit(solution)/shard_map/ppermute | solution.py:40
  59.2 7.7 %collective-permute-start.7 = (bf16[4,4,4,24,768]{4,3,2,1,0:T(8,128)(2,1)}, bf16[4,4,4,24,768]{4,3,2,1,0:T(8,128)(2,1)}, u32[]{:S(2)}, u32[]{:S(2)}) collective-permute-start(bf16[4,4,4,24,768]{4,3,2,1,0:T(8,128)(2,1)} %pad_maximum_fusion.1), channel_id=1, source_target_pairs={{0,4},{4,0},{8,12},{12,8},{16,20},{20,16},{24,28},{28,24},{32,36},... | collective-permute-start | bytes 7077896 | tf_op jit(solution)/shard_map/ppermute | solution.py:58
  77.1 3.6 %slice-start = ((s8[4718592]{0:T(1024)(128)(4,1)}), s8[4194304]{0:T(1024)(128)(4,1)S(1)}, s32[]{:S(2)}) async-start(s8[4718592]{0:T(1024)(128)(4,1)} %bitcast.181), calls=%async_computation.1 | async-start | bytes 8388608
  77.1 3.7 %slice-start.1 = ((s8[4718592]{0:T(1024)(128)(4,1)}), s8[524288]{0:T(1024)(128)(4,1)S(1)}, s32[]{:S(2)}) async-start(s8[4718592]{0:T(1024)(128)(4,1)} %bitcast.181), calls=%async_computation.2 | async-start | bytes 1048576
  92.4 16.5 %collective-permute-start.8 = (bf16[2,192,128]{2,1,0:T(8,128)(2,1)S(1)}, bf16[2,192,128]{2,1,0:T(8,128)(2,1)S(1)}, u32[]{:S(2)}, u32[]{:S(2)}) collective-permute-start(bf16[2,192,128]{2,1,0:T(8,128)(2,1)S(1)} %get-tuple-element.19), channel_id=1, source_target_pairs={{0,1},{1,2},{2,3},{3,0},{4,5},{5,6},{6,7},{7,4},{8,9},{9,10},{10,1... | collective-permute-start | bytes 294920 | tf_op jit(solution)/shard_map/ppermute | solution.py:77
  93.8 15.4 %collective-permute-start.9 = (bf16[2,192,128]{2,1,0:T(8,128)(2,1)S(1)}, bf16[2,192,128]{2,1,0:T(8,128)(2,1)S(1)}, u32[]{:S(2)}, u32[]{:S(2)}) collective-permute-start(bf16[2,192,128]{2,1,0:T(8,128)(2,1)S(1)} %get-tuple-element.20), channel_id=1, source_target_pairs={{0,3},{1,0},{2,1},{3,2},{4,7},{5,4},{6,5},{7,6},{8,11},{9,8},{10,9... | collective-permute-start | bytes 294920 | tf_op jit(solution)/shard_map/ppermute | solution.py:77
  95.3 14.3 %collective-permute-start.10 = (bf16[2,192,128]{2,1,0:T(8,128)(2,1)S(1)}, bf16[2,192,128]{2,1,0:T(8,128)(2,1)S(1)}, u32[]{:S(2)}, u32[]{:S(2)}) collective-permute-start(bf16[2,192,128]{2,1,0:T(8,128)(2,1)S(1)} %get-tuple-element.21), channel_id=1, source_target_pairs={{0,2},{1,3},{2,0},{3,1},{4,6},{5,7},{6,4},{7,5},{8,10},{9,11},{10,... | collective-permute-start | bytes 294920 | tf_op jit(solution)/shard_map/ppermute | solution.py:77
  100.3 11.6 %collective-permute-start.11 = (bf16[2,192,256]{2,1,0:T(8,128)(2,1)S(1)}, bf16[2,192,256]{2,1,0:T(8,128)(2,1)S(1)}, u32[]{:S(2)}, u32[]{:S(2)}) collective-permute-start(bf16[2,192,256]{2,1,0:T(8,128)(2,1)S(1)} %get-tuple-element.26), channel_id=1, source_target_pairs={{0,1},{1,2},{2,3},{3,0},{4,5},{5,6},{6,7},{7,4},{8,9},{9,10},{10,1... | collective-permute-start | bytes 589832 | tf_op jit(solution)/shard_map/ppermute | solution.py:77
  100.8 12.7 %collective-permute-start.12 = (bf16[2,192,256]{2,1,0:T(8,128)(2,1)S(1)}, bf16[2,192,256]{2,1,0:T(8,128)(2,1)S(1)}, u32[]{:S(2)}, u32[]{:S(2)}) collective-permute-start(bf16[2,192,256]{2,1,0:T(8,128)(2,1)S(1)} %get-tuple-element.27), channel_id=1, source_target_pairs={{0,3},{1,0},{2,1},{3,2},{4,7},{5,4},{6,5},{7,6},{8,11},{9,8},{10,9... | collective-permute-start | bytes 589832 | tf_op jit(solution)/shard_map/ppermute | solution.py:77
  108.9 6.2 %collective-permute-start.13 = (bf16[2,192,256]{2,1,0:T(8,128)(2,1)S(1)}, bf16[2,192,256]{2,1,0:T(8,128)(2,1)S(1)}, u32[]{:S(2)}, u32[]{:S(2)}) collective-permute-start(bf16[2,192,256]{2,1,0:T(8,128)(2,1)S(1)} %get-tuple-element.28), channel_id=1, source_target_pairs={{0,2},{1,3},{2,0},{3,1},{4,6},{5,7},{6,4},{7,5},{8,10},{9,11},{10,... | collective-permute-start | bytes 589832 | tf_op jit(solution)/shard_map/ppermute | solution.py:77
  109.2 16.0 %collective-permute-start.14 = (bf16[2,192,384]{2,1,0:T(8,128)(2,1)S(1)}, bf16[2,192,384]{2,1,0:T(8,128)(2,1)S(1)}, u32[]{:S(2)}, u32[]{:S(2)}) collective-permute-start(bf16[2,192,384]{2,1,0:T(8,128)(2,1)S(1)} %get-tuple-element.37), channel_id=1, source_target_pairs={{0,1},{1,2},{2,3},{3,0},{4,5},{5,6},{6,7},{7,4},{8,9},{9,10},{10,1... | collective-permute-start | bytes 884744 | tf_op jit(solution)/shard_map/ppermute | solution.py:77
  109.6 15.6 %collective-permute-start.15 = (bf16[2,192,384]{2,1,0:T(8,128)(2,1)S(1)}, bf16[2,192,384]{2,1,0:T(8,128)(2,1)S(1)}, u32[]{:S(2)}, u32[]{:S(2)}) collective-permute-start(bf16[2,192,384]{2,1,0:T(8,128)(2,1)S(1)} %get-tuple-element.38), channel_id=1, source_target_pairs={{0,3},{1,0},{2,1},{3,2},{4,7},{5,4},{6,5},{7,6},{8,11},{9,8},{10,9... | collective-permute-start | bytes 884744 | tf_op jit(solution)/shard_map/ppermute | solution.py:77
  111.9 16.1 %collective-permute-start.16 = (bf16[2,192,384]{2,1,0:T(8,128)(2,1)S(1)}, bf16[2,192,384]{2,1,0:T(8,128)(2,1)S(1)}, u32[]{:S(2)}, u32[]{:S(2)}) collective-permute-start(bf16[2,192,384]{2,1,0:T(8,128)(2,1)S(1)} %get-tuple-element.39), channel_id=1, source_target_pairs={{0,2},{1,3},{2,0},{3,1},{4,6},{5,7},{6,4},{7,5},{8,10},{9,11},{10,... | collective-permute-start | bytes 884744 | tf_op jit(solution)/shard_map/ppermute | solution.py:77
  115.1 14.0 %copy-start.1 = (bf16[2,768,768]{2,1,0:T(8,128)(2,1)S(1)}, bf16[2,768,768]{2,1,0:T(8,128)(2,1)}, u32[]{:S(2)}) copy-start(bf16[2,768,768]{2,1,0:T(8,128)(2,1)} %param.3) | copy-start | bytes 7077892

commit v17 on v13

--- a/solution.py
+++ b/solution.py
@@ -9,7 +9,7 @@
 
 
 RING = 4
-CHUNKS = 6
+CHUNKS = 3
 
 
 def ring_axis(stage, core):
@@ -54,20 +54,16 @@
     picked = pieces.at[owned_slots].get(mode="promise_in_bounds")
     first = ring_gather(picked, sizes, 1, direct_far=True)
     both = ring_gather(first, sizes, 2)
-    swap = [(q, q ^ 1) for q in range(devices)]
-    other = lax.ppermute(both, PAIR, swap)
     chips = nz * nx
-    stacked = jnp.concatenate(
-        [both.reshape((chips,) + both.shape[2:]), other.reshape((chips,) + both.shape[2:])], axis=0
-    )
+    stacked = lax.all_gather(both, "core", axis=0, tiled=False)
+    stacked = stacked.reshape((nc * chips,) + both.shape[2:])
     z = lax.axis_index("z")
     x = lax.axis_index("x")
-    core = lax.axis_index("core")
     q = jnp.arange(devices, dtype=jnp.int32)
     zq, xq, cq = q // (nx * nc), (q // nc) % nx, q % nc
     dz, dx = (zq - z) % nz, (xq - x) % nx
     inner = jnp.where(cq == 0, dz * nx + dx, dx * nz + dz)
-    index = jnp.where(cq == core, 0, chips) + inner
+    index = cq * chips + inner
     ordered = stacked.at[index].get(mode="promise_in_bounds")
     ordered = jnp.transpose(ordered, (1, 0, 2, 3))
     return ordered.reshape(slots, rows, cols)

time: 142 us -> 142 us (level)
  the two profiles are of different devices: /device:TPU:0 before, /device:TPU:1 now
where the time goes in v17:
time: 142 us; the launch traced here: 140 us
  waiting for transfers between devices  64.6 us (45%)
  starting transfers between devices  28.4 us (20%)
  matrix products  17.7 us (12%)
  between operations  13.7 us (10%)
  local copies, waits for them, and re-layouts  10.9 us (8%)
  other arithmetic  4.9 us (3%)
    all_to_all x1, waiting for transfers between devices, gather_slots(): pieces = lax.all_to_all(pieces, PAIR, 0, 0, tiled=True)  17.8 us
    all_gather x1, waiting for transfers between devices, gather_slots(): stacked = lax.all_gather(both, 'core', axis=0, tiled=False)  16.6 us
    ppermute x9, starting transfers between devices, shifted(): lax.ppermute(value, 'vgrp', [(g, (g + step) % groups) for g in range(grou...  11 us
    ppermute x9, waiting for transfers between devices, shifted(): lax.ppermute(value, 'vgrp', [(g, (g + step) % groups) for g in range(grou...  10.8 us
    dot_general x12, matrix products, columns(): jnp.einsum('pad,bd->pab', half_product, vectors[slot, lo:hi], preferred_e...  9.72 us
    all_to_all x1, starting transfers between devices, gather_slots(): pieces = lax.all_to_all(pieces, PAIR, 0, 0, tiled=True)  9.55 us
    dot_general x4, matrix products, on_device(): jnp.einsum('ac,pcd->pad', vectors[slot], amplitudes, preferred_element_ty...  8.01 us
    ppermute x2, waiting for transfers between devices, ring_gather(): from_next = lax.ppermute(piece, PAIR, ring_perm(sizes, stage, -1))  7.2 us
  transfers between devices with their start and end apart: 18, of which 11 were waited for; matrix products, arithmetic and copies ran while one was open for 5% of the time, Pallas kernels for 0%

profile of v17, /device:TPU:1, one launch (start us, length us, event | category | flops | bytes accessed | tf_op | source)
XLA Modules:
  0.0 140.2 jit_solution(7025840156675971797)
XLA Ops:
  6.5 9.6 %all-to-all-start = ((bf16[32,24,768]{2,1,0:T(8,128)(2,1)}), bf16[32,24,768]{2,1,0:T(8,128)(2,1)S(1)}, u32[]{:S(2)}, u32[]{:S(2)}) async-start(bf16[32,24,768]{2,1,0:T(8,128)(2,1)} %bitcast.206), calls=%async_computation | async-start | bytes 2359296 | tf_op jit(solution)/shard_map/all_to_all | solution.py:53
  16.9 17.8 %all-to-all-done = bf16[32,24,768]{2,1,0:T(8,128)(2,1)S(1)} async-done(((bf16[32,24,768]{2,1,0:T(8,128)(2,1)}), bf16[32,24,768]{2,1,0:T(8,128)(2,1)S(1)}, u32[]{:S(2)}, u32[]{:S(2)}) %all-to-all-start) | async-done | bytes 1179680 | tf_op jit(solution)/shard_map/all_to_all | solution.py:53
  34.6 1.2 gather_fusion
  35.8 1.1 collective-permute-start.1
  36.9 1.2 collective-permute-start
  38.4 3.5 %collective-permute-done.1 = bf16[4,24,768]{2,1,0:T(8,128)(2,1)S(1)} collective-permute-done((bf16[4,24,768]{2,1,0:T(8,128)(2,1)}, bf16[4,24,768]{2,1,0:T(8,128)(2,1)S(1)}, u32[]{:S(2)}, u32[]{:S(2)}) %collective-permute-start.1) | collective-permute-done | bytes 147488 | tf_op jit(solution)/shard_map/ppermute | solution.py:38
  41.9 1.6 %collective-permute-done.2 = bf16[4,24,768]{2,1,0:T(8,128)(2,1)S(1)} collective-permute-done((bf16[4,24,768]{2,1,0:T(8,128)(2,1)}, bf16[4,24,768]{2,1,0:T(8,128)(2,1)S(1)}, u32[]{:S(2)}, u32[]{:S(2)}) %collective-permute-start.2) | collective-permute-done | bytes 147488 | tf_op jit(solution)/shard_map/ppermute | solution.py:35
  43.5 1.0 fusion.30
  44.5 1.9 %collective-permute-start.3 = (bf16[4,4,24,768]{3,2,1,0:T(8,128)(2,1)S(1)}, bf16[4,4,24,768]{3,2,1,0:T(8,128)(2,1)S(1)}, u32[]{:S(2)}, u32[]{:S(2)}) collective-permute-start(bf16[4,4,24,768]{3,2,1,0:T(8,128)(2,1)S(1)} %get-tuple-element.47), channel_id=1, source_target_pairs={{0,96},{4,28},{8,104},{12,4},{16,112},{20,12},{24,120},{28,20},{32... | collective-permute-start | bytes 1769480 | tf_op jit(solution)/shard_map/ppermute | solution.py:36
  46.4 7.2 %collective-permute-done.3 = bf16[4,4,24,768]{3,2,1,0:T(8,128)(2,1)S(1)} collective-permute-done((bf16[4,4,24,768]{3,2,1,0:T(8,128)(2,1)S(1)}, bf16[4,4,24,768]{3,2,1,0:T(8,128)(2,1)S(1)}, u32[]{:S(2)}, u32[]{:S(2)}) %collective-permute-start.3) | collective-permute-done | bytes 589856 | tf_op jit(solution)/shard_map/ppermute | solution.py:36
  53.6 3.1 %collective-permute-start.6 = (bf16[2,4,24,768]{3,2,1,0:T(8,128)(2,1)S(1)}, bf16[2,4,24,768]{3,2,1,0:T(8,128)(2,1)S(1)}, u32[]{:S(2)}, u32[]{:S(2)}) collective-permute-start(bf16[2,4,24,768]{3,2,1,0:T(8,128)(2,1)S(1)} %slice.81), channel_id=1, source_target_pairs={{0,96},{4,28},{8,104},{12,4},{16,112},{20,12},{24,120},{28,20},{32... | collective-permute-start | bytes 884744 | tf_op jit(solution)/shard_map/ppermute | solution.py:41
  57.0 3.4 %collective-permute-done.6 = bf16[2,4,24,768]{3,2,1,0:T(8,128)(2,1)S(1)} collective-permute-done((bf16[2,4,24,768]{3,2,1,0:T(8,128)(2,1)S(1)}, bf16[2,4,24,768]{3,2,1,0:T(8,128)(2,1)S(1)}, u32[]{:S(2)}, u32[]{:S(2)}) %collective-permute-start.6) | collective-permute-done | bytes 294944 | tf_op jit(solution)/shard_map/ppermute | solution.py:41
  60.4 3.7 %collective-permute-done.5 = bf16[2,4,24,768]{3,2,1,0:T(8,128)(2,1)S(1)} collective-permute-done((bf16[2,4,24,768]{3,2,1,0:T(8,128)(2,1)S(1)}, bf16[2,4,24,768]{3,2,1,0:T(8,128)(2,1)S(1)}, u32[]{:S(2)}, u32[]{:S(2)}) %collective-permute-start.5) | collective-permute-done | bytes 294944 | tf_op jit(solution)/shard_map/ppermute | solution.py:40
  64.1 1.7 %pad_maximum_fusion = bf16[4,4,4,24,768]{4,3,2,1,0:T(8,128)(2,1)} fusion(bf16[1,4,4,24,768]{4,3,2,1,0:T(8,128)(2,1)S(1)} %bitcast.201, bf16[1,4,4,24,768]{4,3,2,1,0:T(8,128)(2,1)S(1)} %maximum_bitcast_fusion, bf16[1,4,4,24,768]{4,3,2,1,0:T(8,128)(2,1)S(1)} %bitcast.200, bf16[1,4,4,24,768]{4,3,2,1,0:T(8,128)(2,1)S(1)} %get-tuple-element.46), kind=kLoop, calls=%fused_computation.2 | loop fusion | flops 3538944 | bytes 4718592 | tf_op jit(solution)/shard_map/stack | solution.py:43
  66.0 16.6 %all-gather.3.cloned.1.call-done = bf16[8,4,4,24,768]{4,3,2,1,0:T(8,128)(2,1)} async-done(((bf16[4,4,4,24,768]{4,3,2,1,0:T(8,128)(2,1)}), bf16[8,4,4,24,768]{4,3,2,1,0:T(8,128)(2,1)}) %all-gather.3.cloned.1.call-update) | async-done | bytes 4718608 | tf_op jit(solution)/shard_map/all_gather | solution.py:58
  82.6 5.4 %gather_fusion.1 = bf16[32,4,24,768]{3,2,1,0:T(8,128)(2,1)} fusion(bf16[32,4,24,768]{3,2,1,0:T(8,128)(2,1)} %bitcast.193, s32[1024]{0:T(1024)S(1)} %pad_clamp_fusion), kind=kCustom, calls=%fused_computation.1 | custom fusion | bytes 9437312 | tf_op jit(solution)/shard_map/gather | solution.py:67
  87.9 2.8 %copy.23 = bf16[4,32,24,768]{3,2,1,0:T(8,128)(2,1)S(1)} copy(bf16[4,32,24,768]{3,2,0,1:T(8,128)(2,1)} %bitcast.179) | data formatting | bytes 9437184 | tf_op jit(solution)/shard_map/transpose | solution.py:68
  90.7 1.0 copy-done.1
  92.0 2.0 %convert_bitcast_fusion.1 = bf16[2,768,768]{2,1,0:T(8,128)(2,1)S(1)} fusion(bf16[768,768,1]{1,0,2:T(8,128)(2,1)S(1)} %bitcast.205, bf16[2,768,768]{2,1,0:T(8,128)(2,1)S(1)} %copy-done), kind=kOutput, calls=%fused_computation.4 | convolution fusion | flops 1813118976 | bytes 5898240 | tf_op jit(solution)/shard_map/ac,pcd->pad/dot_general | solution.py:113
  94.0 2.0 %convert_bitcast_fusion = bf16[2,768,768]{2,1,0:T(8,128)(2,1)S(1)} fusion(bf16[768,768,1]{1,0,2:T(8,128)(2,1)S(1)} %bitcast.204, bf16[2,768,768]{2,1,0:T(8,128)(2,1)S(1)} %copy-done), kind=kOutput, calls=%fused_computation.3 | convolution fusion | flops 1813118976 | bytes 5898240 | tf_op jit(solution)/shard_map/ac,pcd->pad/dot_general | solution.py:113
  96.0 2.0 %convert_bitcast_fusion.2 = bf16[2,768,768]{2,1,0:T(8,128)(2,1)S(1)} fusion(bf16[768,768,1]{1,0,2:T(8,128)(2,1)S(1)} %bitcast.203, bf16[2,768,768]{2,1,0:T(8,128)(2,1)S(1)} %copy-done), kind=kOutput, calls=%fused_computation.5 | convolution fusion | flops 1813118976 | bytes 5898240 | tf_op jit(solution)/shard_map/ac,pcd->pad/dot_general | solution.py:113
  98.0 2.0 %convert_bitcast_fusion.3 = bf16[2,768,768]{2,1,0:T(8,128)(2,1)S(1)} fusion(bf16[768,768,1]{1,0,2:T(8,128)(2,1)S(1)} %bitcast.202, bf16[2,768,768]{2,1,0:T(8,128)(2,1)S(1)} %copy-done), kind=kOutput, calls=%fused_computation.6 | convolution fusion | flops 1813118976 | bytes 5898240 | tf_op jit(solution)/shard_map/ac,pcd->pad/dot_general | solution.py:113
  103.4 1.4 collective-permute-start.7
  104.8 1.4 collective-permute-start.8
  106.2 1.6 %collective-permute-start.9 = (bf16[2,192,256]{2,1,0:T(8,128)(2,1)S(1)}, bf16[2,192,256]{2,1,0:T(8,128)(2,1)S(1)}, u32[]{:S(2)}, u32[]{:S(2)}) collective-permute-start(bf16[2,192,256]{2,1,0:T(8,128)(2,1)S(1)} %get-tuple-element.21), channel_id=1, source_target_pairs={{0,2},{1,3},{2,0},{3,1},{4,6},{5,7},{6,4},{7,5},{8,10},{9,11},{10,... | collective-permute-start | bytes 589832 | tf_op jit(solution)/shard_map/ppermute | solution.py:73
  111.5 2.4 %collective-permute-start.11 = (bf16[2,192,256]{2,1,0:T(8,128)(2,1)S(1)}, bf16[2,192,256]{2,1,0:T(8,128)(2,1)S(1)}, u32[]{:S(2)}, u32[]{:S(2)}) collective-permute-start(bf16[2,192,256]{2,1,0:T(8,128)(2,1)S(1)} %get-tuple-element.27), channel_id=1, source_target_pairs={{0,3},{1,0},{2,1},{3,2},{4,7},{5,4},{6,5},{7,6},{8,11},{9,8},{10,9... | collective-permute-start | bytes 589832 | tf_op jit(solution)/shard_map/ppermute | solution.py:73
  117.9 2.2 %collective-permute-start.14 = (bf16[2,192,256]{2,1,0:T(8,128)(2,1)S(1)}, bf16[2,192,256]{2,1,0:T(8,128)(2,1)S(1)}, u32[]{:S(2)}, u32[]{:S(2)}) collective-permute-start(bf16[2,192,256]{2,1,0:T(8,128)(2,1)S(1)} %get-tuple-element.38), channel_id=1, source_target_pairs={{0,3},{1,0},{2,1},{3,2},{4,7},{5,4},{6,5},{7,6},{8,11},{9,8},{10,9... | collective-permute-start | bytes 589832 | tf_op jit(solution)/shard_map/ppermute | solution.py:73
  120.9 1.0 collective-permute-start.15
  121.9 1.8 %collective-permute-done.12 = bf16[2,192,256]{2,1,0:T(8,128)(2,1)S(1)} collective-permute-done((bf16[2,192,256]{2,1,0:T(8,128)(2,1)S(1)}, bf16[2,192,256]{2,1,0:T(8,128)(2,1)S(1)}, u32[]{:S(2)}, u32[]{:S(2)}) %collective-permute-start.12) | collective-permute-done | bytes 196640 | tf_op jit(solution)/shard_map/ppermute | solution.py:73
  123.8 7.3 %collective-permute-done.13 = bf16[2,192,256]{2,1,0:T(8,128)(2,1)S(1)} collective-permute-done((bf16[2,192,256]{2,1,0:T(8,128)(2,1)S(1)}, bf16[2,192,256]{2,1,0:T(8,128)(2,1)S(1)}, u32[]{:S(2)}, u32[]{:S(2)}) %collective-permute-start.13) | collective-permute-done | bytes 196640 | tf_op jit(solution)/shard_map/ppermute | solution.py:73
  131.1 1.0 collective-permute-done.15
  132.3 1.1 pad_maximum_fusion.1
  (45 shorter events, 13.7 us)
Async XLA Ops:
  6.5 85.5 %copy-start = (bf16[2,768,768]{2,1,0:T(8,128)(2,1)S(1)}, bf16[2,768,768]{2,1,0:T(8,128)(2,1)}, u32[]{:S(2)}) copy-start(bf16[2,768,768]{2,1,0:T(8,128)(2,1)} %param.3) | copy-start | bytes 7077892
  6.5 28.1 %all-to-all-start = ((bf16[32,24,768]{2,1,0:T(8,128)(2,1)}), bf16[32,24,768]{2,1,0:T(8,128)(2,1)S(1)}, u32[]{:S(2)}, u32[]{:S(2)}) async-start(bf16[32,24,768]{2,1,0:T(8,128)(2,1)} %bitcast.206), calls=%async_computation | async-start | bytes 2359296 | tf_op jit(solution)/shard_map/all_to_all | solution.py:53
  16.1 66.5 %all-gather.3.cloned.1.call-start = ((), (), s32[]{:S(2)}) async-start(), calls=%async_computation.1 | async-start | bytes 7077888 | tf_op jit(solution)/shard_map/all_gather | solution.py:58
  35.8 6.0 %collective-permute-start.1 = (bf16[4,24,768]{2,1,0:T(8,128)(2,1)}, bf16[4,24,768]{2,1,0:T(8,128)(2,1)S(1)}, u32[]{:S(2)}, u32[]{:S(2)}) collective-permute-start(bf16[4,24,768]{2,1,0:T(8,128)(2,1)} %gather_fusion), channel_id=1, source_target_pairs={{0,16},{4,68},{8,24},{12,76},{16,0},{20,84},{24,8},{28,92},{32,48}... | collective-permute-start | bytes 442376 | tf_op jit(solution)/shard_map/ppermute | solution.py:38
  36.9 4.9 %collective-permute-start = (bf16[4,24,768]{2,1,0:T(8,128)(2,1)}, bf16[4,24,768]{2,1,0:T(8,128)(2,1)S(1)}, u32[]{:S(2)}, u32[]{:S(2)}) collective-permute-start(bf16[4,24,768]{2,1,0:T(8,128)(2,1)} %gather_fusion), channel_id=1, source_target_pairs={{0,24},{4,100},{8,0},{12,108},{16,8},{20,116},{24,16},{28,124},{32... | collective-permute-start | bytes 442376 | tf_op jit(solution)/shard_map/ppermute | solution.py:36
  38.1 5.4 %collective-permute-start.2 = (bf16[4,24,768]{2,1,0:T(8,128)(2,1)}, bf16[4,24,768]{2,1,0:T(8,128)(2,1)S(1)}, u32[]{:S(2)}, u32[]{:S(2)}) collective-permute-start(bf16[4,24,768]{2,1,0:T(8,128)(2,1)} %gather_fusion), channel_id=1, source_target_pairs={{0,8},{4,36},{8,16},{12,44},{16,24},{20,52},{24,0},{28,60},{32,40}... | collective-permute-start | bytes 442376 | tf_op jit(solution)/shard_map/ppermute | solution.py:35
  44.5 9.1 %collective-permute-start.3 = (bf16[4,4,24,768]{3,2,1,0:T(8,128)(2,1)S(1)}, bf16[4,4,24,768]{3,2,1,0:T(8,128)(2,1)S(1)}, u32[]{:S(2)}, u32[]{:S(2)}) collective-permute-start(bf16[4,4,24,768]{3,2,1,0:T(8,128)(2,1)S(1)} %get-tuple-element.47), channel_id=1, source_target_pairs={{0,96},{4,28},{8,104},{12,4},{16,112},{20,12},{24,120},{28,20},{32... | collective-permute-start | bytes 1769480 | tf_op jit(solution)/shard_map/ppermute | solution.py:36
  46.4 10.3 %collective-permute-start.4 = (bf16[4,4,24,768]{3,2,1,0:T(8,128)(2,1)S(1)}, bf16[4,4,24,768]{3,2,1,0:T(8,128)(2,1)S(1)}, u32[]{:S(2)}, u32[]{:S(2)}) collective-permute-start(bf16[4,4,24,768]{3,2,1,0:T(8,128)(2,1)S(1)} %get-tuple-element.47), channel_id=1, source_target_pairs={{0,32},{4,12},{8,40},{12,20},{16,48},{20,28},{24,56},{28,4},{32,64... | collective-permute-start | bytes 1769480 | tf_op jit(solution)/shard_map/ppermute | solution.py:35
  53.6 6.8 %collective-permute-start.6 = (bf16[2,4,24,768]{3,2,1,0:T(8,128)(2,1)S(1)}, bf16[2,4,24,768]{3,2,1,0:T(8,128)(2,1)S(1)}, u32[]{:S(2)}, u32[]{:S(2)}) collective-permute-start(bf16[2,4,24,768]{3,2,1,0:T(8,128)(2,1)S(1)} %slice.81), channel_id=1, source_target_pairs={{0,96},{4,28},{8,104},{12,4},{16,112},{20,12},{24,120},{28,20},{32... | collective-permute-start | bytes 884744 | tf_op jit(solution)/shard_map/ppermute | solution.py:41
  56.7 7.3 %collective-permute-start.5 = (bf16[2,4,24,768]{3,2,1,0:T(8,128)(2,1)S(1)}, bf16[2,4,24,768]{3,2,1,0:T(8,128)(2,1)S(1)}, u32[]{:S(2)}, u32[]{:S(2)}) collective-permute-start(bf16[2,4,24,768]{3,2,1,0:T(8,128)(2,1)S(1)} %slice.80), channel_id=1, source_target_pairs={{0,32},{4,12},{8,40},{12,20},{16,48},{20,28},{24,56},{28,4},{32,64... | collective-permute-start | bytes 884744 | tf_op jit(solution)/shard_map/ppermute | solution.py:40
  87.9 3.8 %copy-start.1 = (bf16[32,4,24,768]{3,2,1,0:T(8,128)(2,1)S(1)}, bf16[32,4,24,768]{3,2,1,0:T(8,128)(2,1)}, u32[]{:S(2)}) copy-start(bf16[32,4,24,768]{3,2,1,0:T(8,128)(2,1)} %gather_fusion.1) | copy-start | bytes 14155780
  103.4 13.8 %collective-permute-start.7 = (bf16[2,192,256]{2,1,0:T(8,128)(2,1)S(1)}, bf16[2,192,256]{2,1,0:T(8,128)(2,1)S(1)}, u32[]{:S(2)}, u32[]{:S(2)}) collective-permute-start(bf16[2,192,256]{2,1,0:T(8,128)(2,1)S(1)} %get-tuple-element.19), channel_id=1, source_target_pairs={{0,1},{1,2},{2,3},{3,0},{4,5},{5,6},{6,7},{7,4},{8,9},{9,10},{10,1... | collective-permute-start | bytes 589832 | tf_op jit(solution)/shard_map/ppermute | solution.py:73
  104.8 12.7 %collective-permute-start.8 = (bf16[2,192,256]{2,1,0:T(8,128)(2,1)S(1)}, bf16[2,192,256]{2,1,0:T(8,128)(2,1)S(1)}, u32[]{:S(2)}, u32[]{:S(2)}) collective-permute-start(bf16[2,192,256]{2,1,0:T(8,128)(2,1)S(1)} %get-tuple-element.20), channel_id=1, source_target_pairs={{0,3},{1,0},{2,1},{3,2},{4,7},{5,4},{6,5},{7,6},{8,11},{9,8},{10,9... | collective-permute-start | bytes 589832 | tf_op jit(solution)/shard_map/ppermute | solution.py:73
  106.2 11.7 %collective-permute-start.9 = (bf16[2,192,256]{2,1,0:T(8,128)(2,1)S(1)}, bf16[2,192,256]{2,1,0:T(8,128)(2,1)S(1)}, u32[]{:S(2)}, u32[]{:S(2)}) collective-permute-start(bf16[2,192,256]{2,1,0:T(8,128)(2,1)S(1)} %get-tuple-element.21), channel_id=1, source_target_pairs={{0,2},{1,3},{2,0},{3,1},{4,6},{5,7},{6,4},{7,5},{8,10},{9,11},{10,... | collective-permute-start | bytes 589832 | tf_op jit(solution)/shard_map/ppermute | solution.py:73
  111.1 9.8 %collective-permute-start.10 = (bf16[2,192,256]{2,1,0:T(8,128)(2,1)S(1)}, bf16[2,192,256]{2,1,0:T(8,128)(2,1)S(1)}, u32[]{:S(2)}, u32[]{:S(2)}) collective-permute-start(bf16[2,192,256]{2,1,0:T(8,128)(2,1)S(1)} %get-tuple-element.26), channel_id=1, source_target_pairs={{0,1},{1,2},{2,3},{3,0},{4,5},{5,6},{6,7},{7,4},{8,9},{9,10},{10,1... | collective-permute-start | bytes 589832 | tf_op jit(solution)/shard_map/ppermute | solution.py:73
  111.5 10.4 %collective-permute-start.11 = (bf16[2,192,256]{2,1,0:T(8,128)(2,1)S(1)}, bf16[2,192,256]{2,1,0:T(8,128)(2,1)S(1)}, u32[]{:S(2)}, u32[]{:S(2)}) collective-permute-start(bf16[2,192,256]{2,1,0:T(8,128)(2,1)S(1)} %get-tuple-element.27), channel_id=1, source_target_pairs={{0,3},{1,0},{2,1},{3,2},{4,7},{5,4},{6,5},{7,6},{8,11},{9,8},{10,9... | collective-permute-start | bytes 589832 | tf_op jit(solution)/shard_map/ppermute | solution.py:73
  117.2 6.5 %collective-permute-start.12 = (bf16[2,192,256]{2,1,0:T(8,128)(2,1)S(1)}, bf16[2,192,256]{2,1,0:T(8,128)(2,1)S(1)}, u32[]{:S(2)}, u32[]{:S(2)}) collective-permute-start(bf16[2,192,256]{2,1,0:T(8,128)(2,1)S(1)} %get-tuple-element.28), channel_id=1, source_target_pairs={{0,2},{1,3},{2,0},{3,1},{4,6},{5,7},{6,4},{7,5},{8,10},{9,11},{10,... | collective-permute-start | bytes 589832 | tf_op jit(solution)/shard_map/ppermute | solution.py:73
  117.5 13.7 %collective-permute-start.13 = (bf16[2,192,256]{2,1,0:T(8,128)(2,1)S(1)}, bf16[2,192,256]{2,1,0:T(8,128)(2,1)S(1)}, u32[]{:S(2)}, u32[]{:S(2)}) collective-permute-start(bf16[2,192,256]{2,1,0:T(8,128)(2,1)S(1)} %get-tuple-element.37), channel_id=1, source_target_pairs={{0,1},{1,2},{2,3},{3,0},{4,5},{5,6},{6,7},{7,4},{8,9},{9,10},{10,1... | collective-permute-start | bytes 589832 | tf_op jit(solution)/shard_map/ppermute | solution.py:73
  117.9 13.2 %collective-permute-start.14 = (bf16[2,192,256]{2,1,0:T(8,128)(2,1)S(1)}, bf16[2,192,256]{2,1,0:T(8,128)(2,1)S(1)}, u32[]{:S(2)}, u32[]{:S(2)}) collective-permute-start(bf16[2,192,256]{2,1,0:T(8,128)(2,1)S(1)} %get-tuple-element.38), channel_id=1, source_target_pairs={{0,3},{1,0},{2,1},{3,2},{4,7},{5,4},{6,5},{7,6},{8,11},{9,8},{10,9... | collective-permute-start | bytes 589832 | tf_op jit(solution)/shard_map/ppermute | solution.py:73
  120.9 11.3 %collective-permute-start.15 = (bf16[2,192,256]{2,1,0:T(8,128)(2,1)S(1)}, bf16[2,192,256]{2,1,0:T(8,128)(2,1)S(1)}, u32[]{:S(2)}, u32[]{:S(2)}) collective-permute-start(bf16[2,192,256]{2,1,0:T(8,128)(2,1)S(1)} %get-tuple-element.39), channel_id=1, source_target_pairs={{0,2},{1,3},{2,0},{3,1},{4,6},{5,7},{6,4},{7,5},{8,10},{9,11},{10,... | collective-permute-start | bytes 589832 | tf_op jit(solution)/shard_map/ppermute | solution.py:73
Sparse Core Ops, SparseCore 0:
  66.0 16.5 all-gather.2

commit v18 on v17

--- a/solution.py
+++ b/solution.py
@@ -40,7 +40,7 @@
         far_low = lax.ppermute(from_prev[:half], PAIR, ring_perm(sizes, stage, 1))
         far_high = lax.ppermute(from_next[half:], PAIR, ring_perm(sizes, stage, -1))
         far = jnp.concatenate([far_low, far_high], axis=0)
-    return jnp.stack([piece, from_next, far, from_prev], axis=0)
+    return [piece, from_next, far, from_prev]
 
 
 def gather_slots(own_vector, owned_slots, sizes):
@@ -52,18 +52,20 @@
     pieces = own_vector.reshape(devices, piece, cols)
     pieces = lax.all_to_all(pieces, PAIR, 0, 0, tiled=True)
     picked = pieces.at[owned_slots].get(mode="promise_in_bounds")
-    first = ring_gather(picked, sizes, 1, direct_far=True)
+    first = jnp.stack(ring_gather(picked, sizes, 1, direct_far=True), axis=0)
     both = ring_gather(first, sizes, 2)
+    swap = [(q, q ^ 1) for q in range(devices)]
+    other = [lax.ppermute(part, PAIR, swap) for part in both]
     chips = nz * nx
-    stacked = lax.all_gather(both, "core", axis=0, tiled=False)
-    stacked = stacked.reshape((nc * chips,) + both.shape[2:])
+    stacked = jnp.concatenate(both + other, axis=0)
     z = lax.axis_index("z")
     x = lax.axis_index("x")
+    core = lax.axis_index("core")
     q = jnp.arange(devices, dtype=jnp.int32)
     zq, xq, cq = q // (nx * nc), (q // nc) % nx, q % nc
     dz, dx = (zq - z) % nz, (xq - x) % nx
     inner = jnp.where(cq == 0, dz * nx + dx, dx * nz + dz)
-    index = cq * chips + inner
+    index = jnp.where(cq == core, 0, chips) + inner
     ordered = stacked.at[index].get(mode="promise_in_bounds")
     ordered = jnp.transpose(ordered, (1, 0, 2, 3))
     return ordered.reshape(slots, rows, cols)

time: 142 us -> 118 us (0.83)
  waiting for transfers between devices: 64.6 us -> 35.6 us
  between operations: 13.7 us -> 0.34 us
  starting transfers between devices: 28.4 us -> 38.9 us
  local copies, waits for them, and re-layouts: 10.9 us -> 21.1 us
  other arithmetic: 4.9 us -> 3.14 us
    all_gather x1 -> x0, waiting for transfers between devices: 16.6 us -> none  [gather_slots(): stacked = lax.all_gather(both, 'core', axis=0, tiled=False)]
    ppermute x0 -> x4, starting transfers between devices: none -> 10.3 us  [gather_slots(): other = [lax.ppermute(part, PAIR, swap) for part in both]]
    unnamed x4 -> x15, local copies, waits for them, and re-layouts: 0.96 us -> 10.3 us
    ppermute x2, waiting for transfers between devices: 7.2 us -> 0.01 us  [ring_gather(): from_next = lax.ppermute(piece, PAIR, ring_perm(sizes, stage, -1))]
    ppermute x1, waiting for transfers between devices: 3.69 us -> 0.01 us  [ring_gather(): far_low = lax.ppermute(from_prev[:half], PAIR, ring_perm(sizes, stage, 1))]
    ppermute x1, waiting for transfers between devices: 3.38 us -> 0.01 us  [ring_gather(): far_high = lax.ppermute(from_next[half:], PAIR, ring_perm(sizes, stage, -1))]
    another operation x3 -> x1, other arithmetic: 2.79 us -> 0.98 us  [gather_slots(): first = jnp.stack(ring_gather(picked, sizes, 1, direct_far=True), axis=0)]
    ppermute x2, waiting for transfers between devices: 1.63 us -> 3.21 us  [ring_gather(): from_prev = lax.ppermute(piece, PAIR, ring_perm(sizes, stage, 1))]
  transfers between devices with their start and end apart: 18 -> 21, of which waited for: 11 -> 8; matrix products, arithmetic and copies ran while one was open for 5% -> 15% of each run, Pallas kernels for 0% -> 0%
where the time goes in v18:
time: 118 us; the launch traced here: 117 us
  starting transfers between devices  38.9 us (33%)
  waiting for transfers between devices  35.6 us (30%)
  local copies, waits for them, and re-layouts  21.1 us (18%)
  matrix products  17.7 us (15%)
  other arithmetic  3.14 us (3%)
    all_to_all x1, waiting for transfers between devices, gather_slots(): pieces = lax.all_to_all(pieces, PAIR, 0, 0, tiled=True)  17.8 us
    ppermute x9, waiting for transfers between devices, shifted(): lax.ppermute(value, 'vgrp', [(g, (g + step) % groups) for g in range(grou...  11.2 us
    ppermute x9, starting transfers between devices, shifted(): lax.ppermute(value, 'vgrp', [(g, (g + step) % groups) for g in range(grou...  11 us
    unnamed x15, local copies, waits for them, and re-layouts  10.3 us
    ppermute x4, starting transfers between devices, gather_slots(): other = [lax.ppermute(part, PAIR, swap) for part in both]  10.3 us
    dot_general x12, matrix products, columns(): jnp.einsum('pad,bd->pab', half_product, vectors[slot, lo:hi], preferred_e...  9.72 us
    all_to_all x1, starting transfers between devices, gather_slots(): pieces = lax.all_to_all(pieces, PAIR, 0, 0, tiled=True)  9.55 us
    dot_general x4, matrix products, on_device(): jnp.einsum('ac,pcd->pad', vectors[slot], amplitudes, preferred_element_ty...  8.01 us
  transfers between devices with their start and end apart: 21, of which 8 were waited for; matrix products, arithmetic and copies ran while one was open for 15% of the time, Pallas kernels for 0%

profile of v18, /device:TPU:1, one launch (start us, length us, event | category | flops | bytes accessed | tf_op | source)
XLA Modules:
  0.0 116.8 jit_solution(10350788220732600473)
XLA Ops:
  0.0 9.6 %all-to-all-start = ((bf16[32,24,768]{2,1,0:T(8,128)(2,1)}), bf16[32,24,768]{2,1,0:T(8,128)(2,1)S(1)}, u32[]{:S(2)}, u32[]{:S(2)}) async-start(bf16[32,24,768]{2,1,0:T(8,128)(2,1)} %bitcast.201), calls=%async_computation | async-start | bytes 2359296 | tf_op jit(solution)/shard_map/all_to_all | solution.py:53
  10.3 17.8 %all-to-all-done = bf16[32,24,768]{2,1,0:T(8,128)(2,1)S(1)} async-done(((bf16[32,24,768]{2,1,0:T(8,128)(2,1)}), bf16[32,24,768]{2,1,0:T(8,128)(2,1)S(1)}, u32[]{:S(2)}, u32[]{:S(2)}) %all-to-all-start) | async-done | bytes 1179680 | tf_op jit(solution)/shard_map/all_to_all | solution.py:53
  28.1 1.2 %gather_fusion = bf16[4,24,768]{2,1,0:T(8,128)(2,1)} fusion(bf16[32,24,768]{2,1,0:T(8,128)(2,1)S(1)} %all-to-all-done, s32[1024]{0:T(1024)S(1)} %pad_clamp_fusion.1), kind=kCustom, calls=%fused_computation | custom fusion | bytes 294928 | tf_op jit(solution)/shard_map/gather | solution.py:54
  29.3 1.1 collective-permute-start.1
  30.4 1.2 collective-permute-start
  31.9 3.4 %collective-permute-done.1 = bf16[4,24,768]{2,1,0:T(8,128)(2,1)S(1)} collective-permute-done((bf16[4,24,768]{2,1,0:T(8,128)(2,1)}, bf16[4,24,768]{2,1,0:T(8,128)(2,1)S(1)}, u32[]{:S(2)}, u32[]{:S(2)}) %collective-permute-start.1) | collective-permute-done | bytes 147488 | tf_op jit(solution)/shard_map/ppermute | solution.py:38
  35.3 1.6 %collective-permute-done.2 = bf16[4,24,768]{2,1,0:T(8,128)(2,1)S(1)} collective-permute-done((bf16[4,24,768]{2,1,0:T(8,128)(2,1)}, bf16[4,24,768]{2,1,0:T(8,128)(2,1)S(1)}, u32[]{:S(2)}, u32[]{:S(2)}) %collective-permute-start.2) | collective-permute-done | bytes 147488 | tf_op jit(solution)/shard_map/ppermute | solution.py:35
  36.9 1.0 pad_maximum_fusion.1
  37.9 1.1 collective-permute-start.4
  39.0 1.7 %collective-permute-start.3 = (bf16[4,4,24,768]{3,2,1,0:T(8,128)(2,1)S(1)}, bf16[4,4,24,768]{3,2,1,0:T(8,128)(2,1)S(1)}, u32[]{:S(2)}, u32[]{:S(2)}) collective-permute-start(bf16[4,4,24,768]{3,2,1,0:T(8,128)(2,1)S(1)} %pad_maximum_fusion.1), channel_id=1, source_target_pairs={{0,96},{4,28},{8,104},{12,4},{16,112},{20,12},{24,120},{28,20},{32... | collective-permute-start | bytes 1769480 | tf_op jit(solution)/shard_map/ppermute | solution.py:36
  40.7 1.6 %constant_dynamic-update-slice_fusion.11 = bf16[32,4,24,768]{3,2,1,0:T(8,128)(2,1)} fusion(bf16[4,24,768]{2,1,0:T(8,128)(2,1)} %gather_fusion), kind=kLoop, calls=%fused_computation.68 | loop fusion | bytes 294912
  42.3 3.1 %collective-permute-start.7 = (bf16[4,4,24,768]{3,2,1,0:T(8,128)(2,1)S(1)}, bf16[4,4,24,768]{3,2,1,0:T(8,128)(2,1)S(1)}, u32[]{:S(2)}, u32[]{:S(2)}) collective-permute-start(bf16[4,4,24,768]{3,2,1,0:T(8,128)(2,1)S(1)} %pad_maximum_fusion.1), channel_id=1, source_target_pairs={{0,4},{4,0},{8,12},{12,8},{16,20},{20,16},{24,28},{28,24},{32,36},... | collective-permute-start | bytes 1769480 | tf_op jit(solution)/shard_map/ppermute | solution.py:58
  46.7 1.6 %collective-permute-done.4 = bf16[4,4,24,768]{3,2,1,0:T(8,128)(2,1)S(1)} collective-permute-done((bf16[4,4,24,768]{3,2,1,0:T(8,128)(2,1)S(1)}, bf16[4,4,24,768]{3,2,1,0:T(8,128)(2,1)S(1)}, u32[]{:S(2)}, u32[]{:S(2)}) %collective-permute-start.4) | collective-permute-done | bytes 589856 | tf_op jit(solution)/shard_map/ppermute | solution.py:35
  48.4 2.7 %collective-permute-start.6 = (bf16[2,4,24,768]{3,2,1,0:T(8,128)(2,1)S(1)}, bf16[2,4,24,768]{3,2,1,0:T(8,128)(2,1)S(1)}, u32[]{:S(2)}, u32[]{:S(2)}) collective-permute-start(bf16[2,4,24,768]{3,2,1,0:T(8,128)(2,1)S(1)} %slice.81), channel_id=1, source_target_pairs={{0,96},{4,28},{8,104},{12,4},{16,112},{20,12},{24,120},{28,20},{32... | collective-permute-start | bytes 884744 | tf_op jit(solution)/shard_map/ppermute | solution.py:41
  51.8 3.9 %collective-permute-start.10 = (bf16[4,4,24,768]{3,2,1,0:T(8,128)(2,1)S(1)}, bf16[4,4,24,768]{3,2,1,0:T(8,128)(2,1)S(1)}, u32[]{:S(2)}, u32[]{:S(2)}) collective-permute-start(bf16[4,4,24,768]{3,2,1,0:T(8,128)(2,1)S(1)} %collective-permute-done.4), channel_id=1, source_target_pairs={{0,4},{4,0},{8,12},{12,8},{16,20},{20,16},{24,28},{28,24},{32,36},... | collective-permute-start | bytes 1769480 | tf_op jit(solution)/shard_map/ppermute | solution.py:58
  56.6 3.3 %collective-permute-start.9 = (bf16[4,4,24,768]{3,2,1,0:T(8,128)(2,1)S(1)}, bf16[4,4,24,768]{3,2,1,0:T(8,128)(2,1)S(1)}, u32[]{:S(2)}, u32[]{:S(2)}) collective-permute-start(bf16[4,4,24,768]{3,2,1,0:T(8,128)(2,1)S(1)} %pad_maximum_fusion.2), channel_id=1, source_target_pairs={{0,4},{4,0},{8,12},{12,8},{16,20},{20,16},{24,28},{28,24},{32,36},... | collective-permute-start | bytes 1769480 | tf_op jit(solution)/shard_map/ppermute | solution.py:58
  65.7 5.4 %gather_fusion.1 = bf16[32,4,24,768]{3,2,1,0:T(8,128)(2,1)} fusion(bf16[32,4,24,768]{3,2,1,0:T(8,128)(2,1)} %constant_dynamic-update-slice_fusion, s32[1024]{0:T(1024)S(1)} %pad_clamp_fusion), kind=kCustom, calls=%fused_computation.1 | custom fusion | bytes 9437312 | tf_op jit(solution)/shard_map/gather | solution.py:69
  71.1 2.8 %copy.13 = bf16[4,32,24,768]{3,2,1,0:T(8,128)(2,1)S(1)} copy(bf16[4,32,24,768]{3,2,0,1:T(8,128)(2,1)} %bitcast.176) | data formatting | bytes 9437184 | tf_op jit(solution)/shard_map/transpose | solution.py:70
  73.9 1.0 copy-done.1
  75.2 2.0 %convert_bitcast_fusion.1 = bf16[2,768,768]{2,1,0:T(8,128)(2,1)S(1)} fusion(bf16[768,768,1]{1,0,2:T(8,128)(2,1)S(1)} %bitcast.200, bf16[2,768,768]{2,1,0:T(8,128)(2,1)S(1)} %copy-done), kind=kOutput, calls=%fused_computation.3 | convolution fusion | flops 1813118976 | bytes 5898240 | tf_op jit(solution)/shard_map/ac,pcd->pad/dot_general | solution.py:115
  77.2 2.0 %convert_bitcast_fusion = bf16[2,768,768]{2,1,0:T(8,128)(2,1)S(1)} fusion(bf16[768,768,1]{1,0,2:T(8,128)(2,1)S(1)} %bitcast.199, bf16[2,768,768]{2,1,0:T(8,128)(2,1)S(1)} %copy-done), kind=kOutput, calls=%fused_computation.2 | convolution fusion | flops 1813118976 | bytes 5898240 | tf_op jit(solution)/shard_map/ac,pcd->pad/dot_general | solution.py:115
  79.2 2.0 %convert_bitcast_fusion.2 = bf16[2,768,768]{2,1,0:T(8,128)(2,1)S(1)} fusion(bf16[768,768,1]{1,0,2:T(8,128)(2,1)S(1)} %bitcast.198, bf16[2,768,768]{2,1,0:T(8,128)(2,1)S(1)} %copy-done), kind=kOutput, calls=%fused_computation.4 | convolution fusion | flops 1813118976 | bytes 5898240 | tf_op jit(solution)/shard_map/ac,pcd->pad/dot_general | solution.py:115
  81.2 2.0 %convert_bitcast_fusion.3 = bf16[2,768,768]{2,1,0:T(8,128)(2,1)S(1)} fusion(bf16[768,768,1]{1,0,2:T(8,128)(2,1)S(1)} %bitcast.197, bf16[2,768,768]{2,1,0:T(8,128)(2,1)S(1)} %copy-done), kind=kOutput, calls=%fused_computation.5 | convolution fusion | flops 1813118976 | bytes 5898240 | tf_op jit(solution)/shard_map/ac,pcd->pad/dot_general | solution.py:115
  86.6 1.4 %collective-permute-start.11 = (bf16[2,192,256]{2,1,0:T(8,128)(2,1)S(1)}, bf16[2,192,256]{2,1,0:T(8,128)(2,1)S(1)}, u32[]{:S(2)}, u32[]{:S(2)}) collective-permute-start(bf16[2,192,256]{2,1,0:T(8,128)(2,1)S(1)} %get-tuple-element.19), channel_id=1, source_target_pairs={{0,1},{1,2},{2,3},{3,0},{4,5},{5,6},{6,7},{7,4},{8,9},{9,10},{10,1... | collective-permute-start | bytes 589832 | tf_op jit(solution)/shard_map/ppermute | solution.py:75
  87.9 1.5 %collective-permute-start.12 = (bf16[2,192,256]{2,1,0:T(8,128)(2,1)S(1)}, bf16[2,192,256]{2,1,0:T(8,128)(2,1)S(1)}, u32[]{:S(2)}, u32[]{:S(2)}) collective-permute-start(bf16[2,192,256]{2,1,0:T(8,128)(2,1)S(1)} %get-tuple-element.20), channel_id=1, source_target_pairs={{0,3},{1,0},{2,1},{3,2},{4,7},{5,4},{6,5},{7,6},{8,11},{9,8},{10,9... | collective-permute-start | bytes 589832 | tf_op jit(solution)/shard_map/ppermute | solution.py:75
  89.4 1.6 %collective-permute-start.13 = (bf16[2,192,256]{2,1,0:T(8,128)(2,1)S(1)}, bf16[2,192,256]{2,1,0:T(8,128)(2,1)S(1)}, u32[]{:S(2)}, u32[]{:S(2)}) collective-permute-start(bf16[2,192,256]{2,1,0:T(8,128)(2,1)S(1)} %get-tuple-element.21), channel_id=1, source_target_pairs={{0,2},{1,3},{2,0},{3,1},{4,6},{5,7},{6,4},{7,5},{8,10},{9,11},{10,... | collective-permute-start | bytes 589832 | tf_op jit(solution)/shard_map/ppermute | solution.py:75
  94.8 2.3 %collective-permute-start.15 = (bf16[2,192,256]{2,1,0:T(8,128)(2,1)S(1)}, bf16[2,192,256]{2,1,0:T(8,128)(2,1)S(1)}, u32[]{:S(2)}, u32[]{:S(2)}) collective-permute-start(bf16[2,192,256]{2,1,0:T(8,128)(2,1)S(1)} %get-tuple-element.27), channel_id=1, source_target_pairs={{0,3},{1,0},{2,1},{3,2},{4,7},{5,4},{6,5},{7,6},{8,11},{9,8},{10,9... | collective-permute-start | bytes 589832 | tf_op jit(solution)/shard_map/ppermute | solution.py:75
  101.1 2.3 %collective-permute-start.18 = (bf16[2,192,256]{2,1,0:T(8,128)(2,1)S(1)}, bf16[2,192,256]{2,1,0:T(8,128)(2,1)S(1)}, u32[]{:S(2)}, u32[]{:S(2)}) collective-permute-start(bf16[2,192,256]{2,1,0:T(8,128)(2,1)S(1)} %get-tuple-element.38), channel_id=1, source_target_pairs={{0,3},{1,0},{2,1},{3,2},{4,7},{5,4},{6,5},{7,6},{8,11},{9,8},{10,9... | collective-permute-start | bytes 589832 | tf_op jit(solution)/shard_map/ppermute | solution.py:75
  105.2 2.0 %collective-permute-done.16 = bf16[2,192,256]{2,1,0:T(8,128)(2,1)S(1)} collective-permute-done((bf16[2,192,256]{2,1,0:T(8,128)(2,1)S(1)}, bf16[2,192,256]{2,1,0:T(8,128)(2,1)S(1)}, u32[]{:S(2)}, u32[]{:S(2)}) %collective-permute-start.16) | collective-permute-done | bytes 196640 | tf_op jit(solution)/shard_map/ppermute | solution.py:75
  107.3 7.1 %collective-permute-done.17 = bf16[2,192,256]{2,1,0:T(8,128)(2,1)S(1)} collective-permute-done((bf16[2,192,256]{2,1,0:T(8,128)(2,1)S(1)}, bf16[2,192,256]{2,1,0:T(8,128)(2,1)S(1)}, u32[]{:S(2)}, u32[]{:S(2)}) %collective-permute-start.17) | collective-permute-done | bytes 196640 | tf_op jit(solution)/shard_map/ppermute | solution.py:75
  114.4 1.2 %collective-permute-done.19 = bf16[2,192,256]{2,1,0:T(8,128)(2,1)S(1)} collective-permute-done((bf16[2,192,256]{2,1,0:T(8,128)(2,1)S(1)}, bf16[2,192,256]{2,1,0:T(8,128)(2,1)S(1)}, u32[]{:S(2)}, u32[]{:S(2)}) %collective-permute-start.19) | collective-permute-done | bytes 196640 | tf_op jit(solution)/shard_map/ppermute | solution.py:75
  115.7 1.1 pad_maximum_fusion
  (61 shorter events, 23.2 us)
Async XLA Ops:
  0.0 75.2 %copy-start = (bf16[2,768,768]{2,1,0:T(8,128)(2,1)S(1)}, bf16[2,768,768]{2,1,0:T(8,128)(2,1)}, u32[]{:S(2)}) copy-start(bf16[2,768,768]{2,1,0:T(8,128)(2,1)} %param.3) | copy-start | bytes 7077892
  0.0 28.1 %all-to-all-start = ((bf16[32,24,768]{2,1,0:T(8,128)(2,1)}), bf16[32,24,768]{2,1,0:T(8,128)(2,1)S(1)}, u32[]{:S(2)}, u32[]{:S(2)}) async-start(bf16[32,24,768]{2,1,0:T(8,128)(2,1)} %bitcast.201), calls=%async_computation | async-start | bytes 2359296 | tf_op jit(solution)/shard_map/all_to_all | solution.py:53
  29.3 6.0 %collective-permute-start.1 = (bf16[4,24,768]{2,1,0:T(8,128)(2,1)}, bf16[4,24,768]{2,1,0:T(8,128)(2,1)S(1)}, u32[]{:S(2)}, u32[]{:S(2)}) collective-permute-start(bf16[4,24,768]{2,1,0:T(8,128)(2,1)} %gather_fusion), channel_id=1, source_target_pairs={{0,16},{4,68},{8,24},{12,76},{16,0},{20,84},{24,8},{28,92},{32,48}... | collective-permute-start | bytes 442376 | tf_op jit(solution)/shard_map/ppermute | solution.py:38
  30.4 4.9 %collective-permute-start = (bf16[4,24,768]{2,1,0:T(8,128)(2,1)}, bf16[4,24,768]{2,1,0:T(8,128)(2,1)S(1)}, u32[]{:S(2)}, u32[]{:S(2)}) collective-permute-start(bf16[4,24,768]{2,1,0:T(8,128)(2,1)} %gather_fusion), channel_id=1, source_target_pairs={{0,24},{4,100},{8,0},{12,108},{16,8},{20,116},{24,16},{28,124},{32... | collective-permute-start | bytes 442376 | tf_op jit(solution)/shard_map/ppermute | solution.py:36
  31.5 5.4 %collective-permute-start.2 = (bf16[4,24,768]{2,1,0:T(8,128)(2,1)}, bf16[4,24,768]{2,1,0:T(8,128)(2,1)S(1)}, u32[]{:S(2)}, u32[]{:S(2)}) collective-permute-start(bf16[4,24,768]{2,1,0:T(8,128)(2,1)} %gather_fusion), channel_id=1, source_target_pairs={{0,8},{4,36},{8,16},{12,44},{16,24},{20,52},{24,0},{28,60},{32,40}... | collective-permute-start | bytes 442376 | tf_op jit(solution)/shard_map/ppermute | solution.py:35
  37.9 10.3 %collective-permute-start.4 = (bf16[4,4,24,768]{3,2,1,0:T(8,128)(2,1)S(1)}, bf16[4,4,24,768]{3,2,1,0:T(8,128)(2,1)S(1)}, u32[]{:S(2)}, u32[]{:S(2)}) collective-permute-start(bf16[4,4,24,768]{3,2,1,0:T(8,128)(2,1)S(1)} %pad_maximum_fusion.1), channel_id=1, source_target_pairs={{0,32},{4,12},{8,40},{12,20},{16,48},{20,28},{24,56},{28,4},{32,64... | collective-permute-start | bytes 1769480 | tf_op jit(solution)/shard_map/ppermute | solution.py:35
  39.0 9.4 %collective-permute-start.3 = (bf16[4,4,24,768]{3,2,1,0:T(8,128)(2,1)S(1)}, bf16[4,4,24,768]{3,2,1,0:T(8,128)(2,1)S(1)}, u32[]{:S(2)}, u32[]{:S(2)}) collective-permute-start(bf16[4,4,24,768]{3,2,1,0:T(8,128)(2,1)S(1)} %pad_maximum_fusion.1), channel_id=1, source_target_pairs={{0,96},{4,28},{8,104},{12,4},{16,112},{20,12},{24,120},{28,20},{32... | collective-permute-start | bytes 1769480 | tf_op jit(solution)/shard_map/ppermute | solution.py:36
  42.3 20.0 %collective-permute-start.7 = (bf16[4,4,24,768]{3,2,1,0:T(8,128)(2,1)S(1)}, bf16[4,4,24,768]{3,2,1,0:T(8,128)(2,1)S(1)}, u32[]{:S(2)}, u32[]{:S(2)}) collective-permute-start(bf16[4,4,24,768]{3,2,1,0:T(8,128)(2,1)S(1)} %pad_maximum_fusion.1), channel_id=1, source_target_pairs={{0,4},{4,0},{8,12},{12,8},{16,20},{20,16},{24,28},{28,24},{32,36},... | collective-permute-start | bytes 1769480 | tf_op jit(solution)/shard_map/ppermute | solution.py:58
  48.3 8.3 %collective-permute-start.5 = (bf16[2,4,24,768]{3,2,1,0:T(8,128)(2,1)S(1)}, bf16[2,4,24,768]{3,2,1,0:T(8,128)(2,1)S(1)}, u32[]{:S(2)}, u32[]{:S(2)}) collective-permute-start(bf16[2,4,24,768]{3,2,1,0:T(8,128)(2,1)S(1)} %slice.80), channel_id=1, source_target_pairs={{0,32},{4,12},{8,40},{12,20},{16,48},{20,28},{24,56},{28,4},{32,64... | collective-permute-start | bytes 884744 | tf_op jit(solution)/shard_map/ppermute | solution.py:40
  48.4 8.2 %collective-permute-start.6 = (bf16[2,4,24,768]{3,2,1,0:T(8,128)(2,1)S(1)}, bf16[2,4,24,768]{3,2,1,0:T(8,128)(2,1)S(1)}, u32[]{:S(2)}, u32[]{:S(2)}) collective-permute-start(bf16[2,4,24,768]{3,2,1,0:T(8,128)(2,1)S(1)} %slice.81), channel_id=1, source_target_pairs={{0,96},{4,28},{8,104},{12,4},{16,112},{20,12},{24,120},{28,20},{32... | collective-permute-start | bytes 884744 | tf_op jit(solution)/shard_map/ppermute | solution.py:41
  51.8 13.1 %collective-permute-start.10 = (bf16[4,4,24,768]{3,2,1,0:T(8,128)(2,1)S(1)}, bf16[4,4,24,768]{3,2,1,0:T(8,128)(2,1)S(1)}, u32[]{:S(2)}, u32[]{:S(2)}) collective-permute-start(bf16[4,4,24,768]{3,2,1,0:T(8,128)(2,1)S(1)} %collective-permute-done.4), channel_id=1, source_target_pairs={{0,4},{4,0},{8,12},{12,8},{16,20},{20,16},{24,28},{28,24},{32,36},... | collective-permute-start | bytes 1769480 | tf_op jit(solution)/shard_map/ppermute | solution.py:58
  55.7 7.4 %collective-permute-start.8 = (bf16[4,4,24,768]{3,2,1,0:T(8,128)(2,1)S(1)}, bf16[4,4,24,768]{3,2,1,0:T(8,128)(2,1)S(1)}, u32[]{:S(2)}, u32[]{:S(2)}) collective-permute-start(bf16[4,4,24,768]{3,2,1,0:T(8,128)(2,1)S(1)} %collective-permute-done.3), channel_id=1, source_target_pairs={{0,4},{4,0},{8,12},{12,8},{16,20},{20,16},{24,28},{28,24},{32,36},... | collective-permute-start | bytes 1769480 | tf_op jit(solution)/shard_map/ppermute | solution.py:58
  56.6 7.4 %collective-permute-start.9 = (bf16[4,4,24,768]{3,2,1,0:T(8,128)(2,1)S(1)}, bf16[4,4,24,768]{3,2,1,0:T(8,128)(2,1)S(1)}, u32[]{:S(2)}, u32[]{:S(2)}) collective-permute-start(bf16[4,4,24,768]{3,2,1,0:T(8,128)(2,1)S(1)} %pad_maximum_fusion.2), channel_id=1, source_target_pairs={{0,4},{4,0},{8,12},{12,8},{16,20},{20,16},{24,28},{28,24},{32,36},... | collective-permute-start | bytes 1769480 | tf_op jit(solution)/shard_map/ppermute | solution.py:58
  71.1 3.8 %copy-start.1 = (bf16[32,4,24,768]{3,2,1,0:T(8,128)(2,1)S(1)}, bf16[32,4,24,768]{3,2,1,0:T(8,128)(2,1)}, u32[]{:S(2)}) copy-start(bf16[32,4,24,768]{3,2,1,0:T(8,128)(2,1)} %gather_fusion.1) | copy-start | bytes 14155780
  86.6 13.9 %collective-permute-start.11 = (bf16[2,192,256]{2,1,0:T(8,128)(2,1)S(1)}, bf16[2,192,256]{2,1,0:T(8,128)(2,1)S(1)}, u32[]{:S(2)}, u32[]{:S(2)}) collective-permute-start(bf16[2,192,256]{2,1,0:T(8,128)(2,1)S(1)} %get-tuple-element.19), channel_id=1, source_target_pairs={{0,1},{1,2},{2,3},{3,0},{4,5},{5,6},{6,7},{7,4},{8,9},{9,10},{10,1... | collective-permute-start | bytes 589832 | tf_op jit(solution)/shard_map/ppermute | solution.py:75
  87.9 12.8 %collective-permute-start.12 = (bf16[2,192,256]{2,1,0:T(8,128)(2,1)S(1)}, bf16[2,192,256]{2,1,0:T(8,128)(2,1)S(1)}, u32[]{:S(2)}, u32[]{:S(2)}) collective-permute-start(bf16[2,192,256]{2,1,0:T(8,128)(2,1)S(1)} %get-tuple-element.20), channel_id=1, source_target_pairs={{0,3},{1,0},{2,1},{3,2},{4,7},{5,4},{6,5},{7,6},{8,11},{9,8},{10,9... | collective-permute-start | bytes 589832 | tf_op jit(solution)/shard_map/ppermute | solution.py:75
  89.4 11.7 %collective-permute-start.13 = (bf16[2,192,256]{2,1,0:T(8,128)(2,1)S(1)}, bf16[2,192,256]{2,1,0:T(8,128)(2,1)S(1)}, u32[]{:S(2)}, u32[]{:S(2)}) collective-permute-start(bf16[2,192,256]{2,1,0:T(8,128)(2,1)S(1)} %get-tuple-element.21), channel_id=1, source_target_pairs={{0,2},{1,3},{2,0},{3,1},{4,6},{5,7},{6,4},{7,5},{8,10},{9,11},{10,... | collective-permute-start | bytes 589832 | tf_op jit(solution)/shard_map/ppermute | solution.py:75
  94.3 10.0 %collective-permute-start.14 = (bf16[2,192,256]{2,1,0:T(8,128)(2,1)S(1)}, bf16[2,192,256]{2,1,0:T(8,128)(2,1)S(1)}, u32[]{:S(2)}, u32[]{:S(2)}) collective-permute-start(bf16[2,192,256]{2,1,0:T(8,128)(2,1)S(1)} %get-tuple-element.26), channel_id=1, source_target_pairs={{0,1},{1,2},{2,3},{3,0},{4,5},{5,6},{6,7},{7,4},{8,9},{9,10},{10,1... | collective-permute-start | bytes 589832 | tf_op jit(solution)/shard_map/ppermute | solution.py:75
  94.8 10.3 %collective-permute-start.15 = (bf16[2,192,256]{2,1,0:T(8,128)(2,1)S(1)}, bf16[2,192,256]{2,1,0:T(8,128)(2,1)S(1)}, u32[]{:S(2)}, u32[]{:S(2)}) collective-permute-start(bf16[2,192,256]{2,1,0:T(8,128)(2,1)S(1)} %get-tuple-element.27), channel_id=1, source_target_pairs={{0,3},{1,0},{2,1},{3,2},{4,7},{5,4},{6,5},{7,6},{8,11},{9,8},{10,9... | collective-permute-start | bytes 589832 | tf_op jit(solution)/shard_map/ppermute | solution.py:75
  100.5 6.7 %collective-permute-start.16 = (bf16[2,192,256]{2,1,0:T(8,128)(2,1)S(1)}, bf16[2,192,256]{2,1,0:T(8,128)(2,1)S(1)}, u32[]{:S(2)}, u32[]{:S(2)}) collective-permute-start(bf16[2,192,256]{2,1,0:T(8,128)(2,1)S(1)} %get-tuple-element.28), channel_id=1, source_target_pairs={{0,2},{1,3},{2,0},{3,1},{4,6},{5,7},{6,4},{7,5},{8,10},{9,11},{10,... | collective-permute-start | bytes 589832 | tf_op jit(solution)/shard_map/ppermute | solution.py:75
  100.7 13.7 %collective-permute-start.17 = (bf16[2,192,256]{2,1,0:T(8,128)(2,1)S(1)}, bf16[2,192,256]{2,1,0:T(8,128)(2,1)S(1)}, u32[]{:S(2)}, u32[]{:S(2)}) collective-permute-start(bf16[2,192,256]{2,1,0:T(8,128)(2,1)S(1)} %get-tuple-element.37), channel_id=1, source_target_pairs={{0,1},{1,2},{2,3},{3,0},{4,5},{5,6},{6,7},{7,4},{8,9},{9,10},{10,1... | collective-permute-start | bytes 589832 | tf_op jit(solution)/shard_map/ppermute | solution.py:75
  101.1 13.3 %collective-permute-start.18 = (bf16[2,192,256]{2,1,0:T(8,128)(2,1)S(1)}, bf16[2,192,256]{2,1,0:T(8,128)(2,1)S(1)}, u32[]{:S(2)}, u32[]{:S(2)}) collective-permute-start(bf16[2,192,256]{2,1,0:T(8,128)(2,1)S(1)} %get-tuple-element.38), channel_id=1, source_target_pairs={{0,3},{1,0},{2,1},{3,2},{4,7},{5,4},{6,5},{7,6},{8,11},{9,8},{10,9... | collective-permute-start | bytes 589832 | tf_op jit(solution)/shard_map/ppermute | solution.py:75
  104.3 11.3 %collective-permute-start.19 = (bf16[2,192,256]{2,1,0:T(8,128)(2,1)S(1)}, bf16[2,192,256]{2,1,0:T(8,128)(2,1)S(1)}, u32[]{:S(2)}, u32[]{:S(2)}) collective-permute-start(bf16[2,192,256]{2,1,0:T(8,128)(2,1)S(1)} %get-tuple-element.39), channel_id=1, source_target_pairs={{0,2},{1,3},{2,0},{3,1},{4,6},{5,7},{6,4},{7,5},{8,10},{9,11},{10,... | collective-permute-start | bytes 589832 | tf_op jit(solution)/shard_map/ppermute | solution.py:75

commit v19 on v18

--- a/solution.py
+++ b/solution.py
@@ -56,18 +56,17 @@
     both = ring_gather(first, sizes, 2)
     swap = [(q, q ^ 1) for q in range(devices)]
     other = [lax.ppermute(part, PAIR, swap) for part in both]
-    chips = nz * nx
-    stacked = jnp.concatenate(both + other, axis=0)
     z = lax.axis_index("z")
     x = lax.axis_index("x")
     core = lax.axis_index("core")
-    q = jnp.arange(devices, dtype=jnp.int32)
-    zq, xq, cq = q // (nx * nc), (q // nc) % nx, q % nc
-    dz, dx = (zq - z) % nz, (xq - x) % nx
-    inner = jnp.where(cq == 0, dz * nx + dx, dx * nz + dz)
-    index = jnp.where(cq == core, 0, chips) + inner
-    ordered = stacked.at[index].get(mode="promise_in_bounds")
-    ordered = jnp.transpose(ordered, (1, 0, 2, 3))
+    ordered = jnp.zeros((slots, devices, piece, cols), own_vector.dtype)
+    for c, parts in ((core, both), (1 - core, other)):
+        for outer, part in enumerate(parts):
+            for inner in range(part.shape[0]):
+                dz = jnp.where(c == 0, outer, inner)
+                dx = jnp.where(c == 0, inner, outer)
+                q = (((z + dz) % nz) * nx + (x + dx) % nx) * nc + c
+                ordered = lax.dynamic_update_slice(ordered, part[inner][:, None], (0, q, 0, 0))
     return ordered.reshape(slots, rows, cols)
 
 

time: 118 us -> 104 us (0.88)
  local copies, waits for them, and re-layouts: 21.1 us -> 2.63 us
  waiting for transfers between devices: 35.6 us -> 42.5 us
  starting transfers between devices: 38.9 us -> 34.8 us
  between operations: 0.34 us -> 1.66 us
    unnamed x15 -> x4, local copies, waits for them, and re-layouts: 10.3 us -> 0.01 us
    ppermute x2, waiting for transfers between devices: 3.21 us -> 11.3 us  [ring_gather(): from_prev = lax.ppermute(piece, PAIR, ring_perm(sizes, stage, 1))]
    gather x1 -> x0, local copies, waits for them, and re-layouts: 5.38 us -> none  [gather_slots(): ordered = stacked.at[index].get(mode='promise_in_bounds')]
    ppermute x4, starting transfers between devices: 10.3 us -> 5.16 us  [gather_slots(): other = [lax.ppermute(part, PAIR, swap) for part in both]]
    ppermute x1, waiting for transfers between devices: 3.37 us -> 0.01 us  [ring_gather(): far = lax.ppermute(piece, PAIR, ring_perm(sizes, stage, 2))]
    transpose x1 -> x0, local copies, waits for them, and re-layouts: 2.79 us -> none  [gather_slots(): ordered = jnp.transpose(ordered, (1, 0, 2, 3))]
    ppermute x1, waiting for transfers between devices: 0.01 us -> 2.71 us  [ring_gather(): far_low = lax.ppermute(from_prev[:half], PAIR, ring_perm(sizes, stage, 1))]
    ppermute x4, waiting for transfers between devices: 0.01 us -> 1.22 us  [gather_slots(): other = [lax.ppermute(part, PAIR, swap) for part in both]]
  transfers between devices with their start and end apart: 21 -> 21, of which waited for: 8 -> 10; matrix products, arithmetic and copies ran while one was open for 15% -> 8% of each run, Pallas kernels for 0% -> 0%
where the time goes in v19:
time: 104 us; the launch traced here: 102 us
  waiting for transfers between devices  42.5 us (41%)
  starting transfers between devices  34.8 us (33%)
  matrix products  18 us (17%)
  local copies, waits for them, and re-layouts  2.63 us (3%)
  other arithmetic  2.21 us (2%)
  between operations  1.66 us (2%)
    all_to_all x1, waiting for transfers between devices, gather_slots(): pieces = lax.all_to_all(pieces, PAIR, 0, 0, tiled=True)  16.7 us
    ppermute x9, starting transfers between devices, shifted(): lax.ppermute(value, 'vgrp', [(g, (g + step) % groups) for g in range(grou...  11.5 us
    ppermute x2, waiting for transfers between devices, ring_gather(): from_prev = lax.ppermute(piece, PAIR, ring_perm(sizes, stage, 1))  11.3 us
    dot_general x12, matrix products, columns(): jnp.einsum('pad,bd->pab', half_product, vectors[slot, lo:hi], preferred_e...  10 us
    ppermute x9, waiting for transfers between devices, shifted(): lax.ppermute(value, 'vgrp', [(g, (g + step) % groups) for g in range(grou...  9.99 us
    all_to_all x1, starting transfers between devices, gather_slots(): pieces = lax.all_to_all(pieces, PAIR, 0, 0, tiled=True)  9.55 us
    dot_general x4, matrix products, on_device(): jnp.einsum('ac,pcd->pad', vectors[slot], amplitudes, preferred_element_ty...  8 us
    ppermute x4, starting transfers between devices, gather_slots(): other = [lax.ppermute(part, PAIR, swap) for part in both]  5.16 us
  transfers between devices with their start and end apart: 21, of which 10 were waited for; matrix products, arithmetic and copies ran while one was open for 8% of the time, Pallas kernels for 0%

profile of v19, /device:TPU:1, one launch (start us, length us, event | category | flops | bytes accessed | tf_op | source)
XLA Modules:
  0.0 101.8 jit_solution(11594264065822031102)
XLA Ops:
  0.0 9.6 %all-to-all-start = ((bf16[32,24,768]{2,1,0:T(8,128)(2,1)}), bf16[32,24,768]{2,1,0:T(8,128)(2,1)S(1)}, u32[]{:S(2)}, u32[]{:S(2)}) async-start(bf16[32,24,768]{2,1,0:T(8,128)(2,1)} %bitcast.374), calls=%async_computation | async-start | bytes 2359296 | tf_op jit(solution)/shard_map/all_to_all | solution.py:53
  11.4 16.7 %all-to-all-done = bf16[32,24,768]{2,1,0:T(8,128)(2,1)S(1)} async-done(((bf16[32,24,768]{2,1,0:T(8,128)(2,1)}), bf16[32,24,768]{2,1,0:T(8,128)(2,1)S(1)}, u32[]{:S(2)}, u32[]{:S(2)}) %all-to-all-start) | async-done | bytes 1179680 | tf_op jit(solution)/shard_map/all_to_all | solution.py:53
  28.1 1.2 %gather_fusion = bf16[4,24,768]{2,1,0:T(8,128)(2,1)} fusion(bf16[32,24,768]{2,1,0:T(8,128)(2,1)S(1)} %all-to-all-done, s32[1024]{0:T(1024)S(1)} %pad_clamp_fusion), kind=kCustom, calls=%fused_computation | custom fusion | bytes 294928 | tf_op jit(solution)/shard_map/gather | solution.py:54
  29.3 1.7 %collective-permute-start.1 = (bf16[4,24,768]{2,1,0:T(8,128)(2,1)}, bf16[4,24,768]{2,1,0:T(8,128)(2,1)S(1)}, u32[]{:S(2)}, u32[]{:S(2)}) collective-permute-start(bf16[4,24,768]{2,1,0:T(8,128)(2,1)} %gather_fusion), channel_id=1, source_target_pairs={{0,16},{4,68},{8,24},{12,76},{16,0},{20,84},{24,8},{28,92},{32,48}... | collective-permute-start | bytes 442376 | tf_op jit(solution)/shard_map/ppermute | solution.py:38
  31.0 1.4 %collective-permute-start = (bf16[4,24,768]{2,1,0:T(8,128)(2,1)}, bf16[4,24,768]{2,1,0:T(8,128)(2,1)S(1)}, u32[]{:S(2)}, u32[]{:S(2)}) collective-permute-start(bf16[4,24,768]{2,1,0:T(8,128)(2,1)} %gather_fusion), channel_id=1, source_target_pairs={{0,24},{4,100},{8,0},{12,108},{16,8},{20,116},{24,16},{28,124},{32... | collective-permute-start | bytes 442376 | tf_op jit(solution)/shard_map/ppermute | solution.py:36
  32.8 3.8 %collective-permute-done.2 = bf16[4,24,768]{2,1,0:T(8,128)(2,1)S(1)} collective-permute-done((bf16[4,24,768]{2,1,0:T(8,128)(2,1)}, bf16[4,24,768]{2,1,0:T(8,128)(2,1)S(1)}, u32[]{:S(2)}, u32[]{:S(2)}) %collective-permute-start.2) | collective-permute-done | bytes 147488 | tf_op jit(solution)/shard_map/ppermute | solution.py:35
  37.3 1.6 %collective-permute-start.7 = (bf16[4,4,24,768]{3,2,1,0:T(8,128)(2,1)S(1)}, bf16[4,4,24,768]{3,2,1,0:T(8,128)(2,1)S(1)}, u32[]{:S(2)}, u32[]{:S(2)}) collective-permute-start(bf16[4,4,24,768]{3,2,1,0:T(8,128)(2,1)S(1)} %pad_maximum_fusion.1), channel_id=1, source_target_pairs={{0,4},{4,0},{8,12},{12,8},{16,20},{20,16},{24,28},{28,24},{32,36},... | collective-permute-start | bytes 1769480 | tf_op jit(solution)/shard_map/ppermute | solution.py:58
  39.3 2.3 %collective-permute-start.3 = (bf16[4,4,24,768]{3,2,1,0:T(8,128)(2,1)S(1)}, bf16[4,4,24,768]{3,2,1,0:T(8,128)(2,1)S(1)}, u32[]{:S(2)}, u32[]{:S(2)}) collective-permute-start(bf16[4,4,24,768]{3,2,1,0:T(8,128)(2,1)S(1)} %pad_maximum_fusion.1), channel_id=1, source_target_pairs={{0,96},{4,28},{8,104},{12,4},{16,112},{20,12},{24,120},{28,20},{32... | collective-permute-start | bytes 1769480 | tf_op jit(solution)/shard_map/ppermute | solution.py:36
  41.6 7.5 %collective-permute-done.4 = bf16[4,4,24,768]{3,2,1,0:T(8,128)(2,1)S(1)} collective-permute-done((bf16[4,4,24,768]{3,2,1,0:T(8,128)(2,1)S(1)}, bf16[4,4,24,768]{3,2,1,0:T(8,128)(2,1)S(1)}, u32[]{:S(2)}, u32[]{:S(2)}) %collective-permute-start.4) | collective-permute-done | bytes 589856 | tf_op jit(solution)/shard_map/ppermute | solution.py:35
  49.3 2.7 %collective-permute-start.6 = (bf16[2,4,24,768]{3,2,1,0:T(8,128)(2,1)S(1)}, bf16[2,4,24,768]{3,2,1,0:T(8,128)(2,1)S(1)}, u32[]{:S(2)}, u32[]{:S(2)}) collective-permute-start(bf16[2,4,24,768]{3,2,1,0:T(8,128)(2,1)S(1)} %slice.197), channel_id=1, source_target_pairs={{0,96},{4,28},{8,104},{12,4},{16,112},{20,12},{24,120},{28,20},{32... | collective-permute-start | bytes 884744 | tf_op jit(solution)/shard_map/ppermute | solution.py:41
  52.0 1.5 %collective-permute-start.10 = (bf16[4,4,24,768]{3,2,1,0:T(8,128)(2,1)S(1)}, bf16[4,4,24,768]{3,2,1,0:T(8,128)(2,1)S(1)}, u32[]{:S(2)}, u32[]{:S(2)}) collective-permute-start(bf16[4,4,24,768]{3,2,1,0:T(8,128)(2,1)S(1)} %collective-permute-done.4), channel_id=1, source_target_pairs={{0,4},{4,0},{8,12},{12,8},{16,20},{20,16},{24,28},{28,24},{32,36},... | collective-permute-start | bytes 1769480 | tf_op jit(solution)/shard_map/ppermute | solution.py:58
  53.6 2.7 %collective-permute-done.5 = bf16[2,4,24,768]{3,2,1,0:T(8,128)(2,1)S(1)} collective-permute-done((bf16[2,4,24,768]{3,2,1,0:T(8,128)(2,1)S(1)}, bf16[2,4,24,768]{3,2,1,0:T(8,128)(2,1)S(1)}, u32[]{:S(2)}, u32[]{:S(2)}) %collective-permute-start.5) | collective-permute-done | bytes 294944 | tf_op jit(solution)/shard_map/ppermute | solution.py:40
  56.3 2.1 %collective-permute-start.9 = (bf16[4,4,24,768]{3,2,1,0:T(8,128)(2,1)S(1)}, bf16[4,4,24,768]{3,2,1,0:T(8,128)(2,1)S(1)}, u32[]{:S(2)}, u32[]{:S(2)}) collective-permute-start(bf16[4,4,24,768]{3,2,1,0:T(8,128)(2,1)S(1)} %pad_maximum_fusion.2), channel_id=1, source_target_pairs={{0,4},{4,0},{8,12},{12,8},{16,20},{20,16},{24,28},{28,24},{32,36},... | collective-permute-start | bytes 1769480 | tf_op jit(solution)/shard_map/ppermute | solution.py:58
  58.8 1.2 %collective-permute-done.9 = bf16[4,4,24,768]{3,2,1,0:T(8,128)(2,1)S(1)} collective-permute-done((bf16[4,4,24,768]{3,2,1,0:T(8,128)(2,1)S(1)}, bf16[4,4,24,768]{3,2,1,0:T(8,128)(2,1)S(1)}, u32[]{:S(2)}, u32[]{:S(2)}) %collective-permute-start.9) | collective-permute-done | bytes 589856 | tf_op jit(solution)/shard_map/ppermute | solution.py:58
  60.6 2.0 %convert_bitcast_fusion.1 = bf16[2,768,768]{2,1,0:T(8,128)(2,1)S(1)} fusion(bf16[768,768,1]{1,0,2:T(8,128)(2,1)S(1)} %bitcast.373, bf16[2,768,768]{2,1,0:T(8,128)(2,1)S(1)} %copy-done), kind=kOutput, calls=%fused_computation.2 | convolution fusion | flops 1813118976 | bytes 5898240 | tf_op jit(solution)/shard_map/ac,pcd->pad/dot_general | solution.py:114
  62.6 2.0 %convert_bitcast_fusion = bf16[2,768,768]{2,1,0:T(8,128)(2,1)S(1)} fusion(bf16[768,768,1]{1,0,2:T(8,128)(2,1)S(1)} %bitcast.372, bf16[2,768,768]{2,1,0:T(8,128)(2,1)S(1)} %copy-done), kind=kOutput, calls=%fused_computation.1 | convolution fusion | flops 1813118976 | bytes 5898240 | tf_op jit(solution)/shard_map/ac,pcd->pad/dot_general | solution.py:114
  64.6 2.0 %convert_bitcast_fusion.2 = bf16[2,768,768]{2,1,0:T(8,128)(2,1)S(1)} fusion(bf16[768,768,1]{1,0,2:T(8,128)(2,1)S(1)} %bitcast.371, bf16[2,768,768]{2,1,0:T(8,128)(2,1)S(1)} %copy-done), kind=kOutput, calls=%fused_computation.3 | convolution fusion | flops 1813118976 | bytes 5898240 | tf_op jit(solution)/shard_map/ac,pcd->pad/dot_general | solution.py:114
  66.6 2.0 %convert_bitcast_fusion.3 = bf16[2,768,768]{2,1,0:T(8,128)(2,1)S(1)} fusion(bf16[768,768,1]{1,0,2:T(8,128)(2,1)S(1)} %bitcast.370, bf16[2,768,768]{2,1,0:T(8,128)(2,1)S(1)} %copy-done), kind=kOutput, calls=%fused_computation.4 | convolution fusion | flops 1813118976 | bytes 5898240 | tf_op jit(solution)/shard_map/ac,pcd->pad/dot_general | solution.py:114
  68.6 0.8 fusion.6
  71.0 0.9 add_add_fusion.2
  72.0 1.4 %collective-permute-start.11 = (bf16[2,192,256]{2,1,0:T(8,128)(2,1)S(1)}, bf16[2,192,256]{2,1,0:T(8,128)(2,1)S(1)}, u32[]{:S(2)}, u32[]{:S(2)}) collective-permute-start(bf16[2,192,256]{2,1,0:T(8,128)(2,1)S(1)} %get-tuple-element.19), channel_id=1, source_target_pairs={{0,1},{1,2},{2,3},{3,0},{4,5},{5,6},{6,7},{7,4},{8,9},{9,10},{10,1... | collective-permute-start | bytes 589832 | tf_op jit(solution)/shard_map/ppermute | solution.py:74
  73.4 1.5 %collective-permute-start.12 = (bf16[2,192,256]{2,1,0:T(8,128)(2,1)S(1)}, bf16[2,192,256]{2,1,0:T(8,128)(2,1)S(1)}, u32[]{:S(2)}, u32[]{:S(2)}) collective-permute-start(bf16[2,192,256]{2,1,0:T(8,128)(2,1)S(1)} %get-tuple-element.20), channel_id=1, source_target_pairs={{0,3},{1,0},{2,1},{3,2},{4,7},{5,4},{6,5},{7,6},{8,11},{9,8},{10,9... | collective-permute-start | bytes 589832 | tf_op jit(solution)/shard_map/ppermute | solution.py:74
  74.9 1.6 %collective-permute-start.13 = (bf16[2,192,256]{2,1,0:T(8,128)(2,1)S(1)}, bf16[2,192,256]{2,1,0:T(8,128)(2,1)S(1)}, u32[]{:S(2)}, u32[]{:S(2)}) collective-permute-start(bf16[2,192,256]{2,1,0:T(8,128)(2,1)S(1)} %get-tuple-element.21), channel_id=1, source_target_pairs={{0,2},{1,3},{2,0},{3,1},{4,6},{5,7},{6,4},{7,5},{8,10},{9,11},{10,... | collective-permute-start | bytes 589832 | tf_op jit(solution)/shard_map/ppermute | solution.py:74
  77.3 0.8 fusion.4
  78.9 0.9 add_add_fusion.1
  80.4 2.3 %collective-permute-start.15 = (bf16[2,192,256]{2,1,0:T(8,128)(2,1)S(1)}, bf16[2,192,256]{2,1,0:T(8,128)(2,1)S(1)}, u32[]{:S(2)}, u32[]{:S(2)}) collective-permute-start(bf16[2,192,256]{2,1,0:T(8,128)(2,1)S(1)} %get-tuple-element.27), channel_id=1, source_target_pairs={{0,3},{1,0},{2,1},{3,2},{4,7},{5,4},{6,5},{7,6},{8,11},{9,8},{10,9... | collective-permute-start | bytes 589832 | tf_op jit(solution)/shard_map/ppermute | solution.py:74
  85.1 0.9 add_add_fusion
  86.8 2.3 %collective-permute-start.18 = (bf16[2,192,256]{2,1,0:T(8,128)(2,1)S(1)}, bf16[2,192,256]{2,1,0:T(8,128)(2,1)S(1)}, u32[]{:S(2)}, u32[]{:S(2)}) collective-permute-start(bf16[2,192,256]{2,1,0:T(8,128)(2,1)S(1)} %get-tuple-element.38), channel_id=1, source_target_pairs={{0,3},{1,0},{2,1},{3,2},{4,7},{5,4},{6,5},{7,6},{8,11},{9,8},{10,9... | collective-permute-start | bytes 589832 | tf_op jit(solution)/shard_map/ppermute | solution.py:74
  89.5 1.3 %collective-permute-start.19 = (bf16[2,192,256]{2,1,0:T(8,128)(2,1)S(1)}, bf16[2,192,256]{2,1,0:T(8,128)(2,1)S(1)}, u32[]{:S(2)}, u32[]{:S(2)}) collective-permute-start(bf16[2,192,256]{2,1,0:T(8,128)(2,1)S(1)} %get-tuple-element.39), channel_id=1, source_target_pairs={{0,2},{1,3},{2,0},{3,1},{4,6},{5,7},{6,4},{7,5},{8,10},{9,11},{10,... | collective-permute-start | bytes 589832 | tf_op jit(solution)/shard_map/ppermute | solution.py:74
  90.9 1.5 %collective-permute-done.16 = bf16[2,192,256]{2,1,0:T(8,128)(2,1)S(1)} collective-permute-done((bf16[2,192,256]{2,1,0:T(8,128)(2,1)S(1)}, bf16[2,192,256]{2,1,0:T(8,128)(2,1)S(1)}, u32[]{:S(2)}, u32[]{:S(2)}) %collective-permute-start.16) | collective-permute-done | bytes 196640 | tf_op jit(solution)/shard_map/ppermute | solution.py:74
  92.5 7.9 %collective-permute-done.17 = bf16[2,192,256]{2,1,0:T(8,128)(2,1)S(1)} collective-permute-done((bf16[2,192,256]{2,1,0:T(8,128)(2,1)S(1)}, bf16[2,192,256]{2,1,0:T(8,128)(2,1)S(1)}, u32[]{:S(2)}, u32[]{:S(2)}) %collective-permute-start.17) | collective-permute-done | bytes 196640 | tf_op jit(solution)/shard_map/ppermute | solution.py:74
  100.7 1.1 %pad_maximum_fusion = f32[2,192,768]{2,1,0:T(8,128)} fusion(f32[2,192,256]{2,1,0:T(8,128)S(1)} %fusion.9, f32[2,192,256]{2,1,0:T(8,128)S(1)} %fusion.10, f32[2,192,256]{2,1,0:T(8,128)S(1)} %fusion.11), kind=kLoop, calls=%fused_computation.8 | loop fusion | flops 589824 | bytes 2359296 | tf_op jit(solution)/shard_map/concatenate | solution.py:127
  (78 shorter events, 11.0 us)
Async XLA Ops:
  0.0 60.5 %copy-start = (bf16[2,768,768]{2,1,0:T(8,128)(2,1)S(1)}, bf16[2,768,768]{2,1,0:T(8,128)(2,1)}, u32[]{:S(2)}) copy-start(bf16[2,768,768]{2,1,0:T(8,128)(2,1)} %param.3) | copy-start | bytes 7077892
  0.0 28.1 %all-to-all-start = ((bf16[32,24,768]{2,1,0:T(8,128)(2,1)}), bf16[32,24,768]{2,1,0:T(8,128)(2,1)S(1)}, u32[]{:S(2)}, u32[]{:S(2)}) async-start(bf16[32,24,768]{2,1,0:T(8,128)(2,1)} %bitcast.374), calls=%async_computation | async-start | bytes 2359296 | tf_op jit(solution)/shard_map/all_to_all | solution.py:53
  29.3 3.5 %copy-start.1 = (bf16[4,24,768]{2,1,0:T(8,128)(2,1)S(1)}, bf16[4,24,768]{2,1,0:T(8,128)(2,1)}, u32[]{:S(2)}) copy-start(bf16[4,24,768]{2,1,0:T(8,128)(2,1)} %gather_fusion) | copy-start | bytes 442372
  29.3 7.3 %collective-permute-start.2 = (bf16[4,24,768]{2,1,0:T(8,128)(2,1)}, bf16[4,24,768]{2,1,0:T(8,128)(2,1)S(1)}, u32[]{:S(2)}, u32[]{:S(2)}) collective-permute-start(bf16[4,24,768]{2,1,0:T(8,128)(2,1)} %gather_fusion), channel_id=1, source_target_pairs={{0,8},{4,36},{8,16},{12,44},{16,24},{20,52},{24,0},{28,60},{32,40}... | collective-permute-start | bytes 442376 | tf_op jit(solution)/shard_map/ppermute | solution.py:35
  29.3 7.3 %collective-permute-start.1 = (bf16[4,24,768]{2,1,0:T(8,128)(2,1)}, bf16[4,24,768]{2,1,0:T(8,128)(2,1)S(1)}, u32[]{:S(2)}, u32[]{:S(2)}) collective-permute-start(bf16[4,24,768]{2,1,0:T(8,128)(2,1)} %gather_fusion), channel_id=1, source_target_pairs={{0,16},{4,68},{8,24},{12,76},{16,0},{20,84},{24,8},{28,92},{32,48}... | collective-permute-start | bytes 442376 | tf_op jit(solution)/shard_map/ppermute | solution.py:38
  31.0 6.1 %collective-permute-start = (bf16[4,24,768]{2,1,0:T(8,128)(2,1)}, bf16[4,24,768]{2,1,0:T(8,128)(2,1)S(1)}, u32[]{:S(2)}, u32[]{:S(2)}) collective-permute-start(bf16[4,24,768]{2,1,0:T(8,128)(2,1)} %gather_fusion), channel_id=1, source_target_pairs={{0,24},{4,100},{8,0},{12,108},{16,8},{20,116},{24,16},{28,124},{32... | collective-permute-start | bytes 442376 | tf_op jit(solution)/shard_map/ppermute | solution.py:36
  37.3 21.3 %collective-permute-start.7 = (bf16[4,4,24,768]{3,2,1,0:T(8,128)(2,1)S(1)}, bf16[4,4,24,768]{3,2,1,0:T(8,128)(2,1)S(1)}, u32[]{:S(2)}, u32[]{:S(2)}) collective-permute-start(bf16[4,4,24,768]{3,2,1,0:T(8,128)(2,1)S(1)} %pad_maximum_fusion.1), channel_id=1, source_target_pairs={{0,4},{4,0},{8,12},{12,8},{16,20},{20,16},{24,28},{28,24},{32,36},... | collective-permute-start | bytes 1769480 | tf_op jit(solution)/shard_map/ppermute | solution.py:58
  38.9 10.2 %collective-permute-start.4 = (bf16[4,4,24,768]{3,2,1,0:T(8,128)(2,1)S(1)}, bf16[4,4,24,768]{3,2,1,0:T(8,128)(2,1)S(1)}, u32[]{:S(2)}, u32[]{:S(2)}) collective-permute-start(bf16[4,4,24,768]{3,2,1,0:T(8,128)(2,1)S(1)} %pad_maximum_fusion.1), channel_id=1, source_target_pairs={{0,32},{4,12},{8,40},{12,20},{16,48},{20,28},{24,56},{28,4},{32,64... | collective-permute-start | bytes 1769480 | tf_op jit(solution)/shard_map/ppermute | solution.py:35
  39.3 10.0 %collective-permute-start.3 = (bf16[4,4,24,768]{3,2,1,0:T(8,128)(2,1)S(1)}, bf16[4,4,24,768]{3,2,1,0:T(8,128)(2,1)S(1)}, u32[]{:S(2)}, u32[]{:S(2)}) collective-permute-start(bf16[4,4,24,768]{3,2,1,0:T(8,128)(2,1)S(1)} %pad_maximum_fusion.1), channel_id=1, source_target_pairs={{0,96},{4,28},{8,104},{12,4},{16,112},{20,12},{24,120},{28,20},{32... | collective-permute-start | bytes 1769480 | tf_op jit(solution)/shard_map/ppermute | solution.py:36
  49.1 7.1 %collective-permute-start.5 = (bf16[2,4,24,768]{3,2,1,0:T(8,128)(2,1)S(1)}, bf16[2,4,24,768]{3,2,1,0:T(8,128)(2,1)S(1)}, u32[]{:S(2)}, u32[]{:S(2)}) collective-permute-start(bf16[2,4,24,768]{3,2,1,0:T(8,128)(2,1)S(1)} %slice.194), channel_id=1, source_target_pairs={{0,32},{4,12},{8,40},{12,20},{16,48},{20,28},{24,56},{28,4},{32,64... | collective-permute-start | bytes 884744 | tf_op jit(solution)/shard_map/ppermute | solution.py:40
  49.3 7.0 %collective-permute-start.6 = (bf16[2,4,24,768]{3,2,1,0:T(8,128)(2,1)S(1)}, bf16[2,4,24,768]{3,2,1,0:T(8,128)(2,1)S(1)}, u32[]{:S(2)}, u32[]{:S(2)}) collective-permute-start(bf16[2,4,24,768]{3,2,1,0:T(8,128)(2,1)S(1)} %slice.197), channel_id=1, source_target_pairs={{0,96},{4,28},{8,104},{12,4},{16,112},{20,12},{24,120},{28,20},{32... | collective-permute-start | bytes 884744 | tf_op jit(solution)/shard_map/ppermute | solution.py:41
  52.0 8.1 %collective-permute-start.10 = (bf16[4,4,24,768]{3,2,1,0:T(8,128)(2,1)S(1)}, bf16[4,4,24,768]{3,2,1,0:T(8,128)(2,1)S(1)}, u32[]{:S(2)}, u32[]{:S(2)}) collective-permute-start(bf16[4,4,24,768]{3,2,1,0:T(8,128)(2,1)S(1)} %collective-permute-done.4), channel_id=1, source_target_pairs={{0,4},{4,0},{8,12},{12,8},{16,20},{20,16},{24,28},{28,24},{32,36},... | collective-permute-start | bytes 1769480 | tf_op jit(solution)/shard_map/ppermute | solution.py:58
  53.5 5.2 %collective-permute-start.8 = (bf16[4,4,24,768]{3,2,1,0:T(8,128)(2,1)S(1)}, bf16[4,4,24,768]{3,2,1,0:T(8,128)(2,1)S(1)}, u32[]{:S(2)}, u32[]{:S(2)}) collective-permute-start(bf16[4,4,24,768]{3,2,1,0:T(8,128)(2,1)S(1)} %collective-permute-done.3), channel_id=1, source_target_pairs={{0,4},{4,0},{8,12},{12,8},{16,20},{20,16},{24,28},{28,24},{32,36},... | collective-permute-start | bytes 1769480 | tf_op jit(solution)/shard_map/ppermute | solution.py:58
  56.3 3.7 %collective-permute-start.9 = (bf16[4,4,24,768]{3,2,1,0:T(8,128)(2,1)S(1)}, bf16[4,4,24,768]{3,2,1,0:T(8,128)(2,1)S(1)}, u32[]{:S(2)}, u32[]{:S(2)}) collective-permute-start(bf16[4,4,24,768]{3,2,1,0:T(8,128)(2,1)S(1)} %pad_maximum_fusion.2), channel_id=1, source_target_pairs={{0,4},{4,0},{8,12},{12,8},{16,20},{20,16},{24,28},{28,24},{32,36},... | collective-permute-start | bytes 1769480 | tf_op jit(solution)/shard_map/ppermute | solution.py:58
  72.0 14.1 %collective-permute-start.11 = (bf16[2,192,256]{2,1,0:T(8,128)(2,1)S(1)}, bf16[2,192,256]{2,1,0:T(8,128)(2,1)S(1)}, u32[]{:S(2)}, u32[]{:S(2)}) collective-permute-start(bf16[2,192,256]{2,1,0:T(8,128)(2,1)S(1)} %get-tuple-element.19), channel_id=1, source_target_pairs={{0,1},{1,2},{2,3},{3,0},{4,5},{5,6},{6,7},{7,4},{8,9},{9,10},{10,1... | collective-permute-start | bytes 589832 | tf_op jit(solution)/shard_map/ppermute | solution.py:74
  73.4 13.0 %collective-permute-start.12 = (bf16[2,192,256]{2,1,0:T(8,128)(2,1)S(1)}, bf16[2,192,256]{2,1,0:T(8,128)(2,1)S(1)}, u32[]{:S(2)}, u32[]{:S(2)}) collective-permute-start(bf16[2,192,256]{2,1,0:T(8,128)(2,1)S(1)} %get-tuple-element.20), channel_id=1, source_target_pairs={{0,3},{1,0},{2,1},{3,2},{4,7},{5,4},{6,5},{7,6},{8,11},{9,8},{10,9... | collective-permute-start | bytes 589832 | tf_op jit(solution)/shard_map/ppermute | solution.py:74
  74.9 11.9 %collective-permute-start.13 = (bf16[2,192,256]{2,1,0:T(8,128)(2,1)S(1)}, bf16[2,192,256]{2,1,0:T(8,128)(2,1)S(1)}, u32[]{:S(2)}, u32[]{:S(2)}) collective-permute-start(bf16[2,192,256]{2,1,0:T(8,128)(2,1)S(1)} %get-tuple-element.21), channel_id=1, source_target_pairs={{0,2},{1,3},{2,0},{3,1},{4,6},{5,7},{6,4},{7,5},{8,10},{9,11},{10,... | collective-permute-start | bytes 589832 | tf_op jit(solution)/shard_map/ppermute | solution.py:74
  79.9 9.6 %collective-permute-start.14 = (bf16[2,192,256]{2,1,0:T(8,128)(2,1)S(1)}, bf16[2,192,256]{2,1,0:T(8,128)(2,1)S(1)}, u32[]{:S(2)}, u32[]{:S(2)}) collective-permute-start(bf16[2,192,256]{2,1,0:T(8,128)(2,1)S(1)} %get-tuple-element.26), channel_id=1, source_target_pairs={{0,1},{1,2},{2,3},{3,0},{4,5},{5,6},{6,7},{7,4},{8,9},{9,10},{10,1... | collective-permute-start | bytes 589832 | tf_op jit(solution)/shard_map/ppermute | solution.py:74
  80.4 10.5 %collective-permute-start.15 = (bf16[2,192,256]{2,1,0:T(8,128)(2,1)S(1)}, bf16[2,192,256]{2,1,0:T(8,128)(2,1)S(1)}, u32[]{:S(2)}, u32[]{:S(2)}) collective-permute-start(bf16[2,192,256]{2,1,0:T(8,128)(2,1)S(1)} %get-tuple-element.27), channel_id=1, source_target_pairs={{0,3},{1,0},{2,1},{3,2},{4,7},{5,4},{6,5},{7,6},{8,11},{9,8},{10,9... | collective-permute-start | bytes 589832 | tf_op jit(solution)/shard_map/ppermute | solution.py:74
  86.2 6.2 %collective-permute-start.16 = (bf16[2,192,256]{2,1,0:T(8,128)(2,1)S(1)}, bf16[2,192,256]{2,1,0:T(8,128)(2,1)S(1)}, u32[]{:S(2)}, u32[]{:S(2)}) collective-permute-start(bf16[2,192,256]{2,1,0:T(8,128)(2,1)S(1)} %get-tuple-element.28), channel_id=1, source_target_pairs={{0,2},{1,3},{2,0},{3,1},{4,6},{5,7},{6,4},{7,5},{8,10},{9,11},{10,... | collective-permute-start | bytes 589832 | tf_op jit(solution)/shard_map/ppermute | solution.py:74
  86.4 13.9 %collective-permute-start.17 = (bf16[2,192,256]{2,1,0:T(8,128)(2,1)S(1)}, bf16[2,192,256]{2,1,0:T(8,128)(2,1)S(1)}, u32[]{:S(2)}, u32[]{:S(2)}) collective-permute-start(bf16[2,192,256]{2,1,0:T(8,128)(2,1)S(1)} %get-tuple-element.37), channel_id=1, source_target_pairs={{0,1},{1,2},{2,3},{3,0},{4,5},{5,6},{6,7},{7,4},{8,9},{9,10},{10,1... | collective-permute-start | bytes 589832 | tf_op jit(solution)/shard_map/ppermute | solution.py:74
  86.8 13.5 %collective-permute-start.18 = (bf16[2,192,256]{2,1,0:T(8,128)(2,1)S(1)}, bf16[2,192,256]{2,1,0:T(8,128)(2,1)S(1)}, u32[]{:S(2)}, u32[]{:S(2)}) collective-permute-start(bf16[2,192,256]{2,1,0:T(8,128)(2,1)S(1)} %get-tuple-element.38), channel_id=1, source_target_pairs={{0,3},{1,0},{2,1},{3,2},{4,7},{5,4},{6,5},{7,6},{8,11},{9,8},{10,9... | collective-permute-start | bytes 589832 | tf_op jit(solution)/shard_map/ppermute | solution.py:74
  89.5 11.1 %collective-permute-start.19 = (bf16[2,192,256]{2,1,0:T(8,128)(2,1)S(1)}, bf16[2,192,256]{2,1,0:T(8,128)(2,1)S(1)}, u32[]{:S(2)}, u32[]{:S(2)}) collective-permute-start(bf16[2,192,256]{2,1,0:T(8,128)(2,1)S(1)} %get-tuple-element.39), channel_id=1, source_target_pairs={{0,2},{1,3},{2,0},{3,1},{4,6},{5,7},{6,4},{7,5},{8,10},{9,11},{10,... | collective-permute-start | bytes 589832 | tf_op jit(solution)/shard_map/ppermute | solution.py:74

commit v20 on v19

--- a/solution.py
+++ b/solution.py
@@ -52,7 +52,9 @@
     pieces = own_vector.reshape(devices, piece, cols)
     pieces = lax.all_to_all(pieces, PAIR, 0, 0, tiled=True)
     picked = pieces.at[owned_slots].get(mode="promise_in_bounds")
-    first = jnp.stack(ring_gather(picked, sizes, 1, direct_far=True), axis=0)
+    first = jnp.zeros((RING,) + picked.shape, picked.dtype)
+    for offset, part in enumerate(ring_gather(picked, sizes, 1, direct_far=True)):
+        first = lax.dynamic_update_slice(first, part[None], (offset, 0, 0, 0))
     both = ring_gather(first, sizes, 2)
     swap = [(q, q ^ 1) for q in range(devices)]
     other = [lax.ppermute(part, PAIR, swap) for part in both]
@@ -117,14 +119,17 @@
         for slot in range(vectors.shape[0])
     )
     width = vectors.shape[1] // CHUNKS
-    outs = []
+    result = None
     for chunk in range(CHUNKS):
         cut = columns(halves, vectors, chunk * width, (chunk + 1) * width)
         own, owed = prepare(cut, vgrp, groups)
         if chunk < CHUNKS - 1:
             halves, owed = lax.optimization_barrier((halves, owed))
-        outs.append(exchange(own, owed, groups))
-    return jnp.concatenate(outs, axis=2)
+        part = exchange(own, owed, groups)
+        if result is None:
+            result = jnp.zeros(part.shape[:2] + (vectors.shape[1],), part.dtype)
+        result = lax.dynamic_update_slice(result, part, (0, 0, chunk * width))
+    return result
 
 
 def solution(mesh):

time: 104 us -> 103 us (level)
  waiting for transfers between devices: 42.5 us -> 44 us
  starting transfers between devices: 34.8 us -> 33.4 us
  local copies, waits for them, and re-layouts: 2.63 us -> 3.73 us
  between operations: 1.66 us -> 0.56 us
    ppermute x2, waiting for transfers between devices: 11.3 us -> 8.71 us  [ring_gather(): from_prev = lax.ppermute(piece, PAIR, ring_perm(sizes, stage, 1))]
    ppermute x1, waiting for transfers between devices: 0.01 us -> 2.14 us  [ring_gather(): far = lax.ppermute(piece, PAIR, ring_perm(sizes, stage, 2))]
    all_to_all x1, waiting for transfers between devices: 16.7 us -> 17.8 us  [gather_slots(): pieces = lax.all_to_all(pieces, PAIR, 0, 0, tiled=True)]
    dynamic_update_slice x0 -> x5, local copies, waits for them, and re-layouts: none -> 1.09 us  [the longest x4 1.01 us: gather_slots(): first = lax.dynamic_update_slice(first, part[None], (offset, 0, 0, 0))]
    concatenate x1 -> x0, other arithmetic: 1.09 us -> none  [on_device(): return jnp.concatenate(outs, axis=2)]
  transfers between devices with their start and end apart: 21 -> 21, of which waited for: 10 -> 11; matrix products, arithmetic and copies ran while one was open for 8% -> 10% of each run, Pallas kernels for 0% -> 0%
where the time goes in v20:
time: 103 us; the launch traced here: 102 us
  waiting for transfers between devices  44 us (43%)
  starting transfers between devices  33.4 us (32%)
  matrix products  18 us (17%)
  local copies, waits for them, and re-layouts  3.73 us (4%)
  other arithmetic  1.79 us (2%)
    all_to_all x1, waiting for transfers between devices, gather_slots(): pieces = lax.all_to_all(pieces, PAIR, 0, 0, tiled=True)  17.8 us
    ppermute x9, starting transfers between devices, shifted(): lax.ppermute(value, 'vgrp', [(g, (g + step) % groups) for g in range(grou...  11.6 us
    dot_general x12, matrix products, columns(): jnp.einsum('pad,bd->pab', half_product, vectors[slot, lo:hi], preferred_e...  10 us
    ppermute x9, waiting for transfers between devices, shifted(): lax.ppermute(value, 'vgrp', [(g, (g + step) % groups) for g in range(grou...  9.82 us
    all_to_all x1, starting transfers between devices, gather_slots(): pieces = lax.all_to_all(pieces, PAIR, 0, 0, tiled=True)  9.55 us
    ppermute x2, waiting for transfers between devices, ring_gather(): from_prev = lax.ppermute(piece, PAIR, ring_perm(sizes, stage, 1))  8.71 us
    dot_general x4, matrix products, on_device(): jnp.einsum('ac,pcd->pad', vectors[slot], amplitudes, preferred_element_ty...  8.01 us
    ppermute x4, starting transfers between devices, gather_slots(): other = [lax.ppermute(part, PAIR, swap) for part in both]  4.92 us
  transfers between devices with their start and end apart: 21, of which 11 were waited for; matrix products, arithmetic and copies ran while one was open for 10% of the time, Pallas kernels for 0%

profile of v20, /device:TPU:1, one launch (start us, length us, event | category | flops | bytes accessed | tf_op | source)
XLA Modules:
  0.0 101.6 jit_solution(3823638772137609458)
XLA Ops:
  0.0 9.6 %all-to-all-start = ((bf16[32,24,768]{2,1,0:T(8,128)(2,1)}), bf16[32,24,768]{2,1,0:T(8,128)(2,1)S(1)}, u32[]{:S(2)}, u32[]{:S(2)}) async-start(bf16[32,24,768]{2,1,0:T(8,128)(2,1)} %bitcast.386), calls=%async_computation | async-start | bytes 2359296 | tf_op jit(solution)/shard_map/all_to_all | solution.py:53
  10.3 17.8 %all-to-all-done = bf16[32,24,768]{2,1,0:T(8,128)(2,1)S(1)} async-done(((bf16[32,24,768]{2,1,0:T(8,128)(2,1)}), bf16[32,24,768]{2,1,0:T(8,128)(2,1)S(1)}, u32[]{:S(2)}, u32[]{:S(2)}) %all-to-all-start) | async-done | bytes 1179680 | tf_op jit(solution)/shard_map/all_to_all | solution.py:53
  28.1 1.2 %gather_fusion = bf16[4,24,768]{2,1,0:T(8,128)(2,1)} fusion(bf16[32,24,768]{2,1,0:T(8,128)(2,1)S(1)} %all-to-all-done, s32[1024]{0:T(1024)S(1)} %pad_clamp_fusion), kind=kCustom, calls=%fused_computation | custom fusion | bytes 294928 | tf_op jit(solution)/shard_map/gather | solution.py:54
  29.9 1.1 %collective-permute-start.1 = (bf16[4,24,768]{2,1,0:T(8,128)(2,1)}, bf16[4,24,768]{2,1,0:T(8,128)(2,1)S(1)}, u32[]{:S(2)}, u32[]{:S(2)}) collective-permute-start(bf16[4,24,768]{2,1,0:T(8,128)(2,1)} %gather_fusion), channel_id=1, source_target_pairs={{0,16},{4,68},{8,24},{12,76},{16,0},{20,84},{24,8},{28,92},{32,48}... | collective-permute-start | bytes 442376 | tf_op jit(solution)/shard_map/ppermute | solution.py:38
  31.2 1.0 dynamic_update_slice.117
  32.2 1.6 %collective-permute-done = bf16[4,24,768]{2,1,0:T(8,128)(2,1)S(1)} collective-permute-done((bf16[4,24,768]{2,1,0:T(8,128)(2,1)}, bf16[4,24,768]{2,1,0:T(8,128)(2,1)S(1)}, u32[]{:S(2)}, u32[]{:S(2)}) %collective-permute-start) | collective-permute-done | bytes 147488 | tf_op jit(solution)/shard_map/ppermute | solution.py:36
  33.8 2.1 %collective-permute-done.1 = bf16[4,24,768]{2,1,0:T(8,128)(2,1)S(1)} collective-permute-done((bf16[4,24,768]{2,1,0:T(8,128)(2,1)}, bf16[4,24,768]{2,1,0:T(8,128)(2,1)S(1)}, u32[]{:S(2)}, u32[]{:S(2)}) %collective-permute-start.1) | collective-permute-done | bytes 147488 | tf_op jit(solution)/shard_map/ppermute | solution.py:38
  36.0 1.6 %collective-permute-done.2 = bf16[4,24,768]{2,1,0:T(8,128)(2,1)S(1)} collective-permute-done((bf16[4,24,768]{2,1,0:T(8,128)(2,1)}, bf16[4,24,768]{2,1,0:T(8,128)(2,1)S(1)}, u32[]{:S(2)}, u32[]{:S(2)}) %collective-permute-start.2) | collective-permute-done | bytes 147488 | tf_op jit(solution)/shard_map/ppermute | solution.py:35
  37.6 1.4 %collective-permute-start.7 = (bf16[4,4,24,768]{3,2,1,0:T(8,128)(2,1)S(1)}, bf16[4,4,24,768]{3,2,1,0:T(8,128)(2,1)S(1)}, u32[]{:S(2)}, u32[]{:S(2)}) collective-permute-start(bf16[4,4,24,768]{3,2,1,0:T(8,128)(2,1)S(1)} %bitcast_dynamic-update-slice_fusion.1), channel_id=1, source_target_pairs={{0,4},{4,0},{8,12},{12,8},{16,20},{20,16},{24,28},{28,24},{32,36},... | collective-permute-start | bytes 1769480 | tf_op jit(solution)/shard_map/ppermute | solution.py:60
  39.0 2.6 %collective-permute-start.3 = (bf16[4,4,24,768]{3,2,1,0:T(8,128)(2,1)S(1)}, bf16[4,4,24,768]{3,2,1,0:T(8,128)(2,1)S(1)}, u32[]{:S(2)}, u32[]{:S(2)}) collective-permute-start(bf16[4,4,24,768]{3,2,1,0:T(8,128)(2,1)S(1)} %bitcast_dynamic-update-slice_fusion.1), channel_id=1, source_target_pairs={{0,96},{4,28},{8,104},{12,4},{16,112},{20,12},{24,120},{28,20},{32... | collective-permute-start | bytes 1769480 | tf_op jit(solution)/shard_map/ppermute | solution.py:36
  42.0 7.1 %collective-permute-done.4 = bf16[4,4,24,768]{3,2,1,0:T(8,128)(2,1)S(1)} collective-permute-done((bf16[4,4,24,768]{3,2,1,0:T(8,128)(2,1)S(1)}, bf16[4,4,24,768]{3,2,1,0:T(8,128)(2,1)S(1)}, u32[]{:S(2)}, u32[]{:S(2)}) %collective-permute-start.4) | collective-permute-done | bytes 589856 | tf_op jit(solution)/shard_map/ppermute | solution.py:35
  49.3 2.7 %collective-permute-start.6 = (bf16[2,4,24,768]{3,2,1,0:T(8,128)(2,1)S(1)}, bf16[2,4,24,768]{3,2,1,0:T(8,128)(2,1)S(1)}, u32[]{:S(2)}, u32[]{:S(2)}) collective-permute-start(bf16[2,4,24,768]{3,2,1,0:T(8,128)(2,1)S(1)} %slice.213), channel_id=1, source_target_pairs={{0,96},{4,28},{8,104},{12,4},{16,112},{20,12},{24,120},{28,20},{32... | collective-permute-start | bytes 884744 | tf_op jit(solution)/shard_map/ppermute | solution.py:41
  52.0 1.5 %collective-permute-start.10 = (bf16[4,4,24,768]{3,2,1,0:T(8,128)(2,1)S(1)}, bf16[4,4,24,768]{3,2,1,0:T(8,128)(2,1)S(1)}, u32[]{:S(2)}, u32[]{:S(2)}) collective-permute-start(bf16[4,4,24,768]{3,2,1,0:T(8,128)(2,1)S(1)} %collective-permute-done.4), channel_id=1, source_target_pairs={{0,4},{4,0},{8,12},{12,8},{16,20},{20,16},{24,28},{28,24},{32,36},... | collective-permute-start | bytes 1769480 | tf_op jit(solution)/shard_map/ppermute | solution.py:60
  53.6 2.7 %collective-permute-done.5 = bf16[2,4,24,768]{3,2,1,0:T(8,128)(2,1)S(1)} collective-permute-done((bf16[2,4,24,768]{3,2,1,0:T(8,128)(2,1)S(1)}, bf16[2,4,24,768]{3,2,1,0:T(8,128)(2,1)S(1)}, u32[]{:S(2)}, u32[]{:S(2)}) %collective-permute-start.5) | collective-permute-done | bytes 294944 | tf_op jit(solution)/shard_map/ppermute | solution.py:40
  56.4 2.1 %collective-permute-start.9 = (bf16[4,4,24,768]{3,2,1,0:T(8,128)(2,1)S(1)}, bf16[4,4,24,768]{3,2,1,0:T(8,128)(2,1)S(1)}, u32[]{:S(2)}, u32[]{:S(2)}) collective-permute-start(bf16[4,4,24,768]{3,2,1,0:T(8,128)(2,1)S(1)} %pad_maximum_fusion), channel_id=1, source_target_pairs={{0,4},{4,0},{8,12},{12,8},{16,20},{20,16},{24,28},{28,24},{32,36},... | collective-permute-start | bytes 1769480 | tf_op jit(solution)/shard_map/ppermute | solution.py:60
  58.9 1.2 %collective-permute-done.9 = bf16[4,4,24,768]{3,2,1,0:T(8,128)(2,1)S(1)} collective-permute-done((bf16[4,4,24,768]{3,2,1,0:T(8,128)(2,1)S(1)}, bf16[4,4,24,768]{3,2,1,0:T(8,128)(2,1)S(1)}, u32[]{:S(2)}, u32[]{:S(2)}) %collective-permute-start.9) | collective-permute-done | bytes 589856 | tf_op jit(solution)/shard_map/ppermute | solution.py:60
  60.6 2.0 %convert_bitcast_fusion.1 = bf16[2,768,768]{2,1,0:T(8,128)(2,1)S(1)} fusion(bf16[768,768,1]{1,0,2:T(8,128)(2,1)S(1)} %bitcast.385, bf16[2,768,768]{2,1,0:T(8,128)(2,1)S(1)} %copy-done), kind=kOutput, calls=%fused_computation.2 | convolution fusion | flops 1813118976 | bytes 5898240 | tf_op jit(solution)/shard_map/ac,pcd->pad/dot_general | solution.py:116
  62.6 2.0 %convert_bitcast_fusion = bf16[2,768,768]{2,1,0:T(8,128)(2,1)S(1)} fusion(bf16[768,768,1]{1,0,2:T(8,128)(2,1)S(1)} %bitcast.384, bf16[2,768,768]{2,1,0:T(8,128)(2,1)S(1)} %copy-done), kind=kOutput, calls=%fused_computation.1 | convolution fusion | flops 1813118976 | bytes 5898240 | tf_op jit(solution)/shard_map/ac,pcd->pad/dot_general | solution.py:116
  64.6 2.0 %convert_bitcast_fusion.2 = bf16[2,768,768]{2,1,0:T(8,128)(2,1)S(1)} fusion(bf16[768,768,1]{1,0,2:T(8,128)(2,1)S(1)} %bitcast.383, bf16[2,768,768]{2,1,0:T(8,128)(2,1)S(1)} %copy-done), kind=kOutput, calls=%fused_computation.3 | convolution fusion | flops 1813118976 | bytes 5898240 | tf_op jit(solution)/shard_map/ac,pcd->pad/dot_general | solution.py:116
  66.7 2.0 %convert_bitcast_fusion.3 = bf16[2,768,768]{2,1,0:T(8,128)(2,1)S(1)} fusion(bf16[768,768,1]{1,0,2:T(8,128)(2,1)S(1)} %bitcast.382, bf16[2,768,768]{2,1,0:T(8,128)(2,1)S(1)} %copy-done), kind=kOutput, calls=%fused_computation.4 | convolution fusion | flops 1813118976 | bytes 5898240 | tf_op jit(solution)/shard_map/ac,pcd->pad/dot_general | solution.py:116
  71.1 0.9 add_add_fusion.2
  72.1 1.4 %collective-permute-start.11 = (bf16[2,192,256]{2,1,0:T(8,128)(2,1)S(1)}, bf16[2,192,256]{2,1,0:T(8,128)(2,1)S(1)}, u32[]{:S(2)}, u32[]{:S(2)}) collective-permute-start(bf16[2,192,256]{2,1,0:T(8,128)(2,1)S(1)} %get-tuple-element.19), channel_id=1, source_target_pairs={{0,1},{1,2},{2,3},{3,0},{4,5},{5,6},{6,7},{7,4},{8,9},{9,10},{10,1... | collective-permute-start | bytes 589832 | tf_op jit(solution)/shard_map/ppermute | solution.py:76
  73.5 1.5 %collective-permute-start.12 = (bf16[2,192,256]{2,1,0:T(8,128)(2,1)S(1)}, bf16[2,192,256]{2,1,0:T(8,128)(2,1)S(1)}, u32[]{:S(2)}, u32[]{:S(2)}) collective-permute-start(bf16[2,192,256]{2,1,0:T(8,128)(2,1)S(1)} %get-tuple-element.20), channel_id=1, source_target_pairs={{0,3},{1,0},{2,1},{3,2},{4,7},{5,4},{6,5},{7,6},{8,11},{9,8},{10,9... | collective-permute-start | bytes 589832 | tf_op jit(solution)/shard_map/ppermute | solution.py:76
  75.0 1.6 %collective-permute-start.13 = (bf16[2,192,256]{2,1,0:T(8,128)(2,1)S(1)}, bf16[2,192,256]{2,1,0:T(8,128)(2,1)S(1)}, u32[]{:S(2)}, u32[]{:S(2)}) collective-permute-start(bf16[2,192,256]{2,1,0:T(8,128)(2,1)S(1)} %get-tuple-element.21), channel_id=1, source_target_pairs={{0,2},{1,3},{2,0},{3,1},{4,6},{5,7},{6,4},{7,5},{8,10},{9,11},{10,... | collective-permute-start | bytes 589832 | tf_op jit(solution)/shard_map/ppermute | solution.py:76
  79.0 0.9 add_add_fusion.1
  80.5 2.3 %collective-permute-start.15 = (bf16[2,192,256]{2,1,0:T(8,128)(2,1)S(1)}, bf16[2,192,256]{2,1,0:T(8,128)(2,1)S(1)}, u32[]{:S(2)}, u32[]{:S(2)}) collective-permute-start(bf16[2,192,256]{2,1,0:T(8,128)(2,1)S(1)} %get-tuple-element.27), channel_id=1, source_target_pairs={{0,3},{1,0},{2,1},{3,2},{4,7},{5,4},{6,5},{7,6},{8,11},{9,8},{10,9... | collective-permute-start | bytes 589832 | tf_op jit(solution)/shard_map/ppermute | solution.py:76
  85.2 0.9 add_add_fusion
  86.9 2.3 %collective-permute-start.18 = (bf16[2,192,256]{2,1,0:T(8,128)(2,1)S(1)}, bf16[2,192,256]{2,1,0:T(8,128)(2,1)S(1)}, u32[]{:S(2)}, u32[]{:S(2)}) collective-permute-start(bf16[2,192,256]{2,1,0:T(8,128)(2,1)S(1)} %get-tuple-element.38), channel_id=1, source_target_pairs={{0,3},{1,0},{2,1},{3,2},{4,7},{5,4},{6,5},{7,6},{8,11},{9,8},{10,9... | collective-permute-start | bytes 589832 | tf_op jit(solution)/shard_map/ppermute | solution.py:76
  89.6 1.4 %collective-permute-start.19 = (bf16[2,192,256]{2,1,0:T(8,128)(2,1)S(1)}, bf16[2,192,256]{2,1,0:T(8,128)(2,1)S(1)}, u32[]{:S(2)}, u32[]{:S(2)}) collective-permute-start(bf16[2,192,256]{2,1,0:T(8,128)(2,1)S(1)} %get-tuple-element.39), channel_id=1, source_target_pairs={{0,2},{1,3},{2,0},{3,1},{4,6},{5,7},{6,4},{7,5},{8,10},{9,11},{10,... | collective-permute-start | bytes 589832 | tf_op jit(solution)/shard_map/ppermute | solution.py:76
  91.0 1.4 %collective-permute-done.16 = bf16[2,192,256]{2,1,0:T(8,128)(2,1)S(1)} collective-permute-done((bf16[2,192,256]{2,1,0:T(8,128)(2,1)S(1)}, bf16[2,192,256]{2,1,0:T(8,128)(2,1)S(1)}, u32[]{:S(2)}, u32[]{:S(2)}) %collective-permute-start.16) | collective-permute-done | bytes 196640 | tf_op jit(solution)/shard_map/ppermute | solution.py:76
  92.5 7.9 %collective-permute-done.17 = bf16[2,192,256]{2,1,0:T(8,128)(2,1)S(1)} collective-permute-done((bf16[2,192,256]{2,1,0:T(8,128)(2,1)S(1)}, bf16[2,192,256]{2,1,0:T(8,128)(2,1)S(1)}, u32[]{:S(2)}, u32[]{:S(2)}) %collective-permute-start.17) | collective-permute-done | bytes 196640 | tf_op jit(solution)/shard_map/ppermute | solution.py:76
  100.7 0.8 fusion.10
  (81 shorter events, 12.4 us)
Async XLA Ops:
  0.0 60.6 %copy-start = (bf16[2,768,768]{2,1,0:T(8,128)(2,1)S(1)}, bf16[2,768,768]{2,1,0:T(8,128)(2,1)}, u32[]{:S(2)}) copy-start(bf16[2,768,768]{2,1,0:T(8,128)(2,1)} %param.3) | copy-start | bytes 7077892
  0.0 28.1 %all-to-all-start = ((bf16[32,24,768]{2,1,0:T(8,128)(2,1)}), bf16[32,24,768]{2,1,0:T(8,128)(2,1)S(1)}, u32[]{:S(2)}, u32[]{:S(2)}) async-start(bf16[32,24,768]{2,1,0:T(8,128)(2,1)} %bitcast.386), calls=%async_computation | async-start | bytes 2359296 | tf_op jit(solution)/shard_map/all_to_all | solution.py:53
  29.3 4.5 %collective-permute-start = (bf16[4,24,768]{2,1,0:T(8,128)(2,1)}, bf16[4,24,768]{2,1,0:T(8,128)(2,1)S(1)}, u32[]{:S(2)}, u32[]{:S(2)}) collective-permute-start(bf16[4,24,768]{2,1,0:T(8,128)(2,1)} %gather_fusion), channel_id=1, source_target_pairs={{0,24},{4,100},{8,0},{12,108},{16,8},{20,116},{24,16},{28,124},{32... | collective-permute-start | bytes 442376 | tf_op jit(solution)/shard_map/ppermute | solution.py:36
  29.9 6.1 %collective-permute-start.1 = (bf16[4,24,768]{2,1,0:T(8,128)(2,1)}, bf16[4,24,768]{2,1,0:T(8,128)(2,1)S(1)}, u32[]{:S(2)}, u32[]{:S(2)}) collective-permute-start(bf16[4,24,768]{2,1,0:T(8,128)(2,1)} %gather_fusion), channel_id=1, source_target_pairs={{0,16},{4,68},{8,24},{12,76},{16,0},{20,84},{24,8},{28,92},{32,48}... | collective-permute-start | bytes 442376 | tf_op jit(solution)/shard_map/ppermute | solution.py:38
  31.0 6.5 %collective-permute-start.2 = (bf16[4,24,768]{2,1,0:T(8,128)(2,1)}, bf16[4,24,768]{2,1,0:T(8,128)(2,1)S(1)}, u32[]{:S(2)}, u32[]{:S(2)}) collective-permute-start(bf16[4,24,768]{2,1,0:T(8,128)(2,1)} %gather_fusion), channel_id=1, source_target_pairs={{0,8},{4,36},{8,16},{12,44},{16,24},{20,52},{24,0},{28,60},{32,40}... | collective-permute-start | bytes 442376 | tf_op jit(solution)/shard_map/ppermute | solution.py:35
  37.6 21.1 %collective-permute-start.7 = (bf16[4,4,24,768]{3,2,1,0:T(8,128)(2,1)S(1)}, bf16[4,4,24,768]{3,2,1,0:T(8,128)(2,1)S(1)}, u32[]{:S(2)}, u32[]{:S(2)}) collective-permute-start(bf16[4,4,24,768]{3,2,1,0:T(8,128)(2,1)S(1)} %bitcast_dynamic-update-slice_fusion.1), channel_id=1, source_target_pairs={{0,4},{4,0},{8,12},{12,8},{16,20},{20,16},{24,28},{28,24},{32,36},... | collective-permute-start | bytes 1769480 | tf_op jit(solution)/shard_map/ppermute | solution.py:60
  38.9 10.2 %collective-permute-start.4 = (bf16[4,4,24,768]{3,2,1,0:T(8,128)(2,1)S(1)}, bf16[4,4,24,768]{3,2,1,0:T(8,128)(2,1)S(1)}, u32[]{:S(2)}, u32[]{:S(2)}) collective-permute-start(bf16[4,4,24,768]{3,2,1,0:T(8,128)(2,1)S(1)} %bitcast_dynamic-update-slice_fusion.1), channel_id=1, source_target_pairs={{0,32},{4,12},{8,40},{12,20},{16,48},{20,28},{24,56},{28,4},{32,64... | collective-permute-start | bytes 1769480 | tf_op jit(solution)/shard_map/ppermute | solution.py:35
  39.0 10.3 %collective-permute-start.3 = (bf16[4,4,24,768]{3,2,1,0:T(8,128)(2,1)S(1)}, bf16[4,4,24,768]{3,2,1,0:T(8,128)(2,1)S(1)}, u32[]{:S(2)}, u32[]{:S(2)}) collective-permute-start(bf16[4,4,24,768]{3,2,1,0:T(8,128)(2,1)S(1)} %bitcast_dynamic-update-slice_fusion.1), channel_id=1, source_target_pairs={{0,96},{4,28},{8,104},{12,4},{16,112},{20,12},{24,120},{28,20},{32... | collective-permute-start | bytes 1769480 | tf_op jit(solution)/shard_map/ppermute | solution.py:36
  49.2 7.1 %collective-permute-start.5 = (bf16[2,4,24,768]{3,2,1,0:T(8,128)(2,1)S(1)}, bf16[2,4,24,768]{3,2,1,0:T(8,128)(2,1)S(1)}, u32[]{:S(2)}, u32[]{:S(2)}) collective-permute-start(bf16[2,4,24,768]{3,2,1,0:T(8,128)(2,1)S(1)} %slice.210), channel_id=1, source_target_pairs={{0,32},{4,12},{8,40},{12,20},{16,48},{20,28},{24,56},{28,4},{32,64... | collective-permute-start | bytes 884744 | tf_op jit(solution)/shard_map/ppermute | solution.py:40
  49.3 7.0 %collective-permute-start.6 = (bf16[2,4,24,768]{3,2,1,0:T(8,128)(2,1)S(1)}, bf16[2,4,24,768]{3,2,1,0:T(8,128)(2,1)S(1)}, u32[]{:S(2)}, u32[]{:S(2)}) collective-permute-start(bf16[2,4,24,768]{3,2,1,0:T(8,128)(2,1)S(1)} %slice.213), channel_id=1, source_target_pairs={{0,96},{4,28},{8,104},{12,4},{16,112},{20,12},{24,120},{28,20},{32... | collective-permute-start | bytes 884744 | tf_op jit(solution)/shard_map/ppermute | solution.py:41
  52.0 8.1 %collective-permute-start.10 = (bf16[4,4,24,768]{3,2,1,0:T(8,128)(2,1)S(1)}, bf16[4,4,24,768]{3,2,1,0:T(8,128)(2,1)S(1)}, u32[]{:S(2)}, u32[]{:S(2)}) collective-permute-start(bf16[4,4,24,768]{3,2,1,0:T(8,128)(2,1)S(1)} %collective-permute-done.4), channel_id=1, source_target_pairs={{0,4},{4,0},{8,12},{12,8},{16,20},{20,16},{24,28},{28,24},{32,36},... | collective-permute-start | bytes 1769480 | tf_op jit(solution)/shard_map/ppermute | solution.py:60
  53.5 5.2 %collective-permute-start.8 = (bf16[4,4,24,768]{3,2,1,0:T(8,128)(2,1)S(1)}, bf16[4,4,24,768]{3,2,1,0:T(8,128)(2,1)S(1)}, u32[]{:S(2)}, u32[]{:S(2)}) collective-permute-start(bf16[4,4,24,768]{3,2,1,0:T(8,128)(2,1)S(1)} %collective-permute-done.3), channel_id=1, source_target_pairs={{0,4},{4,0},{8,12},{12,8},{16,20},{20,16},{24,28},{28,24},{32,36},... | collective-permute-start | bytes 1769480 | tf_op jit(solution)/shard_map/ppermute | solution.py:60
  56.4 3.7 %collective-permute-start.9 = (bf16[4,4,24,768]{3,2,1,0:T(8,128)(2,1)S(1)}, bf16[4,4,24,768]{3,2,1,0:T(8,128)(2,1)S(1)}, u32[]{:S(2)}, u32[]{:S(2)}) collective-permute-start(bf16[4,4,24,768]{3,2,1,0:T(8,128)(2,1)S(1)} %pad_maximum_fusion), channel_id=1, source_target_pairs={{0,4},{4,0},{8,12},{12,8},{16,20},{20,16},{24,28},{28,24},{32,36},... | collective-permute-start | bytes 1769480 | tf_op jit(solution)/shard_map/ppermute | solution.py:60
  72.1 14.1 %collective-permute-start.11 = (bf16[2,192,256]{2,1,0:T(8,128)(2,1)S(1)}, bf16[2,192,256]{2,1,0:T(8,128)(2,1)S(1)}, u32[]{:S(2)}, u32[]{:S(2)}) collective-permute-start(bf16[2,192,256]{2,1,0:T(8,128)(2,1)S(1)} %get-tuple-element.19), channel_id=1, source_target_pairs={{0,1},{1,2},{2,3},{3,0},{4,5},{5,6},{6,7},{7,4},{8,9},{9,10},{10,1... | collective-permute-start | bytes 589832 | tf_op jit(solution)/shard_map/ppermute | solution.py:76
  73.5 13.0 %collective-permute-start.12 = (bf16[2,192,256]{2,1,0:T(8,128)(2,1)S(1)}, bf16[2,192,256]{2,1,0:T(8,128)(2,1)S(1)}, u32[]{:S(2)}, u32[]{:S(2)}) collective-permute-start(bf16[2,192,256]{2,1,0:T(8,128)(2,1)S(1)} %get-tuple-element.20), channel_id=1, source_target_pairs={{0,3},{1,0},{2,1},{3,2},{4,7},{5,4},{6,5},{7,6},{8,11},{9,8},{10,9... | collective-permute-start | bytes 589832 | tf_op jit(solution)/shard_map/ppermute | solution.py:76
  75.0 11.9 %collective-permute-start.13 = (bf16[2,192,256]{2,1,0:T(8,128)(2,1)S(1)}, bf16[2,192,256]{2,1,0:T(8,128)(2,1)S(1)}, u32[]{:S(2)}, u32[]{:S(2)}) collective-permute-start(bf16[2,192,256]{2,1,0:T(8,128)(2,1)S(1)} %get-tuple-element.21), channel_id=1, source_target_pairs={{0,2},{1,3},{2,0},{3,1},{4,6},{5,7},{6,4},{7,5},{8,10},{9,11},{10,... | collective-permute-start | bytes 589832 | tf_op jit(solution)/shard_map/ppermute | solution.py:76
  80.0 9.6 %collective-permute-start.14 = (bf16[2,192,256]{2,1,0:T(8,128)(2,1)S(1)}, bf16[2,192,256]{2,1,0:T(8,128)(2,1)S(1)}, u32[]{:S(2)}, u32[]{:S(2)}) collective-permute-start(bf16[2,192,256]{2,1,0:T(8,128)(2,1)S(1)} %get-tuple-element.26), channel_id=1, source_target_pairs={{0,1},{1,2},{2,3},{3,0},{4,5},{5,6},{6,7},{7,4},{8,9},{9,10},{10,1... | collective-permute-start | bytes 589832 | tf_op jit(solution)/shard_map/ppermute | solution.py:76
  80.5 10.6 %collective-permute-start.15 = (bf16[2,192,256]{2,1,0:T(8,128)(2,1)S(1)}, bf16[2,192,256]{2,1,0:T(8,128)(2,1)S(1)}, u32[]{:S(2)}, u32[]{:S(2)}) collective-permute-start(bf16[2,192,256]{2,1,0:T(8,128)(2,1)S(1)} %get-tuple-element.27), channel_id=1, source_target_pairs={{0,3},{1,0},{2,1},{3,2},{4,7},{5,4},{6,5},{7,6},{8,11},{9,8},{10,9... | collective-permute-start | bytes 589832 | tf_op jit(solution)/shard_map/ppermute | solution.py:76
  86.2 6.2 %collective-permute-start.16 = (bf16[2,192,256]{2,1,0:T(8,128)(2,1)S(1)}, bf16[2,192,256]{2,1,0:T(8,128)(2,1)S(1)}, u32[]{:S(2)}, u32[]{:S(2)}) collective-permute-start(bf16[2,192,256]{2,1,0:T(8,128)(2,1)S(1)} %get-tuple-element.28), channel_id=1, source_target_pairs={{0,2},{1,3},{2,0},{3,1},{4,6},{5,7},{6,4},{7,5},{8,10},{9,11},{10,... | collective-permute-start | bytes 589832 | tf_op jit(solution)/shard_map/ppermute | solution.py:76
  86.5 13.9 %collective-permute-start.17 = (bf16[2,192,256]{2,1,0:T(8,128)(2,1)S(1)}, bf16[2,192,256]{2,1,0:T(8,128)(2,1)S(1)}, u32[]{:S(2)}, u32[]{:S(2)}) collective-permute-start(bf16[2,192,256]{2,1,0:T(8,128)(2,1)S(1)} %get-tuple-element.37), channel_id=1, source_target_pairs={{0,1},{1,2},{2,3},{3,0},{4,5},{5,6},{6,7},{7,4},{8,9},{9,10},{10,1... | collective-permute-start | bytes 589832 | tf_op jit(solution)/shard_map/ppermute | solution.py:76
  86.9 13.5 %collective-permute-start.18 = (bf16[2,192,256]{2,1,0:T(8,128)(2,1)S(1)}, bf16[2,192,256]{2,1,0:T(8,128)(2,1)S(1)}, u32[]{:S(2)}, u32[]{:S(2)}) collective-permute-start(bf16[2,192,256]{2,1,0:T(8,128)(2,1)S(1)} %get-tuple-element.38), channel_id=1, source_target_pairs={{0,3},{1,0},{2,1},{3,2},{4,7},{5,4},{6,5},{7,6},{8,11},{9,8},{10,9... | collective-permute-start | bytes 589832 | tf_op jit(solution)/shard_map/ppermute | solution.py:76
  89.6 11.1 %collective-permute-start.19 = (bf16[2,192,256]{2,1,0:T(8,128)(2,1)S(1)}, bf16[2,192,256]{2,1,0:T(8,128)(2,1)S(1)}, u32[]{:S(2)}, u32[]{:S(2)}) collective-permute-start(bf16[2,192,256]{2,1,0:T(8,128)(2,1)S(1)} %get-tuple-element.39), channel_id=1, source_target_pairs={{0,2},{1,3},{2,0},{3,1},{4,6},{5,7},{6,4},{7,5},{8,10},{9,11},{10,... | collective-permute-start | bytes 589832 | tf_op jit(solution)/shard_map/ppermute | solution.py:76
  92.5 8.2 %copy-start.1 = (f32[2,192,768]{2,1,0:T(8,128)}, f32[2,192,768]{2,1,0:T(8,128)S(1)}, u32[]{:S(2)}) copy-start(f32[2,192,768]{2,1,0:T(8,128)S(1)} %fusion.12) | copy-start | bytes 3538948
